TPU v7x, 256 devices: a whole 4x4x8 slice. The times are simulated.
256 devices in a mesh: tm: 64 (over z, x, core), wafer: 4 (over y).
Axes of the slice: x: 4, y: 4, z: 8, core: 2. Of those that a mesh axis runs over, the one named last changes fastest.
Arguments:
- timestream: bfloat16 [1024, 262144], P('wafer', 'tm'), may hold values from -6 to 6
- sample_weight: bfloat16 [1024, 262144], P('wafer', 'tm'), may hold values from 0 to 4
- response: float32 [3, 1024], replicated, may hold values from -1 to 1
- band_filter: bfloat16 [256, 256], replicated, may hold values from -0.375 to 0.375
- whiten: bfloat16 [7, 1024, 1024], P(None, ('tm', 'wafer')), as said below
- group_wafer: int32 [64], replicated, may hold values from 0 to 6
- pointing: bfloat16 [1024, 6, 256, 256], P(('tm', 'wafer')), may hold values from -0.15625 to 0.15625
- tile_list: int32 [1024, 6], P(('tm', 'wafer')), may hold values from 0 to 2047, as said below
- tile_home: int32 [2048], replicated, may hold values from 0 to 2047, as said below
- solution: float32 [2048, 3, 256], P('tm'), may hold values from -6 to 6
- direction: float32 [2048, 3, 256], P('tm'), may hold values from -6 to 6
- cg_scalars: float32 [2], replicated, may hold values from 0.5 to 1.5
Outputs:
- solution_next: float32 [2048, 3, 256], P('tm')
- residual_next: float32 [2048, 3, 256], P('tm')
- direction_next: float32 [2048, 3, 256], P('tm')
Inputs may be any that keep to these rules, and one draw needn't show every extreme that they name: `tile_list`: the tiles named in the spans of one device (one index of tm and one of wafer) are all different; among them at most 2 have their row tile_home on one index of tm, and in every draw, for each index of wafer, some index of tm owns exactly 2 tiles named by every device of that wafer index. A permutation: row tile_home[i] of a map holds sky tile i. `whiten`: each whitening matrix is symmetric.
All inputs are finite; a program needn't handle non-finite values.
Results may differ from a plain program's by a relative error of at most 0.0033.
The roundings to bfloat16 on the way count: a program that leaves them out, or rounds other values in their place, can miss the bound.
Values may be sent and summed in bfloat16 or wider, within the bound.
No kernel may reach another device: no remote copies, remote signals or barrier semaphores. Data moves between devices by JAX's collectives and lax.ppermute only.
A program may use at most 128 MiB of HBM per device.

v0:
```python
import jax
import jax.numpy as jnp
from jax import lax
from jax.sharding import PartitionSpec as P


def shards(
    timestream,
    sample_weight,
    response,
    band_filter,
    whiten,
    group_wafer,
    pointing,
    tile_list,
    tile_home,
    solution,
    direction,
    cg_scalars,
):
    precise_mode = lax.Precision.HIGHEST
    tm_count = lax.axis_size("tm")
    tm_index = lax.axis_index("tm")
    step_size = cg_scalars[0]
    blend_weight = cg_scalars[1]
    updated = solution + step_size * direction
    short_map = updated.astype(jnp.bfloat16)
    tiles_own, comp_count, pixel_count = solution.shape
    spans_here, per_span = tile_list.shape
    samples = band_filter.shape[0]
    det_total = whiten.shape[2]
    row_count = spans_here * per_span
    capacity = max(2, (row_count + tm_count - 1) // tm_count)
    tile_ids = tile_list.reshape(row_count)
    home_rows = jnp.take(tile_home, tile_ids, axis=0)
    owners = home_rows // tiles_own
    local_slot = home_rows % tiles_own
    positions = jnp.arange(row_count, dtype=jnp.int32)
    earlier = (owners[:, None] == owners[None, :]) & (positions[None, :] < positions[:, None])
    before_count = jnp.sum(earlier.astype(jnp.int32), axis=1)
    targets = owners * capacity + before_count
    placing = targets[:, None] == jnp.arange(tm_count * capacity, dtype=jnp.int32)[None, :]
    requests = jnp.sum(jnp.where(placing, local_slot[:, None], 0), axis=0)
    requests = requests.reshape(tm_count, capacity)
    asked_slots = lax.all_to_all(requests, "tm", split_axis=0, concat_axis=0, tiled=True)
    served = jnp.take(short_map, asked_slots, axis=0)
    replies, asked_slots = (
        lax.all_to_all(served, "tm", split_axis=0, concat_axis=0, tiled=True),
        asked_slots,
    )
    fetched = jnp.take(
        replies.reshape(tm_count * capacity, comp_count, pixel_count), targets, axis=0
    )
    fetched = fetched.reshape(spans_here, per_span, comp_count, pixel_count)
    signal_parts = jnp.einsum(
        "cktp,ckjp->cjt", pointing, fetched, preferred_element_type=jnp.float32
    )
    wafer_pick = group_wafer[tm_index]
    matrix = lax.dynamic_index_in_dim(
        lax.all_gather(whiten, ("tm", "wafer"), axis=1, tiled=True), wafer_pick, 0, keepdims=False
    )
    columns, column_weights = (
        lax.all_to_all(timestream, "wafer", split_axis=1, concat_axis=0, tiled=True),
        lax.all_to_all(sample_weight, "wafer", split_axis=1, concat_axis=0, tiled=True),
    )
    column_weights = column_weights.astype(jnp.float32).reshape(det_total, spans_here, samples)
    signal = jnp.einsum("jd,cjt->dct", response, signal_parts, precision=precise_mode)
    errors = (
        (columns.astype(jnp.float32).reshape(det_total, spans_here, samples) - signal)
        * column_weights
    ).astype(jnp.bfloat16)
    filtered = jnp.dot(
        errors.reshape(det_total * spans_here, samples),
        band_filter,
        preferred_element_type=jnp.float32,
    )
    filtered = filtered.astype(jnp.bfloat16).reshape(det_total, spans_here * samples)
    whitened = jnp.dot(matrix, filtered, preferred_element_type=jnp.float32).astype(jnp.bfloat16)
    smoothed = lax.dot_general(
        whitened.reshape(det_total * spans_here, samples),
        band_filter,
        (((1,), (1,)), ((), ())),
        preferred_element_type=jnp.float32,
    )
    smoothed = smoothed.astype(jnp.bfloat16).reshape(det_total, spans_here, samples)
    stokes = jnp.einsum(
        "jd,dct->cjt",
        response,
        smoothed.astype(jnp.float32) * column_weights,
        precision=precise_mode,
    )
    stokes_short = stokes.astype(jnp.bfloat16)
    partial_value = jnp.einsum(
        "cjt,cktp->ckjp", stokes_short, pointing, preferred_element_type=jnp.float32
    )
    partial_value = partial_value.reshape(row_count, comp_count * pixel_count)
    outgoing = jnp.dot(placing.astype(jnp.float32).T, partial_value, precision=precise_mode)
    outgoing = outgoing.reshape(tm_count, capacity, comp_count, pixel_count)
    arrived = lax.all_to_all(outgoing, "tm", split_axis=0, concat_axis=0, tiled=True)
    slot_hits = (
        asked_slots.reshape(-1)[None, :] == jnp.arange(tiles_own, dtype=jnp.int32)[:, None]
    ).astype(jnp.float32)
    owned_sum = jnp.dot(
        slot_hits,
        arrived.reshape(tm_count * capacity, comp_count * pixel_count),
        precision=precise_mode,
    )
    owned_sum = owned_sum.reshape(tiles_own, comp_count, pixel_count)
    summed = lax.psum(owned_sum, "wafer")
    residual_next = summed * float(det_total) ** (-0.5)
    direction_next = residual_next + blend_weight * direction
    return (updated, residual_next, direction_next)


def solution(mesh):
    in_specs = (
        P("wafer", "tm"),
        P("wafer", "tm"),
        P(),
        P(),
        P(None, ("tm", "wafer"), None),
        P(),
        P(("tm", "wafer"), None, None, None),
        P(("tm", "wafer"), None),
        P(),
        P("tm", None, None),
        P("tm", None, None),
        P(),
    )
    out_specs = (P("tm", None, None), P("tm", None, None), P("tm", None, None))
    return jax.shard_map(shards, mesh=mesh, in_specs=in_specs, out_specs=out_specs, check_vma=False)
```

profile of v0, /device:TPU:2, one launch (start us, length us, event | category | flops | bytes accessed | tf_op | source)
XLA Modules:
  0.0 281.9 jit_solution(5731134282750877064)
XLA Ops:
  7.2 1.6 copy.111
  8.9 0.8 reshape.319
  9.6 0.8 reshape.318
  10.4 1.4 gather_fusion
  11.8 0.2 convert_reduce_fusion
  12.0 0.1 select_reduce_fusion
  12.1 0.8 all_to_all.36
  12.9 12.0 %all-to-all-start = ((s32[64,1,2]{2,1,0:T(1,128)}), s32[64,1,2]{2,1,0:T(1,128)S(1)}, u32[]{:S(2)}, u32[]{:S(2)}) async-start(s32[64,1,2]{2,1,0:T(1,128)} %bitcast.2), calls=%async_computation | async-start | bytes 65536 | tf_op jit(solution)/shard_map/all_to_all | solution.py:45
  24.9 1.4 fusion.34
  26.3 2.4 fusion.33
  28.7 4.8 %all-to-all-done = s32[64,1,2]{2,1,0:T(1,128)S(1)} async-done(((s32[64,1,2]{2,1,0:T(1,128)}), s32[64,1,2]{2,1,0:T(1,128)S(1)}, u32[]{:S(2)}, u32[]{:S(2)}) %all-to-all-start) | async-done | bytes 544 | tf_op jit(solution)/shard_map/all_to_all | solution.py:45
  33.5 0.1 copy.116
  33.7 0.1 copy.118
  33.8 0.1 reshape.339
  33.9 0.1 copy-done.3
  34.1 0.8 gather_fusion.1
  34.9 0.9 broadcast_select_fusion
  35.9 5.5 %all-to-all-start.2 = ((bf16[64,2,3,256]{3,1,2,0:T(2,128)(2,1)}), bf16[64,2,3,256]{3,1,2,0:T(2,128)(2,1)S(1)}, u32[]{:S(2)}, u32[]{:S(2)}) async-start(bf16[64,2,3,256]{3,1,2,0:T(2,128)(2,1)} %broadcast_select_fusion), calls=%async_computation.2 | async-start | bytes 393216 | tf_op jit(solution)/shard_map/all_to_all | solution.py:48
  41.4 4.1 %copy.113 = bf16[256,4096]{0,1:T(8,128)(2,1)} copy(bf16[256,4096]{1,0:T(8,128)(2,1)} %param.12) | data formatting | bytes 4194304 | tf_op args[0]
  45.5 7.3 %all-to-all-done.2 = bf16[64,2,3,256]{3,1,2,0:T(2,128)(2,1)S(1)} async-done(((bf16[64,2,3,256]{3,1,2,0:T(2,128)(2,1)}), bf16[64,2,3,256]{3,1,2,0:T(2,128)(2,1)S(1)}, u32[]{:S(2)}, u32[]{:S(2)}) %all-to-all-start.2) | async-done | bytes 196640 | tf_op jit(solution)/shard_map/all_to_all | solution.py:48
  52.7 4.5 %all-to-all-start.1 = ((bf16[256,4,1024]{0,2,1:T(8,128)(2,1)}), bf16[256,4,1024]{0,2,1:T(8,128)(2,1)}, u32[]{:S(2)}, u32[]{:S(2)}) async-start(bf16[256,4,1024]{0,2,1:T(8,128)(2,1)} %bitcast.99), calls=%async_computation.1 | async-start | bytes 4194304 | tf_op jit(solution)/shard_map/all_to_all | solution.py:63
  57.2 4.1 %copy.123 = bf16[256,4096]{0,1:T(8,128)(2,1)} copy(bf16[256,4096]{1,0:T(8,128)(2,1)} %param.13) | data formatting | bytes 4194304 | tf_op args[1]
  61.3 25.7 %all-to-all-done.1 = bf16[256,4,1024]{0,2,1:T(8,128)(2,1)} async-done(((bf16[256,4,1024]{0,2,1:T(8,128)(2,1)}), bf16[256,4,1024]{0,2,1:T(8,128)(2,1)}, u32[]{:S(2)}, u32[]{:S(2)}) %all-to-all-start.1) | async-done | bytes 2097184 | tf_op jit(solution)/shard_map/all_to_all | solution.py:63
  87.1 4.6 %all-to-all-start.3 = ((bf16[256,4,1024]{0,2,1:T(8,128)(2,1)}), bf16[256,4,1024]{0,2,1:T(8,128)(2,1)}, u32[]{:S(2)}, u32[]{:S(2)}) async-start(bf16[256,4,1024]{0,2,1:T(8,128)(2,1)} %bitcast.98), calls=%async_computation.3 | async-start | bytes 4194304 | tf_op jit(solution)/shard_map/all_to_all | solution.py:64
  91.7 0.1 reduce_sum.24
  91.8 0.1 gather.19
  91.9 0.6 dynamic_slice.7
  94.5 0.8 copy.120
  95.3 1.6 gather_fusion.2
  96.9 0.9 convolution_bitcast_fusion
  97.9 2.0 convert_bitcast_fusion.1
  99.8 4.8 %copy.114 = f32[4,256,1024]{1,0,2:T(4,128)} copy(f32[4,256,1024]{1,2,0:T(8,128)S(1)} %convert_bitcast_fusion.1) | data formatting | bytes 8388608 | tf_op jit(solution)/shard_map/convert_element_type | solution.py:69
  104.7 5.8 %reshape.326 = f32[1024,4,256]{0,2,1:T(8,128)} reshape(f32[4,256,1024]{1,0,2:T(4,128)} %copy.114) | data formatting | bytes 8388608 | tf_op jit(solution)/shard_map/convert_element_type | solution.py:69
  110.5 20.1 %all-to-all-done.3 = bf16[256,4,1024]{0,2,1:T(8,128)(2,1)} async-done(((bf16[256,4,1024]{0,2,1:T(8,128)(2,1)}), bf16[256,4,1024]{0,2,1:T(8,128)(2,1)}, u32[]{:S(2)}, u32[]{:S(2)}) %all-to-all-start.3) | async-done | bytes 2097184 | tf_op jit(solution)/shard_map/all_to_all | solution.py:64
  130.6 2.2 convert_bitcast_fusion
  132.8 4.7 %copy.124 = f32[4,256,1024]{1,0,2:T(4,128)} copy(f32[4,256,1024]{1,2,0:T(8,128)S(1)} %convert_bitcast_fusion) | data formatting | bytes 8388608 | tf_op jit(solution)/shard_map/convert_element_type | solution.py:66
  137.4 5.9 %reshape.327 = f32[1024,4,256]{0,2,1:T(8,128)} reshape(f32[4,256,1024]{1,0,2:T(4,128)} %copy.124) | data formatting | bytes 8388608 | tf_op jit(solution)/shard_map/convert_element_type | solution.py:66
  143.3 7.2 %fusion.2 = bf16[1024,4,256]{0,2,1:T(8,128)(2,1)} fusion(f32[1024,4,256]{0,2,1:T(8,128)} %reshape.327, f32[1024,4,256]{0,2,1:T(8,128)} %reshape.326, f32[4,3,256]{2,1,0:T(4,128)S(1)} %convolution_bitcast_fusion, f32[3,1024]{1,0:T(4,128)S(1)} %copy-done.4), kind=kOutput, calls=%fused_computation.8 | convolution fusion | flops 40894464 | bytes 10510336 | tf_op jit(solution)/shard_map/jd,cjt->dct/dot_general | solution.py:67
  150.5 4.3 %copy.125 = bf16[1024,4,256]{2,1,0:T(4,128)(2,1)} copy(bf16[1024,4,256]{0,2,1:T(8,128)(2,1)} %fusion.2) | data formatting | bytes 4194304 | tf_op jit(solution)/shard_map/convert_element_type | solution.py:71
  154.8 4.1 %reshape.321 = bf16[4096,256]{1,0:T(8,128)(2,1)} reshape(bf16[1024,4,256]{2,1,0:T(4,128)(2,1)} %copy.125) | data formatting | bytes 4194304 | tf_op jit(solution)/shard_map/reshape | solution.py:73
  158.9 3.6 %convolution_convert_fusion.1 = bf16[4096,256]{1,0:T(8,128)(2,1)} fusion(bf16[4096,256]{1,0:T(8,128)(2,1)} %reshape.321, bf16[256,256]{1,0:T(8,128)(2,1)S(1)} %copy-done.2), kind=kOutput, calls=%fused_computation.5 | convolution fusion | flops 537919488 | bytes 4325376 | tf_op jit(solution)/shard_map/dot_general | solution.py:72
  162.5 4.4 %reshape.322 = bf16[1024,1024]{1,0:T(8,128)(2,1)} reshape(bf16[4096,256]{1,0:T(8,128)(2,1)} %convolution_convert_fusion.1) | data formatting | bytes 4194304 | tf_op jit(solution)/shard_map/reshape | solution.py:77
  166.9 7.8 %constant_dynamic-slice_fusion = bf16[1,1024,1024]{2,0,1:T(2,128)(2,1)S(1)} fusion(bf16[7,1024,1024]{2,0,1:T(8,128)(2,1)} %all-gather.2.cloned.1.call-done, s32[]{:T(128)S(6)} %select_n.167), kind=kLoop, calls=%fused_computation.81 | loop fusion | bytes 4194308 | tf_op jit(solution)/shard_map/jit(dynamic_index_in_dim)/dynamic_slice | solution.py:59
  174.7 3.7 %fusion.6 = bf16[1024,1024]{1,0:T(8,128)(2,1)} fusion(bf16[1024,1024]{1,0:T(8,128)(2,1)S(1)} %copy-done.1, bf16[1,1024,1024]{2,0,1:T(2,128)(2,1)S(1)} %constant_dynamic-slice_fusion), kind=kOutput, calls=%fused_computation.15 | convolution fusion | flops 2148532224 | bytes 6291456 | tf_op jit(solution)/shard_map/dot_general | solution.py:78
  178.4 4.4 %reshape.323 = bf16[4096,256]{1,0:T(8,128)(2,1)} reshape(bf16[1024,1024]{1,0:T(8,128)(2,1)} %fusion.6) | data formatting | bytes 4194304 | tf_op jit(solution)/shard_map/reshape | solution.py:80
  182.8 4.3 %fusion = f32[4096,256]{1,0:T(8,128)} fusion(bf16[4096,256]{1,0:T(8,128)(2,1)} %reshape.323, bf16[256,256]{1,0:T(8,128)(2,1)S(1)} %copy-done.2), kind=kOutput, calls=%fused_computation.4 | convolution fusion | flops 538968064 | bytes 6422528 | tf_op jit(solution)/shard_map/dot_general | solution.py:79
  187.0 5.2 %reshape.328 = f32[1024,4,256]{2,1,0:T(4,128)} reshape(f32[4096,256]{1,0:T(8,128)} %fusion) | data formatting | bytes 8388608 | tf_op jit(solution)/shard_map/convert_element_type | solution.py:89
  192.3 5.2 %copy.126 = f32[1024,4,256]{0,2,1:T(8,128)} copy(f32[1024,4,256]{2,1,0:T(4,128)} %reshape.328) | data formatting | bytes 8388608 | tf_op jit(solution)/shard_map/convert_element_type | solution.py:89
  197.5 7.2 %fusion.10 = bf16[4,256,3,1]{1,2,3,0:T(4,128)(2,1)S(1)} fusion(f32[1024,4,256]{0,2,1:T(8,128)} %copy.126, f32[1024,4,256]{0,2,1:T(8,128)} %reshape.327, f32[3,1024]{1,0:T(4,128)S(1)} %copy-done.4), kind=kOutput, calls=%fused_computation.18 | convolution fusion | flops 38800384 | bytes 8407040 | tf_op jit(solution)/shard_map/jd,dct->cjt/dot_general | solution.py:86
  204.7 0.5 fusion.35
  205.2 0.4 fusion.13
  205.7 1.1 copy.129
  206.7 6.5 %all-to-all-start.4 = ((f32[64,2,3,256]{3,1,2,0:T(2,128)}), f32[64,2,3,256]{3,1,2,0:T(2,128)S(1)}, u32[]{:S(2)}, u32[]{:S(2)}) async-start(f32[64,2,3,256]{3,1,2,0:T(2,128)} %copy.129), calls=%async_computation.4 | async-start | bytes 786432 | tf_op jit(solution)/shard_map/all_to_all | solution.py:99
  213.2 0.5 broadcast.425
  213.7 2.1 reduce.3
  215.8 0.9 eq.71
  216.7 11.3 %all-to-all-done.4 = f32[64,2,3,256]{3,1,2,0:T(2,128)S(1)} async-done(((f32[64,2,3,256]{3,1,2,0:T(2,128)}), f32[64,2,3,256]{3,1,2,0:T(2,128)S(1)}, u32[]{:S(2)}, u32[]{:S(2)}) %all-to-all-start.4) | async-done | bytes 393248 | tf_op jit(solution)/shard_map/all_to_all | solution.py:99
  228.0 0.1 copy.130
  228.2 0.8 copy.141
  229.0 1.1 copy.131
  230.1 1.0 fusion.21
  231.1 1.6 copy.132
  232.7 40.0 %all-reduce.2.cloned.1.call-done = f32[32,3,256]{2,0,1:T(8,128)} async-done(((f32[32,3,256]{2,0,1:T(8,128)}), f32[32,3,256]{2,0,1:T(8,128)}) %all-reduce.2.cloned.1.call-update) | async-done | bytes 98320 | tf_op jit(solution)/shard_map/psum | solution.py:109
  272.7 2.3 multiply_add_fusion
  (31 shorter events, 0.4 us)
Async XLA Ops:
  7.2 89.8 %copy-start = (bf16[4,6,256,256]{3,2,1,0:T(8,128)(2,1)S(1)}, bf16[4,6,256,256]{3,2,1,0:T(8,128)(2,1)}, u32[]{:S(2)}) copy-start(bf16[4,6,256,256]{3,2,1,0:T(8,128)(2,1)} %param.18) | copy-start | bytes 9437188
  7.2 159.7 %all-gather.2.cloned.1.call-start = ((), (), s32[]{:S(2)}) async-start(), calls=%async_computation.5 | async-start | bytes 16842752 | tf_op jit(solution)/shard_map/all_gather | solution.py:60
  12.9 20.6 %all-to-all-start = ((s32[64,1,2]{2,1,0:T(1,128)}), s32[64,1,2]{2,1,0:T(1,128)S(1)}, u32[]{:S(2)}, u32[]{:S(2)}) async-start(s32[64,1,2]{2,1,0:T(1,128)} %bitcast.2), calls=%async_computation | async-start | bytes 65536 | tf_op jit(solution)/shard_map/all_to_all | solution.py:45
  33.5 0.6 copy-start.3
  35.9 16.9 %all-to-all-start.2 = ((bf16[64,2,3,256]{3,1,2,0:T(2,128)(2,1)}), bf16[64,2,3,256]{3,1,2,0:T(2,128)(2,1)S(1)}, u32[]{:S(2)}, u32[]{:S(2)}) async-start(bf16[64,2,3,256]{3,1,2,0:T(2,128)(2,1)} %broadcast_select_fusion), calls=%async_computation.2 | async-start | bytes 393216 | tf_op jit(solution)/shard_map/all_to_all | solution.py:48
  52.7 34.3 %all-to-all-start.1 = ((bf16[256,4,1024]{0,2,1:T(8,128)(2,1)}), bf16[256,4,1024]{0,2,1:T(8,128)(2,1)}, u32[]{:S(2)}, u32[]{:S(2)}) async-start(bf16[256,4,1024]{0,2,1:T(8,128)(2,1)} %bitcast.99), calls=%async_computation.1 | async-start | bytes 4194304 | tf_op jit(solution)/shard_map/all_to_all | solution.py:63
  61.3 30.6 %copy-start.6 = (s32[64]{0:T(128)S(1)}, s32[64]{0:T(128)}, u32[]{:S(2)}) copy-start(s32[64]{0:T(128)} %param.17) | copy-start | bytes 772
  61.3 33.1 %copy-start.5 = (s32[4,6]{1,0:T(4,128)S(1)}, s32[4,6]{1,0:T(4,128)}, u32[]{:S(2)}) copy-start(s32[4,6]{1,0:T(4,128)} %param.19) | copy-start | bytes 292
  87.1 43.5 %all-to-all-start.3 = ((bf16[256,4,1024]{0,2,1:T(8,128)(2,1)}), bf16[256,4,1024]{0,2,1:T(8,128)(2,1)}, u32[]{:S(2)}, u32[]{:S(2)}) async-start(bf16[256,4,1024]{0,2,1:T(8,128)(2,1)} %bitcast.98), calls=%async_computation.3 | async-start | bytes 4194304 | tf_op jit(solution)/shard_map/all_to_all | solution.py:64
  137.4 5.9 %copy-start.4 = (f32[3,1024]{1,0:T(4,128)S(1)}, f32[3,1024]{1,0:T(4,128)}, u32[]{:S(2)}) copy-start(f32[3,1024]{1,0:T(4,128)} %param.14) | copy-start | bytes 36868
  154.8 4.1 %copy-start.2 = (bf16[256,256]{1,0:T(8,128)(2,1)S(1)}, bf16[256,256]{1,0:T(8,128)(2,1)}, u32[]{:S(2)}) copy-start(bf16[256,256]{1,0:T(8,128)(2,1)} %param.15) | copy-start | bytes 393220
  166.9 7.8 %copy-start.1 = (bf16[1024,1024]{1,0:T(8,128)(2,1)S(1)}, bf16[1024,1024]{1,0:T(8,128)(2,1)}, u32[]{:S(2)}) copy-start(bf16[1024,1024]{1,0:T(8,128)(2,1)} %reshape.322) | copy-start | bytes 6291460
  206.7 21.3 %all-to-all-start.4 = ((f32[64,2,3,256]{3,1,2,0:T(2,128)}), f32[64,2,3,256]{3,1,2,0:T(2,128)S(1)}, u32[]{:S(2)}, u32[]{:S(2)}) async-start(f32[64,2,3,256]{3,1,2,0:T(2,128)} %copy.129), calls=%async_computation.4 | async-start | bytes 786432 | tf_op jit(solution)/shard_map/all_to_all | solution.py:99
  213.2 59.5 %all-reduce.2.cloned.1.call-start = ((), (), s32[]{:S(2)}) async-start(), calls=%async_computation.6 | async-start | bytes 196608 | tf_op jit(solution)/shard_map/psum | solution.py:109
Sparse Core Ops, SparseCore 0:
  12.2 136.2 all-gather.1
  231.3 41.4 all-reduce.1
where the time goes:
time: 284 us; the launch traced here: 282 us
  waiting for transfers between devices  109 us (38%)
  local copies, waits for them, and re-layouts  82.1 us (29%)
  starting transfers between devices  33.2 us (12%)
  matrix products  28.8 us (10%)
  between operations  16.2 us (6%)
  other arithmetic  12.3 us (4%)
    psum x1, waiting for transfers between devices, shards(): summed = lax.psum(owned_sum, 'wafer')  40 us
    all_to_all x1, waiting for transfers between devices, shards(): lax.all_to_all(timestream, 'wafer', split_axis=1, concat_axis=0, tiled=True)  25.7 us
    all_to_all x1, waiting for transfers between devices, shards(): lax.all_to_all(sample_weight, 'wafer', split_axis=1, concat_axis=0, tiled...  20.1 us
    unnamed x19, local copies, waits for them, and re-layouts  12.4 us
    all_to_all x1, starting transfers between devices, shards(): lax.all_to_all(requests, 'tm', split_axis=0, concat_axis=0, tiled=True)  12 us
    all_to_all x1, waiting for transfers between devices, shards(): lax.all_to_all(outgoing, 'tm', split_axis=0, concat_axis=0, tiled=True)  11.3 us
    convert_element_type x2, local copies, waits for them, and re-layouts, shards(): columns.astype(jnp.float32).reshape(det_total, spans_here, samples) - signal  10.7 us
    convert_element_type x2, local copies, waits for them, and re-layouts, shards(): column_weights.astype(jnp.float32).reshape(det_total, spans_here, samples)  10.6 us
  transfers between devices with their start and end apart: 7, of which 6 were waited for; matrix products, arithmetic and copies ran while one was open for 27% of the time, Pallas kernels for 0%

commit v1 on v0

--- a/solution.py
+++ b/solution.py
@@ -55,10 +55,10 @@
     signal_parts = jnp.einsum(
         "cktp,ckjp->cjt", pointing, fetched, preferred_element_type=jnp.float32
     )
-    wafer_pick = group_wafer[tm_index]
-    matrix = lax.dynamic_index_in_dim(
-        lax.all_gather(whiten, ("tm", "wafer"), axis=1, tiled=True), wafer_pick, 0, keepdims=False
-    )
+    block_rows = lax.all_gather(whiten, "wafer", axis=1, tiled=True)
+    sent_blocks = jnp.take(block_rows, group_wafer, axis=0)
+    matrix = lax.all_to_all(sent_blocks, "tm", split_axis=0, concat_axis=0, tiled=True)
+    matrix = matrix.reshape(det_total, det_total)
     columns, column_weights = (
         lax.all_to_all(timestream, "wafer", split_axis=1, concat_axis=0, tiled=True),
         lax.all_to_all(sample_weight, "wafer", split_axis=1, concat_axis=0, tiled=True),

time: 284 us -> 299 us (1.053)
  blocking collectives: 0 us -> 32.8 us
  waiting for transfers between devices: 109 us -> 86 us
  starting transfers between devices: 33.2 us -> 43.8 us
  local copies, waits for them, and re-layouts: 82.1 us -> 74.8 us
    all_gather x0 -> x1, blocking collectives: none -> 32.8 us  [shards(): block_rows = lax.all_gather(whiten, 'wafer', axis=1, tiled=True)]
    all_to_all x1, waiting for transfers between devices: 25.7 us -> 0.01 us  [shards(): lax.all_to_all(timestream, 'wafer', split_axis=1, concat_axis=0, tiled=True)]
    dynamic_slice x2 -> x0, local copies, waits for them, and re-layouts: 8.34 us -> none  [the longest x1 7.75 us: shards(): lax.dynamic_index_in_dim(lax.all_gather(whiten, ('tm', 'wafer'), axis=1,...]
    all_to_all x0 -> x1, starting transfers between devices: none -> 6.71 us  [shards(): lax.all_to_all(sent_blocks, 'tm', split_axis=0, concat_axis=0, tiled=True)]
    all_to_all x1, starting transfers between devices: 6.46 us -> 10.4 us  [shards(): lax.all_to_all(outgoing, 'tm', split_axis=0, concat_axis=0, tiled=True)]
    select_n x0 -> x2, other arithmetic: none -> 3.15 us  [shards(): sent_blocks = jnp.take(block_rows, group_wafer, axis=0)]
    unnamed x19 -> x23, local copies, waits for them, and re-layouts: 12.4 us -> 11.4 us
  transfers between devices with their start and end apart: 7 -> 7, of which waited for: 6 -> 5; matrix products, arithmetic and copies ran while one was open for 27% -> 25% of each run, Pallas kernels for 0% -> 0%
where the time goes in v1:
time: 299 us; the launch traced here: 298 us
  waiting for transfers between devices  86 us (29%)
  local copies, waits for them, and re-layouts  74.8 us (25%)
  starting transfers between devices  43.8 us (15%)
  blocking collectives  32.8 us (11%)
  matrix products  30.9 us (10%)
  other arithmetic  15.2 us (5%)
  between operations  14.3 us (5%)
    psum x1, waiting for transfers between devices, shards(): summed = lax.psum(owned_sum, 'wafer')  40.1 us
    all_gather x1, blocking collectives, shards(): block_rows = lax.all_gather(whiten, 'wafer', axis=1, tiled=True)  32.8 us
    all_to_all x1, waiting for transfers between devices, shards(): lax.all_to_all(sample_weight, 'wafer', split_axis=1, concat_axis=0, tiled...  22.9 us
    all_to_all x1, starting transfers between devices, shards(): lax.all_to_all(requests, 'tm', split_axis=0, concat_axis=0, tiled=True)  12 us
    unnamed x23, local copies, waits for them, and re-layouts  11.4 us
    all_to_all x1, waiting for transfers between devices, shards(): lax.all_to_all(outgoing, 'tm', split_axis=0, concat_axis=0, tiled=True)  11.2 us
    convert_element_type x2, local copies, waits for them, and re-layouts, shards(): columns.astype(jnp.float32).reshape(det_total, spans_here, samples) - signal  10.5 us
    convert_element_type x2, local copies, waits for them, and re-layouts, shards(): column_weights.astype(jnp.float32).reshape(det_total, spans_here, samples)  10.5 us
  transfers between devices with their start and end apart: 7, of which 5 were waited for; matrix products, arithmetic and copies ran while one was open for 25% of the time, Pallas kernels for 0%

profile of v1, /device:TPU:2, one launch (start us, length us, event | category | flops | bytes accessed | tf_op | source)
XLA Modules:
  0.0 297.6 jit_solution(12162273992266911379)
XLA Ops:
  7.2 0.9 reshape.327
  8.1 0.8 reshape.326
  8.9 1.4 gather_fusion
  10.3 0.2 convert_reduce_fusion
  10.5 0.1 select_reduce_fusion
  10.6 0.8 all_to_all.39
  11.4 12.0 %all-to-all-start = ((s32[64,1,2]{2,1,0:T(1,128)}), s32[64,1,2]{2,1,0:T(1,128)S(1)}, u32[]{:S(2)}, u32[]{:S(2)}) async-start(s32[64,1,2]{2,1,0:T(1,128)} %bitcast.2), calls=%async_computation | async-start | bytes 65536 | tf_op jit(solution)/shard_map/all_to_all | solution.py:45
  23.4 1.3 fusion.32
  24.7 2.4 fusion.31
  27.1 4.9 %all-to-all-done = s32[64,1,2]{2,1,0:T(1,128)S(1)} async-done(((s32[64,1,2]{2,1,0:T(1,128)}), s32[64,1,2]{2,1,0:T(1,128)S(1)}, u32[]{:S(2)}, u32[]{:S(2)}) %all-to-all-start) | async-done | bytes 544 | tf_op jit(solution)/shard_map/all_to_all | solution.py:45
  32.0 0.1 copy.118
  32.1 0.1 reshape.356
  32.3 0.1 copy.116
  32.4 0.2 copy-done.4
  32.6 0.8 gather_fusion.2
  33.4 0.9 broadcast_select_fusion.1
  34.3 5.5 %all-to-all-start.3 = ((bf16[64,2,3,256]{3,1,2,0:T(2,128)(2,1)}), bf16[64,2,3,256]{3,1,2,0:T(2,128)(2,1)S(1)}, u32[]{:S(2)}, u32[]{:S(2)}) async-start(bf16[64,2,3,256]{3,1,2,0:T(2,128)(2,1)} %broadcast_select_fusion.1), calls=%async_computation.3 | async-start | bytes 393216 | tf_op jit(solution)/shard_map/all_to_all | solution.py:48
  39.9 4.1 %copy.123 = bf16[256,4096]{0,1:T(8,128)(2,1)} copy(bf16[256,4096]{1,0:T(8,128)(2,1)} %param.13) | data formatting | bytes 4194304 | tf_op args[1]
  43.9 6.9 %all-to-all-done.3 = bf16[64,2,3,256]{3,1,2,0:T(2,128)(2,1)S(1)} async-done(((bf16[64,2,3,256]{3,1,2,0:T(2,128)(2,1)}), bf16[64,2,3,256]{3,1,2,0:T(2,128)(2,1)S(1)}, u32[]{:S(2)}, u32[]{:S(2)}) %all-to-all-start.3) | async-done | bytes 196640 | tf_op jit(solution)/shard_map/all_to_all | solution.py:48
  50.9 0.7 copy-done.1
  51.5 4.5 %all-to-all-start.4 = ((bf16[256,4,1024]{0,2,1:T(8,128)(2,1)}), bf16[256,4,1024]{0,2,1:T(8,128)(2,1)}, u32[]{:S(2)}, u32[]{:S(2)}) async-start(bf16[256,4,1024]{0,2,1:T(8,128)(2,1)} %bitcast.95), calls=%async_computation.4 | async-start | bytes 4194304 | tf_op jit(solution)/shard_map/all_to_all | solution.py:64
  56.0 4.1 %copy.113 = bf16[256,4096]{0,1:T(8,128)(2,1)} copy(bf16[256,4096]{1,0:T(8,128)(2,1)} %param.12) | data formatting | bytes 4194304 | tf_op args[0]
  60.1 22.9 %all-to-all-done.4 = bf16[256,4,1024]{0,2,1:T(8,128)(2,1)} async-done(((bf16[256,4,1024]{0,2,1:T(8,128)(2,1)}), bf16[256,4,1024]{0,2,1:T(8,128)(2,1)}, u32[]{:S(2)}, u32[]{:S(2)}) %all-to-all-start.4) | async-done | bytes 2097184 | tf_op jit(solution)/shard_map/all_to_all | solution.py:64
  82.9 4.6 %all-to-all-start.2 = ((bf16[256,4,1024]{0,2,1:T(8,128)(2,1)}), bf16[256,4,1024]{0,2,1:T(8,128)(2,1)}, u32[]{:S(2)}, u32[]{:S(2)}) async-start(bf16[256,4,1024]{0,2,1:T(8,128)(2,1)} %bitcast.94), calls=%async_computation.2 | async-start | bytes 4194304 | tf_op jit(solution)/shard_map/all_to_all | solution.py:63
  87.6 32.8 %all_gather.3 = bf16[7,16,1024]{2,0,1:T(8,128)(2,1)S(1)} all-gather(bf16[7,4,1024]{2,0,1:T(8,128)(2,1)S(1)} %copy.111), channel_id=1, replica_groups=mesh['tm'=64,'wafer'=4] {'wafer'}, dimensions={1}, use_global_device_ids=true | all-gather | bytes 286720 | tf_op jit(solution)/shard_map/all_gather | solution.py:58
  120.4 0.1 copy.112
  120.6 2.0 gather_fusion.1
  122.6 3.1 %broadcast_select_fusion = bf16[64,16,1024]{2,1,0:T(8,128)(2,1)} fusion(bf16[64,16,1024]{2,1,0:T(8,128)(2,1)} %gather_fusion.1, pred[64]{0:T(512)(128)(4,1)S(1)} %compare_and_fusion.2), kind=kLoop, calls=%fused_computation.14 | loop fusion | flops 1048576 | bytes 4194368 | tf_op jit(solution)/shard_map/jit(_take)/select_n | solution.py:59
  125.8 6.7 %all-to-all-start.1 = ((bf16[64,16,1024]{2,1,0:T(8,128)(2,1)}), bf16[64,16,1024]{2,1,0:T(8,128)(2,1)}, u32[]{:S(2)}, u32[]{:S(2)}) async-start(bf16[64,16,1024]{2,1,0:T(8,128)(2,1)} %broadcast_select_fusion), calls=%async_computation.1 | async-start | bytes 4194304 | tf_op jit(solution)/shard_map/all_to_all | solution.py:60
  132.7 0.8 copy.120
  133.5 1.6 gather_fusion.3
  135.2 0.9 convolution_bitcast_fusion
  136.1 2.0 convert_bitcast_fusion
  138.0 4.7 %copy.124 = f32[4,256,1024]{1,0,2:T(4,128)} copy(f32[4,256,1024]{1,2,0:T(8,128)S(1)} %convert_bitcast_fusion) | data formatting | bytes 8388608 | tf_op jit(solution)/shard_map/convert_element_type | solution.py:66
  142.7 5.8 %reshape.336 = f32[1024,4,256]{0,2,1:T(8,128)} reshape(f32[4,256,1024]{1,0,2:T(4,128)} %copy.124) | data formatting | bytes 8388608 | tf_op jit(solution)/shard_map/convert_element_type | solution.py:66
  148.5 2.0 convert_bitcast_fusion.1
  150.5 4.7 %copy.114 = f32[4,256,1024]{1,0,2:T(4,128)} copy(f32[4,256,1024]{1,2,0:T(8,128)S(1)} %convert_bitcast_fusion.1) | data formatting | bytes 8388608 | tf_op jit(solution)/shard_map/convert_element_type | solution.py:69
  155.2 5.8 %reshape.335 = f32[1024,4,256]{0,2,1:T(8,128)} reshape(f32[4,256,1024]{1,0,2:T(4,128)} %copy.114) | data formatting | bytes 8388608 | tf_op jit(solution)/shard_map/convert_element_type | solution.py:69
  161.0 7.1 %fusion.2 = bf16[1024,4,256]{0,2,1:T(8,128)(2,1)} fusion(f32[1024,4,256]{0,2,1:T(8,128)} %reshape.336, f32[1024,4,256]{0,2,1:T(8,128)} %reshape.335, f32[4,3,256]{2,1,0:T(4,128)S(1)} %convolution_bitcast_fusion, f32[3,1024]{1,0:T(4,128)S(1)} %copy-done.5), kind=kOutput, calls=%fused_computation.9 | convolution fusion | flops 40894464 | bytes 10510336 | tf_op jit(solution)/shard_map/jd,cjt->dct/dot_general | solution.py:67
  168.1 4.2 %copy.125 = bf16[1024,4,256]{2,1,0:T(4,128)(2,1)} copy(bf16[1024,4,256]{0,2,1:T(8,128)(2,1)} %fusion.2) | data formatting | bytes 4194304 | tf_op jit(solution)/shard_map/convert_element_type | solution.py:71
  172.3 4.0 %reshape.330 = bf16[4096,256]{1,0:T(8,128)(2,1)} reshape(bf16[1024,4,256]{2,1,0:T(4,128)(2,1)} %copy.125) | data formatting | bytes 4194304 | tf_op jit(solution)/shard_map/reshape | solution.py:73
  176.3 3.6 %convolution_convert_fusion.1 = bf16[4096,256]{1,0:T(8,128)(2,1)} fusion(bf16[4096,256]{1,0:T(8,128)(2,1)} %reshape.330, bf16[256,256]{1,0:T(8,128)(2,1)S(1)} %copy-done.3), kind=kOutput, calls=%fused_computation.6 | convolution fusion | flops 537919488 | bytes 4325376 | tf_op jit(solution)/shard_map/dot_general | solution.py:72
  180.0 4.4 %reshape.331 = bf16[1024,1024]{1,0:T(8,128)(2,1)} reshape(bf16[4096,256]{1,0:T(8,128)(2,1)} %convolution_convert_fusion.1) | data formatting | bytes 4194304 | tf_op jit(solution)/shard_map/reshape | solution.py:77
  184.3 5.9 %convolution_convert_fusion.2 = bf16[1024,1024]{1,0:T(8,128)(2,1)} fusion(bf16[1024,1024]{1,0:T(8,128)(2,1)} %bitcast.6, bf16[1024,1024]{1,0:T(8,128)(2,1)} %reshape.331), kind=kOutput, calls=%fused_computation.15 | convolution fusion | flops 2148532224 | bytes 6291456 | tf_op jit(solution)/shard_map/dot_general | solution.py:78
  190.2 4.4 %reshape.332 = bf16[4096,256]{1,0:T(8,128)(2,1)} reshape(bf16[1024,1024]{1,0:T(8,128)(2,1)} %convolution_convert_fusion.2) | data formatting | bytes 4194304 | tf_op jit(solution)/shard_map/reshape | solution.py:80
  194.6 4.3 %fusion = f32[4096,256]{1,0:T(8,128)} fusion(bf16[4096,256]{1,0:T(8,128)(2,1)} %reshape.332, bf16[256,256]{1,0:T(8,128)(2,1)S(1)} %copy-done.3), kind=kOutput, calls=%fused_computation.5 | convolution fusion | flops 538968064 | bytes 6422528 | tf_op jit(solution)/shard_map/dot_general | solution.py:79
  199.0 5.2 %reshape.337 = f32[1024,4,256]{2,1,0:T(4,128)} reshape(f32[4096,256]{1,0:T(8,128)} %fusion) | data formatting | bytes 8388608 | tf_op jit(solution)/shard_map/convert_element_type | solution.py:89
  204.2 5.3 %copy.126 = f32[1024,4,256]{0,2,1:T(8,128)} copy(f32[1024,4,256]{2,1,0:T(4,128)} %reshape.337) | data formatting | bytes 8388608 | tf_op jit(solution)/shard_map/convert_element_type | solution.py:89
  209.4 7.2 %fusion.8 = bf16[4,256,3,1]{1,2,3,0:T(4,128)(2,1)S(1)} fusion(f32[1024,4,256]{0,2,1:T(8,128)} %copy.126, f32[1024,4,256]{0,2,1:T(8,128)} %reshape.336, f32[3,1024]{1,0:T(4,128)S(1)} %copy-done.5), kind=kOutput, calls=%fused_computation.18 | convolution fusion | flops 38800384 | bytes 8407040 | tf_op jit(solution)/shard_map/jd,dct->cjt/dot_general | solution.py:86
  216.6 0.5 fusion.33
  217.1 0.4 fusion.11
  217.6 1.1 copy.129
  218.6 10.4 %all-to-all-start.5 = ((f32[64,2,3,256]{3,1,2,0:T(2,128)}), f32[64,2,3,256]{3,1,2,0:T(2,128)S(1)}, u32[]{:S(2)}, u32[]{:S(2)}) async-start(f32[64,2,3,256]{3,1,2,0:T(2,128)} %copy.129), calls=%async_computation.5 | async-start | bytes 786432 | tf_op jit(solution)/shard_map/all_to_all | solution.py:99
  229.1 0.5 broadcast.432
  229.6 2.1 reduce.3
  231.7 0.9 eq.71
  232.6 11.2 %all-to-all-done.5 = f32[64,2,3,256]{3,1,2,0:T(2,128)S(1)} async-done(((f32[64,2,3,256]{3,1,2,0:T(2,128)}), f32[64,2,3,256]{3,1,2,0:T(2,128)S(1)}, u32[]{:S(2)}, u32[]{:S(2)}) %all-to-all-start.5) | async-done | bytes 393248 | tf_op jit(solution)/shard_map/all_to_all | solution.py:99
  243.7 0.1 copy.130
  243.9 0.8 copy.140
  244.7 1.1 copy.131
  245.9 1.0 fusion.19
  246.9 1.6 copy.132
  248.4 40.1 %all-reduce.2.cloned.1.call-done = f32[32,3,256]{2,0,1:T(8,128)} async-done(((f32[32,3,256]{2,0,1:T(8,128)}), f32[32,3,256]{2,0,1:T(8,128)}) %all-reduce.2.cloned.1.call-update) | async-done | bytes 98320 | tf_op jit(solution)/shard_map/psum | solution.py:109
  288.6 2.2 multiply_add_fusion
  (39 shorter events, 0.6 us)
Async XLA Ops:
  7.2 128.0 %copy-start = (bf16[4,6,256,256]{3,2,1,0:T(8,128)(2,1)S(1)}, bf16[4,6,256,256]{3,2,1,0:T(8,128)(2,1)}, u32[]{:S(2)}) copy-start(bf16[4,6,256,256]{3,2,1,0:T(8,128)(2,1)} %param.18) | copy-start | bytes 9437188
  11.4 20.6 %all-to-all-start = ((s32[64,1,2]{2,1,0:T(1,128)}), s32[64,1,2]{2,1,0:T(1,128)S(1)}, u32[]{:S(2)}, u32[]{:S(2)}) async-start(s32[64,1,2]{2,1,0:T(1,128)} %bitcast.2), calls=%async_computation | async-start | bytes 65536 | tf_op jit(solution)/shard_map/all_to_all | solution.py:45
  31.9 0.6 copy-start.4
  34.3 16.5 %all-to-all-start.3 = ((bf16[64,2,3,256]{3,1,2,0:T(2,128)(2,1)}), bf16[64,2,3,256]{3,1,2,0:T(2,128)(2,1)S(1)}, u32[]{:S(2)}, u32[]{:S(2)}) async-start(bf16[64,2,3,256]{3,1,2,0:T(2,128)(2,1)} %broadcast_select_fusion.1), calls=%async_computation.3 | async-start | bytes 393216 | tf_op jit(solution)/shard_map/all_to_all | solution.py:48
  50.9 0.7 copy-start.1
  51.5 31.4 %all-to-all-start.4 = ((bf16[256,4,1024]{0,2,1:T(8,128)(2,1)}), bf16[256,4,1024]{0,2,1:T(8,128)(2,1)}, u32[]{:S(2)}, u32[]{:S(2)}) async-start(bf16[256,4,1024]{0,2,1:T(8,128)(2,1)} %bitcast.95), calls=%async_computation.4 | async-start | bytes 4194304 | tf_op jit(solution)/shard_map/all_to_all | solution.py:64
  82.9 4.6 %copy-start.6 = (bf16[7,4,1024]{2,1,0:T(4,128)(2,1)S(1)}, bf16[7,4,1024]{2,1,0:T(4,128)(2,1)}, u32[]{:S(2)}) copy-start(bf16[7,4,1024]{2,1,0:T(4,128)(2,1)} %param.16) | copy-start | bytes 172036
  82.9 37.6 %copy-start.8 = (s32[64]{0:T(128)S(1)}, s32[64]{0:T(128)}, u32[]{:S(2)}) copy-start(s32[64]{0:T(128)} %param.17) | copy-start | bytes 772
  82.9 42.8 %all-to-all-start.2 = ((bf16[256,4,1024]{0,2,1:T(8,128)(2,1)}), bf16[256,4,1024]{0,2,1:T(8,128)(2,1)}, u32[]{:S(2)}, u32[]{:S(2)}) async-start(bf16[256,4,1024]{0,2,1:T(8,128)(2,1)} %bitcast.94), calls=%async_computation.2 | async-start | bytes 4194304 | tf_op jit(solution)/shard_map/all_to_all | solution.py:63
  125.8 6.9 %copy-start.7 = (s32[4,6]{1,0:T(4,128)S(1)}, s32[4,6]{1,0:T(4,128)}, u32[]{:S(2)}) copy-start(s32[4,6]{1,0:T(4,128)} %param.19) | copy-start | bytes 292
  125.8 7.0 %copy-start.2 = (bf16[64,2,3,256]{3,1,2,0:T(2,128)(2,1)S(1)}, bf16[64,2,3,256]{3,1,2,0:T(2,128)(2,1)}, u32[]{:S(2)}) copy-start(bf16[64,2,3,256]{3,1,2,0:T(2,128)(2,1)} %copy-done.1) | copy-start | bytes 589828
  125.8 58.6 %all-to-all-start.1 = ((bf16[64,16,1024]{2,1,0:T(8,128)(2,1)}), bf16[64,16,1024]{2,1,0:T(8,128)(2,1)}, u32[]{:S(2)}, u32[]{:S(2)}) async-start(bf16[64,16,1024]{2,1,0:T(8,128)(2,1)} %broadcast_select_fusion), calls=%async_computation.1 | async-start | bytes 4194304 | tf_op jit(solution)/shard_map/all_to_all | solution.py:60
  155.2 5.8 %copy-start.5 = (f32[3,1024]{1,0:T(4,128)S(1)}, f32[3,1024]{1,0:T(4,128)}, u32[]{:S(2)}) copy-start(f32[3,1024]{1,0:T(4,128)} %param.14) | copy-start | bytes 36868
  172.3 4.0 %copy-start.3 = (bf16[256,256]{1,0:T(8,128)(2,1)S(1)}, bf16[256,256]{1,0:T(8,128)(2,1)}, u32[]{:S(2)}) copy-start(bf16[256,256]{1,0:T(8,128)(2,1)} %param.15) | copy-start | bytes 393220
  218.6 25.1 %all-to-all-start.5 = ((f32[64,2,3,256]{3,1,2,0:T(2,128)}), f32[64,2,3,256]{3,1,2,0:T(2,128)S(1)}, u32[]{:S(2)}, u32[]{:S(2)}) async-start(f32[64,2,3,256]{3,1,2,0:T(2,128)} %copy.129), calls=%async_computation.5 | async-start | bytes 786432 | tf_op jit(solution)/shard_map/all_to_all | solution.py:99
  229.0 59.6 %all-reduce.2.cloned.1.call-start = ((), (), s32[]{:S(2)}) async-start(), calls=%async_computation.6 | async-start | bytes 196608 | tf_op jit(solution)/shard_map/psum | solution.py:109
Sparse Core Ops, SparseCore 0:
  247.0 41.5 all-reduce.1

commit v2 on v1

--- a/solution.py
+++ b/solution.py
@@ -2,6 +2,27 @@
 import jax.numpy as jnp
 from jax import lax
 from jax.sharding import PartitionSpec as P
+
+
+def wafer_gather(x, axis):
+    spot = lax.axis_index("wafer")
+    size = lax.axis_size("wafer")
+    bit = 1
+    while bit < size:
+        other = lax.ppermute(x, "wafer", [(i, i ^ bit) for i in range(size)])
+        low = (spot & bit) == 0
+        x = jnp.where(low, jnp.concatenate([x, other], axis), jnp.concatenate([other, x], axis))
+        bit *= 2
+    return x
+
+
+def wafer_sum(x):
+    size = lax.axis_size("wafer")
+    bit = 1
+    while bit < size:
+        x = x + lax.ppermute(x, "wafer", [(i, i ^ bit) for i in range(size)])
+        bit *= 2
+    return x
 
 
 def shards(
@@ -55,7 +76,7 @@
     signal_parts = jnp.einsum(
         "cktp,ckjp->cjt", pointing, fetched, preferred_element_type=jnp.float32
     )
-    block_rows = lax.all_gather(whiten, "wafer", axis=1, tiled=True)
+    block_rows = wafer_gather(whiten, 1)
     sent_blocks = jnp.take(block_rows, group_wafer, axis=0)
     matrix = lax.all_to_all(sent_blocks, "tm", split_axis=0, concat_axis=0, tiled=True)
     matrix = matrix.reshape(det_total, det_total)
@@ -106,7 +127,7 @@
         precision=precise_mode,
     )
     owned_sum = owned_sum.reshape(tiles_own, comp_count, pixel_count)
-    summed = lax.psum(owned_sum, "wafer")
+    summed = wafer_sum(owned_sum)
     residual_next = summed * float(det_total) ** (-0.5)
     direction_next = residual_next + blend_weight * direction
     return (updated, residual_next, direction_next)

time: 299 us -> 255 us (0.85)
  blocking collectives: 32.8 us -> 0 us
  between operations: 14.3 us -> 0.84 us
  starting transfers between devices: 43.8 us -> 51.6 us
  waiting for transfers between devices: 86 us -> 79.7 us
    psum x1 -> x0, waiting for transfers between devices: 40.1 us -> none  [shards(): summed = lax.psum(owned_sum, 'wafer')]
    ppermute x0 -> x4, waiting for transfers between devices: none -> 33.8 us  [the longest x2 27.4 us: wafer_gather(): other = lax.ppermute(x, 'wafer', [(i, i ^ bit) for i in range(size)])]
    all_gather x1 -> x0, blocking collectives: 32.8 us -> none  [shards(): block_rows = lax.all_gather(whiten, 'wafer', axis=1, tiled=True)]
    ppermute x0 -> x4, starting transfers between devices: none -> 7.9 us  [the longest x2 4.73 us: wafer_gather(): other = lax.ppermute(x, 'wafer', [(i, i ^ bit) for i in range(size)])]
    unnamed x23 -> x22, local copies, waits for them, and re-layouts: 11.4 us -> 11.4 us
  transfers between devices with their start and end apart: 7 -> 10, of which waited for: 5 -> 8; matrix products, arithmetic and copies ran while one was open for 25% -> 30% of each run, Pallas kernels for 0% -> 0%
where the time goes in v2:
time: 255 us; the launch traced here: 253 us
  waiting for transfers between devices  79.7 us (31%)
  local copies, waits for them, and re-layouts  74.6 us (29%)
  starting transfers between devices  51.6 us (20%)
  matrix products  30.3 us (12%)
  other arithmetic  16.3 us (6%)
    ppermute x2, waiting for transfers between devices, wafer_gather(): other = lax.ppermute(x, 'wafer', [(i, i ^ bit) for i in range(size)])  27.4 us
    all_to_all x1, waiting for transfers between devices, shards(): lax.all_to_all(sample_weight, 'wafer', split_axis=1, concat_axis=0, tiled...  22.9 us
    all_to_all x1, starting transfers between devices, shards(): lax.all_to_all(requests, 'tm', split_axis=0, concat_axis=0, tiled=True)  12 us
    unnamed x22, local copies, waits for them, and re-layouts  11.4 us
    all_to_all x1, waiting for transfers between devices, shards(): lax.all_to_all(outgoing, 'tm', split_axis=0, concat_axis=0, tiled=True)  11.2 us
    convert_element_type x2, local copies, waits for them, and re-layouts, shards(): columns.astype(jnp.float32).reshape(det_total, spans_here, samples) - signal  10.5 us
    convert_element_type x2, local copies, waits for them, and re-layouts, shards(): smoothed.astype(jnp.float32) * column_weights  10.5 us
    convert_element_type x2, local copies, waits for them, and re-layouts, shards(): column_weights.astype(jnp.float32).reshape(det_total, spans_here, samples)  10.5 us
  transfers between devices with their start and end apart: 10, of which 8 were waited for; matrix products, arithmetic and copies ran while one was open for 30% of the time, Pallas kernels for 0%

profile of v2, /device:TPU:2, one launch (start us, length us, event | category | flops | bytes accessed | tf_op | source)
XLA Modules:
  0.0 253.4 jit_solution(1870328873468114112)
XLA Ops:
  0.6 0.9 reshape.327
  1.6 0.8 reshape.326
  2.4 1.4 gather_fusion
  3.8 0.2 convert_reduce_fusion
  4.1 0.8 all_to_all.39
  4.8 12.0 %all-to-all-start = ((s32[64,1,2]{2,1,0:T(1,128)}), s32[64,1,2]{2,1,0:T(1,128)S(1)}, u32[]{:S(2)}, u32[]{:S(2)}) async-start(s32[64,1,2]{2,1,0:T(1,128)} %bitcast.2), calls=%async_computation | async-start | bytes 65536 | tf_op jit(solution)/shard_map/all_to_all | solution.py:66
  16.9 1.3 fusion.32
  18.2 2.4 fusion.31
  20.6 4.8 %all-to-all-done = s32[64,1,2]{2,1,0:T(1,128)S(1)} async-done(((s32[64,1,2]{2,1,0:T(1,128)}), s32[64,1,2]{2,1,0:T(1,128)S(1)}, u32[]{:S(2)}, u32[]{:S(2)}) %all-to-all-start) | async-done | bytes 544 | tf_op jit(solution)/shard_map/all_to_all | solution.py:66
  26.0 0.8 gather_fusion.2
  26.9 0.9 broadcast_select_fusion.1
  27.8 5.5 %all-to-all-start.3 = ((bf16[64,2,3,256]{3,1,2,0:T(2,128)(2,1)}), bf16[64,2,3,256]{3,1,2,0:T(2,128)(2,1)S(1)}, u32[]{:S(2)}, u32[]{:S(2)}) async-start(bf16[64,2,3,256]{3,1,2,0:T(2,128)(2,1)} %broadcast_select_fusion.1), calls=%async_computation.3 | async-start | bytes 393216 | tf_op jit(solution)/shard_map/all_to_all | solution.py:69
  33.3 4.1 %copy.94 = bf16[256,4096]{0,1:T(8,128)(2,1)} copy(bf16[256,4096]{1,0:T(8,128)(2,1)} %param.13) | data formatting | bytes 4194304 | tf_op args[1]
  37.4 6.9 %all-to-all-done.3 = bf16[64,2,3,256]{3,1,2,0:T(2,128)(2,1)S(1)} async-done(((bf16[64,2,3,256]{3,1,2,0:T(2,128)(2,1)}), bf16[64,2,3,256]{3,1,2,0:T(2,128)(2,1)S(1)}, u32[]{:S(2)}, u32[]{:S(2)}) %all-to-all-start.3) | async-done | bytes 196640 | tf_op jit(solution)/shard_map/all_to_all | solution.py:69
  44.3 0.7 copy-done.1
  45.0 4.5 %all-to-all-start.4 = ((bf16[256,4,1024]{0,2,1:T(8,128)(2,1)}), bf16[256,4,1024]{0,2,1:T(8,128)(2,1)}, u32[]{:S(2)}, u32[]{:S(2)}) async-start(bf16[256,4,1024]{0,2,1:T(8,128)(2,1)} %bitcast.95), calls=%async_computation.4 | async-start | bytes 4194304 | tf_op jit(solution)/shard_map/all_to_all | solution.py:85
  49.5 4.1 %copy.84 = bf16[256,4096]{0,1:T(8,128)(2,1)} copy(bf16[256,4096]{1,0:T(8,128)(2,1)} %param.12) | data formatting | bytes 4194304 | tf_op args[0]
  53.5 22.9 %all-to-all-done.4 = bf16[256,4,1024]{0,2,1:T(8,128)(2,1)} async-done(((bf16[256,4,1024]{0,2,1:T(8,128)(2,1)}), bf16[256,4,1024]{0,2,1:T(8,128)(2,1)}, u32[]{:S(2)}, u32[]{:S(2)}) %all-to-all-start.4) | async-done | bytes 2097184 | tf_op jit(solution)/shard_map/all_to_all | solution.py:85
  76.4 4.6 %all-to-all-start.2 = ((bf16[256,4,1024]{0,2,1:T(8,128)(2,1)}), bf16[256,4,1024]{0,2,1:T(8,128)(2,1)}, u32[]{:S(2)}, u32[]{:S(2)}) async-start(bf16[256,4,1024]{0,2,1:T(8,128)(2,1)} %bitcast.94), calls=%async_computation.2 | async-start | bytes 4194304 | tf_op jit(solution)/shard_map/all_to_all | solution.py:84
  81.1 2.0 collective-permute-start
  83.0 23.7 %collective-permute-done = bf16[7,4,1024]{2,1,0:T(4,128)(2,1)S(1)} collective-permute-done((bf16[7,4,1024]{2,1,0:T(4,128)(2,1)S(1)}, bf16[7,4,1024]{2,1,0:T(4,128)(2,1)S(1)}, u32[]{:S(2)}, u32[]{:S(2)}) %collective-permute-start) | collective-permute-done | bytes 57376 | tf_op jit(solution)/shard_map/ppermute | solution.py:12
  106.8 2.8 %collective-permute-start.1 = (bf16[7,8,1024]{2,1,0:T(8,128)(2,1)S(1)}, bf16[7,8,1024]{2,1,0:T(8,128)(2,1)}, u32[]{:S(2)}, u32[]{:S(2)}) collective-permute-start(bf16[7,8,1024]{2,1,0:T(8,128)(2,1)S(1)} %maximum_select_fusion.1), channel_id=1, source_target_pairs={{0,2},{1,3},{2,0},{3,1},{4,6},{5,7},{6,4},{7,5},{8,10},{9,11},{10,... | collective-permute-start | bytes 344072 | tf_op jit(solution)/shard_map/ppermute | solution.py:12
  109.6 3.7 %collective-permute-done.1 = bf16[7,8,1024]{2,1,0:T(8,128)(2,1)} collective-permute-done((bf16[7,8,1024]{2,1,0:T(8,128)(2,1)S(1)}, bf16[7,8,1024]{2,1,0:T(8,128)(2,1)}, u32[]{:S(2)}, u32[]{:S(2)}) %collective-permute-start.1) | collective-permute-done | bytes 114720 | tf_op jit(solution)/shard_map/ppermute | solution.py:12
  113.3 1.0 maximum_select_fusion
  114.3 2.0 gather_fusion.1
  116.3 3.2 %broadcast_select_fusion = bf16[64,16,1024]{2,1,0:T(8,128)(2,1)} fusion(bf16[64,16,1024]{2,1,0:T(8,128)(2,1)} %gather_fusion.1, pred[64]{0:T(512)(128)(4,1)S(1)} %compare_and_fusion.2), kind=kLoop, calls=%fused_computation.14 | loop fusion | flops 1048576 | bytes 4194368 | tf_op jit(solution)/shard_map/jit(_take)/select_n | solution.py:80
  119.5 6.7 %all-to-all-start.1 = ((bf16[64,16,1024]{2,1,0:T(8,128)(2,1)}), bf16[64,16,1024]{2,1,0:T(8,128)(2,1)}, u32[]{:S(2)}, u32[]{:S(2)}) async-start(bf16[64,16,1024]{2,1,0:T(8,128)(2,1)} %broadcast_select_fusion), calls=%async_computation.1 | async-start | bytes 4194304 | tf_op jit(solution)/shard_map/all_to_all | solution.py:81
  126.5 0.8 copy.91
  127.3 1.6 gather_fusion.3
  128.9 0.9 convolution_bitcast_fusion
  129.8 2.0 convert_bitcast_fusion
  131.8 4.7 %copy.95 = f32[4,256,1024]{1,0,2:T(4,128)} copy(f32[4,256,1024]{1,2,0:T(8,128)S(1)} %convert_bitcast_fusion) | data formatting | bytes 8388608 | tf_op jit(solution)/shard_map/convert_element_type | solution.py:87
  136.5 5.8 %reshape.336 = f32[1024,4,256]{0,2,1:T(8,128)} reshape(f32[4,256,1024]{1,0,2:T(4,128)} %copy.95) | data formatting | bytes 8388608 | tf_op jit(solution)/shard_map/convert_element_type | solution.py:87
  142.3 2.0 convert_bitcast_fusion.1
  144.2 4.7 %copy.85 = f32[4,256,1024]{1,0,2:T(4,128)} copy(f32[4,256,1024]{1,2,0:T(8,128)S(1)} %convert_bitcast_fusion.1) | data formatting | bytes 8388608 | tf_op jit(solution)/shard_map/convert_element_type | solution.py:90
  148.9 5.9 %reshape.335 = f32[1024,4,256]{0,2,1:T(8,128)} reshape(f32[4,256,1024]{1,0,2:T(4,128)} %copy.85) | data formatting | bytes 8388608 | tf_op jit(solution)/shard_map/convert_element_type | solution.py:90
  154.7 7.1 %fusion.2 = bf16[1024,4,256]{0,2,1:T(8,128)(2,1)} fusion(f32[1024,4,256]{0,2,1:T(8,128)} %reshape.336, f32[1024,4,256]{0,2,1:T(8,128)} %reshape.335, f32[4,3,256]{2,1,0:T(4,128)S(1)} %convolution_bitcast_fusion, f32[3,1024]{1,0:T(4,128)S(1)} %copy-done.5), kind=kOutput, calls=%fused_computation.9 | convolution fusion | flops 40894464 | bytes 10510336 | tf_op jit(solution)/shard_map/jd,cjt->dct/dot_general | solution.py:88
  161.8 4.3 %copy.96 = bf16[1024,4,256]{2,1,0:T(4,128)(2,1)} copy(bf16[1024,4,256]{0,2,1:T(8,128)(2,1)} %fusion.2) | data formatting | bytes 4194304 | tf_op jit(solution)/shard_map/convert_element_type | solution.py:92
  166.1 4.0 %reshape.330 = bf16[4096,256]{1,0:T(8,128)(2,1)} reshape(bf16[1024,4,256]{2,1,0:T(4,128)(2,1)} %copy.96) | data formatting | bytes 4194304 | tf_op jit(solution)/shard_map/reshape | solution.py:94
  170.1 3.7 %convolution_convert_fusion.1 = bf16[4096,256]{1,0:T(8,128)(2,1)} fusion(bf16[4096,256]{1,0:T(8,128)(2,1)} %reshape.330, bf16[256,256]{1,0:T(8,128)(2,1)S(1)} %copy-done.3), kind=kOutput, calls=%fused_computation.6 | convolution fusion | flops 537919488 | bytes 4325376 | tf_op jit(solution)/shard_map/dot_general | solution.py:93
  173.7 4.4 %reshape.331 = bf16[1024,1024]{1,0:T(8,128)(2,1)} reshape(bf16[4096,256]{1,0:T(8,128)(2,1)} %convolution_convert_fusion.1) | data formatting | bytes 4194304 | tf_op jit(solution)/shard_map/reshape | solution.py:98
  178.1 5.9 %convolution_convert_fusion.2 = bf16[1024,1024]{1,0:T(8,128)(2,1)} fusion(bf16[1024,1024]{1,0:T(8,128)(2,1)} %bitcast.6, bf16[1024,1024]{1,0:T(8,128)(2,1)} %reshape.331), kind=kOutput, calls=%fused_computation.15 | convolution fusion | flops 2148532224 | bytes 6291456 | tf_op jit(solution)/shard_map/dot_general | solution.py:99
  184.0 4.4 %reshape.332 = bf16[4096,256]{1,0:T(8,128)(2,1)} reshape(bf16[1024,1024]{1,0:T(8,128)(2,1)} %convolution_convert_fusion.2) | data formatting | bytes 4194304 | tf_op jit(solution)/shard_map/reshape | solution.py:101
  188.4 4.3 %fusion = f32[4096,256]{1,0:T(8,128)} fusion(bf16[4096,256]{1,0:T(8,128)(2,1)} %reshape.332, bf16[256,256]{1,0:T(8,128)(2,1)S(1)} %copy-done.3), kind=kOutput, calls=%fused_computation.5 | convolution fusion | flops 538968064 | bytes 6422528 | tf_op jit(solution)/shard_map/dot_general | solution.py:100
  192.8 5.2 %reshape.337 = f32[1024,4,256]{2,1,0:T(4,128)} reshape(f32[4096,256]{1,0:T(8,128)} %fusion) | data formatting | bytes 8388608 | tf_op jit(solution)/shard_map/convert_element_type | solution.py:110
  198.0 5.3 %copy.97 = f32[1024,4,256]{0,2,1:T(8,128)} copy(f32[1024,4,256]{2,1,0:T(4,128)} %reshape.337) | data formatting | bytes 8388608 | tf_op jit(solution)/shard_map/convert_element_type | solution.py:110
  203.2 7.2 %fusion.8 = bf16[4,256,3,1]{1,2,3,0:T(4,128)(2,1)S(1)} fusion(f32[1024,4,256]{0,2,1:T(8,128)} %copy.97, f32[1024,4,256]{0,2,1:T(8,128)} %reshape.336, f32[3,1024]{1,0:T(4,128)S(1)} %copy-done.5), kind=kOutput, calls=%fused_computation.18 | convolution fusion | flops 38800384 | bytes 8407040 | tf_op jit(solution)/shard_map/jd,dct->cjt/dot_general | solution.py:107
  210.4 0.5 fusion.33
  210.9 0.4 fusion.11
  211.4 1.1 copy.100
  212.4 10.4 %all-to-all-start.5 = ((f32[64,2,3,256]{3,1,2,0:T(2,128)}), f32[64,2,3,256]{3,1,2,0:T(2,128)S(1)}, u32[]{:S(2)}, u32[]{:S(2)}) async-start(f32[64,2,3,256]{3,1,2,0:T(2,128)} %copy.100), calls=%async_computation.5 | async-start | bytes 786432 | tf_op jit(solution)/shard_map/all_to_all | solution.py:120
  222.8 0.5 broadcast.444
  223.4 2.1 reduce.3
  225.5 0.9 eq.77
  226.3 11.2 %all-to-all-done.5 = f32[64,2,3,256]{3,1,2,0:T(2,128)S(1)} async-done(((f32[64,2,3,256]{3,1,2,0:T(2,128)}), f32[64,2,3,256]{3,1,2,0:T(2,128)S(1)}, u32[]{:S(2)}, u32[]{:S(2)}) %all-to-all-start.5) | async-done | bytes 393248 | tf_op jit(solution)/shard_map/all_to_all | solution.py:120
  237.7 0.8 copy.111
  238.5 1.1 copy.102
  239.7 0.3 fusion.19
  240.0 0.4 collective-permute-start.2
  240.4 4.5 %collective-permute-done.2 = f32[32,3,256]{2,0,1:T(8,128)S(1)} collective-permute-done((f32[32,3,256]{2,0,1:T(8,128)S(1)}, f32[32,3,256]{2,0,1:T(8,128)S(1)}, u32[]{:S(2)}, u32[]{:S(2)}) %collective-permute-start.2) | collective-permute-done | bytes 98336 | tf_op jit(solution)/shard_map/ppermute | solution.py:23
  245.0 2.8 %collective-permute-start.3 = (f32[32,3,256]{2,0,1:T(8,128)S(1)}, f32[32,3,256]{2,0,1:T(8,128)S(1)}, u32[]{:S(2)}, u32[]{:S(2)}) collective-permute-start(f32[32,3,256]{2,0,1:T(8,128)S(1)} %add.165), channel_id=1, source_target_pairs={{0,2},{1,3},{2,0},{3,1},{4,6},{5,7},{6,4},{7,5},{8,10},{9,11},{10,... | collective-permute-start | bytes 294920 | tf_op jit(solution)/shard_map/ppermute | solution.py:23
  247.7 1.6 copy.103
  249.3 1.9 collective-permute-done.3
  251.2 2.2 multiply_add_fusion
  (44 shorter events, 1.3 us)
Async XLA Ops:
  0.6 128.3 %copy-start = (bf16[4,6,256,256]{3,2,1,0:T(8,128)(2,1)S(1)}, bf16[4,6,256,256]{3,2,1,0:T(8,128)(2,1)}, u32[]{:S(2)}) copy-start(bf16[4,6,256,256]{3,2,1,0:T(8,128)(2,1)} %param.18) | copy-start | bytes 9437188
  4.8 20.6 %all-to-all-start = ((s32[64,1,2]{2,1,0:T(1,128)}), s32[64,1,2]{2,1,0:T(1,128)S(1)}, u32[]{:S(2)}, u32[]{:S(2)}) async-start(s32[64,1,2]{2,1,0:T(1,128)} %bitcast.2), calls=%async_computation | async-start | bytes 65536 | tf_op jit(solution)/shard_map/all_to_all | solution.py:66
  25.4 0.6 copy-start.4
  27.8 16.5 %all-to-all-start.3 = ((bf16[64,2,3,256]{3,1,2,0:T(2,128)(2,1)}), bf16[64,2,3,256]{3,1,2,0:T(2,128)(2,1)S(1)}, u32[]{:S(2)}, u32[]{:S(2)}) async-start(bf16[64,2,3,256]{3,1,2,0:T(2,128)(2,1)} %broadcast_select_fusion.1), calls=%async_computation.3 | async-start | bytes 393216 | tf_op jit(solution)/shard_map/all_to_all | solution.py:69
  44.3 0.7 copy-start.1
  45.0 31.4 %all-to-all-start.4 = ((bf16[256,4,1024]{0,2,1:T(8,128)(2,1)}), bf16[256,4,1024]{0,2,1:T(8,128)(2,1)}, u32[]{:S(2)}, u32[]{:S(2)}) async-start(bf16[256,4,1024]{0,2,1:T(8,128)(2,1)} %bitcast.95), calls=%async_computation.4 | async-start | bytes 4194304 | tf_op jit(solution)/shard_map/all_to_all | solution.py:85
  76.4 4.6 %copy-start.6 = (bf16[7,4,1024]{2,1,0:T(4,128)(2,1)S(1)}, bf16[7,4,1024]{2,1,0:T(4,128)(2,1)}, u32[]{:S(2)}) copy-start(bf16[7,4,1024]{2,1,0:T(4,128)(2,1)} %param.16) | copy-start | bytes 172036
  76.4 6.6 %copy-start.8 = (s32[64]{0:T(128)S(1)}, s32[64]{0:T(128)}, u32[]{:S(2)}) copy-start(s32[64]{0:T(128)} %param.17) | copy-start | bytes 772
  76.4 43.1 %all-to-all-start.2 = ((bf16[256,4,1024]{0,2,1:T(8,128)(2,1)}), bf16[256,4,1024]{0,2,1:T(8,128)(2,1)}, u32[]{:S(2)}, u32[]{:S(2)}) async-start(bf16[256,4,1024]{0,2,1:T(8,128)(2,1)} %bitcast.94), calls=%async_computation.2 | async-start | bytes 4194304 | tf_op jit(solution)/shard_map/all_to_all | solution.py:84
  81.1 25.6 %collective-permute-start = (bf16[7,4,1024]{2,1,0:T(4,128)(2,1)S(1)}, bf16[7,4,1024]{2,1,0:T(4,128)(2,1)S(1)}, u32[]{:S(2)}, u32[]{:S(2)}) collective-permute-start(bf16[7,4,1024]{2,1,0:T(4,128)(2,1)S(1)} %copy-done.6), channel_id=1, source_target_pairs={{0,1},{1,0},{2,3},{3,2},{4,5},{5,4},{6,7},{7,6},{8,9},{9,8},{10,11... | collective-permute-start | bytes 172040 | tf_op jit(solution)/shard_map/ppermute | solution.py:12
  106.8 6.5 %collective-permute-start.1 = (bf16[7,8,1024]{2,1,0:T(8,128)(2,1)S(1)}, bf16[7,8,1024]{2,1,0:T(8,128)(2,1)}, u32[]{:S(2)}, u32[]{:S(2)}) collective-permute-start(bf16[7,8,1024]{2,1,0:T(8,128)(2,1)S(1)} %maximum_select_fusion.1), channel_id=1, source_target_pairs={{0,2},{1,3},{2,0},{3,1},{4,6},{5,7},{6,4},{7,5},{8,10},{9,11},{10,... | collective-permute-start | bytes 344072 | tf_op jit(solution)/shard_map/ppermute | solution.py:12
  119.5 6.9 %copy-start.7 = (s32[4,6]{1,0:T(4,128)S(1)}, s32[4,6]{1,0:T(4,128)}, u32[]{:S(2)}) copy-start(s32[4,6]{1,0:T(4,128)} %param.19) | copy-start | bytes 292
  119.5 7.0 %copy-start.2 = (bf16[64,2,3,256]{3,1,2,0:T(2,128)(2,1)S(1)}, bf16[64,2,3,256]{3,1,2,0:T(2,128)(2,1)}, u32[]{:S(2)}) copy-start(bf16[64,2,3,256]{3,1,2,0:T(2,128)(2,1)} %copy-done.1) | copy-start | bytes 589828
  119.5 58.6 %all-to-all-start.1 = ((bf16[64,16,1024]{2,1,0:T(8,128)(2,1)}), bf16[64,16,1024]{2,1,0:T(8,128)(2,1)}, u32[]{:S(2)}, u32[]{:S(2)}) async-start(bf16[64,16,1024]{2,1,0:T(8,128)(2,1)} %broadcast_select_fusion), calls=%async_computation.1 | async-start | bytes 4194304 | tf_op jit(solution)/shard_map/all_to_all | solution.py:81
  148.9 5.9 %copy-start.5 = (f32[3,1024]{1,0:T(4,128)S(1)}, f32[3,1024]{1,0:T(4,128)}, u32[]{:S(2)}) copy-start(f32[3,1024]{1,0:T(4,128)} %param.14) | copy-start | bytes 36868
  166.1 4.0 %copy-start.3 = (bf16[256,256]{1,0:T(8,128)(2,1)S(1)}, bf16[256,256]{1,0:T(8,128)(2,1)}, u32[]{:S(2)}) copy-start(bf16[256,256]{1,0:T(8,128)(2,1)} %param.15) | copy-start | bytes 393220
  212.4 25.1 %all-to-all-start.5 = ((f32[64,2,3,256]{3,1,2,0:T(2,128)}), f32[64,2,3,256]{3,1,2,0:T(2,128)S(1)}, u32[]{:S(2)}, u32[]{:S(2)}) async-start(f32[64,2,3,256]{3,1,2,0:T(2,128)} %copy.100), calls=%async_computation.5 | async-start | bytes 786432 | tf_op jit(solution)/shard_map/all_to_all | solution.py:120
  240.0 5.0 %collective-permute-start.2 = (f32[32,3,256]{2,0,1:T(8,128)S(1)}, f32[32,3,256]{2,0,1:T(8,128)S(1)}, u32[]{:S(2)}, u32[]{:S(2)}) collective-permute-start(f32[32,3,256]{2,0,1:T(8,128)S(1)} %fusion.19), channel_id=1, source_target_pairs={{0,1},{1,0},{2,3},{3,2},{4,5},{5,4},{6,7},{7,6},{8,9},{9,8},{10,11... | collective-permute-start | bytes 294920 | tf_op jit(solution)/shard_map/ppermute | solution.py:23
  245.0 6.2 %collective-permute-start.3 = (f32[32,3,256]{2,0,1:T(8,128)S(1)}, f32[32,3,256]{2,0,1:T(8,128)S(1)}, u32[]{:S(2)}, u32[]{:S(2)}) collective-permute-start(f32[32,3,256]{2,0,1:T(8,128)S(1)} %add.165), channel_id=1, source_target_pairs={{0,2},{1,3},{2,0},{3,1},{4,6},{5,7},{6,4},{7,5},{8,10},{9,11},{10,... | collective-permute-start | bytes 294920 | tf_op jit(solution)/shard_map/ppermute | solution.py:23

commit v3 on v2

--- a/solution.py
+++ b/solution.py
@@ -14,6 +14,20 @@
         x = jnp.where(low, jnp.concatenate([x, other], axis), jnp.concatenate([other, x], axis))
         bit *= 2
     return x
+
+
+def wafer_columns(x):
+    spot = lax.axis_index("wafer")
+    size = lax.axis_size("wafer")
+    width = x.shape[1] // size
+    pieces = [lax.dynamic_slice_in_dim(x, spot * width, width, 1)]
+    for shift in range(1, size):
+        target = (spot + shift) % size
+        piece = lax.dynamic_slice_in_dim(x, target * width, width, 1)
+        pieces.append(lax.ppermute(piece, "wafer", [(i, (i + shift) % size) for i in range(size)]))
+    stacked = jnp.stack(pieces)
+    order = (spot - jnp.arange(size, dtype=jnp.int32)) % size
+    return jnp.take(stacked, order, axis=0).reshape(size * x.shape[0], width)
 
 
 def wafer_sum(x):
@@ -80,37 +94,24 @@
     sent_blocks = jnp.take(block_rows, group_wafer, axis=0)
     matrix = lax.all_to_all(sent_blocks, "tm", split_axis=0, concat_axis=0, tiled=True)
     matrix = matrix.reshape(det_total, det_total)
-    columns, column_weights = (
-        lax.all_to_all(timestream, "wafer", split_axis=1, concat_axis=0, tiled=True),
-        lax.all_to_all(sample_weight, "wafer", split_axis=1, concat_axis=0, tiled=True),
-    )
-    column_weights = column_weights.astype(jnp.float32).reshape(det_total, spans_here, samples)
-    signal = jnp.einsum("jd,cjt->dct", response, signal_parts, precision=precise_mode)
-    errors = (
-        (columns.astype(jnp.float32).reshape(det_total, spans_here, samples) - signal)
-        * column_weights
-    ).astype(jnp.bfloat16)
-    filtered = jnp.dot(
-        errors.reshape(det_total * spans_here, samples),
-        band_filter,
-        preferred_element_type=jnp.float32,
-    )
-    filtered = filtered.astype(jnp.bfloat16).reshape(det_total, spans_here * samples)
+    columns = wafer_columns(timestream)
+    column_weights = wafer_columns(sample_weight).astype(jnp.float32)
+    width = spans_here * samples
+    parts_flat = jnp.transpose(signal_parts, (1, 0, 2)).reshape(comp_count, width)
+    signal = jnp.einsum("jd,js->ds", response, parts_flat, precision=precise_mode)
+    errors = ((columns.astype(jnp.float32) - signal) * column_weights).astype(jnp.bfloat16)
+    block_id = jnp.arange(width, dtype=jnp.int32) // samples
+    same_span = block_id[:, None] == block_id[None, :]
+    filter_blocks = jnp.where(same_span, jnp.tile(band_filter, (spans_here, spans_here)), jnp.zeros((), band_filter.dtype))
+    filtered = jnp.dot(errors, filter_blocks, preferred_element_type=jnp.float32).astype(jnp.bfloat16)
     whitened = jnp.dot(matrix, filtered, preferred_element_type=jnp.float32).astype(jnp.bfloat16)
     smoothed = lax.dot_general(
-        whitened.reshape(det_total * spans_here, samples),
-        band_filter,
-        (((1,), (1,)), ((), ())),
-        preferred_element_type=jnp.float32,
+        whitened, filter_blocks, (((1,), (1,)), ((), ())), preferred_element_type=jnp.float32
+    ).astype(jnp.bfloat16)
+    stokes = jnp.einsum(
+        "jd,ds->js", response, smoothed.astype(jnp.float32) * column_weights, precision=precise_mode
     )
-    smoothed = smoothed.astype(jnp.bfloat16).reshape(det_total, spans_here, samples)
-    stokes = jnp.einsum(
-        "jd,dct->cjt",
-        response,
-        smoothed.astype(jnp.float32) * column_weights,
-        precision=precise_mode,
-    )
-    stokes_short = stokes.astype(jnp.bfloat16)
+    stokes_short = jnp.transpose(stokes.reshape(comp_count, spans_here, samples), (1, 0, 2)).astype(jnp.bfloat16)
     partial_value = jnp.einsum(
         "cjt,cktp->ckjp", stokes_short, pointing, preferred_element_type=jnp.float32
     )

time: 255 us -> 195 us (0.76)
  waiting for transfers between devices: 79.7 us -> 40.3 us
  local copies, waits for them, and re-layouts: 74.6 us -> 40.8 us
  other arithmetic: 16.3 us -> 30.3 us
    ppermute x2, waiting for transfers between devices: 27.4 us -> 0.01 us  [wafer_gather(): other = lax.ppermute(x, 'wafer', [(i, i ^ bit) for i in range(size)])]
    convert_element_type x7 -> x2, local copies, waits for them, and re-layouts: 35.7 us -> 10.8 us  [the longest x1 5.45 us: shards(): columns.astype(jnp.float32) - signal]
    all_to_all x2 -> x0, waiting for transfers between devices: 22.9 us -> none  [the longest x1 22.9 us: shards(): lax.all_to_all(sample_weight, 'wafer', split_axis=1, concat_axis=0, tiled...]
    reshape x3 -> x0, local copies, waits for them, and re-layouts: 12.8 us -> none  [the longest x1 4.42 us: shards(): whitened.reshape(det_total * spans_here, samples)]
    ppermute x0 -> x6, waiting for transfers between devices: none -> 12.1 us  [wafer_columns(): lax.ppermute(piece, 'wafer', [(i, (i + shift) % size) for i in range(size)])]
    all_to_all x2 -> x0, starting transfers between devices: 9.1 us -> none  [the longest x1 4.63 us: shards(): lax.all_to_all(timestream, 'wafer', split_axis=1, concat_axis=0, tiled=True)]
    ppermute x0 -> x6, starting transfers between devices: none -> 8.51 us  [wafer_columns(): lax.ppermute(piece, 'wafer', [(i, (i + shift) % size) for i in range(size)])]
    gather x0 -> x2, local copies, waits for them, and re-layouts: none -> 7.25 us  [wafer_columns(): return jnp.take(stacked, order, axis=0).reshape(size * x.shape[0], width)]
  transfers between devices with their start and end apart: 10 -> 14, of which waited for: 8 -> 7; matrix products, arithmetic and copies ran while one was open for 30% -> 37% of each run, Pallas kernels for 0% -> 0%
where the time goes in v3:
time: 195 us; the launch traced here: 194 us
  starting transfers between devices  53.7 us (28%)
  local copies, waits for them, and re-layouts  40.8 us (21%)
  waiting for transfers between devices  40.3 us (21%)
  other arithmetic  30.3 us (16%)
  matrix products  27.9 us (14%)
    all_to_all x1, starting transfers between devices, shards(): lax.all_to_all(served, 'tm', split_axis=0, concat_axis=0, tiled=True)  12.2 us
    ppermute x6, waiting for transfers between devices, wafer_columns(): lax.ppermute(piece, 'wafer', [(i, (i + shift) % size) for i in range(size)])  12.1 us
    all_to_all x1, starting transfers between devices, shards(): lax.all_to_all(requests, 'tm', split_axis=0, concat_axis=0, tiled=True)  12 us
    all_to_all x1, waiting for transfers between devices, shards(): lax.all_to_all(outgoing, 'tm', split_axis=0, concat_axis=0, tiled=True)  11.2 us
    all_to_all x1, starting transfers between devices, shards(): lax.all_to_all(outgoing, 'tm', split_axis=0, concat_axis=0, tiled=True)  10.4 us
    dot_general x1, matrix products, shards(): lax.dot_general(whitened, filter_blocks, (((1,), (1,)), ((), ())), prefer...  8.76 us
    ppermute x6, starting transfers between devices, wafer_columns(): lax.ppermute(piece, 'wafer', [(i, (i + shift) % size) for i in range(size)])  8.51 us
    ppermute x2, waiting for transfers between devices, wafer_sum(): x = x + lax.ppermute(x, 'wafer', [(i, i ^ bit) for i in range(size)])  7.41 us
  transfers between devices with their start and end apart: 14, of which 7 were waited for; matrix products, arithmetic and copies ran while one was open for 37% of the time, Pallas kernels for 0%

profile of v3, /device:TPU:2, one launch (start us, length us, event | category | flops | bytes accessed | tf_op | source)
XLA Modules:
  0.0 194.1 jit_solution(5065176384599629947)
XLA Ops:
  0.8 3.1 %dynamic-slice_bitcast_fusion = (bf16[1,256,1024]{2,1,0:T(8,128)(2,1)}, bf16[256,1024]{1,0:T(8,128)(2,1)}, bf16[256,1024]{1,0:T(8,128)(2,1)}, bf16[256,1024]{1,0:T(8,128)(2,1)}) fusion(bf16[256,4096]{1,0:T(8,128)(2,1)} %param.15, s32[]{:T(128)S(6)} %select_n.258, s32[]{:T(128)S(6)} %select_n.260, s32[]{:T(128)S(6)} %select_n.264, s32[]{:T(128)S(6)} %select_n.262), kind=kLoop, calls=%fused_computation.27 | loop fusion | bytes 4194320 | tf_op jit(solution)/shard_map/stack | solution.py:28
  3.8 1.6 collective-permute-start.5
  5.4 2.9 %collective-permute-start.6 = (bf16[256,1024]{1,0:T(8,128)(2,1)}, bf16[256,1024]{1,0:T(8,128)(2,1)}, u32[]{:S(2)}, u32[]{:S(2)}) collective-permute-start(bf16[256,1024]{1,0:T(8,128)(2,1)} %get-tuple-element.29), channel_id=1, source_target_pairs={{0,2},{1,3},{2,0},{3,1},{4,6},{5,7},{6,4},{7,5},{8,10},{9,11},{10,... | collective-permute-start | bytes 1572872 | tf_op jit(solution)/shard_map/ppermute | solution.py:27
  8.3 1.3 collective-permute-start.7
  9.8 0.4 copy-done.14
  10.3 0.7 gather_fusion
  11.0 0.2 convert_reduce_fusion
  11.3 0.8 all_to_all.19
  12.1 12.0 %all-to-all-start = ((s32[64,1,2]{2,1,0:T(1,128)}), s32[64,1,2]{2,1,0:T(1,128)S(1)}, u32[]{:S(2)}, u32[]{:S(2)}) async-start(s32[64,1,2]{2,1,0:T(1,128)} %bitcast.2), calls=%async_computation | async-start | bytes 65536 | tf_op jit(solution)/shard_map/all_to_all | solution.py:80
  24.1 0.8 collective-permute-start
  24.9 0.5 compare_and_fusion.3
  25.4 0.6 fusion.47
  26.0 1.4 fusion.46
  27.5 5.2 %all-to-all-done = s32[64,1,2]{2,1,0:T(1,128)S(1)} async-done(((s32[64,1,2]{2,1,0:T(1,128)}), s32[64,1,2]{2,1,0:T(1,128)S(1)}, u32[]{:S(2)}, u32[]{:S(2)}) %all-to-all-start) | async-done | bytes 544 | tf_op jit(solution)/shard_map/all_to_all | solution.py:80
  33.1 0.2 copy-done.5
  33.3 0.8 gather_fusion.2
  34.1 1.7 maximum_select_fusion.1
  35.8 1.2 collective-permute-start.1
  37.0 0.9 broadcast_select_fusion.3
  37.9 12.2 %all-to-all-start.2 = ((bf16[64,2,3,256]{3,1,2,0:T(2,128)(2,1)}), bf16[64,2,3,256]{3,1,2,0:T(2,128)(2,1)}, u32[]{:S(2)}, u32[]{:S(2)}) async-start(bf16[64,2,3,256]{3,1,2,0:T(2,128)(2,1)} %broadcast_select_fusion.3), calls=%async_computation.2 | async-start | bytes 393216 | tf_op jit(solution)/shard_map/all_to_all | solution.py:83
  50.1 1.1 maximum_select_fusion
  51.2 2.0 %gather_fusion.1 = bf16[64,16,1024]{2,1,0:T(8,128)(2,1)} fusion(bf16[7,16,1024]{2,1,0:T(8,128)(2,1)S(1)} %maximum_select_fusion, s32[1024]{0:T(1024)S(1)} %pad_clamp_fusion.3), kind=kCustom, calls=%fused_computation.3 | custom fusion | bytes 4194560 | tf_op jit(solution)/shard_map/jit(_take)/gather | solution.py:94
  53.3 3.2 %broadcast_select_fusion.2 = bf16[64,16,1024]{2,1,0:T(8,128)(2,1)} fusion(bf16[64,16,1024]{2,1,0:T(8,128)(2,1)} %gather_fusion.1, pred[64]{0:T(512)(128)(4,1)S(1)} %copy-done.18), kind=kLoop, calls=%fused_computation.24 | loop fusion | flops 1048576 | bytes 4194368 | tf_op jit(solution)/shard_map/jit(_take)/select_n | solution.py:94
  56.4 4.4 %all-to-all-done.2 = bf16[64,2,3,256]{3,1,2,0:T(2,128)(2,1)} async-done(((bf16[64,2,3,256]{3,1,2,0:T(2,128)(2,1)}), bf16[64,2,3,256]{3,1,2,0:T(2,128)(2,1)}, u32[]{:S(2)}, u32[]{:S(2)}) %all-to-all-start.2) | async-done | bytes 196640 | tf_op jit(solution)/shard_map/all_to_all | solution.py:83
  60.9 6.5 %all-to-all-start.1 = ((bf16[64,16,1024]{2,1,0:T(8,128)(2,1)}), bf16[64,16,1024]{2,1,0:T(8,128)(2,1)}, u32[]{:S(2)}, u32[]{:S(2)}) async-start(bf16[64,16,1024]{2,1,0:T(8,128)(2,1)} %broadcast_select_fusion.2), calls=%async_computation.1 | async-start | bytes 4194304 | tf_op jit(solution)/shard_map/all_to_all | solution.py:95
  67.4 2.9 %dynamic-slice_bitcast_fusion.1 = (bf16[1,256,1024]{2,1,0:T(8,128)(2,1)}, bf16[256,1024]{1,0:T(8,128)(2,1)}, bf16[256,1024]{1,0:T(8,128)(2,1)}, bf16[256,1024]{1,0:T(8,128)(2,1)}) fusion(bf16[256,4096]{1,0:T(8,128)(2,1)} %param.14, s32[]{:T(128)S(6)} %select_n.258, s32[]{:T(128)S(6)} %select_n.260, s32[]{:T(128)S(6)} %select_n.264, s32[]{:T(128)S(6)} %select_n.262), kind=kLoop, calls=%fused_computation.28 | loop fusion | bytes 4194320 | tf_op jit(solution)/shard_map/stack | solution.py:28
  70.3 2.0 %collective-permute-start.2 = (bf16[256,1024]{1,0:T(8,128)(2,1)}, bf16[256,1024]{1,0:T(8,128)(2,1)}, u32[]{:S(2)}, u32[]{:S(2)}) collective-permute-start(bf16[256,1024]{1,0:T(8,128)(2,1)} %get-tuple-element.23), channel_id=1, source_target_pairs={{0,1},{1,2},{2,3},{3,0},{4,5},{5,6},{6,7},{7,4},{8,9},{9,10},{10,1... | collective-permute-start | bytes 1572872 | tf_op jit(solution)/shard_map/ppermute | solution.py:27
  72.6 0.7 collective-permute-start.3
  73.3 0.5 tile.4
  73.9 1.8 copy.91
  75.7 1.0 copy.75
  76.7 0.6 gather_fusion.3
  77.3 0.9 fusion.20
  78.4 3.0 %pad_maximum_fusion.1 = bf16[4,256,1024]{2,1,0:T(8,128)(2,1)} fusion(bf16[1,256,1024]{2,1,0:T(8,128)(2,1)} %bitcast.28, bf16[1,256,1024]{2,1,0:T(8,128)(2,1)} %bitcast.27, bf16[1,256,1024]{2,1,0:T(8,128)(2,1)} %bitcast.26, bf16[1,256,1024]{2,1,0:T(8,128)(2,1)S(1)} %copy-done.3), kind=kLoop, calls=%fused_computation.14 | loop fusion | flops 3145728 | bytes 4194304 | tf_op jit(solution)/shard_map/stack | solution.py:28
  81.3 3.6 %gather_fusion.5 = bf16[4,256,1024]{2,1,0:T(8,128)(2,1)} fusion(bf16[4,256,1024]{2,1,0:T(8,128)(2,1)} %pad_maximum_fusion.1, s32[1024]{0:T(1024)S(1)} %pad_clamp_fusion.2), kind=kCustom, calls=%fused_computation.1.clone | custom fusion | bytes 4194320 | tf_op jit(solution)/shard_map/jit(_take)/gather | solution.py:30
  84.9 0.5 collective-permute-done.4
  85.4 11.6 %collective-permute-done.2 = bf16[256,1024]{1,0:T(8,128)(2,1)} collective-permute-done((bf16[256,1024]{1,0:T(8,128)(2,1)}, bf16[256,1024]{1,0:T(8,128)(2,1)}, u32[]{:S(2)}, u32[]{:S(2)}) %collective-permute-start.2) | collective-permute-done | bytes 524320 | tf_op jit(solution)/shard_map/ppermute | solution.py:27
  97.0 3.1 %pad_maximum_fusion = bf16[4,256,1024]{2,1,0:T(8,128)(2,1)} fusion(bf16[1,256,1024]{2,1,0:T(8,128)(2,1)} %bitcast.10, bf16[1,256,1024]{2,1,0:T(8,128)(2,1)} %bitcast.9, bf16[1,256,1024]{2,1,0:T(8,128)(2,1)} %bitcast.8, bf16[1,256,1024]{2,1,0:T(8,128)(2,1)} %get-tuple-element.22), kind=kLoop, calls=%fused_computation.13 | loop fusion | flops 3145728 | bytes 4194304 | tf_op jit(solution)/shard_map/stack | solution.py:28
  100.2 3.6 %gather_fusion.4 = bf16[4,256,1024]{2,1,0:T(8,128)(2,1)} fusion(bf16[4,256,1024]{2,1,0:T(8,128)(2,1)} %pad_maximum_fusion, s32[1024]{0:T(1024)S(1)} %pad_clamp_fusion.2), kind=kCustom, calls=%fused_computation.clone | custom fusion | bytes 4194320 | tf_op jit(solution)/shard_map/jit(_take)/gather | solution.py:30
  103.8 4.0 %broadcast_select_fusion.1 = (bf16[4,256,1024]{2,1,0:T(8,128)(2,1)S(1)}, bf16[4,256,1024]{2,1,0:T(8,128)(2,1)}) fusion(bf16[4,256,1024]{2,1,0:T(8,128)(2,1)} %gather_fusion.4, pred[4]{0:T(512)(128)(4,1)S(1)} %compare_and_fusion, bf16[4,256,1024]{2,1,0:T(8,128)(2,1)} %gather_fusion.5), kind=kLoop, calls=%fused_computation.23 | loop fusion | flops 2097152 | bytes 8388612 | tf_op jit(solution)/shard_map/jit(_take)/select_n | solution.py:30
  107.8 2.6 %bitcast_convert_fusion.1 = f32[1024,1024]{1,0:T(8,128)} fusion(bf16[4,256,1024]{2,1,0:T(8,128)(2,1)S(1)} %get-tuple-element.30), kind=kLoop, calls=%fused_computation.16 | loop fusion | flops 1048576 | bytes 6291456 | tf_op jit(solution)/shard_map/convert_element_type | solution.py:102
  110.4 5.4 %copy.88 = f32[1024,1024]{0,1:T(8,128)} copy(f32[1024,1024]{1,0:T(8,128)} %bitcast_convert_fusion.1) | data formatting | bytes 8388608 | tf_op jit(solution)/shard_map/convert_element_type | solution.py:102
  115.8 4.1 %bitcast_convert_fusion = f32[1024,1024]{1,0:T(8,128)} fusion(bf16[4,256,1024]{2,1,0:T(8,128)(2,1)} %get-tuple-element.31), kind=kLoop, calls=%fused_computation.15 | loop fusion | flops 1048576 | bytes 6291456 | tf_op jit(solution)/shard_map/convert_element_type | solution.py:98
  119.9 5.4 %copy.89 = f32[1024,1024]{0,1:T(8,128)} copy(f32[1024,1024]{1,0:T(8,128)} %bitcast_convert_fusion) | data formatting | bytes 8388608 | tf_op jit(solution)/shard_map/convert_element_type | solution.py:98
  125.2 6.2 %fusion.1 = bf16[1024,1024]{0,1:T(8,128)(2,1)S(1)} fusion(f32[1024,1024]{0,1:T(8,128)} %copy.89, f32[1024,1024]{0,1:T(8,128)} %copy.88, f32[3,1024]{1,0:T(4,128)S(1)} %bitcast.115, f32[3,1024]{1,0:T(4,128)S(1)} %copy-done.8), kind=kOutput, calls=%fused_computation.8 | convolution fusion | flops 40894464 | bytes 10510336 | tf_op jit(solution)/shard_map/jd,js->ds/dot_general | solution.py:101
  131.5 4.0 %fusion.17 = bf16[1024,1024]{1,0:T(8,128)(2,1)} fusion(bf16[1024,1024]{0,1:T(8,128)(2,1)S(1)} %fusion.1, bf16[1024,1024]{1,0:T(8,128)(2,1)S(1)} %bitcast.108, s32[1024]{0:T(1024)S(1)} %add_select_fusion), kind=kOutput, calls=%fused_computation.26 | convolution fusion | flops 2149580800 | bytes 6295552 | tf_op jit(solution)/shard_map/dot_general | solution.py:106
  135.5 8.8 %fusion.6 = bf16[1024,1024]{0,1:T(8,128)(2,1)} fusion(bf16[1024,1024]{1,0:T(8,128)(2,1)} %bitcast.6, bf16[1024,1024]{1,0:T(8,128)(2,1)} %fusion.17, bf16[1024,1024]{1,0:T(8,128)(2,1)} %bitcast.107, s32[1024]{0:T(1024)S(1)} %add_select_fusion), kind=kOutput, calls=%fused_computation.18 | convolution fusion | flops 4298113024 | bytes 8392704 | tf_op jit(solution)/shard_map/dot_general | solution.py:108
  144.3 6.7 %fusion.10 = bf16[1024,3]{0,1:T(4,128)(2,1)S(1)} fusion(f32[3,1024]{1,0:T(4,128)S(1)} %copy-done.8, f32[1024,1024]{0,1:T(8,128)} %copy.89, bf16[1024,1024]{0,1:T(8,128)(2,1)} %fusion.6), kind=kOutput, calls=%fused_computation.25 | convolution fusion | flops 39848960 | bytes 6309888 | tf_op jit(solution)/shard_map/jd,ds->js/dot_general | solution.py:111
  151.0 0.5 fusion.48
  151.6 0.4 fusion.18
  152.1 1.1 copy.80
  153.1 10.4 %all-to-all-start.3 = ((f32[64,2,3,256]{3,1,2,0:T(2,128)}), f32[64,2,3,256]{3,1,2,0:T(2,128)S(1)}, u32[]{:S(2)}, u32[]{:S(2)}) async-start(f32[64,2,3,256]{3,1,2,0:T(2,128)} %copy.80), calls=%async_computation.3 | async-start | bytes 786432 | tf_op jit(solution)/shard_map/all_to_all | solution.py:121
  163.5 0.5 broadcast.545
  164.0 2.1 %reduce.3 = s32[64,2]{1,0:T(8,128)} reduce(s32[64,1,2]{2,1,0:T(1,128)} %copy-done.5, s32[]{:T(128)} %broadcast.545), dimensions={1}, to_apply=%all_to_all.20.reduce_sub_computation.3 | reduce | bytes 1028 | tf_op jit(solution)/shard_map/all_to_all | solution.py:80
  166.1 0.9 eq.100
  167.0 11.2 %all-to-all-done.3 = f32[64,2,3,256]{3,1,2,0:T(2,128)S(1)} async-done(((f32[64,2,3,256]{3,1,2,0:T(2,128)}), f32[64,2,3,256]{3,1,2,0:T(2,128)S(1)}, u32[]{:S(2)}, u32[]{:S(2)}) %all-to-all-start.3) | async-done | bytes 393248 | tf_op jit(solution)/shard_map/all_to_all | solution.py:121
  178.4 0.8 copy.93
  179.2 1.1 copy.82
  180.4 0.3 fusion.27
  180.8 4.9 %collective-permute-done.8 = f32[32,3,256]{2,0,1:T(8,128)S(1)} collective-permute-done((f32[32,3,256]{2,0,1:T(8,128)S(1)}, f32[32,3,256]{2,0,1:T(8,128)S(1)}, u32[]{:S(2)}, u32[]{:S(2)}) %collective-permute-start.8) | collective-permute-done | bytes 98336 | tf_op jit(solution)/shard_map/ppermute | solution.py:37
  185.7 2.1 %collective-permute-start.9 = (f32[32,3,256]{2,0,1:T(8,128)S(1)}, f32[32,3,256]{2,0,1:T(8,128)S(1)}, u32[]{:S(2)}, u32[]{:S(2)}) collective-permute-start(f32[32,3,256]{2,0,1:T(8,128)S(1)} %add.237), channel_id=1, source_target_pairs={{0,2},{1,3},{2,0},{3,1},{4,6},{5,7},{6,4},{7,5},{8,10},{9,11},{10,... | collective-permute-start | bytes 294920 | tf_op jit(solution)/shard_map/ppermute | solution.py:37
  187.8 1.6 copy.83
  189.3 2.5 %collective-permute-done.9 = f32[32,3,256]{2,0,1:T(8,128)S(1)} collective-permute-done((f32[32,3,256]{2,0,1:T(8,128)S(1)}, f32[32,3,256]{2,0,1:T(8,128)S(1)}, u32[]{:S(2)}, u32[]{:S(2)}) %collective-permute-start.9) | collective-permute-done | bytes 98336 | tf_op jit(solution)/shard_map/ppermute | solution.py:37
  191.9 2.2 %multiply_add_fusion = (f32[32,3,256]{2,0,1:T(8,128)}, f32[32,3,256]{2,0,1:T(8,128)}) fusion(f32[32,3,256]{2,0,1:T(8,128)} %param.24, f32[]{:T(128)} %bitcast.40, f32[32,3,256]{2,0,1:T(8,128)S(1)} %add.237, f32[32,3,256]{2,0,1:T(8,128)S(1)} %collective-permute-done.9), kind=kLoop, calls=%fused_computation.34 | loop fusion | flops 98304 | bytes 491524 | tf_op jit(solution)/shard_map/add | solution.py:133
  (75 shorter events, 1.5 us)
Async XLA Ops:
  0.6 76.7 %copy-start = (bf16[4,6,256,256]{3,2,1,0:T(8,128)(2,1)S(1)}, bf16[4,6,256,256]{3,2,1,0:T(8,128)(2,1)}, u32[]{:S(2)}) copy-start(bf16[4,6,256,256]{3,2,1,0:T(8,128)(2,1)} %param.20) | copy-start | bytes 9437188
  0.7 9.0 %copy-start.10 = (s32[4,6]{1,0:T(4,128)S(1)}, s32[4,6]{1,0:T(4,128)}, u32[]{:S(2)}) copy-start(s32[4,6]{1,0:T(4,128)} %param.21) | copy-start | bytes 292
  0.7 9.6 %copy-start.1 = (s32[2048]{0:T(1024)S(1)}, s32[2048]{0:T(1024)}, u32[]{:S(2)}) copy-start(s32[2048]{0:T(1024)} %param.22) | copy-start | bytes 24580
  0.7 23.4 %copy-start.9 = (bf16[7,4,1024]{2,1,0:T(4,128)(2,1)S(1)}, bf16[7,4,1024]{2,1,0:T(4,128)(2,1)}, u32[]{:S(2)}) copy-start(bf16[7,4,1024]{2,1,0:T(4,128)(2,1)} %param.18) | copy-start | bytes 172036
  0.7 24.1 %copy-start.19 = (s32[64]{0:T(128)S(1)}, s32[64]{0:T(128)}, u32[]{:S(2)}) copy-start(s32[64]{0:T(128)} %param.19) | copy-start | bytes 772
  0.7 24.6 %copy-start.13 = (f32[2]{0:T(128)S(1)}, f32[2]{0:T(128)}, u32[]{:S(2)}) copy-start(f32[2]{0:T(128)} %param.25) | copy-start | bytes 28
  0.7 25.3 %copy-start.4 = (f32[32,3,256]{2,0,1:T(8,128)S(1)}, f32[32,3,256]{2,0,1:T(8,128)}, u32[]{:S(2)}) copy-start(f32[32,3,256]{2,0,1:T(8,128)} %param.24) | copy-start | bytes 294916
  0.8 25.3 %copy-start.7 = (f32[32,3,256]{2,0,1:T(8,128)S(1)}, f32[32,3,256]{2,0,1:T(8,128)}, u32[]{:S(2)}) copy-start(f32[32,3,256]{2,0,1:T(8,128)} %param.23) | copy-start | bytes 294916
  3.8 68.8 %collective-permute-start.5 = (bf16[256,1024]{1,0:T(8,128)(2,1)}, bf16[256,1024]{1,0:T(8,128)(2,1)}, u32[]{:S(2)}, u32[]{:S(2)}) collective-permute-start(bf16[256,1024]{1,0:T(8,128)(2,1)} %get-tuple-element.27), channel_id=1, source_target_pairs={{0,1},{1,2},{2,3},{3,0},{4,5},{5,6},{6,7},{7,4},{8,9},{9,10},{10,1... | collective-permute-start | bytes 1572872 | tf_op jit(solution)/shard_map/ppermute | solution.py:27
  5.4 72.9 %collective-permute-start.6 = (bf16[256,1024]{1,0:T(8,128)(2,1)}, bf16[256,1024]{1,0:T(8,128)(2,1)}, u32[]{:S(2)}, u32[]{:S(2)}) collective-permute-start(bf16[256,1024]{1,0:T(8,128)(2,1)} %get-tuple-element.29), channel_id=1, source_target_pairs={{0,2},{1,3},{2,0},{3,1},{4,6},{5,7},{6,4},{7,5},{8,10},{9,11},{10,... | collective-permute-start | bytes 1572872 | tf_op jit(solution)/shard_map/ppermute | solution.py:27
  8.3 70.0 %collective-permute-start.7 = (bf16[256,1024]{1,0:T(8,128)(2,1)}, bf16[256,1024]{1,0:T(8,128)(2,1)}, u32[]{:S(2)}, u32[]{:S(2)}) collective-permute-start(bf16[256,1024]{1,0:T(8,128)(2,1)} %get-tuple-element.28), channel_id=1, source_target_pairs={{0,3},{1,0},{2,1},{3,2},{4,7},{5,4},{6,5},{7,6},{8,11},{9,8},{10,9... | collective-permute-start | bytes 1572872 | tf_op jit(solution)/shard_map/ppermute | solution.py:27
  9.7 0.5 copy-start.14
  11.2 21.7 %copy-start.11 = (s32[24]{0:T(128)}, s32[24]{0:T(128)S(1)}, u32[]{:S(2)}) copy-start(s32[24]{0:T(128)S(1)} %convert_reduce_fusion) | copy-start | bytes 292
  11.2 0.9 copy-start.16
  12.1 20.6 %all-to-all-start = ((s32[64,1,2]{2,1,0:T(1,128)}), s32[64,1,2]{2,1,0:T(1,128)S(1)}, u32[]{:S(2)}, u32[]{:S(2)}) async-start(s32[64,1,2]{2,1,0:T(1,128)} %bitcast.2), calls=%async_computation | async-start | bytes 65536 | tf_op jit(solution)/shard_map/all_to_all | solution.py:80
  24.1 10.0 %collective-permute-start = (bf16[7,4,1024]{2,1,0:T(4,128)(2,1)S(1)}, bf16[7,4,1024]{2,1,0:T(4,128)(2,1)}, u32[]{:S(2)}, u32[]{:S(2)}) collective-permute-start(bf16[7,4,1024]{2,1,0:T(4,128)(2,1)S(1)} %copy-done.9), channel_id=1, source_target_pairs={{0,1},{1,0},{2,3},{3,2},{4,5},{5,4},{6,7},{7,6},{8,9},{9,8},{10,11... | collective-permute-start | bytes 172040 | tf_op jit(solution)/shard_map/ppermute | solution.py:12
  32.6 0.6 copy-start.5
  35.8 14.3 %collective-permute-start.1 = (bf16[7,8,1024]{2,1,0:T(8,128)(2,1)}, bf16[7,8,1024]{2,1,0:T(8,128)(2,1)}, u32[]{:S(2)}, u32[]{:S(2)}) collective-permute-start(bf16[7,8,1024]{2,1,0:T(8,128)(2,1)} %maximum_select_fusion.1), channel_id=1, source_target_pairs={{0,2},{1,3},{2,0},{3,1},{4,6},{5,7},{6,4},{7,5},{8,10},{9,11},{10,... | collective-permute-start | bytes 344072 | tf_op jit(solution)/shard_map/ppermute | solution.py:12
  37.9 23.0 %all-to-all-start.2 = ((bf16[64,2,3,256]{3,1,2,0:T(2,128)(2,1)}), bf16[64,2,3,256]{3,1,2,0:T(2,128)(2,1)}, u32[]{:S(2)}, u32[]{:S(2)}) async-start(bf16[64,2,3,256]{3,1,2,0:T(2,128)(2,1)} %broadcast_select_fusion.3), calls=%async_computation.2 | async-start | bytes 393216 | tf_op jit(solution)/shard_map/all_to_all | solution.py:83
  51.2 2.0 %copy-start.18 = (pred[64]{0:T(512)(128)(4,1)S(1)}, pred[64]{0:T(512)(128)(4,1)}, u32[]{:S(2)}) copy-start(pred[64]{0:T(512)(128)(4,1)} %compare_and_fusion.3) | copy-start | bytes 196
  60.9 74.6 %all-to-all-start.1 = ((bf16[64,16,1024]{2,1,0:T(8,128)(2,1)}), bf16[64,16,1024]{2,1,0:T(8,128)(2,1)}, u32[]{:S(2)}, u32[]{:S(2)}) async-start(bf16[64,16,1024]{2,1,0:T(8,128)(2,1)} %broadcast_select_fusion.2), calls=%async_computation.1 | async-start | bytes 4194304 | tf_op jit(solution)/shard_map/all_to_all | solution.py:95
  67.4 5.0 %copy-start.12 = (s32[24]{0:T(128)S(1)}, s32[24]{0:T(128)}, u32[]{:S(2)}) copy-start(s32[24]{0:T(128)} %copy-done.11) | copy-start | bytes 292
  67.4 5.2 %copy-start.15 = (s32[24,1]{0,1:T(1,128)S(1)}, s32[24,1]{0,1:T(1,128)}, u32[]{:S(2)}) copy-start(s32[24,1]{0,1:T(1,128)} %copy-done.14) | copy-start | bytes 292
  67.4 6.0 %copy-start.6 = (bf16[256,256]{1,0:T(8,128)(2,1)S(1)}, bf16[256,256]{1,0:T(8,128)(2,1)}, u32[]{:S(2)}) copy-start(bf16[256,256]{1,0:T(8,128)(2,1)} %param.17) | copy-start | bytes 393220
  70.3 15.1 %collective-permute-start.4 = (bf16[256,1024]{1,0:T(8,128)(2,1)}, bf16[256,1024]{1,0:T(8,128)(2,1)}, u32[]{:S(2)}, u32[]{:S(2)}) collective-permute-start(bf16[256,1024]{1,0:T(8,128)(2,1)} %get-tuple-element.24), channel_id=1, source_target_pairs={{0,3},{1,0},{2,1},{3,2},{4,7},{5,4},{6,5},{7,6},{8,11},{9,8},{10,9... | collective-permute-start | bytes 1572872 | tf_op jit(solution)/shard_map/ppermute | solution.py:27
  70.3 26.7 %collective-permute-start.2 = (bf16[256,1024]{1,0:T(8,128)(2,1)}, bf16[256,1024]{1,0:T(8,128)(2,1)}, u32[]{:S(2)}, u32[]{:S(2)}) collective-permute-start(bf16[256,1024]{1,0:T(8,128)(2,1)} %get-tuple-element.23), channel_id=1, source_target_pairs={{0,1},{1,2},{2,3},{3,0},{4,5},{5,6},{6,7},{7,4},{8,9},{9,10},{10,1... | collective-permute-start | bytes 1572872 | tf_op jit(solution)/shard_map/ppermute | solution.py:27
  72.6 24.4 %collective-permute-start.3 = (bf16[256,1024]{1,0:T(8,128)(2,1)}, bf16[256,1024]{1,0:T(8,128)(2,1)}, u32[]{:S(2)}, u32[]{:S(2)}) collective-permute-start(bf16[256,1024]{1,0:T(8,128)(2,1)} %get-tuple-element.25), channel_id=1, source_target_pairs={{0,2},{1,3},{2,0},{3,1},{4,6},{5,7},{6,4},{7,5},{8,10},{9,11},{10,... | collective-permute-start | bytes 1572872 | tf_op jit(solution)/shard_map/ppermute | solution.py:27
  77.3 1.0 copy-start.3
  119.9 5.4 %copy-start.8 = (f32[3,1024]{1,0:T(4,128)S(1)}, f32[3,1024]{1,0:T(4,128)}, u32[]{:S(2)}) copy-start(f32[3,1024]{1,0:T(4,128)} %param.16) | copy-start | bytes 36868
  125.2 6.2 %copy-start.2 = (bf16[128,8,4,256]{3,1,2,0:T(8,128)(2,1)S(1)}, bf16[128,8,4,256]{3,1,2,0:T(8,128)(2,1)}, u32[]{:S(2)}) copy-start(bf16[128,8,4,256]{3,1,2,0:T(8,128)(2,1)} %copy.91) | copy-start | bytes 6291460
  150.9 0.7 copy-start.17
  153.1 25.1 %all-to-all-start.3 = ((f32[64,2,3,256]{3,1,2,0:T(2,128)}), f32[64,2,3,256]{3,1,2,0:T(2,128)S(1)}, u32[]{:S(2)}, u32[]{:S(2)}) async-start(f32[64,2,3,256]{3,1,2,0:T(2,128)} %copy.80), calls=%async_computation.3 | async-start | bytes 786432 | tf_op jit(solution)/shard_map/all_to_all | solution.py:121
  180.7 5.0 %collective-permute-start.8 = (f32[32,3,256]{2,0,1:T(8,128)S(1)}, f32[32,3,256]{2,0,1:T(8,128)S(1)}, u32[]{:S(2)}, u32[]{:S(2)}) collective-permute-start(f32[32,3,256]{2,0,1:T(8,128)S(1)} %fusion.27), channel_id=1, source_target_pairs={{0,1},{1,0},{2,3},{3,2},{4,5},{5,4},{6,7},{7,6},{8,9},{9,8},{10,11... | collective-permute-start | bytes 294920 | tf_op jit(solution)/shard_map/ppermute | solution.py:37
  185.7 6.2 %collective-permute-start.9 = (f32[32,3,256]{2,0,1:T(8,128)S(1)}, f32[32,3,256]{2,0,1:T(8,128)S(1)}, u32[]{:S(2)}, u32[]{:S(2)}) collective-permute-start(f32[32,3,256]{2,0,1:T(8,128)S(1)} %add.237), channel_id=1, source_target_pairs={{0,2},{1,3},{2,0},{3,1},{4,6},{5,7},{6,4},{7,5},{8,10},{9,11},{10,... | collective-permute-start | bytes 294920 | tf_op jit(solution)/shard_map/ppermute | solution.py:37

commit v4 on v3

--- a/solution.py
+++ b/solution.py
@@ -25,9 +25,12 @@
         target = (spot + shift) % size
         piece = lax.dynamic_slice_in_dim(x, target * width, width, 1)
         pieces.append(lax.ppermute(piece, "wafer", [(i, (i + shift) % size) for i in range(size)]))
-    stacked = jnp.stack(pieces)
-    order = (spot - jnp.arange(size, dtype=jnp.int32)) % size
-    return jnp.take(stacked, order, axis=0).reshape(size * x.shape[0], width)
+    rows = x.shape[0]
+    placed = jnp.zeros((size, rows, width), x.dtype)
+    for shift, piece in enumerate(pieces):
+        source = (spot - shift) % size
+        placed = lax.dynamic_update_slice_in_dim(placed, piece[None], source, 0)
+    return placed.reshape(size * rows, width)
 
 
 def wafer_sum(x):
@@ -98,7 +101,7 @@
     column_weights = wafer_columns(sample_weight).astype(jnp.float32)
     width = spans_here * samples
     parts_flat = jnp.transpose(signal_parts, (1, 0, 2)).reshape(comp_count, width)
-    signal = jnp.einsum("jd,js->ds", response, parts_flat, precision=precise_mode)
+    signal = sum(response[j][:, None] * parts_flat[j][None, :] for j in range(comp_count))
     errors = ((columns.astype(jnp.float32) - signal) * column_weights).astype(jnp.bfloat16)
     block_id = jnp.arange(width, dtype=jnp.int32) // samples
     same_span = block_id[:, None] == block_id[None, :]
@@ -108,9 +111,8 @@
     smoothed = lax.dot_general(
         whitened, filter_blocks, (((1,), (1,)), ((), ())), preferred_element_type=jnp.float32
     ).astype(jnp.bfloat16)
-    stokes = jnp.einsum(
-        "jd,ds->js", response, smoothed.astype(jnp.float32) * column_weights, precision=precise_mode
-    )
+    weighted = smoothed.astype(jnp.float32) * column_weights
+    stokes = jnp.stack([jnp.sum(response[j][:, None] * weighted, axis=0) for j in range(comp_count)])
     stokes_short = jnp.transpose(stokes.reshape(comp_count, spans_here, samples), (1, 0, 2)).astype(jnp.bfloat16)
     partial_value = jnp.einsum(
         "cjt,cktp->ckjp", stokes_short, pointing, preferred_element_type=jnp.float32

time: 195 us -> 176 us (0.903)
  matrix products: 27.9 us -> 14.3 us
  other arithmetic: 30.3 us -> 22.8 us
  starting transfers between devices: 53.7 us -> 56.7 us
  waiting for transfers between devices: 40.3 us -> 37.8 us
    dynamic_update_slice x0 -> x8, local copies, waits for them, and re-layouts: none -> 14 us  [wafer_columns(): placed = lax.dynamic_update_slice_in_dim(placed, piece[None], source, 0)]
    dot_general x2 -> x0, matrix products: 12.9 us -> none  [the longest x1 6.67 us: shards(): jnp.einsum('jd,ds->js', response, smoothed.astype(jnp.float32) * column_w...]
    all_to_all x1, waiting for transfers between devices: 0.01 us -> 11.5 us  [shards(): lax.all_to_all(sent_blocks, 'tm', split_axis=0, concat_axis=0, tiled=True)]
    convert_element_type x2 -> x0, local copies, waits for them, and re-layouts: 10.8 us -> none  [the longest x1 5.45 us: shards(): columns.astype(jnp.float32) - signal]
    ppermute x6, waiting for transfers between devices: 12.1 us -> 2.05 us  [wafer_columns(): lax.ppermute(piece, 'wafer', [(i, (i + shift) % size) for i in range(size)])]
    gather x2 -> x0, local copies, waits for them, and re-layouts: 7.25 us -> none  [wafer_columns(): return jnp.take(stacked, order, axis=0).reshape(size * x.shape[0], width)]
    another operation x2 -> x0, other arithmetic: 6.07 us -> none  [wafer_columns(): stacked = jnp.stack(pieces)]
    all_to_all x1, waiting for transfers between devices: 5.19 us -> 0.01 us  [shards(): lax.all_to_all(requests, 'tm', split_axis=0, concat_axis=0, tiled=True)]
  transfers between devices with their start and end apart: 14 -> 14, of which waited for: 7 -> 7; matrix products, arithmetic and copies ran while one was open for 37% -> 34% of each run, Pallas kernels for 0% -> 0%
where the time goes in v4:
time: 176 us; the launch traced here: 174 us
  starting transfers between devices  56.7 us (32%)
  local copies, waits for them, and re-layouts  41.6 us (24%)
  waiting for transfers between devices  37.8 us (21%)
  other arithmetic  22.8 us (13%)
  matrix products  14.3 us (8%)
    dynamic_update_slice x8, local copies, waits for them, and re-layouts, wafer_columns(): placed = lax.dynamic_update_slice_in_dim(placed, piece[None], source, 0)  14 us
    all_to_all x1, starting transfers between devices, shards(): lax.all_to_all(served, 'tm', split_axis=0, concat_axis=0, tiled=True)  12.2 us
    all_to_all x1, starting transfers between devices, shards(): lax.all_to_all(requests, 'tm', split_axis=0, concat_axis=0, tiled=True)  12 us
    all_to_all x1, waiting for transfers between devices, shards(): lax.all_to_all(sent_blocks, 'tm', split_axis=0, concat_axis=0, tiled=True)  11.5 us
    ppermute x6, starting transfers between devices, wafer_columns(): lax.ppermute(piece, 'wafer', [(i, (i + shift) % size) for i in range(size)])  11.4 us
    all_to_all x1, waiting for transfers between devices, shards(): lax.all_to_all(outgoing, 'tm', split_axis=0, concat_axis=0, tiled=True)  11.2 us
    dot_general x1, matrix products, shards(): lax.dot_general(whitened, filter_blocks, (((1,), (1,)), ((), ())), prefer...  8.42 us
    unnamed x44, local copies, waits for them, and re-layouts  7.99 us
  transfers between devices with their start and end apart: 14, of which 7 were waited for; matrix products, arithmetic and copies ran while one was open for 34% of the time, Pallas kernels for 0%

profile of v4, /device:TPU:2, one launch (start us, length us, event | category | flops | bytes accessed | tf_op | source)
XLA Modules:
  0.0 174.4 jit_solution(5402493257210464654)
XLA Ops:
  0.7 2.7 %constant_dynamic-slice_fusion.3 = (bf16[256,1024]{1,0:T(8,128)(2,1)}, bf16[256,1024]{1,0:T(8,128)(2,1)}, bf16[256,1024]{1,0:T(8,128)(2,1)}) fusion(bf16[256,4096]{1,0:T(8,128)(2,1)} %param.12, s32[]{:T(128)S(6)} %select_n.310, s32[]{:T(128)S(6)} %select_n.302, s32[]{:T(128)S(6)} %select_n.306), kind=kLoop, calls=%fused_computation.79 | loop fusion | bytes 3145740 | tf_op jit(solution)/shard_map/dynamic_slice | solution.py:26
  3.5 1.7 collective-permute-start.2
  5.1 2.9 %collective-permute-start.3 = (bf16[256,1024]{1,0:T(8,128)(2,1)}, bf16[256,1024]{1,0:T(8,128)(2,1)}, u32[]{:S(2)}, u32[]{:S(2)}) collective-permute-start(bf16[256,1024]{1,0:T(8,128)(2,1)} %get-tuple-element.32), channel_id=1, source_target_pairs={{0,2},{1,3},{2,0},{3,1},{4,6},{5,7},{6,4},{7,5},{8,10},{9,11},{10,... | collective-permute-start | bytes 1572872 | tf_op jit(solution)/shard_map/ppermute | solution.py:27
  8.0 1.3 collective-permute-start.4
  9.4 1.2 constant_dynamic-slice_fusion
  10.6 0.7 collective-permute-start.5
  11.4 0.7 gather_fusion
  12.5 0.8 all_to_all.19
  13.2 12.0 %all-to-all-start = ((s32[64,1,2]{2,1,0:T(1,128)}), s32[64,1,2]{2,1,0:T(1,128)S(1)}, u32[]{:S(2)}, u32[]{:S(2)}) async-start(s32[64,1,2]{2,1,0:T(1,128)} %bitcast.2), calls=%async_computation | async-start | bytes 65536 | tf_op jit(solution)/shard_map/all_to_all | solution.py:83
  25.4 0.5 fusion.38
  25.9 0.6 compare_and_fusion.2
  26.5 0.6 add_select_fusion
  27.1 0.6 fusion.45
  27.8 1.6 broadcast.577.clone.1
  29.4 1.9 %bitcast_dynamic-update-slice_fusion.7 = bf16[4,256,1024]{2,1,0:T(8,128)(2,1)} fusion(bf16[4,256,1024]{2,1,0:T(8,128)(2,1)} %broadcast.577.clone.1, s32[]{:T(128)S(6)} %select_n.300, bf16[256,4096]{1,0:T(8,128)(2,1)} %param.12, s32[]{:T(128)S(6)} %select_n.298), kind=kLoop, calls=%fused_computation.27 | loop fusion | bytes 1048584 | tf_op jit(solution)/shard_map/dynamic_update_slice | solution.py:32
  31.2 1.4 fusion.43
  32.7 0.6 pad_clamp_fusion.2
  33.3 0.7 gather.24
  34.6 0.8 gather_fusion.2
  35.5 4.8 %collective-permute-done = bf16[7,4,1024]{2,1,0:T(4,128)(2,1)} collective-permute-done((bf16[7,4,1024]{2,1,0:T(4,128)(2,1)S(1)}, bf16[7,4,1024]{2,1,0:T(4,128)(2,1)}, u32[]{:S(2)}, u32[]{:S(2)}) %collective-permute-start) | collective-permute-done | bytes 57376 | tf_op jit(solution)/shard_map/ppermute | solution.py:12
  40.3 1.7 maximum_select_fusion.1
  41.9 2.9 %collective-permute-start.1 = (bf16[7,8,1024]{2,1,0:T(8,128)(2,1)}, bf16[7,8,1024]{2,1,0:T(8,128)(2,1)}, u32[]{:S(2)}, u32[]{:S(2)}) collective-permute-start(bf16[7,8,1024]{2,1,0:T(8,128)(2,1)} %maximum_select_fusion.1), channel_id=1, source_target_pairs={{0,2},{1,3},{2,0},{3,1},{4,6},{5,7},{6,4},{7,5},{8,10},{9,11},{10,... | collective-permute-start | bytes 344072 | tf_op jit(solution)/shard_map/ppermute | solution.py:12
  44.8 0.9 broadcast_select_fusion.1
  45.8 12.2 %all-to-all-start.2 = ((bf16[64,2,3,256]{3,1,2,0:T(2,128)(2,1)}), bf16[64,2,3,256]{3,1,2,0:T(2,128)(2,1)}, u32[]{:S(2)}, u32[]{:S(2)}) async-start(bf16[64,2,3,256]{3,1,2,0:T(2,128)(2,1)} %broadcast_select_fusion.1), calls=%async_computation.2 | async-start | bytes 393216 | tf_op jit(solution)/shard_map/all_to_all | solution.py:86
  58.0 0.7 collective-permute-start.6
  58.7 1.1 maximum_select_fusion
  59.8 2.2 %gather_fusion.1 = bf16[64,16,1024]{2,1,0:T(8,128)(2,1)} fusion(bf16[7,16,1024]{2,1,0:T(8,128)(2,1)S(1)} %maximum_select_fusion, s32[1024]{0:T(1024)} %pad_clamp_fusion.2), kind=kCustom, calls=%fused_computation.1 | custom fusion | bytes 4194560 | tf_op jit(solution)/shard_map/jit(_take)/gather | solution.py:97
  62.0 3.2 %broadcast_select_fusion = bf16[64,16,1024]{2,1,0:T(8,128)(2,1)} fusion(bf16[64,16,1024]{2,1,0:T(8,128)(2,1)} %gather_fusion.1, pred[64]{0:T(512)(128)(4,1)S(1)} %copy-done.18), kind=kLoop, calls=%fused_computation.17 | loop fusion | flops 1048576 | bytes 4194368 | tf_op jit(solution)/shard_map/jit(_take)/select_n | solution.py:97
  65.3 3.5 %all-to-all-done.2 = bf16[64,2,3,256]{3,1,2,0:T(2,128)(2,1)} async-done(((bf16[64,2,3,256]{3,1,2,0:T(2,128)(2,1)}), bf16[64,2,3,256]{3,1,2,0:T(2,128)(2,1)}, u32[]{:S(2)}, u32[]{:S(2)}) %all-to-all-start.2) | async-done | bytes 196640 | tf_op jit(solution)/shard_map/all_to_all | solution.py:86
  68.7 7.0 %all-to-all-start.1 = ((bf16[64,16,1024]{2,1,0:T(8,128)(2,1)}), bf16[64,16,1024]{2,1,0:T(8,128)(2,1)}, u32[]{:S(2)}, u32[]{:S(2)}) async-start(bf16[64,16,1024]{2,1,0:T(8,128)(2,1)} %broadcast_select_fusion), calls=%async_computation.1 | async-start | bytes 4194304 | tf_op jit(solution)/shard_map/all_to_all | solution.py:98
  75.8 1.6 broadcast.577.clone
  77.5 1.9 %bitcast_dynamic-update-slice_fusion.3 = bf16[4,256,1024]{2,1,0:T(8,128)(2,1)} fusion(bf16[4,256,1024]{2,1,0:T(8,128)(2,1)} %broadcast.577.clone, s32[]{:T(128)S(6)} %select_n.300, bf16[256,4096]{1,0:T(8,128)(2,1)} %param.13, s32[]{:T(128)S(6)} %select_n.298), kind=kLoop, calls=%fused_computation.23 | loop fusion | bytes 1048584 | tf_op jit(solution)/shard_map/dynamic_update_slice | solution.py:32
  79.4 4.2 %compare_select_fusion.1 = bf16[4,256,4,256]{3,2,1,0:T(4,128)(2,1)} fusion(s32[4,256]{1,0:T(4,128)S(1)} %add_select_fusion.1, bf16[256,256]{1,0:T(8,128)(2,1)S(1)} %copy-done.5), kind=kLoop, calls=%fused_computation.10 | loop fusion | flops 2097152 | bytes 2232320 | tf_op jit(solution)/shard_map/jit(_where)/select_n | solution.py:108
  83.6 3.4 %copy.86 = bf16[128,8,4,256]{3,1,2,0:T(8,128)(2,1)} copy(bf16[128,8,4,256]{3,2,1,0:T(4,128)(2,1)} %bitcast.105) | data formatting | bytes 4194304
  87.1 0.5 tile.4
  87.6 1.8 %copy.87 = bf16[128,8,4,256]{3,1,2,0:T(8,128)(2,1)} copy(bf16[128,8,4,256]{3,2,1,0:T(4,128)(2,1)S(1)} %bitcast.106) | data formatting | bytes 4194304
  89.4 1.0 copy.73
  90.4 0.6 gather_fusion.3
  91.1 0.9 convolution_bitcast_fusion
  92.1 4.1 %collective-permute-start.7 = (bf16[256,1024]{1,0:T(8,128)(2,1)S(1)}, bf16[256,1024]{1,0:T(8,128)(2,1)S(1)}, u32[]{:S(2)}, u32[]{:S(2)}) collective-permute-start(bf16[256,1024]{1,0:T(8,128)(2,1)S(1)} %copy-done.4), channel_id=1, source_target_pairs={{0,3},{1,0},{2,1},{3,2},{4,7},{5,4},{6,5},{7,6},{8,11},{9,8},{10,9... | collective-permute-start | bytes 1572872 | tf_op jit(solution)/shard_map/ppermute | solution.py:27
  96.2 1.9 %bitcast_dynamic-update-slice_fusion.6 = bf16[4,256,1024]{2,1,0:T(8,128)(2,1)} fusion(bf16[4,256,1024]{2,1,0:T(8,128)(2,1)} %bitcast_dynamic-update-slice_fusion.7, s32[]{:T(128)S(6)} %select_n.304, bf16[256,1024]{1,0:T(8,128)(2,1)} %collective-permute-done.2), kind=kLoop, calls=%fused_computation.26 | loop fusion | bytes 1048580 | tf_op jit(solution)/shard_map/dynamic_update_slice | solution.py:32
  98.1 1.9 %bitcast_dynamic-update-slice_fusion.2 = bf16[4,256,1024]{2,1,0:T(8,128)(2,1)} fusion(bf16[4,256,1024]{2,1,0:T(8,128)(2,1)} %bitcast_dynamic-update-slice_fusion.3, s32[]{:T(128)S(6)} %select_n.304, bf16[256,1024]{1,0:T(8,128)(2,1)} %collective-permute-done.5), kind=kLoop, calls=%fused_computation.22 | loop fusion | bytes 1048580 | tf_op jit(solution)/shard_map/dynamic_update_slice | solution.py:32
  100.0 1.9 %bitcast_dynamic-update-slice_fusion.5 = bf16[4,256,1024]{2,1,0:T(8,128)(2,1)} fusion(bf16[4,256,1024]{2,1,0:T(8,128)(2,1)} %bitcast_dynamic-update-slice_fusion.6, s32[]{:T(128)S(6)} %select_n.308, bf16[256,1024]{1,0:T(8,128)(2,1)} %collective-permute-done.3), kind=kLoop, calls=%fused_computation.25 | loop fusion | bytes 1048580 | tf_op jit(solution)/shard_map/dynamic_update_slice | solution.py:32
  101.9 1.9 %bitcast_dynamic-update-slice_fusion.1 = bf16[4,256,1024]{2,1,0:T(8,128)(2,1)} fusion(bf16[4,256,1024]{2,1,0:T(8,128)(2,1)} %bitcast_dynamic-update-slice_fusion.2, s32[]{:T(128)S(6)} %select_n.308, bf16[256,1024]{1,0:T(8,128)(2,1)} %collective-permute-done.6), kind=kLoop, calls=%fused_computation.21 | loop fusion | bytes 1048580 | tf_op jit(solution)/shard_map/dynamic_update_slice | solution.py:32
  103.8 1.9 %bitcast_dynamic-update-slice_fusion.4 = bf16[4,256,1024]{2,1,0:T(8,128)(2,1)} fusion(bf16[4,256,1024]{2,1,0:T(8,128)(2,1)} %bitcast_dynamic-update-slice_fusion.5, s32[]{:T(128)S(6)} %select_n.312, bf16[256,1024]{1,0:T(8,128)(2,1)} %collective-permute-done.4), kind=kLoop, calls=%fused_computation.24 | loop fusion | bytes 1048580 | tf_op jit(solution)/shard_map/dynamic_update_slice | solution.py:32
  105.6 2.0 %collective-permute-done.7 = bf16[256,1024]{1,0:T(8,128)(2,1)S(1)} collective-permute-done((bf16[256,1024]{1,0:T(8,128)(2,1)S(1)}, bf16[256,1024]{1,0:T(8,128)(2,1)S(1)}, u32[]{:S(2)}, u32[]{:S(2)}) %collective-permute-start.7) | collective-permute-done | bytes 524320 | tf_op jit(solution)/shard_map/ppermute | solution.py:27
  107.7 0.8 bitcast_dynamic-update-slice_fusion
  108.5 3.2 %multiply_convert_fusion = bf16[4,256,1024]{2,1,0:T(8,128)(2,1)S(1)} fusion(bf16[4,256,1024]{2,1,0:T(8,128)(2,1)} %bitcast_dynamic-update-slice_fusion.4, f32[1024]{0:T(1024)S(1)} %bitcast.118, f32[4,256]{1,0:T(4,128)S(1)} %mul.166, f32[1024]{0:T(1024)S(1)} %bitcast.119, f32[4,256]{1,0:T(4,128)S(1)} %mul.161, f32[1024]{0:T(1024)S(1)} %bitcast.117, ...), kind=kLoop, calls=%fused_computation.8 | loop fusion | flops 10485760 | bytes 6316032 | tf_op jit(solution)/shard_map/convert_element_type | solution.py:105
  111.7 3.7 %fusion.46 = bf16[1024,1024]{1,0:T(8,128)(2,1)} fusion(bf16[1024,1024]{1,0:T(8,128)(2,1)S(1)} %bitcast.110, bf16[1024,1024]{1,0:T(8,128)(2,1)S(1)} %bitcast.109), kind=kOutput, calls=%fused_computation.129 | convolution fusion | flops 2147483648 | bytes 6291456 | tf_op jit(solution)/shard_map/dot_general | solution.py:109
  115.4 11.5 %all-to-all-done.1 = bf16[64,16,1024]{2,1,0:T(8,128)(2,1)} async-done(((bf16[64,16,1024]{2,1,0:T(8,128)(2,1)}), bf16[64,16,1024]{2,1,0:T(8,128)(2,1)}, u32[]{:S(2)}, u32[]{:S(2)}) %all-to-all-start.1) | async-done | bytes 2097184 | tf_op jit(solution)/shard_map/all_to_all | solution.py:98
  126.9 8.4 %multiply_reduce_fusion.2 = (bf16[1024]{0:T(1024)(128)(2,1)S(1)}, bf16[1024]{0:T(1024)(128)(2,1)S(1)}, bf16[1024]{0:T(1024)(128)(2,1)S(1)}) fusion(f32[1024]{0:T(1024)S(1)} %bitcast.122, f32[1024]{0:T(1024)S(1)} %bitcast.121, f32[1024]{0:T(1024)S(1)} %bitcast.120, bf16[4,256,1024]{2,1,0:T(8,128)(2,1)} %bitcast_dynamic-update-slice_fusion, ...), kind=kOutput, calls=%fused_computation.7 | convolution fusion | flops 4308595712 | bytes 8411136 | tf_op jit(solution)/shard_map/dot_general | solution.py:111
  136.4 1.1 copy.78
  137.5 5.4 %all-to-all-start.3 = ((f32[64,2,3,256]{3,1,2,0:T(2,128)}), f32[64,2,3,256]{3,1,2,0:T(2,128)S(1)}, u32[]{:S(2)}, u32[]{:S(2)}) async-start(f32[64,2,3,256]{3,1,2,0:T(2,128)} %copy.78), calls=%async_computation.3 | async-start | bytes 786432 | tf_op jit(solution)/shard_map/all_to_all | solution.py:123
  143.4 2.1 %reduce.15 = s32[64,2]{1,0:T(8,128)} reduce(s32[64,1,2]{2,1,0:T(1,128)} %copy-done.7, s32[]{:T(128)} %broadcast.620), dimensions={1}, to_apply=%all_to_all.20.reduce_sub_computation.3 | reduce | bytes 1028 | tf_op jit(solution)/shard_map/all_to_all | solution.py:83
  145.5 0.9 eq.118
  146.4 11.2 %all-to-all-done.3 = f32[64,2,3,256]{3,1,2,0:T(2,128)S(1)} async-done(((f32[64,2,3,256]{3,1,2,0:T(2,128)}), f32[64,2,3,256]{3,1,2,0:T(2,128)S(1)}, u32[]{:S(2)}, u32[]{:S(2)}) %all-to-all-start.3) | async-done | bytes 393248 | tf_op jit(solution)/shard_map/all_to_all | solution.py:123
  157.8 0.8 copy.89
  158.6 1.1 copy.80
  160.1 2.7 %collective-permute-start.8 = (f32[32,3,256]{2,0,1:T(8,128)S(1)}, f32[32,3,256]{2,0,1:T(8,128)S(1)}, u32[]{:S(2)}, u32[]{:S(2)}) collective-permute-start(f32[32,3,256]{2,0,1:T(8,128)S(1)} %fusion.19), channel_id=1, source_target_pairs={{0,1},{1,0},{2,3},{3,2},{4,5},{5,4},{6,7},{7,6},{8,9},{9,8},{10,11... | collective-permute-start | bytes 294920 | tf_op jit(solution)/shard_map/ppermute | solution.py:40
  162.7 3.2 %collective-permute-done.8 = f32[32,3,256]{2,0,1:T(8,128)S(1)} collective-permute-done((f32[32,3,256]{2,0,1:T(8,128)S(1)}, f32[32,3,256]{2,0,1:T(8,128)S(1)}, u32[]{:S(2)}, u32[]{:S(2)}) %collective-permute-start.8) | collective-permute-done | bytes 98336 | tf_op jit(solution)/shard_map/ppermute | solution.py:40
  165.9 3.0 %collective-permute-start.9 = (f32[32,3,256]{2,0,1:T(8,128)S(1)}, f32[32,3,256]{2,0,1:T(8,128)S(1)}, u32[]{:S(2)}, u32[]{:S(2)}) collective-permute-start(f32[32,3,256]{2,0,1:T(8,128)S(1)} %add.286), channel_id=1, source_target_pairs={{0,2},{1,3},{2,0},{3,1},{4,6},{5,7},{6,4},{7,5},{8,10},{9,11},{10,... | collective-permute-start | bytes 294920 | tf_op jit(solution)/shard_map/ppermute | solution.py:40
  168.9 1.6 copy.81
  170.4 1.7 collective-permute-done.9
  172.1 2.3 %multiply_add_fusion = (f32[32,3,256]{2,0,1:T(8,128)}, f32[32,3,256]{2,0,1:T(8,128)}) fusion(f32[32,3,256]{2,0,1:T(8,128)} %param.22, f32[]{:T(128)} %bitcast.43, f32[32,3,256]{2,0,1:T(8,128)S(1)} %add.286, f32[32,3,256]{2,0,1:T(8,128)S(1)} %collective-permute-done.9), kind=kLoop, calls=%fused_computation.33 | loop fusion | flops 98304 | bytes 491524 | tf_op jit(solution)/shard_map/add | solution.py:135
  (83 shorter events, 3.6 us)
Async XLA Ops:
  0.6 90.4 %copy-start = (bf16[4,6,256,256]{3,2,1,0:T(8,128)(2,1)S(1)}, bf16[4,6,256,256]{3,2,1,0:T(8,128)(2,1)}, u32[]{:S(2)}) copy-start(bf16[4,6,256,256]{3,2,1,0:T(8,128)(2,1)} %param.18) | copy-start | bytes 9437188
  0.7 8.7 %copy-start.2 = (bf16[256,4096]{1,0:T(8,128)(2,1)S(1)}, bf16[256,4096]{1,0:T(8,128)(2,1)}, u32[]{:S(2)}) copy-start(bf16[256,4096]{1,0:T(8,128)(2,1)} %param.13) | copy-start | bytes 6291460
  3.4 7.8 %copy-start.10 = (s32[4,6]{1,0:T(4,128)S(1)}, s32[4,6]{1,0:T(4,128)}, u32[]{:S(2)}) copy-start(s32[4,6]{1,0:T(4,128)} %param.19) | copy-start | bytes 292
  3.4 8.0 %copy-start.1 = (s32[2048]{0:T(1024)S(1)}, s32[2048]{0:T(1024)}, u32[]{:S(2)}) copy-start(s32[2048]{0:T(1024)} %param.20) | copy-start | bytes 24580
  3.5 21.8 %copy-start.9 = (bf16[7,4,1024]{2,1,0:T(4,128)(2,1)S(1)}, bf16[7,4,1024]{2,1,0:T(4,128)(2,1)}, u32[]{:S(2)}) copy-start(bf16[7,4,1024]{2,1,0:T(4,128)(2,1)} %param.16) | copy-start | bytes 172036
  3.5 22.5 %copy-start.19 = (s32[64]{0:T(128)S(1)}, s32[64]{0:T(128)}, u32[]{:S(2)}) copy-start(s32[64]{0:T(128)} %param.17) | copy-start | bytes 772
  3.5 23.7 %copy-start.14 = (f32[2]{0:T(128)S(1)}, f32[2]{0:T(128)}, u32[]{:S(2)}) copy-start(f32[2]{0:T(128)} %param.23) | copy-start | bytes 28
  3.5 88.6 %collective-permute-start.2 = (bf16[256,1024]{1,0:T(8,128)(2,1)}, bf16[256,1024]{1,0:T(8,128)(2,1)}, u32[]{:S(2)}, u32[]{:S(2)}) collective-permute-start(bf16[256,1024]{1,0:T(8,128)(2,1)} %get-tuple-element.31), channel_id=1, source_target_pairs={{0,1},{1,2},{2,3},{3,0},{4,5},{5,6},{6,7},{7,4},{8,9},{9,10},{10,1... | collective-permute-start | bytes 1572872 | tf_op jit(solution)/shard_map/ppermute | solution.py:27
  5.1 94.9 %collective-permute-start.3 = (bf16[256,1024]{1,0:T(8,128)(2,1)}, bf16[256,1024]{1,0:T(8,128)(2,1)}, u32[]{:S(2)}, u32[]{:S(2)}) collective-permute-start(bf16[256,1024]{1,0:T(8,128)(2,1)} %get-tuple-element.32), channel_id=1, source_target_pairs={{0,2},{1,3},{2,0},{3,1},{4,6},{5,7},{6,4},{7,5},{8,10},{9,11},{10,... | collective-permute-start | bytes 1572872 | tf_op jit(solution)/shard_map/ppermute | solution.py:27
  8.0 95.7 %collective-permute-start.4 = (bf16[256,1024]{1,0:T(8,128)(2,1)}, bf16[256,1024]{1,0:T(8,128)(2,1)}, u32[]{:S(2)}, u32[]{:S(2)}) collective-permute-start(bf16[256,1024]{1,0:T(8,128)(2,1)} %get-tuple-element.30), channel_id=1, source_target_pairs={{0,3},{1,0},{2,1},{3,2},{4,7},{5,4},{6,5},{7,6},{8,11},{9,8},{10,9... | collective-permute-start | bytes 1572872 | tf_op jit(solution)/shard_map/ppermute | solution.py:27
  10.6 20.7 %copy-start.6 = (f32[32,3,256]{2,0,1:T(8,128)S(1)}, f32[32,3,256]{2,0,1:T(8,128)}, u32[]{:S(2)}) copy-start(f32[32,3,256]{2,0,1:T(8,128)} %param.22) | copy-start | bytes 294916
  10.6 20.7 %copy-start.8 = (f32[32,3,256]{2,0,1:T(8,128)S(1)}, f32[32,3,256]{2,0,1:T(8,128)}, u32[]{:S(2)}) copy-start(f32[32,3,256]{2,0,1:T(8,128)} %param.21) | copy-start | bytes 294916
  10.6 87.5 %collective-permute-start.5 = (bf16[256,1024]{1,0:T(8,128)(2,1)}, bf16[256,1024]{1,0:T(8,128)(2,1)}, u32[]{:S(2)}, u32[]{:S(2)}) collective-permute-start(bf16[256,1024]{1,0:T(8,128)(2,1)} %get-tuple-element.28), channel_id=1, source_target_pairs={{0,1},{1,2},{2,3},{3,0},{4,5},{5,6},{6,7},{7,4},{8,9},{9,10},{10,1... | collective-permute-start | bytes 1572872 | tf_op jit(solution)/shard_map/ppermute | solution.py:27
  12.4 22.1 %copy-start.16 = (s32[24]{0:T(128)}, s32[24]{0:T(128)S(1)}, u32[]{:S(2)}) copy-start(s32[24]{0:T(128)S(1)} %get-tuple-element.42) | copy-start | bytes 292
  13.2 20.8 %all-to-all-start = ((s32[64,1,2]{2,1,0:T(1,128)}), s32[64,1,2]{2,1,0:T(1,128)S(1)}, u32[]{:S(2)}, u32[]{:S(2)}) async-start(s32[64,1,2]{2,1,0:T(1,128)} %bitcast.2), calls=%async_computation | async-start | bytes 65536 | tf_op jit(solution)/shard_map/all_to_all | solution.py:83
  25.3 15.0 %collective-permute-start = (bf16[7,4,1024]{2,1,0:T(4,128)(2,1)S(1)}, bf16[7,4,1024]{2,1,0:T(4,128)(2,1)}, u32[]{:S(2)}, u32[]{:S(2)}) collective-permute-start(bf16[7,4,1024]{2,1,0:T(4,128)(2,1)S(1)} %copy-done.9), channel_id=1, source_target_pairs={{0,1},{1,0},{2,3},{3,2},{4,5},{5,4},{6,7},{7,6},{8,9},{9,8},{10,11... | collective-permute-start | bytes 172040 | tf_op jit(solution)/shard_map/ppermute | solution.py:12
  34.0 0.6 copy-start.7
  41.9 16.0 %collective-permute-start.1 = (bf16[7,8,1024]{2,1,0:T(8,128)(2,1)}, bf16[7,8,1024]{2,1,0:T(8,128)(2,1)}, u32[]{:S(2)}, u32[]{:S(2)}) collective-permute-start(bf16[7,8,1024]{2,1,0:T(8,128)(2,1)} %maximum_select_fusion.1), channel_id=1, source_target_pairs={{0,2},{1,3},{2,0},{3,1},{4,6},{5,7},{6,4},{7,5},{8,10},{9,11},{10,... | collective-permute-start | bytes 344072 | tf_op jit(solution)/shard_map/ppermute | solution.py:12
  45.8 23.0 %all-to-all-start.2 = ((bf16[64,2,3,256]{3,1,2,0:T(2,128)(2,1)}), bf16[64,2,3,256]{3,1,2,0:T(2,128)(2,1)}, u32[]{:S(2)}, u32[]{:S(2)}) async-start(bf16[64,2,3,256]{3,1,2,0:T(2,128)(2,1)} %broadcast_select_fusion.1), calls=%async_computation.2 | async-start | bytes 393216 | tf_op jit(solution)/shard_map/all_to_all | solution.py:86
  58.0 43.9 %collective-permute-start.6 = (bf16[256,1024]{1,0:T(8,128)(2,1)}, bf16[256,1024]{1,0:T(8,128)(2,1)}, u32[]{:S(2)}, u32[]{:S(2)}) collective-permute-start(bf16[256,1024]{1,0:T(8,128)(2,1)} %get-tuple-element.29), channel_id=1, source_target_pairs={{0,2},{1,3},{2,0},{3,1},{4,6},{5,7},{6,4},{7,5},{8,10},{9,11},{10,... | collective-permute-start | bytes 1572872 | tf_op jit(solution)/shard_map/ppermute | solution.py:27
  59.8 2.2 %copy-start.18 = (pred[64]{0:T(512)(128)(4,1)S(1)}, pred[64]{0:T(512)(128)(4,1)}, u32[]{:S(2)}) copy-start(pred[64]{0:T(512)(128)(4,1)} %compare_and_fusion.2) | copy-start | bytes 196
  65.3 10.5 %copy-start.15 = (s32[24]{0:T(128)S(1)}, s32[24]{0:T(128)}, u32[]{:S(2)}) copy-start(s32[24]{0:T(128)} %fusion.38) | copy-start | bytes 292
  68.7 58.2 %all-to-all-start.1 = ((bf16[64,16,1024]{2,1,0:T(8,128)(2,1)}), bf16[64,16,1024]{2,1,0:T(8,128)(2,1)}, u32[]{:S(2)}, u32[]{:S(2)}) async-start(bf16[64,16,1024]{2,1,0:T(8,128)(2,1)} %broadcast_select_fusion), calls=%async_computation.1 | async-start | bytes 4194304 | tf_op jit(solution)/shard_map/all_to_all | solution.py:98
  75.8 3.5 %copy-start.12 = (s32[4,6]{1,0:T(4,128)S(1)}, s32[4,6]{1,0:T(4,128)}, u32[]{:S(2)}) copy-start(s32[4,6]{1,0:T(4,128)} %gather.24) | copy-start | bytes 292
  75.8 3.6 %copy-start.11 = (f32[3,1024]{1,0:T(4,128)S(1)}, f32[3,1024]{1,0:T(4,128)}, u32[]{:S(2)}) copy-start(f32[3,1024]{1,0:T(4,128)} %param.14) | copy-start | bytes 36868
  75.8 3.6 %copy-start.5 = (bf16[256,256]{1,0:T(8,128)(2,1)S(1)}, bf16[256,256]{1,0:T(8,128)(2,1)}, u32[]{:S(2)}) copy-start(bf16[256,256]{1,0:T(8,128)(2,1)} %param.15) | copy-start | bytes 393220
  91.0 1.0 copy-start.4
  92.1 15.6 %collective-permute-start.7 = (bf16[256,1024]{1,0:T(8,128)(2,1)S(1)}, bf16[256,1024]{1,0:T(8,128)(2,1)S(1)}, u32[]{:S(2)}, u32[]{:S(2)}) collective-permute-start(bf16[256,1024]{1,0:T(8,128)(2,1)S(1)} %copy-done.4), channel_id=1, source_target_pairs={{0,3},{1,0},{2,1},{3,2},{4,7},{5,4},{6,5},{7,6},{8,11},{9,8},{10,9... | collective-permute-start | bytes 1572872 | tf_op jit(solution)/shard_map/ppermute | solution.py:27
  108.5 3.2 %copy-start.3 = (bf16[128,8,4,256]{3,1,2,0:T(8,128)(2,1)S(1)}, bf16[128,8,4,256]{3,1,2,0:T(8,128)(2,1)}, u32[]{:S(2)}) copy-start(bf16[128,8,4,256]{3,1,2,0:T(8,128)(2,1)} %copy.86) | copy-start | bytes 6291460
  111.7 15.2 %copy-start.13 = (s32[1024]{0:T(1024)S(1)}, s32[1024]{0:T(1024)}, u32[]{:S(2)}) copy-start(s32[1024]{0:T(1024)} %add_select_fusion) | copy-start | bytes 12292
  135.3 0.6 copy-start.17
  137.5 20.2 %all-to-all-start.3 = ((f32[64,2,3,256]{3,1,2,0:T(2,128)}), f32[64,2,3,256]{3,1,2,0:T(2,128)S(1)}, u32[]{:S(2)}, u32[]{:S(2)}) async-start(f32[64,2,3,256]{3,1,2,0:T(2,128)} %copy.78), calls=%async_computation.3 | async-start | bytes 786432 | tf_op jit(solution)/shard_map/all_to_all | solution.py:123
  160.1 5.8 %collective-permute-start.8 = (f32[32,3,256]{2,0,1:T(8,128)S(1)}, f32[32,3,256]{2,0,1:T(8,128)S(1)}, u32[]{:S(2)}, u32[]{:S(2)}) collective-permute-start(f32[32,3,256]{2,0,1:T(8,128)S(1)} %fusion.19), channel_id=1, source_target_pairs={{0,1},{1,0},{2,3},{3,2},{4,5},{5,4},{6,7},{7,6},{8,9},{9,8},{10,11... | collective-permute-start | bytes 294920 | tf_op jit(solution)/shard_map/ppermute | solution.py:40
  165.9 6.2 %collective-permute-start.9 = (f32[32,3,256]{2,0,1:T(8,128)S(1)}, f32[32,3,256]{2,0,1:T(8,128)S(1)}, u32[]{:S(2)}, u32[]{:S(2)}) collective-permute-start(f32[32,3,256]{2,0,1:T(8,128)S(1)} %add.286), channel_id=1, source_target_pairs={{0,2},{1,3},{2,0},{3,1},{4,6},{5,7},{6,4},{7,5},{8,10},{9,11},{10,... | collective-permute-start | bytes 294920 | tf_op jit(solution)/shard_map/ppermute | solution.py:40

commit v5 on v4

--- a/solution.py
+++ b/solution.py
@@ -31,6 +31,29 @@
         source = (spot - shift) % size
         placed = lax.dynamic_update_slice_in_dim(placed, piece[None], source, 0)
     return placed.reshape(size * rows, width)
+
+
+def symmetric_gather(block_rows, group_wafer, tm_index, tm_count):
+    _, rows, det_total = block_rows.shape
+    groups = 8
+    lanes = det_total // groups
+    sent_groups = groups // 2 + 1
+    home_group = tm_index // (tm_count // groups)
+    rolled = jnp.roll(block_rows, -home_group * lanes, axis=2)[:, :, : sent_groups * lanes]
+    sent = jnp.take(rolled, group_wafer, axis=0)
+    got = lax.all_to_all(sent, "tm", split_axis=0, concat_axis=0, tiled=True)
+    got = got.reshape(groups, det_total // groups, sent_groups, lanes)
+    band = []
+    for g in range(groups):
+        row = []
+        for h in range(groups):
+            d = (h - g) % groups
+            if d < sent_groups:
+                row.append(got[g, :, d, :])
+            else:
+                row.append(got[h, :, (g - h) % groups, :].T)
+        band.append(jnp.concatenate(row, axis=1))
+    return jnp.concatenate(band, axis=0)
 
 
 def wafer_sum(x):
@@ -94,9 +117,7 @@
         "cktp,ckjp->cjt", pointing, fetched, preferred_element_type=jnp.float32
     )
     block_rows = wafer_gather(whiten, 1)
-    sent_blocks = jnp.take(block_rows, group_wafer, axis=0)
-    matrix = lax.all_to_all(sent_blocks, "tm", split_axis=0, concat_axis=0, tiled=True)
-    matrix = matrix.reshape(det_total, det_total)
+    matrix = symmetric_gather(block_rows, group_wafer, tm_index, tm_count)
     columns = wafer_columns(timestream)
     column_weights = wafer_columns(sample_weight).astype(jnp.float32)
     width = spans_here * samples

time: 176 us -> 299 us (1.70); the launches traced: 174 us -> 293 us
  local copies, waits for them, and re-layouts: 41.6 us -> 169 us
  waiting for transfers between devices: 37.8 us -> 32.1 us
    unnamed x44 -> x140, local copies, waits for them, and re-layouts: 7.99 us -> 121 us
    slice x0 -> x6, local copies, waits for them, and re-layouts: none -> 12.1 us  [the longest x4 8.11 us: symmetric_gather(): row.append(got[h, :, (g - h) % groups, :].T)]
    ppermute x2, waiting for transfers between devices: 4.81 us -> 0.01 us  [wafer_gather(): other = lax.ppermute(x, 'wafer', [(i, i ^ bit) for i in range(size)])]
    reshape x0 -> x1, local copies, waits for them, and re-layouts: none -> 4.09 us  [symmetric_gather(): got = got.reshape(groups, det_total // groups, sent_groups, lanes)]
    dynamic_update_slice x8, local copies, waits for them, and re-layouts: 14 us -> 10.9 us  [wafer_columns(): placed = lax.dynamic_update_slice_in_dim(placed, piece[None], source, 0)]
  transfers between devices with their start and end apart: 14 -> 14, of which waited for: 7 -> 6; matrix products, arithmetic and copies ran while one was open for 34% -> 20% of each run, Pallas kernels for 0% -> 0%
where the time goes in v5:
time: 299 us; the launch traced here: 293 us
  local copies, waits for them, and re-layouts  169 us (57%)
  starting transfers between devices  54.6 us (18%)
  waiting for transfers between devices  32.1 us (11%)
  other arithmetic  22.3 us (7%)
  matrix products  14.3 us (5%)
    unnamed x140, local copies, waits for them, and re-layouts  121 us
    all_to_all x1, starting transfers between devices, shards(): lax.all_to_all(requests, 'tm', split_axis=0, concat_axis=0, tiled=True)  12 us
    ppermute x6, starting transfers between devices, wafer_columns(): lax.ppermute(piece, 'wafer', [(i, (i + shift) % size) for i in range(size)])  11.2 us
    all_to_all x1, waiting for transfers between devices, shards(): lax.all_to_all(outgoing, 'tm', split_axis=0, concat_axis=0, tiled=True)  11.2 us
    dynamic_update_slice x8, local copies, waits for them, and re-layouts, wafer_columns(): placed = lax.dynamic_update_slice_in_dim(placed, piece[None], source, 0)  10.9 us
    all_to_all x1, starting transfers between devices, shards(): lax.all_to_all(served, 'tm', split_axis=0, concat_axis=0, tiled=True)  10.3 us
    all_to_all x1, waiting for transfers between devices, symmetric_gather(): got = lax.all_to_all(sent, 'tm', split_axis=0, concat_axis=0, tiled=True)  8.71 us
    dot_general x1, matrix products, shards(): lax.dot_general(whitened, filter_blocks, (((1,), (1,)), ((), ())), prefer...  8.42 us
  transfers between devices with their start and end apart: 14, of which 6 were waited for; matrix products, arithmetic and copies ran while one was open for 20% of the time, Pallas kernels for 0%

profile of v5, /device:TPU:2, one launch (start us, length us, event | category | flops | bytes accessed | tf_op | source)
XLA Modules:
  0.0 293.5 jit_solution(11997650953820067591)
XLA Ops:
  0.6 1.7 collective-permute-start
  2.3 2.7 constant_dynamic-slice_fusion.3
  5.7 3.1 %collective-permute-start.3 = (bf16[256,1024]{1,0:T(8,128)(2,1)}, bf16[256,1024]{1,0:T(8,128)(2,1)}, u32[]{:S(2)}, u32[]{:S(2)}) collective-permute-start(bf16[256,1024]{1,0:T(8,128)(2,1)} %get-tuple-element.122), channel_id=1, source_target_pairs={{0,2},{1,3},{2,0},{3,1},{4,6},{5,7},{6,4},{7,5},{8,10},{9,11},{10,... | collective-permute-start | bytes 1572872 | tf_op jit(solution)/shard_map/ppermute | solution.py:27
  8.8 1.9 collective-permute-start.4
  14.5 12.0 %all-to-all-start = ((s32[64,1,2]{2,1,0:T(1,128)}), s32[64,1,2]{2,1,0:T(1,128)S(1)}, u32[]{:S(2)}, u32[]{:S(2)}) async-start(s32[64,1,2]{2,1,0:T(1,128)} %bitcast.2), calls=%async_computation | async-start | bytes 65536 | tf_op jit(solution)/shard_map/all_to_all | solution.py:106
  30.6 1.8 broadcast.579.clone
  32.4 1.9 bitcast_dynamic-update-slice_fusion.3
  36.6 4.2 %compare_select_fusion.1 = bf16[4,256,4,256]{3,2,1,0:T(4,128)(2,1)} fusion(s32[4,256]{1,0:T(4,128)S(1)} %add_select_fusion.1, bf16[256,256]{1,0:T(8,128)(2,1)S(1)} %copy-done.8), kind=kLoop, calls=%fused_computation.10 | loop fusion | flops 2097152 | bytes 2232320 | tf_op jit(solution)/shard_map/jit(_where)/select_n | solution.py:129
  42.2 3.4 %copy.1998 = bf16[128,8,4,256]{3,1,2,0:T(8,128)(2,1)} copy(bf16[128,8,4,256]{3,2,1,0:T(4,128)(2,1)} %bitcast.281) | data formatting | bytes 4194304
  46.2 1.9 copy.1999
  49.5 1.7 maximum_select_fusion.1
  53.6 10.3 %all-to-all-start.2 = ((bf16[64,2,3,256]{3,1,2,0:T(2,128)(2,1)}), bf16[64,2,3,256]{3,1,2,0:T(2,128)(2,1)S(1)}, u32[]{:S(2)}, u32[]{:S(2)}) async-start(bf16[64,2,3,256]{3,1,2,0:T(2,128)(2,1)} %copy.1923), calls=%async_computation.2 | async-start | bytes 393216 | tf_op jit(solution)/shard_map/all_to_all | solution.py:109
  63.9 2.3 collective-permute-start.6
  67.4 1.9 gather_fusion.1
  69.3 2.6 broadcast_select_fusion
  71.9 2.8 all-to-all-done.2
  74.7 7.9 %all-to-all-start.1 = ((bf16[64,16,640]{2,1,0:T(8,128)(2,1)}), bf16[64,16,640]{2,1,0:T(8,128)(2,1)}, u32[]{:S(2)}, u32[]{:S(2)}) async-start(bf16[64,16,640]{2,1,0:T(8,128)(2,1)} %broadcast_select_fusion), calls=%async_computation.1 | async-start | bytes 2621440 | tf_op jit(solution)/shard_map/all_to_all | solution.py:44
  83.4 1.7 gather_fusion.3
  86.1 3.2 %collective-permute-start.7 = (bf16[256,1024]{1,0:T(8,128)(2,1)S(1)}, bf16[256,1024]{1,0:T(8,128)(2,1)S(1)}, u32[]{:S(2)}, u32[]{:S(2)}) collective-permute-start(bf16[256,1024]{1,0:T(8,128)(2,1)S(1)} %copy-done.7), channel_id=1, source_target_pairs={{0,3},{1,0},{2,1},{3,2},{4,7},{5,4},{6,5},{7,6},{8,11},{9,8},{10,9... | collective-permute-start | bytes 1572872 | tf_op jit(solution)/shard_map/ppermute | solution.py:27
  90.4 1.9 bitcast_dynamic-update-slice_fusion.2
  93.4 1.9 bitcast_dynamic-update-slice_fusion.1
  96.4 4.4 %collective-permute-done.7 = bf16[256,1024]{1,0:T(8,128)(2,1)S(1)} collective-permute-done((bf16[256,1024]{1,0:T(8,128)(2,1)S(1)}, bf16[256,1024]{1,0:T(8,128)(2,1)S(1)}, u32[]{:S(2)}, u32[]{:S(2)}) %collective-permute-start.7) | collective-permute-done | bytes 524320 | tf_op jit(solution)/shard_map/ppermute | solution.py:27
  101.6 2.9 multiply_convert_fusion
  104.6 3.6 %fusion.50 = bf16[1024,1024]{1,0:T(8,128)(2,1)} fusion(bf16[1024,1024]{1,0:T(8,128)(2,1)S(1)} %bitcast.286, bf16[1024,1024]{1,0:T(8,128)(2,1)S(1)} %bitcast.285), kind=kOutput, calls=%fused_computation.199 | convolution fusion | flops 2147483648 | bytes 6291456 | tf_op jit(solution)/shard_map/dot_general | solution.py:130
  108.2 8.7 %all-to-all-done.1 = bf16[64,16,640]{2,1,0:T(8,128)(2,1)} async-done(((bf16[64,16,640]{2,1,0:T(8,128)(2,1)}), bf16[64,16,640]{2,1,0:T(8,128)(2,1)}, u32[]{:S(2)}, u32[]{:S(2)}) %all-to-all-start.1) | async-done | bytes 1310752 | tf_op jit(solution)/shard_map/all_to_all | solution.py:44
  116.9 4.1 %reshape.443 = bf16[8,128,5,128]{3,2,1,0:T(8,128)(2,1)} reshape(bf16[64,16,640]{2,1,0:T(8,128)(2,1)} %all-to-all-done.1) | data formatting | bytes 2621440 | tf_op jit(solution)/shard_map/reshape | solution.py:45
  121.0 1.9 fusion.47
  122.9 5.1 %fusion.46 = (bf16[1,128,1,128]{3,2,1,0:T(2,128)(2,1)S(1)}, bf16[1,128,1,128]{3,2,1,0:T(2,128)(2,1)}, bf16[1,128,1,128]{3,2,1,0:T(2,128)(2,1)}, bf16[1,128,1,128...) fusion(bf16[8,128,5,128]{3,2,1,0:T(8,128)(2,1)} %reshape.443), kind=kLoop, calls=%fused_computation.194 | loop fusion | bytes 1245184 | tf_op jit(solution)/shard_map/slice | solution.py:54
  128.0 2.1 fusion.45
  130.7 1.6 copy.1976
  133.8 1.6 copy.1979
  136.8 1.6 copy.1982
  139.8 1.6 copy.1890
  142.8 1.6 copy.1980
  154.2 1.6 copy.1983
  155.8 1.5 constant_dynamic-update-slice_fusion.53
  157.3 1.6 copy.1985
  161.7 1.6 copy.1984
  173.1 1.6 copy.1986
  176.1 1.6 copy.1988
  179.9 1.6 copy.1987
  191.3 1.6 copy.1989
  194.3 1.5 copy.1991
  197.3 1.6 copy.1990
  198.9 1.5 constant_dynamic-update-slice_fusion.11
  200.4 1.5 constant_dynamic-update-slice_fusion.43
  208.9 1.6 copy.1992
  210.4 1.5 constant_dynamic-update-slice_fusion.23
  211.9 1.6 copy.1994
  213.5 1.5 constant_dynamic-update-slice_fusion.10
  215.0 1.5 constant_dynamic-update-slice_fusion.33
  216.4 1.6 copy.1993
  218.0 1.5 constant_dynamic-update-slice_fusion.32
  226.5 1.6 copy.1995
  246.7 8.4 %multiply_reduce_fusion.2 = (bf16[1024]{0:T(1024)(128)(2,1)S(1)}, bf16[1024]{0:T(1024)(128)(2,1)S(1)}, bf16[1024]{0:T(1024)(128)(2,1)S(1)}) fusion(f32[1024]{0:T(1024)S(1)} %bitcast.298, f32[1024]{0:T(1024)S(1)} %bitcast.297, f32[1024]{0:T(1024)S(1)} %bitcast.296, bf16[4,256,1024]{2,1,0:T(8,128)(2,1)} %bitcast_dynamic-update-slice_fusion, ...), kind=kOutput, calls=%fused_computation.7 | convolution fusion | flops 4308595712 | bytes 8411136 | tf_op jit(solution)/shard_map/dot_general | solution.py:132
  257.4 5.6 %all-to-all-start.3 = ((f32[64,2,3,256]{3,1,2,0:T(2,128)}), f32[64,2,3,256]{3,1,2,0:T(2,128)S(1)}, u32[]{:S(2)}, u32[]{:S(2)}) async-start(f32[64,2,3,256]{3,1,2,0:T(2,128)} %copy.1929), calls=%async_computation.3 | async-start | bytes 786432 | tf_op jit(solution)/shard_map/all_to_all | solution.py:144
  263.5 2.1 reduce.15
  266.4 11.2 %all-to-all-done.3 = f32[64,2,3,256]{3,1,2,0:T(2,128)S(1)} async-done(((f32[64,2,3,256]{3,1,2,0:T(2,128)}), f32[64,2,3,256]{3,1,2,0:T(2,128)S(1)}, u32[]{:S(2)}, u32[]{:S(2)}) %all-to-all-start.3) | async-done | bytes 393248 | tf_op jit(solution)/shard_map/all_to_all | solution.py:144
  280.1 1.7 collective-permute-start.8
  281.8 3.3 %collective-permute-done.8 = f32[32,3,256]{2,0,1:T(8,128)S(1)} collective-permute-done((f32[32,3,256]{2,0,1:T(8,128)S(1)}, f32[32,3,256]{2,0,1:T(8,128)S(1)}, u32[]{:S(2)}, u32[]{:S(2)}) %collective-permute-start.8) | collective-permute-done | bytes 98336 | tf_op jit(solution)/shard_map/ppermute | solution.py:63
  285.1 3.0 %collective-permute-start.9 = (f32[32,3,256]{2,0,1:T(8,128)S(1)}, f32[32,3,256]{2,0,1:T(8,128)S(1)}, u32[]{:S(2)}, u32[]{:S(2)}) collective-permute-start(f32[32,3,256]{2,0,1:T(8,128)S(1)} %add.299), channel_id=1, source_target_pairs={{0,2},{1,3},{2,0},{3,1},{4,6},{5,7},{6,4},{7,5},{8,10},{9,11},{10,... | collective-permute-start | bytes 294920 | tf_op jit(solution)/shard_map/ppermute | solution.py:63
  288.0 1.6 copy.1932
  289.6 1.7 collective-permute-done.9
  291.3 2.1 multiply_add_fusion
  (189 shorter events, 107.8 us)
Async XLA Ops:
  0.6 84.5 %copy-start = (bf16[4,6,256,256]{3,2,1,0:T(8,128)(2,1)S(1)}, bf16[4,6,256,256]{3,2,1,0:T(8,128)(2,1)}, u32[]{:S(2)}) copy-start(bf16[4,6,256,256]{3,2,1,0:T(8,128)(2,1)} %param.18) | copy-start | bytes 9437188
  0.6 48.8 %collective-permute-start = (bf16[7,4,1024]{2,1,0:T(4,128)(2,1)}, bf16[7,4,1024]{2,1,0:T(4,128)(2,1)}, u32[]{:S(2)}, u32[]{:S(2)}) collective-permute-start(bf16[7,4,1024]{2,1,0:T(4,128)(2,1)} %param.16), channel_id=1, source_target_pairs={{0,1},{1,0},{2,3},{3,2},{4,5},{5,4},{6,7},{7,6},{8,9},{9,8},{10,11... | collective-permute-start | bytes 172040 | tf_op jit(solution)/shard_map/ppermute | solution.py:12
  2.3 8.3 %copy-start.5 = (bf16[256,4096]{1,0:T(8,128)(2,1)S(1)}, bf16[256,4096]{1,0:T(8,128)(2,1)}, u32[]{:S(2)}) copy-start(bf16[256,4096]{1,0:T(8,128)(2,1)} %param.13) | copy-start | bytes 6291460
  5.0 6.9 %copy-start.13 = (s32[4,6]{1,0:T(4,128)S(1)}, s32[4,6]{1,0:T(4,128)}, u32[]{:S(2)}) copy-start(s32[4,6]{1,0:T(4,128)} %param.19) | copy-start | bytes 292
  5.0 7.1 %copy-start.1 = (s32[2048]{0:T(1024)S(1)}, s32[2048]{0:T(1024)}, u32[]{:S(2)}) copy-start(s32[2048]{0:T(1024)} %param.20) | copy-start | bytes 24580
  5.0 21.5 %copy-start.25 = (s32[64]{0:T(128)S(1)}, s32[64]{0:T(128)}, u32[]{:S(2)}) copy-start(s32[64]{0:T(128)} %param.17) | copy-start | bytes 772
  5.0 81.0 %collective-permute-start.2 = (bf16[256,1024]{1,0:T(8,128)(2,1)}, bf16[256,1024]{1,0:T(8,128)(2,1)}, u32[]{:S(2)}, u32[]{:S(2)}) collective-permute-start(bf16[256,1024]{1,0:T(8,128)(2,1)} %get-tuple-element.121), channel_id=1, source_target_pairs={{0,1},{1,2},{2,3},{3,0},{4,5},{5,6},{6,7},{7,4},{8,9},{9,10},{10,1... | collective-permute-start | bytes 1572872 | tf_op jit(solution)/shard_map/ppermute | solution.py:27
  5.7 86.7 %collective-permute-start.3 = (bf16[256,1024]{1,0:T(8,128)(2,1)}, bf16[256,1024]{1,0:T(8,128)(2,1)}, u32[]{:S(2)}, u32[]{:S(2)}) collective-permute-start(bf16[256,1024]{1,0:T(8,128)(2,1)} %get-tuple-element.122), channel_id=1, source_target_pairs={{0,2},{1,3},{2,0},{3,1},{4,6},{5,7},{6,4},{7,5},{8,10},{9,11},{10,... | collective-permute-start | bytes 1572872 | tf_op jit(solution)/shard_map/ppermute | solution.py:27
  8.8 86.6 %collective-permute-start.4 = (bf16[256,1024]{1,0:T(8,128)(2,1)}, bf16[256,1024]{1,0:T(8,128)(2,1)}, u32[]{:S(2)}, u32[]{:S(2)}) collective-permute-start(bf16[256,1024]{1,0:T(8,128)(2,1)} %get-tuple-element.120), channel_id=1, source_target_pairs={{0,3},{1,0},{2,1},{3,2},{4,7},{5,4},{6,5},{7,6},{8,11},{9,8},{10,9... | collective-permute-start | bytes 1572872 | tf_op jit(solution)/shard_map/ppermute | solution.py:27
  11.8 78.6 %collective-permute-start.5 = (bf16[256,1024]{1,0:T(8,128)(2,1)}, bf16[256,1024]{1,0:T(8,128)(2,1)}, u32[]{:S(2)}, u32[]{:S(2)}) collective-permute-start(bf16[256,1024]{1,0:T(8,128)(2,1)} %get-tuple-element.118), channel_id=1, source_target_pairs={{0,1},{1,2},{2,3},{3,0},{4,5},{5,6},{6,7},{7,4},{8,9},{9,10},{10,1... | collective-permute-start | bytes 1572872 | tf_op jit(solution)/shard_map/ppermute | solution.py:27
  13.1 0.6 copy-start.20
  14.5 33.5 %all-to-all-start = ((s32[64,1,2]{2,1,0:T(1,128)}), s32[64,1,2]{2,1,0:T(1,128)S(1)}, u32[]{:S(2)}, u32[]{:S(2)}) async-start(s32[64,1,2]{2,1,0:T(1,128)} %bitcast.2), calls=%async_computation | async-start | bytes 65536 | tf_op jit(solution)/shard_map/all_to_all | solution.py:106
  29.4 4.9 %copy-start.19 = (f32[2]{0:T(128)S(1)}, f32[2]{0:T(128)}, u32[]{:S(2)}) copy-start(f32[2]{0:T(128)} %param.23) | copy-start | bytes 28
  29.4 6.1 %copy-start.14 = (f32[3,1024]{1,0:T(4,128)S(1)}, f32[3,1024]{1,0:T(4,128)}, u32[]{:S(2)}) copy-start(f32[3,1024]{1,0:T(4,128)} %param.14) | copy-start | bytes 36868
  29.4 7.2 %copy-start.8 = (bf16[256,256]{1,0:T(8,128)(2,1)S(1)}, bf16[256,256]{1,0:T(8,128)(2,1)}, u32[]{:S(2)}) copy-start(bf16[256,256]{1,0:T(8,128)(2,1)} %param.15) | copy-start | bytes 393220
  30.5 10.3 %copy-start.3 = (bf16[4,256,1024]{2,1,0:T(8,128)(2,1)}, bf16[4,256,1024]{2,1,0:T(8,128)(2,1)S(1)}, u32[]{:S(2)}) copy-start(bf16[4,256,1024]{2,1,0:T(8,128)(2,1)S(1)} %bitcast_dynamic-update-slice_fusion.7) | copy-start | bytes 6291460
  32.4 8.5 %copy-start.9 = (f32[32,3,256]{2,0,1:T(8,128)S(1)}, f32[32,3,256]{2,0,1:T(8,128)}, u32[]{:S(2)}) copy-start(f32[32,3,256]{2,0,1:T(8,128)} %param.22) | copy-start | bytes 294916
  32.4 8.5 %copy-start.11 = (f32[32,3,256]{2,0,1:T(8,128)S(1)}, f32[32,3,256]{2,0,1:T(8,128)}, u32[]{:S(2)}) copy-start(f32[32,3,256]{2,0,1:T(8,128)} %param.21) | copy-start | bytes 294916
  46.2 3.3 %copy-start.12 = (bf16[7,4,1024]{2,1,0:T(4,128)(2,1)S(1)}, bf16[7,4,1024]{2,1,0:T(4,128)(2,1)}, u32[]{:S(2)}) copy-start(bf16[7,4,1024]{2,1,0:T(4,128)(2,1)} %param.16) | copy-start | bytes 172036
  48.0 0.6 copy-start.10
  51.1 12.7 %collective-permute-start.1 = (bf16[7,8,1024]{2,1,0:T(8,128)(2,1)}, bf16[7,8,1024]{2,1,0:T(8,128)(2,1)}, u32[]{:S(2)}, u32[]{:S(2)}) collective-permute-start(bf16[7,8,1024]{2,1,0:T(8,128)(2,1)} %maximum_select_fusion.1), channel_id=1, source_target_pairs={{0,2},{1,3},{2,0},{3,1},{4,6},{5,7},{6,4},{7,5},{8,10},{9,11},{10,... | collective-permute-start | bytes 344072 | tf_op jit(solution)/shard_map/ppermute | solution.py:12
  52.7 16.6 %copy-start.24 = (pred[64]{0:T(512)(128)(4,1)S(1)}, pred[64]{0:T(512)(128)(4,1)}, u32[]{:S(2)}) copy-start(pred[64]{0:T(512)(128)(4,1)} %compare_and_fusion.2) | copy-start | bytes 196
  53.6 21.1 %all-to-all-start.2 = ((bf16[64,2,3,256]{3,1,2,0:T(2,128)(2,1)}), bf16[64,2,3,256]{3,1,2,0:T(2,128)(2,1)S(1)}, u32[]{:S(2)}, u32[]{:S(2)}) async-start(bf16[64,2,3,256]{3,1,2,0:T(2,128)(2,1)} %copy.1923), calls=%async_computation.2 | async-start | bytes 393216 | tf_op jit(solution)/shard_map/all_to_all | solution.py:109
  63.9 29.5 %collective-permute-start.6 = (bf16[256,1024]{1,0:T(8,128)(2,1)}, bf16[256,1024]{1,0:T(8,128)(2,1)}, u32[]{:S(2)}, u32[]{:S(2)}) collective-permute-start(bf16[256,1024]{1,0:T(8,128)(2,1)} %get-tuple-element.119), channel_id=1, source_target_pairs={{0,2},{1,3},{2,0},{3,1},{4,6},{5,7},{6,4},{7,5},{8,10},{9,11},{10,... | collective-permute-start | bytes 1572872 | tf_op jit(solution)/shard_map/ppermute | solution.py:27
  71.9 13.2 %copy-start.22 = (pred[4,6]{1,0:T(4,128)(4,1)S(1)}, pred[4,6]{1,0:T(4,128)(4,1)}, u32[]{:S(2)}) copy-start(pred[4,6]{1,0:T(4,128)(4,1)} %compare_and_fusion.1) | copy-start | bytes 76
  74.7 42.2 %all-to-all-start.1 = ((bf16[64,16,640]{2,1,0:T(8,128)(2,1)}), bf16[64,16,640]{2,1,0:T(8,128)(2,1)}, u32[]{:S(2)}, u32[]{:S(2)}) async-start(bf16[64,16,640]{2,1,0:T(8,128)(2,1)} %broadcast_select_fusion), calls=%async_computation.1 | async-start | bytes 2621440 | tf_op jit(solution)/shard_map/all_to_all | solution.py:44
  85.1 1.0 copy-start.7
  85.1 4.2 %copy-start.4 = (bf16[4,256,1024]{2,1,0:T(8,128)(2,1)S(1)}, bf16[4,256,1024]{2,1,0:T(8,128)(2,1)}, u32[]{:S(2)}) copy-start(bf16[4,256,1024]{2,1,0:T(8,128)(2,1)} %copy-done.3) | copy-start | bytes 6291460
  86.1 14.7 %collective-permute-start.7 = (bf16[256,1024]{1,0:T(8,128)(2,1)S(1)}, bf16[256,1024]{1,0:T(8,128)(2,1)S(1)}, u32[]{:S(2)}, u32[]{:S(2)}) collective-permute-start(bf16[256,1024]{1,0:T(8,128)(2,1)S(1)} %copy-done.7), channel_id=1, source_target_pairs={{0,3},{1,0},{2,1},{3,2},{4,7},{5,4},{6,5},{7,6},{8,11},{9,8},{10,9... | collective-permute-start | bytes 1572872 | tf_op jit(solution)/shard_map/ppermute | solution.py:27
  101.6 2.9 %copy-start.6 = (bf16[128,8,4,256]{3,1,2,0:T(8,128)(2,1)S(1)}, bf16[128,8,4,256]{3,1,2,0:T(8,128)(2,1)}, u32[]{:S(2)}) copy-start(bf16[128,8,4,256]{3,1,2,0:T(8,128)(2,1)} %copy.1998) | copy-start | bytes 6291460
  121.0 7.0 %copy-start.2 = (bf16[8,128,5,128]{3,2,1,0:T(8,128)(2,1)S(1)}, bf16[8,128,5,128]{3,2,1,0:T(8,128)(2,1)}, u32[]{:S(2)}) copy-start(bf16[8,128,5,128]{3,2,1,0:T(8,128)(2,1)} %reshape.443) | copy-start | bytes 3932164
  185.7 61.1 %copy-start.15 = (f32[1,1024]{1,0:T(1,128)S(1)}, f32[1,1024]{1,0:T(1,128)}, u32[]{:S(2)}) copy-start(f32[1,1024]{1,0:T(1,128)} %get-tuple-element.163) | copy-start | bytes 12292
  185.7 61.1 %copy-start.16 = (f32[1,1024]{1,0:T(1,128)S(1)}, f32[1,1024]{1,0:T(1,128)}, u32[]{:S(2)}) copy-start(f32[1,1024]{1,0:T(1,128)} %get-tuple-element.164) | copy-start | bytes 12292
  185.7 61.1 %copy-start.17 = (f32[1,1024]{1,0:T(1,128)S(1)}, f32[1,1024]{1,0:T(1,128)}, u32[]{:S(2)}) copy-start(f32[1,1024]{1,0:T(1,128)} %get-tuple-element.165) | copy-start | bytes 12292
  185.7 61.1 %copy-start.18 = (s32[1024]{0:T(1024)S(1)}, s32[1024]{0:T(1024)}, u32[]{:S(2)}) copy-start(s32[1024]{0:T(1024)} %add_select_fusion) | copy-start | bytes 12292
  255.2 0.7 copy-start.21
  255.2 0.7 copy-start.23
  257.4 20.3 %all-to-all-start.3 = ((f32[64,2,3,256]{3,1,2,0:T(2,128)}), f32[64,2,3,256]{3,1,2,0:T(2,128)S(1)}, u32[]{:S(2)}, u32[]{:S(2)}) async-start(f32[64,2,3,256]{3,1,2,0:T(2,128)} %copy.1929), calls=%async_computation.3 | async-start | bytes 786432 | tf_op jit(solution)/shard_map/all_to_all | solution.py:144
  280.1 5.0 %collective-permute-start.8 = (f32[32,3,256]{2,0,1:T(8,128)S(1)}, f32[32,3,256]{2,0,1:T(8,128)S(1)}, u32[]{:S(2)}, u32[]{:S(2)}) collective-permute-start(f32[32,3,256]{2,0,1:T(8,128)S(1)} %fusion.20), channel_id=1, source_target_pairs={{0,1},{1,0},{2,3},{3,2},{4,5},{5,4},{6,7},{7,6},{8,9},{9,8},{10,11... | collective-permute-start | bytes 294920 | tf_op jit(solution)/shard_map/ppermute | solution.py:63
  285.1 6.2 %collective-permute-start.9 = (f32[32,3,256]{2,0,1:T(8,128)S(1)}, f32[32,3,256]{2,0,1:T(8,128)S(1)}, u32[]{:S(2)}, u32[]{:S(2)}) collective-permute-start(f32[32,3,256]{2,0,1:T(8,128)S(1)} %add.299), channel_id=1, source_target_pairs={{0,2},{1,3},{2,0},{3,1},{4,6},{5,7},{6,4},{7,5},{8,10},{9,11},{10,... | collective-permute-start | bytes 294920 | tf_op jit(solution)/shard_map/ppermute | solution.py:63

commit v6 on v5

--- a/solution.py
+++ b/solution.py
@@ -43,17 +43,12 @@
     sent = jnp.take(rolled, group_wafer, axis=0)
     got = lax.all_to_all(sent, "tm", split_axis=0, concat_axis=0, tiled=True)
     got = got.reshape(groups, det_total // groups, sent_groups, lanes)
-    band = []
-    for g in range(groups):
-        row = []
-        for h in range(groups):
-            d = (h - g) % groups
-            if d < sent_groups:
-                row.append(got[g, :, d, :])
-            else:
-                row.append(got[h, :, (g - h) % groups, :].T)
-        band.append(jnp.concatenate(row, axis=1))
-    return jnp.concatenate(band, axis=0)
+    padded = jnp.pad(got, ((0, 0), (0, 0), (0, groups - sent_groups), (0, 0)))
+    direct = jnp.stack([jnp.roll(padded[g], g, axis=1) for g in range(groups)])
+    direct = direct.reshape(det_total, det_total)
+    group_of = jnp.arange(det_total, dtype=jnp.int32) // lanes
+    use_direct = (group_of[None, :] - group_of[:, None]) % groups < sent_groups
+    return jnp.where(use_direct, direct, direct.T)
 
 
 def wafer_sum(x):

time: 299 us -> 183 us (0.61); the launches traced: 293 us -> 182 us
  local copies, waits for them, and re-layouts: 169 us -> 55.2 us
  matrix products: 14.3 us -> 18.5 us
  other arithmetic: 22.3 us -> 25.4 us
  waiting for transfers between devices: 32.1 us -> 29.1 us
    unnamed x140 -> x55, local copies, waits for them, and re-layouts: 121 us -> 10.1 us
    slice x6 -> x10, local copies, waits for them, and re-layouts: 12.1 us -> 0.63 us  [symmetric_gather(): direct = jnp.stack([jnp.roll(padded[g], g, axis=1) for g in range(groups)])]
    dot_general x1, matrix products: 3.65 us -> 10.5 us  [shards(): jnp.dot(matrix, filtered, preferred_element_type=jnp.float32)]
    reshape x0 -> x1, local copies, waits for them, and re-layouts: none -> 3.95 us  [symmetric_gather(): direct = direct.reshape(det_total, det_total)]
    dynamic_update_slice x8, local copies, waits for them, and re-layouts: 10.9 us -> 14.2 us  [wafer_columns(): placed = lax.dynamic_update_slice_in_dim(placed, piece[None], source, 0)]
  transfers between devices with their start and end apart: 14 -> 14, of which waited for: 6 -> 6; matrix products, arithmetic and copies ran while one was open for 20% -> 32% of each run, Pallas kernels for 0% -> 0%
where the time goes in v6:
time: 183 us; the launch traced here: 182 us
  local copies, waits for them, and re-layouts  55.2 us (30%)
  starting transfers between devices  52.2 us (29%)
  waiting for transfers between devices  29.1 us (16%)
  other arithmetic  25.4 us (14%)
  matrix products  18.5 us (10%)
    dynamic_update_slice x8, local copies, waits for them, and re-layouts, wafer_columns(): placed = lax.dynamic_update_slice_in_dim(placed, piece[None], source, 0)  14.2 us
    ppermute x6, starting transfers between devices, wafer_columns(): lax.ppermute(piece, 'wafer', [(i, (i + shift) % size) for i in range(size)])  12.5 us
    all_to_all x1, starting transfers between devices, shards(): lax.all_to_all(requests, 'tm', split_axis=0, concat_axis=0, tiled=True)  12 us
    all_to_all x1, waiting for transfers between devices, shards(): lax.all_to_all(outgoing, 'tm', split_axis=0, concat_axis=0, tiled=True)  11.2 us
    dot_general x1, matrix products, shards(): jnp.dot(matrix, filtered, preferred_element_type=jnp.float32)  10.5 us
    all_to_all x1, starting transfers between devices, shards(): lax.all_to_all(served, 'tm', split_axis=0, concat_axis=0, tiled=True)  10.3 us
    unnamed x55, local copies, waits for them, and re-layouts  10.1 us
    all_to_all x1, starting transfers between devices, symmetric_gather(): got = lax.all_to_all(sent, 'tm', split_axis=0, concat_axis=0, tiled=True)  8.72 us
  transfers between devices with their start and end apart: 14, of which 6 were waited for; matrix products, arithmetic and copies ran while one was open for 32% of the time, Pallas kernels for 0%

profile of v6, /device:TPU:2, one launch (start us, length us, event | category | flops | bytes accessed | tf_op | source)
XLA Modules:
  0.0 181.6 jit_solution(1206577866350822326)
XLA Ops:
  0.7 2.7 %constant_dynamic-slice_fusion = (bf16[256,1024]{1,0:T(8,128)(2,1)}, bf16[256,1024]{1,0:T(8,128)(2,1)}, bf16[256,1024]{1,0:T(8,128)(2,1)}) fusion(bf16[256,4096]{1,0:T(8,128)(2,1)} %param.13, s32[]{:T(128)S(6)} %select_n.353, s32[]{:T(128)S(6)} %select_n.345, s32[]{:T(128)S(6)} %select_n.349), kind=kLoop, calls=%fused_computation.118 | loop fusion | bytes 3145740 | tf_op jit(solution)/shard_map/dynamic_slice | solution.py:26
  3.5 1.7 collective-permute-start.5
  5.1 2.9 %collective-permute-start.6 = (bf16[256,1024]{1,0:T(8,128)(2,1)}, bf16[256,1024]{1,0:T(8,128)(2,1)}, u32[]{:S(2)}, u32[]{:S(2)}) collective-permute-start(bf16[256,1024]{1,0:T(8,128)(2,1)} %get-tuple-element.29), channel_id=1, source_target_pairs={{0,2},{1,3},{2,0},{3,1},{4,6},{5,7},{6,4},{7,5},{8,10},{9,11},{10,... | collective-permute-start | bytes 1572872 | tf_op jit(solution)/shard_map/ppermute | solution.py:27
  8.0 1.3 collective-permute-start.7
  9.4 0.7 collective-permute-start
  10.0 1.3 constant_dynamic-slice_fusion.3
  11.3 1.3 collective-permute-start.2
  12.8 0.7 gather_fusion
  13.9 0.8 all_to_all.19
  14.6 12.0 %all-to-all-start = ((s32[64,1,2]{2,1,0:T(1,128)}), s32[64,1,2]{2,1,0:T(1,128)S(1)}, u32[]{:S(2)}, u32[]{:S(2)}) async-start(s32[64,1,2]{2,1,0:T(1,128)} %bitcast.2), calls=%async_computation | async-start | bytes 65536 | tf_op jit(solution)/shard_map/all_to_all | solution.py:101
  27.2 0.6 add_select_fusion.3
  28.5 0.6 add_select_fusion.1
  29.1 0.6 fusion.75
  29.7 0.6 slice_reduce_fusion.2
  30.4 0.6 pad_clamp_fusion.2
  30.9 1.6 broadcast.640.clone
  32.5 2.0 %bitcast_dynamic-update-slice_fusion.3 = bf16[4,256,1024]{2,1,0:T(8,128)(2,1)} fusion(bf16[4,256,1024]{2,1,0:T(8,128)(2,1)} %broadcast.640.clone, s32[]{:T(128)S(6)} %select_n.343, bf16[256,4096]{1,0:T(8,128)(2,1)} %param.13, s32[]{:T(128)S(6)} %select_n.341), kind=kLoop, calls=%fused_computation.38 | loop fusion | bytes 1048584 | tf_op jit(solution)/shard_map/dynamic_update_slice | solution.py:32
  34.5 1.7 broadcast.640.clone.1
  36.1 1.9 %bitcast_dynamic-update-slice_fusion.7 = bf16[4,256,1024]{2,1,0:T(8,128)(2,1)} fusion(bf16[4,256,1024]{2,1,0:T(8,128)(2,1)} %broadcast.640.clone.1, s32[]{:T(128)S(6)} %select_n.343, bf16[256,4096]{1,0:T(8,128)(2,1)} %param.12, s32[]{:T(128)S(6)} %select_n.341), kind=kLoop, calls=%fused_computation.42 | loop fusion | bytes 1048584 | tf_op jit(solution)/shard_map/dynamic_update_slice | solution.py:32
  38.6 4.2 %compare_select_fusion.1 = bf16[4,256,4,256]{3,2,1,0:T(4,128)(2,1)} fusion(s32[4,256]{1,0:T(4,128)S(1)} %add_select_fusion.2, bf16[256,256]{1,0:T(8,128)(2,1)S(1)} %copy-done.5), kind=kLoop, calls=%fused_computation.18 | loop fusion | flops 2097152 | bytes 2232320 | tf_op jit(solution)/shard_map/jit(_where)/select_n | solution.py:124
  42.8 1.4 fusion.72
  44.8 0.8 gather_fusion.2
  45.7 1.7 maximum_select_fusion.1
  47.6 1.0 broadcast_select_fusion.1
  48.6 10.3 %all-to-all-start.2 = ((bf16[64,2,3,256]{3,1,2,0:T(2,128)(2,1)}), bf16[64,2,3,256]{3,1,2,0:T(2,128)(2,1)S(1)}, u32[]{:S(2)}, u32[]{:S(2)}) async-start(bf16[64,2,3,256]{3,1,2,0:T(2,128)(2,1)} %broadcast_select_fusion.1), calls=%async_computation.2 | async-start | bytes 393216 | tf_op jit(solution)/shard_map/all_to_all | solution.py:104
  58.9 3.3 %collective-permute-start.3 = (bf16[256,1024]{1,0:T(8,128)(2,1)}, bf16[256,1024]{1,0:T(8,128)(2,1)}, u32[]{:S(2)}, u32[]{:S(2)}) collective-permute-start(bf16[256,1024]{1,0:T(8,128)(2,1)} %get-tuple-element.32), channel_id=1, source_target_pairs={{0,2},{1,3},{2,0},{3,1},{4,6},{5,7},{6,4},{7,5},{8,10},{9,11},{10,... | collective-permute-start | bytes 1572872 | tf_op jit(solution)/shard_map/ppermute | solution.py:27
  62.2 1.1 maximum_select_fusion
  63.4 1.9 %gather_fusion.1 = bf16[64,16,640]{2,1,0:T(8,128)(2,1)} fusion(bf16[7,16,640]{2,1,0:T(8,128)(2,1)S(1)} %fusion.33, s32[1024]{0:T(1024)} %pad_clamp_fusion.2), kind=kCustom, calls=%fused_computation.1 | custom fusion | bytes 2621696 | tf_op jit(solution)/shard_map/jit(_take)/gather | solution.py:43
  65.3 2.6 %broadcast_select_fusion = bf16[64,16,640]{2,1,0:T(8,128)(2,1)} fusion(bf16[64,16,640]{2,1,0:T(8,128)(2,1)} %gather_fusion.1, pred[64]{0:T(512)(128)(4,1)S(1)} %copy-done.23), kind=kLoop, calls=%fused_computation.32 | loop fusion | flops 655360 | bytes 2621504 | tf_op jit(solution)/shard_map/jit(_take)/select_n | solution.py:43
  67.9 1.8 all-to-all-done.2
  69.7 8.7 %all-to-all-start.1 = ((bf16[64,16,640]{2,1,0:T(8,128)(2,1)}), bf16[64,16,640]{2,1,0:T(8,128)(2,1)}, u32[]{:S(2)}, u32[]{:S(2)}) async-start(bf16[64,16,640]{2,1,0:T(8,128)(2,1)} %broadcast_select_fusion), calls=%async_computation.1 | async-start | bytes 2621440 | tf_op jit(solution)/shard_map/all_to_all | solution.py:44
  78.6 3.4 %copy.92 = bf16[128,8,4,256]{3,1,2,0:T(8,128)(2,1)} copy(bf16[128,8,4,256]{3,2,1,0:T(4,128)(2,1)} %bitcast.159) | data formatting | bytes 4194304
  82.6 1.8 %copy.93 = bf16[128,8,4,256]{3,1,2,0:T(8,128)(2,1)} copy(bf16[128,8,4,256]{3,2,1,0:T(4,128)(2,1)S(1)} %bitcast.160) | data formatting | bytes 4194304
  84.4 0.8 copy.78
  85.2 1.6 gather_fusion.3
  86.8 0.9 convolution_bitcast_fusion
  87.8 1.9 %collective-permute-start.4 = (bf16[256,1024]{1,0:T(8,128)(2,1)S(1)}, bf16[256,1024]{1,0:T(8,128)(2,1)S(1)}, u32[]{:S(2)}, u32[]{:S(2)}) collective-permute-start(bf16[256,1024]{1,0:T(8,128)(2,1)S(1)} %copy-done.4), channel_id=1, source_target_pairs={{0,3},{1,0},{2,1},{3,2},{4,7},{5,4},{6,5},{7,6},{8,11},{9,8},{10,9... | collective-permute-start | bytes 1572872 | tf_op jit(solution)/shard_map/ppermute | solution.py:27
  89.7 1.9 %bitcast_dynamic-update-slice_fusion.2 = bf16[4,256,1024]{2,1,0:T(8,128)(2,1)} fusion(bf16[4,256,1024]{2,1,0:T(8,128)(2,1)} %bitcast_dynamic-update-slice_fusion.3, s32[]{:T(128)S(6)} %select_n.347, bf16[256,1024]{1,0:T(8,128)(2,1)} %collective-permute-done.5), kind=kLoop, calls=%fused_computation.37 | loop fusion | bytes 1048580 | tf_op jit(solution)/shard_map/dynamic_update_slice | solution.py:32
  91.6 1.9 %bitcast_dynamic-update-slice_fusion.6 = bf16[4,256,1024]{2,1,0:T(8,128)(2,1)} fusion(bf16[4,256,1024]{2,1,0:T(8,128)(2,1)} %bitcast_dynamic-update-slice_fusion.7, s32[]{:T(128)S(6)} %select_n.347, bf16[256,1024]{1,0:T(8,128)(2,1)} %collective-permute-done.2), kind=kLoop, calls=%fused_computation.41 | loop fusion | bytes 1048580 | tf_op jit(solution)/shard_map/dynamic_update_slice | solution.py:32
  93.6 1.9 %bitcast_dynamic-update-slice_fusion.1 = bf16[4,256,1024]{2,1,0:T(8,128)(2,1)} fusion(bf16[4,256,1024]{2,1,0:T(8,128)(2,1)} %bitcast_dynamic-update-slice_fusion.2, s32[]{:T(128)S(6)} %select_n.351, bf16[256,1024]{1,0:T(8,128)(2,1)} %collective-permute-done.6), kind=kLoop, calls=%fused_computation.36 | loop fusion | bytes 1048580 | tf_op jit(solution)/shard_map/dynamic_update_slice | solution.py:32
  95.4 1.9 %bitcast_dynamic-update-slice_fusion.5 = bf16[4,256,1024]{2,1,0:T(8,128)(2,1)} fusion(bf16[4,256,1024]{2,1,0:T(8,128)(2,1)} %bitcast_dynamic-update-slice_fusion.6, s32[]{:T(128)S(6)} %select_n.351, bf16[256,1024]{1,0:T(8,128)(2,1)} %collective-permute-done.3), kind=kLoop, calls=%fused_computation.40 | loop fusion | bytes 1048580 | tf_op jit(solution)/shard_map/dynamic_update_slice | solution.py:32
  97.3 1.9 %bitcast_dynamic-update-slice_fusion = bf16[4,256,1024]{2,1,0:T(8,128)(2,1)} fusion(bf16[4,256,1024]{2,1,0:T(8,128)(2,1)} %bitcast_dynamic-update-slice_fusion.1, s32[]{:T(128)S(6)} %select_n.355, bf16[256,1024]{1,0:T(8,128)(2,1)} %collective-permute-done.7), kind=kLoop, calls=%fused_computation.35 | loop fusion | bytes 1048580 | tf_op jit(solution)/shard_map/dynamic_update_slice | solution.py:32
  99.2 2.6 %collective-permute-done.4 = bf16[256,1024]{1,0:T(8,128)(2,1)S(1)} collective-permute-done((bf16[256,1024]{1,0:T(8,128)(2,1)S(1)}, bf16[256,1024]{1,0:T(8,128)(2,1)S(1)}, u32[]{:S(2)}, u32[]{:S(2)}) %collective-permute-start.4) | collective-permute-done | bytes 524320 | tf_op jit(solution)/shard_map/ppermute | solution.py:27
  101.8 0.8 bitcast_dynamic-update-slice_fusion.4
  102.6 4.1 %multiply_convert_fusion = bf16[4,256,1024]{2,1,0:T(8,128)(2,1)} fusion(bf16[4,256,1024]{2,1,0:T(8,128)(2,1)} %bitcast_dynamic-update-slice_fusion.4, f32[1024]{0:T(1024)S(1)} %bitcast.178, f32[4,256]{1,0:T(4,128)S(1)} %mul.170, f32[1024]{0:T(1024)S(1)} %bitcast.179, f32[4,256]{1,0:T(4,128)S(1)} %mul.165, f32[1024]{0:T(1024)S(1)} %bitcast.177, ...), kind=kLoop, calls=%fused_computation.15 | loop fusion | flops 10485760 | bytes 6316032 | tf_op jit(solution)/shard_map/convert_element_type | solution.py:121
  106.7 6.0 %all-to-all-done.1 = bf16[64,16,640]{2,1,0:T(8,128)(2,1)} async-done(((bf16[64,16,640]{2,1,0:T(8,128)(2,1)}), bf16[64,16,640]{2,1,0:T(8,128)(2,1)}, u32[]{:S(2)}, u32[]{:S(2)}) %all-to-all-start.1) | async-done | bytes 1310752 | tf_op jit(solution)/shard_map/all_to_all | solution.py:44
  112.7 4.2 %reshape.470 = bf16[8,128,5,128]{3,2,1,0:T(8,128)(2,1)} reshape(bf16[64,16,640]{2,1,0:T(8,128)(2,1)} %all-to-all-done.1) | data formatting | bytes 2621440 | tf_op jit(solution)/shard_map/reshape | solution.py:45
  116.9 2.0 %fusion.25 = (bf16[128,8,128]{2,1,0:T(8,128)(2,1)S(1)}, bf16[128,8,128]{2,1,0:T(8,128)(2,1)S(1)}, bf16[128,8,128]{2,1,0:T(8,128)(2,1)S(1)}, bf16[128,8,128]{2,1,...) fusion(bf16[8,128,5,128]{3,2,1,0:T(8,128)(2,1)} %reshape.470), kind=kLoop, calls=%fused_computation.61 | loop fusion | bytes 3407872 | tf_op jit(solution)/shard_map/squeeze | solution.py:47
  120.8 2.0 %copy.114 = bf16[128,8,8,128]{3,1,2,0:T(8,128)(2,1)} copy(bf16[128,8,8,128]{3,2,1,0:T(8,128)(2,1)S(1)} %bitcast.162) | data formatting | bytes 4194304
  122.8 4.0 %copy.72 = bf16[1024,1024]{0,1:T(8,128)(2,1)} copy(bf16[1024,1024]{1,0:T(8,128)(2,1)} %bitcast.161) | data formatting | bytes 4194304 | tf_op jit(solution)/shard_map/reshape | solution.py:48
  126.8 10.5 %fusion.6 = bf16[1024,1024]{1,0:T(8,128)(2,1)} fusion(bf16[1024,1024]{0,1:T(8,128)(2,1)} %copy.72, s32[1024]{0:T(1024)S(1)} %copy-done.17, bf16[1024,1024]{1,0:T(8,128)(2,1)} %bitcast.167, bf16[1024,1024]{1,0:T(8,128)(2,1)} %bitcast.166, bf16[128,8,8,128]{3,2,1,0:T(8,128)(2,1)} %bitcast.163), kind=kOutput, calls=%fused_computation.23 | convolution fusion | flops 4310695936 | bytes 10489856 | tf_op jit(solution)/shard_map/dot_general | solution.py:126
  137.4 5.8 %multiply_reduce_fusion.2 = (bf16[1024]{0:T(1024)(128)(2,1)S(1)}, bf16[1024]{0:T(1024)(128)(2,1)S(1)}, bf16[1024]{0:T(1024)(128)(2,1)S(1)}) fusion(f32[1024]{0:T(1024)S(1)} %bitcast.182, f32[1024]{0:T(1024)S(1)} %bitcast.181, f32[1024]{0:T(1024)S(1)} %bitcast.180, bf16[4,256,1024]{2,1,0:T(8,128)(2,1)} %bitcast_dynamic-update-slice_fusion, ...), kind=kOutput, calls=%fused_computation.14 | convolution fusion | flops 2160063488 | bytes 6313984 | tf_op jit(solution)/shard_map/dot_general | solution.py:127
  144.3 1.1 copy.83
  145.4 5.6 %all-to-all-start.3 = ((f32[64,2,3,256]{3,1,2,0:T(2,128)}), f32[64,2,3,256]{3,1,2,0:T(2,128)S(1)}, u32[]{:S(2)}, u32[]{:S(2)}) async-start(f32[64,2,3,256]{3,1,2,0:T(2,128)} %copy.83), calls=%async_computation.3 | async-start | bytes 786432 | tf_op jit(solution)/shard_map/all_to_all | solution.py:139
  151.5 2.1 %reduce.15 = s32[64,2]{1,0:T(8,128)} reduce(s32[64,1,2]{2,1,0:T(1,128)} %copy-done.8, s32[]{:T(128)} %broadcast.687), dimensions={1}, to_apply=%all_to_all.20.reduce_sub_computation.3 | reduce | bytes 1028 | tf_op jit(solution)/shard_map/all_to_all | solution.py:101
  153.6 0.9 eq.123
  154.4 11.2 %all-to-all-done.3 = f32[64,2,3,256]{3,1,2,0:T(2,128)S(1)} async-done(((f32[64,2,3,256]{3,1,2,0:T(2,128)}), f32[64,2,3,256]{3,1,2,0:T(2,128)S(1)}, u32[]{:S(2)}, u32[]{:S(2)}) %all-to-all-start.3) | async-done | bytes 393248 | tf_op jit(solution)/shard_map/all_to_all | solution.py:139
  165.8 0.8 copy.95
  166.6 1.1 copy.85
  168.5 4.5 %collective-permute-done.8 = f32[32,3,256]{2,0,1:T(8,128)S(1)} collective-permute-done((f32[32,3,256]{2,0,1:T(8,128)S(1)}, f32[32,3,256]{2,0,1:T(8,128)S(1)}, u32[]{:S(2)}, u32[]{:S(2)}) %collective-permute-start.8) | collective-permute-done | bytes 98336 | tf_op jit(solution)/shard_map/ppermute | solution.py:58
  173.1 1.7 collective-permute-start.9
  174.8 1.6 copy.86
  176.4 2.9 %collective-permute-done.9 = f32[32,3,256]{2,0,1:T(8,128)S(1)} collective-permute-done((f32[32,3,256]{2,0,1:T(8,128)S(1)}, f32[32,3,256]{2,0,1:T(8,128)S(1)}, u32[]{:S(2)}, u32[]{:S(2)}) %collective-permute-start.9) | collective-permute-done | bytes 98336 | tf_op jit(solution)/shard_map/ppermute | solution.py:58
  179.3 2.3 %multiply_add_fusion = (f32[32,3,256]{2,0,1:T(8,128)}, f32[32,3,256]{2,0,1:T(8,128)}) fusion(f32[32,3,256]{2,0,1:T(8,128)} %param.22, f32[]{:T(128)} %bitcast.57, f32[32,3,256]{2,0,1:T(8,128)S(1)} %add.317, f32[32,3,256]{2,0,1:T(8,128)S(1)} %collective-permute-done.9), kind=kLoop, calls=%fused_computation.81 | loop fusion | flops 98304 | bytes 491524 | tf_op jit(solution)/shard_map/add | solution.py:151
  (116 shorter events, 8.3 us)
Async XLA Ops:
  0.6 86.1 %copy-start = (bf16[4,6,256,256]{3,2,1,0:T(8,128)(2,1)S(1)}, bf16[4,6,256,256]{3,2,1,0:T(8,128)(2,1)}, u32[]{:S(2)}) copy-start(bf16[4,6,256,256]{3,2,1,0:T(8,128)(2,1)} %param.18) | copy-start | bytes 9437188
  0.6 8.7 %copy-start.10 = (bf16[7,4,1024]{2,1,0:T(4,128)(2,1)S(1)}, bf16[7,4,1024]{2,1,0:T(4,128)(2,1)}, u32[]{:S(2)}) copy-start(bf16[7,4,1024]{2,1,0:T(4,128)(2,1)} %param.16) | copy-start | bytes 172036
  0.7 9.3 %copy-start.3 = (bf16[256,4096]{1,0:T(8,128)(2,1)S(1)}, bf16[256,4096]{1,0:T(8,128)(2,1)}, u32[]{:S(2)}) copy-start(bf16[256,4096]{1,0:T(8,128)(2,1)} %param.12) | copy-start | bytes 6291460
  3.4 9.2 %copy-start.11 = (s32[4,6]{1,0:T(4,128)S(1)}, s32[4,6]{1,0:T(4,128)}, u32[]{:S(2)}) copy-start(s32[4,6]{1,0:T(4,128)} %param.19) | copy-start | bytes 292
  3.4 9.4 %copy-start.1 = (s32[2048]{0:T(1024)S(1)}, s32[2048]{0:T(1024)}, u32[]{:S(2)}) copy-start(s32[2048]{0:T(1024)} %param.20) | copy-start | bytes 24580
  3.4 23.2 %copy-start.24 = (s32[64]{0:T(128)S(1)}, s32[64]{0:T(128)}, u32[]{:S(2)}) copy-start(s32[64]{0:T(128)} %param.17) | copy-start | bytes 772
  3.4 25.6 %copy-start.18 = (f32[2]{0:T(128)S(1)}, f32[2]{0:T(128)}, u32[]{:S(2)}) copy-start(f32[2]{0:T(128)} %param.23) | copy-start | bytes 28
  3.4 26.3 %copy-start.12 = (f32[3,1024]{1,0:T(4,128)S(1)}, f32[3,1024]{1,0:T(4,128)}, u32[]{:S(2)}) copy-start(f32[3,1024]{1,0:T(4,128)} %param.14) | copy-start | bytes 36868
  3.5 84.3 %collective-permute-start.5 = (bf16[256,1024]{1,0:T(8,128)(2,1)}, bf16[256,1024]{1,0:T(8,128)(2,1)}, u32[]{:S(2)}, u32[]{:S(2)}) collective-permute-start(bf16[256,1024]{1,0:T(8,128)(2,1)} %get-tuple-element.28), channel_id=1, source_target_pairs={{0,1},{1,2},{2,3},{3,0},{4,5},{5,6},{6,7},{7,4},{8,9},{9,10},{10,1... | collective-permute-start | bytes 1572872 | tf_op jit(solution)/shard_map/ppermute | solution.py:27
  5.1 88.5 %collective-permute-start.6 = (bf16[256,1024]{1,0:T(8,128)(2,1)}, bf16[256,1024]{1,0:T(8,128)(2,1)}, u32[]{:S(2)}, u32[]{:S(2)}) collective-permute-start(bf16[256,1024]{1,0:T(8,128)(2,1)} %get-tuple-element.29), channel_id=1, source_target_pairs={{0,2},{1,3},{2,0},{3,1},{4,6},{5,7},{6,4},{7,5},{8,10},{9,11},{10,... | collective-permute-start | bytes 1572872 | tf_op jit(solution)/shard_map/ppermute | solution.py:27
  8.0 89.3 %collective-permute-start.7 = (bf16[256,1024]{1,0:T(8,128)(2,1)}, bf16[256,1024]{1,0:T(8,128)(2,1)}, u32[]{:S(2)}, u32[]{:S(2)}) collective-permute-start(bf16[256,1024]{1,0:T(8,128)(2,1)} %get-tuple-element.27), channel_id=1, source_target_pairs={{0,3},{1,0},{2,1},{3,2},{4,7},{5,4},{6,5},{7,6},{8,11},{9,8},{10,9... | collective-permute-start | bytes 1572872 | tf_op jit(solution)/shard_map/ppermute | solution.py:27
  9.4 36.3 %collective-permute-start = (bf16[7,4,1024]{2,1,0:T(4,128)(2,1)S(1)}, bf16[7,4,1024]{2,1,0:T(4,128)(2,1)}, u32[]{:S(2)}, u32[]{:S(2)}) collective-permute-start(bf16[7,4,1024]{2,1,0:T(4,128)(2,1)S(1)} %copy-done.10), channel_id=1, source_target_pairs={{0,1},{1,0},{2,3},{3,2},{4,5},{5,4},{6,7},{7,6},{8,9},{9,8},{10,11... | collective-permute-start | bytes 172040 | tf_op jit(solution)/shard_map/ppermute | solution.py:12
  11.3 80.3 %collective-permute-start.2 = (bf16[256,1024]{1,0:T(8,128)(2,1)}, bf16[256,1024]{1,0:T(8,128)(2,1)}, u32[]{:S(2)}, u32[]{:S(2)}) collective-permute-start(bf16[256,1024]{1,0:T(8,128)(2,1)} %get-tuple-element.31), channel_id=1, source_target_pairs={{0,1},{1,2},{2,3},{3,0},{4,5},{5,6},{6,7},{7,4},{8,9},{9,10},{10,1... | collective-permute-start | bytes 1572872 | tf_op jit(solution)/shard_map/ppermute | solution.py:27
  13.8 22.4 %copy-start.20 = (s32[24]{0:T(128)}, s32[24]{0:T(128)S(1)}, u32[]{:S(2)}) copy-start(s32[24]{0:T(128)S(1)} %get-tuple-element.52) | copy-start | bytes 292
  14.6 29.6 %all-to-all-start = ((s32[64,1,2]{2,1,0:T(1,128)}), s32[64,1,2]{2,1,0:T(1,128)S(1)}, u32[]{:S(2)}, u32[]{:S(2)}) async-start(s32[64,1,2]{2,1,0:T(1,128)} %bitcast.2), calls=%async_computation | async-start | bytes 65536 | tf_op jit(solution)/shard_map/all_to_all | solution.py:101
  32.5 6.1 %copy-start.5 = (bf16[256,256]{1,0:T(8,128)(2,1)S(1)}, bf16[256,256]{1,0:T(8,128)(2,1)}, u32[]{:S(2)}) copy-start(bf16[256,256]{1,0:T(8,128)(2,1)} %param.15) | copy-start | bytes 393220
  36.1 6.7 %copy-start.7 = (f32[32,3,256]{2,0,1:T(8,128)S(1)}, f32[32,3,256]{2,0,1:T(8,128)}, u32[]{:S(2)}) copy-start(f32[32,3,256]{2,0,1:T(8,128)} %param.22) | copy-start | bytes 294916
  36.1 6.7 %copy-start.9 = (f32[32,3,256]{2,0,1:T(8,128)S(1)}, f32[32,3,256]{2,0,1:T(8,128)}, u32[]{:S(2)}) copy-start(f32[32,3,256]{2,0,1:T(8,128)} %param.21) | copy-start | bytes 294916
  44.2 0.6 copy-start.8
  47.3 11.5 %collective-permute-start.1 = (bf16[7,8,1024]{2,1,0:T(8,128)(2,1)}, bf16[7,8,1024]{2,1,0:T(8,128)(2,1)}, u32[]{:S(2)}, u32[]{:S(2)}) collective-permute-start(bf16[7,8,1024]{2,1,0:T(8,128)(2,1)} %maximum_select_fusion.1), channel_id=1, source_target_pairs={{0,2},{1,3},{2,0},{3,1},{4,6},{5,7},{6,4},{7,5},{8,10},{9,11},{10,... | collective-permute-start | bytes 344072 | tf_op jit(solution)/shard_map/ppermute | solution.py:12
  47.6 17.7 %copy-start.23 = (pred[64]{0:T(512)(128)(4,1)S(1)}, pred[64]{0:T(512)(128)(4,1)}, u32[]{:S(2)}) copy-start(pred[64]{0:T(512)(128)(4,1)} %compare_and_fusion.2) | copy-start | bytes 196
  48.6 21.1 %all-to-all-start.2 = ((bf16[64,2,3,256]{3,1,2,0:T(2,128)(2,1)}), bf16[64,2,3,256]{3,1,2,0:T(2,128)(2,1)S(1)}, u32[]{:S(2)}, u32[]{:S(2)}) async-start(bf16[64,2,3,256]{3,1,2,0:T(2,128)(2,1)} %broadcast_select_fusion.1), calls=%async_computation.2 | async-start | bytes 393216 | tf_op jit(solution)/shard_map/all_to_all | solution.py:104
  58.9 36.6 %collective-permute-start.3 = (bf16[256,1024]{1,0:T(8,128)(2,1)}, bf16[256,1024]{1,0:T(8,128)(2,1)}, u32[]{:S(2)}, u32[]{:S(2)}) collective-permute-start(bf16[256,1024]{1,0:T(8,128)(2,1)} %get-tuple-element.32), channel_id=1, source_target_pairs={{0,2},{1,3},{2,0},{3,1},{4,6},{5,7},{6,4},{7,5},{8,10},{9,11},{10,... | collective-permute-start | bytes 1572872 | tf_op jit(solution)/shard_map/ppermute | solution.py:27
  65.3 13.1 %copy-start.19 = (s32[24]{0:T(128)S(1)}, s32[24]{0:T(128)}, u32[]{:S(2)}) copy-start(s32[24]{0:T(128)} %fusion.64) | copy-start | bytes 292
  69.7 43.0 %all-to-all-start.1 = ((bf16[64,16,640]{2,1,0:T(8,128)(2,1)}), bf16[64,16,640]{2,1,0:T(8,128)(2,1)}, u32[]{:S(2)}, u32[]{:S(2)}) async-start(bf16[64,16,640]{2,1,0:T(8,128)(2,1)} %broadcast_select_fusion), calls=%async_computation.1 | async-start | bytes 2621440 | tf_op jit(solution)/shard_map/all_to_all | solution.py:44
  78.6 3.4 %copy-start.6 = (bf16[256,256]{1,0:T(8,128)(2,1)S(1)}, bf16[256,256]{1,0:T(8,128)(2,1)}, u32[]{:S(2)}) copy-start(bf16[256,256]{1,0:T(8,128)(2,1)} %param.15) | copy-start | bytes 393220
  82.5 4.2 %copy-start.22 = (pred[4,6]{1,0:T(4,128)(4,1)S(1)}, pred[4,6]{1,0:T(4,128)(4,1)}, u32[]{:S(2)}) copy-start(pred[4,6]{1,0:T(4,128)(4,1)} %compare_and_fusion.1) | copy-start | bytes 76
  86.8 1.0 copy-start.4
  87.8 14.0 %collective-permute-start.4 = (bf16[256,1024]{1,0:T(8,128)(2,1)S(1)}, bf16[256,1024]{1,0:T(8,128)(2,1)S(1)}, u32[]{:S(2)}, u32[]{:S(2)}) collective-permute-start(bf16[256,1024]{1,0:T(8,128)(2,1)S(1)} %copy-done.4), channel_id=1, source_target_pairs={{0,3},{1,0},{2,1},{3,2},{4,7},{5,4},{6,5},{7,6},{8,11},{9,8},{10,9... | collective-permute-start | bytes 1572872 | tf_op jit(solution)/shard_map/ppermute | solution.py:27
  120.8 2.0 %copy-start.2 = (bf16[8,128,8,128]{3,2,1,0:T(8,128)(2,1)}, bf16[8,128,8,128]{3,2,1,0:T(8,128)(2,1)S(1)}, u32[]{:S(2)}) copy-start(bf16[8,128,8,128]{3,2,1,0:T(8,128)(2,1)S(1)} %fusion.32) | copy-start | bytes 6291460
  122.8 4.0 %copy-start.17 = (s32[1024]{0:T(1024)S(1)}, s32[1024]{0:T(1024)}, u32[]{:S(2)}) copy-start(s32[1024]{0:T(1024)} %add_select_fusion.3) | copy-start | bytes 12292
  126.8 10.6 %copy-start.13 = (f32[1,1024]{1,0:T(1,128)S(1)}, f32[1,1024]{1,0:T(1,128)}, u32[]{:S(2)}) copy-start(f32[1,1024]{1,0:T(1,128)} %get-tuple-element.43) | copy-start | bytes 12292
  126.8 10.6 %copy-start.14 = (f32[1,1024]{1,0:T(1,128)S(1)}, f32[1,1024]{1,0:T(1,128)}, u32[]{:S(2)}) copy-start(f32[1,1024]{1,0:T(1,128)} %get-tuple-element.44) | copy-start | bytes 12292
  126.8 10.6 %copy-start.15 = (f32[1,1024]{1,0:T(1,128)S(1)}, f32[1,1024]{1,0:T(1,128)}, u32[]{:S(2)}) copy-start(f32[1,1024]{1,0:T(1,128)} %get-tuple-element.45) | copy-start | bytes 12292
  126.8 10.6 %copy-start.16 = (s32[1024]{0:T(1024)S(1)}, s32[1024]{0:T(1024)}, u32[]{:S(2)}) copy-start(s32[1024]{0:T(1024)} %add_select_fusion.1) | copy-start | bytes 12292
  143.2 0.7 copy-start.21
  145.4 20.3 %all-to-all-start.3 = ((f32[64,2,3,256]{3,1,2,0:T(2,128)}), f32[64,2,3,256]{3,1,2,0:T(2,128)S(1)}, u32[]{:S(2)}, u32[]{:S(2)}) async-start(f32[64,2,3,256]{3,1,2,0:T(2,128)} %copy.83), calls=%async_computation.3 | async-start | bytes 786432 | tf_op jit(solution)/shard_map/all_to_all | solution.py:139
  168.1 5.0 %collective-permute-start.8 = (f32[32,3,256]{2,0,1:T(8,128)S(1)}, f32[32,3,256]{2,0,1:T(8,128)S(1)}, u32[]{:S(2)}, u32[]{:S(2)}) collective-permute-start(f32[32,3,256]{2,0,1:T(8,128)S(1)} %fusion.42), channel_id=1, source_target_pairs={{0,1},{1,0},{2,3},{3,2},{4,5},{5,4},{6,7},{7,6},{8,9},{9,8},{10,11... | collective-permute-start | bytes 294920 | tf_op jit(solution)/shard_map/ppermute | solution.py:58
  173.1 6.2 %collective-permute-start.9 = (f32[32,3,256]{2,0,1:T(8,128)S(1)}, f32[32,3,256]{2,0,1:T(8,128)S(1)}, u32[]{:S(2)}, u32[]{:S(2)}) collective-permute-start(f32[32,3,256]{2,0,1:T(8,128)S(1)} %add.317), channel_id=1, source_target_pairs={{0,2},{1,3},{2,0},{3,1},{4,6},{5,7},{6,4},{7,5},{8,10},{9,11},{10,... | collective-permute-start | bytes 294920 | tf_op jit(solution)/shard_map/ppermute | solution.py:58

commit v7 on v6

--- a/solution.py
+++ b/solution.py
@@ -34,7 +34,7 @@
 
 
 def symmetric_gather(block_rows, group_wafer, tm_index, tm_count):
-    _, rows, det_total = block_rows.shape
+    _, _, det_total = block_rows.shape
     groups = 8
     lanes = det_total // groups
     sent_groups = groups // 2 + 1
@@ -100,10 +100,7 @@
     requests = requests.reshape(tm_count, capacity)
     asked_slots = lax.all_to_all(requests, "tm", split_axis=0, concat_axis=0, tiled=True)
     served = jnp.take(short_map, asked_slots, axis=0)
-    replies, asked_slots = (
-        lax.all_to_all(served, "tm", split_axis=0, concat_axis=0, tiled=True),
-        asked_slots,
-    )
+    replies = lax.all_to_all(served, "tm", split_axis=0, concat_axis=0, tiled=True)
     fetched = jnp.take(
         replies.reshape(tm_count * capacity, comp_count, pixel_count), targets, axis=0
     )
@@ -168,4 +165,5 @@
         P(),
     )
     out_specs = (P("tm", None, None), P("tm", None, None), P("tm", None, None))
+
     return jax.shard_map(shards, mesh=mesh, in_specs=in_specs, out_specs=out_specs, check_vma=False)

time: 183 us -> 183 us (level)
  no operation moved by 1% of the time
where the time goes in v7:
time: 183 us; the launch traced here: 182 us
  local copies, waits for them, and re-layouts  55.2 us (30%)
  starting transfers between devices  52.2 us (29%)
  waiting for transfers between devices  29.1 us (16%)
  other arithmetic  25.4 us (14%)
  matrix products  18.5 us (10%)
    dynamic_update_slice x8, local copies, waits for them, and re-layouts, wafer_columns(): placed = lax.dynamic_update_slice_in_dim(placed, piece[None], source, 0)  14.2 us
    ppermute x6, starting transfers between devices, wafer_columns(): lax.ppermute(piece, 'wafer', [(i, (i + shift) % size) for i in range(size)])  12.5 us
    all_to_all x1, starting transfers between devices, shards(): lax.all_to_all(requests, 'tm', split_axis=0, concat_axis=0, tiled=True)  12 us
    all_to_all x1, waiting for transfers between devices, shards(): lax.all_to_all(outgoing, 'tm', split_axis=0, concat_axis=0, tiled=True)  11.2 us
    dot_general x1, matrix products, shards(): jnp.dot(matrix, filtered, preferred_element_type=jnp.float32)  10.5 us
    all_to_all x1, starting transfers between devices, shards(): lax.all_to_all(served, 'tm', split_axis=0, concat_axis=0, tiled=True)  10.3 us
    unnamed x55, local copies, waits for them, and re-layouts  10.1 us
    all_to_all x1, starting transfers between devices, symmetric_gather(): got = lax.all_to_all(sent, 'tm', split_axis=0, concat_axis=0, tiled=True)  8.72 us
  transfers between devices with their start and end apart: 14, of which 6 were waited for; matrix products, arithmetic and copies ran while one was open for 32% of the time, Pallas kernels for 0%

profile of v7, /device:TPU:2, one launch (start us, length us, event | category | flops | bytes accessed | tf_op | source)
XLA Modules:
  0.0 181.6 jit_solution(1206577866350822326)
XLA Ops:
  0.7 2.7 %constant_dynamic-slice_fusion = (bf16[256,1024]{1,0:T(8,128)(2,1)}, bf16[256,1024]{1,0:T(8,128)(2,1)}, bf16[256,1024]{1,0:T(8,128)(2,1)}) fusion(bf16[256,4096]{1,0:T(8,128)(2,1)} %param.13, s32[]{:T(128)S(6)} %select_n.353, s32[]{:T(128)S(6)} %select_n.345, s32[]{:T(128)S(6)} %select_n.349), kind=kLoop, calls=%fused_computation.118 | loop fusion | bytes 3145740 | tf_op jit(solution)/shard_map/dynamic_slice | solution.py:26
  3.5 1.7 collective-permute-start.5
  5.1 2.9 %collective-permute-start.6 = (bf16[256,1024]{1,0:T(8,128)(2,1)}, bf16[256,1024]{1,0:T(8,128)(2,1)}, u32[]{:S(2)}, u32[]{:S(2)}) collective-permute-start(bf16[256,1024]{1,0:T(8,128)(2,1)} %get-tuple-element.29), channel_id=1, source_target_pairs={{0,2},{1,3},{2,0},{3,1},{4,6},{5,7},{6,4},{7,5},{8,10},{9,11},{10,... | collective-permute-start | bytes 1572872 | tf_op jit(solution)/shard_map/ppermute | solution.py:27
  8.0 1.3 collective-permute-start.7
  9.4 0.7 collective-permute-start
  10.0 1.3 constant_dynamic-slice_fusion.3
  11.3 1.3 collective-permute-start.2
  12.8 0.7 gather_fusion
  13.9 0.8 all_to_all.19
  14.6 12.0 %all-to-all-start = ((s32[64,1,2]{2,1,0:T(1,128)}), s32[64,1,2]{2,1,0:T(1,128)S(1)}, u32[]{:S(2)}, u32[]{:S(2)}) async-start(s32[64,1,2]{2,1,0:T(1,128)} %bitcast.2), calls=%async_computation | async-start | bytes 65536 | tf_op jit(solution)/shard_map/all_to_all | solution.py:101
  27.2 0.6 add_select_fusion.3
  28.5 0.6 add_select_fusion.1
  29.1 0.6 fusion.75
  29.7 0.6 slice_reduce_fusion.2
  30.4 0.6 pad_clamp_fusion.2
  30.9 1.6 broadcast.640.clone
  32.5 2.0 %bitcast_dynamic-update-slice_fusion.3 = bf16[4,256,1024]{2,1,0:T(8,128)(2,1)} fusion(bf16[4,256,1024]{2,1,0:T(8,128)(2,1)} %broadcast.640.clone, s32[]{:T(128)S(6)} %select_n.343, bf16[256,4096]{1,0:T(8,128)(2,1)} %param.13, s32[]{:T(128)S(6)} %select_n.341), kind=kLoop, calls=%fused_computation.38 | loop fusion | bytes 1048584 | tf_op jit(solution)/shard_map/dynamic_update_slice | solution.py:32
  34.5 1.7 broadcast.640.clone.1
  36.1 1.9 %bitcast_dynamic-update-slice_fusion.7 = bf16[4,256,1024]{2,1,0:T(8,128)(2,1)} fusion(bf16[4,256,1024]{2,1,0:T(8,128)(2,1)} %broadcast.640.clone.1, s32[]{:T(128)S(6)} %select_n.343, bf16[256,4096]{1,0:T(8,128)(2,1)} %param.12, s32[]{:T(128)S(6)} %select_n.341), kind=kLoop, calls=%fused_computation.42 | loop fusion | bytes 1048584 | tf_op jit(solution)/shard_map/dynamic_update_slice | solution.py:32
  38.6 4.2 %compare_select_fusion.1 = bf16[4,256,4,256]{3,2,1,0:T(4,128)(2,1)} fusion(s32[4,256]{1,0:T(4,128)S(1)} %add_select_fusion.2, bf16[256,256]{1,0:T(8,128)(2,1)S(1)} %copy-done.5), kind=kLoop, calls=%fused_computation.18 | loop fusion | flops 2097152 | bytes 2232320 | tf_op jit(solution)/shard_map/jit(_where)/select_n | solution.py:121
  42.8 1.4 fusion.72
  44.8 0.8 gather_fusion.2
  45.7 1.7 maximum_select_fusion.1
  47.6 1.0 broadcast_select_fusion.1
  48.6 10.3 %all-to-all-start.2 = ((bf16[64,2,3,256]{3,1,2,0:T(2,128)(2,1)}), bf16[64,2,3,256]{3,1,2,0:T(2,128)(2,1)S(1)}, u32[]{:S(2)}, u32[]{:S(2)}) async-start(bf16[64,2,3,256]{3,1,2,0:T(2,128)(2,1)} %broadcast_select_fusion.1), calls=%async_computation.2 | async-start | bytes 393216 | tf_op jit(solution)/shard_map/all_to_all | solution.py:103
  58.9 3.3 %collective-permute-start.3 = (bf16[256,1024]{1,0:T(8,128)(2,1)}, bf16[256,1024]{1,0:T(8,128)(2,1)}, u32[]{:S(2)}, u32[]{:S(2)}) collective-permute-start(bf16[256,1024]{1,0:T(8,128)(2,1)} %get-tuple-element.32), channel_id=1, source_target_pairs={{0,2},{1,3},{2,0},{3,1},{4,6},{5,7},{6,4},{7,5},{8,10},{9,11},{10,... | collective-permute-start | bytes 1572872 | tf_op jit(solution)/shard_map/ppermute | solution.py:27
  62.2 1.1 maximum_select_fusion
  63.4 1.9 %gather_fusion.1 = bf16[64,16,640]{2,1,0:T(8,128)(2,1)} fusion(bf16[7,16,640]{2,1,0:T(8,128)(2,1)S(1)} %fusion.33, s32[1024]{0:T(1024)} %pad_clamp_fusion.2), kind=kCustom, calls=%fused_computation.1 | custom fusion | bytes 2621696 | tf_op jit(solution)/shard_map/jit(_take)/gather | solution.py:43
  65.3 2.6 %broadcast_select_fusion = bf16[64,16,640]{2,1,0:T(8,128)(2,1)} fusion(bf16[64,16,640]{2,1,0:T(8,128)(2,1)} %gather_fusion.1, pred[64]{0:T(512)(128)(4,1)S(1)} %copy-done.23), kind=kLoop, calls=%fused_computation.32 | loop fusion | flops 655360 | bytes 2621504 | tf_op jit(solution)/shard_map/jit(_take)/select_n | solution.py:43
  67.9 1.8 all-to-all-done.2
  69.7 8.7 %all-to-all-start.1 = ((bf16[64,16,640]{2,1,0:T(8,128)(2,1)}), bf16[64,16,640]{2,1,0:T(8,128)(2,1)}, u32[]{:S(2)}, u32[]{:S(2)}) async-start(bf16[64,16,640]{2,1,0:T(8,128)(2,1)} %broadcast_select_fusion), calls=%async_computation.1 | async-start | bytes 2621440 | tf_op jit(solution)/shard_map/all_to_all | solution.py:44
  78.6 3.4 %copy.92 = bf16[128,8,4,256]{3,1,2,0:T(8,128)(2,1)} copy(bf16[128,8,4,256]{3,2,1,0:T(4,128)(2,1)} %bitcast.159) | data formatting | bytes 4194304
  82.6 1.8 %copy.93 = bf16[128,8,4,256]{3,1,2,0:T(8,128)(2,1)} copy(bf16[128,8,4,256]{3,2,1,0:T(4,128)(2,1)S(1)} %bitcast.160) | data formatting | bytes 4194304
  84.4 0.8 copy.78
  85.2 1.6 gather_fusion.3
  86.8 0.9 convolution_bitcast_fusion
  87.8 1.9 %collective-permute-start.4 = (bf16[256,1024]{1,0:T(8,128)(2,1)S(1)}, bf16[256,1024]{1,0:T(8,128)(2,1)S(1)}, u32[]{:S(2)}, u32[]{:S(2)}) collective-permute-start(bf16[256,1024]{1,0:T(8,128)(2,1)S(1)} %copy-done.4), channel_id=1, source_target_pairs={{0,3},{1,0},{2,1},{3,2},{4,7},{5,4},{6,5},{7,6},{8,11},{9,8},{10,9... | collective-permute-start | bytes 1572872 | tf_op jit(solution)/shard_map/ppermute | solution.py:27
  89.7 1.9 %bitcast_dynamic-update-slice_fusion.2 = bf16[4,256,1024]{2,1,0:T(8,128)(2,1)} fusion(bf16[4,256,1024]{2,1,0:T(8,128)(2,1)} %bitcast_dynamic-update-slice_fusion.3, s32[]{:T(128)S(6)} %select_n.347, bf16[256,1024]{1,0:T(8,128)(2,1)} %collective-permute-done.5), kind=kLoop, calls=%fused_computation.37 | loop fusion | bytes 1048580 | tf_op jit(solution)/shard_map/dynamic_update_slice | solution.py:32
  91.6 1.9 %bitcast_dynamic-update-slice_fusion.6 = bf16[4,256,1024]{2,1,0:T(8,128)(2,1)} fusion(bf16[4,256,1024]{2,1,0:T(8,128)(2,1)} %bitcast_dynamic-update-slice_fusion.7, s32[]{:T(128)S(6)} %select_n.347, bf16[256,1024]{1,0:T(8,128)(2,1)} %collective-permute-done.2), kind=kLoop, calls=%fused_computation.41 | loop fusion | bytes 1048580 | tf_op jit(solution)/shard_map/dynamic_update_slice | solution.py:32
  93.6 1.9 %bitcast_dynamic-update-slice_fusion.1 = bf16[4,256,1024]{2,1,0:T(8,128)(2,1)} fusion(bf16[4,256,1024]{2,1,0:T(8,128)(2,1)} %bitcast_dynamic-update-slice_fusion.2, s32[]{:T(128)S(6)} %select_n.351, bf16[256,1024]{1,0:T(8,128)(2,1)} %collective-permute-done.6), kind=kLoop, calls=%fused_computation.36 | loop fusion | bytes 1048580 | tf_op jit(solution)/shard_map/dynamic_update_slice | solution.py:32
  95.4 1.9 %bitcast_dynamic-update-slice_fusion.5 = bf16[4,256,1024]{2,1,0:T(8,128)(2,1)} fusion(bf16[4,256,1024]{2,1,0:T(8,128)(2,1)} %bitcast_dynamic-update-slice_fusion.6, s32[]{:T(128)S(6)} %select_n.351, bf16[256,1024]{1,0:T(8,128)(2,1)} %collective-permute-done.3), kind=kLoop, calls=%fused_computation.40 | loop fusion | bytes 1048580 | tf_op jit(solution)/shard_map/dynamic_update_slice | solution.py:32
  97.3 1.9 %bitcast_dynamic-update-slice_fusion = bf16[4,256,1024]{2,1,0:T(8,128)(2,1)} fusion(bf16[4,256,1024]{2,1,0:T(8,128)(2,1)} %bitcast_dynamic-update-slice_fusion.1, s32[]{:T(128)S(6)} %select_n.355, bf16[256,1024]{1,0:T(8,128)(2,1)} %collective-permute-done.7), kind=kLoop, calls=%fused_computation.35 | loop fusion | bytes 1048580 | tf_op jit(solution)/shard_map/dynamic_update_slice | solution.py:32
  99.2 2.6 %collective-permute-done.4 = bf16[256,1024]{1,0:T(8,128)(2,1)S(1)} collective-permute-done((bf16[256,1024]{1,0:T(8,128)(2,1)S(1)}, bf16[256,1024]{1,0:T(8,128)(2,1)S(1)}, u32[]{:S(2)}, u32[]{:S(2)}) %collective-permute-start.4) | collective-permute-done | bytes 524320 | tf_op jit(solution)/shard_map/ppermute | solution.py:27
  101.8 0.8 bitcast_dynamic-update-slice_fusion.4
  102.6 4.1 %multiply_convert_fusion = bf16[4,256,1024]{2,1,0:T(8,128)(2,1)} fusion(bf16[4,256,1024]{2,1,0:T(8,128)(2,1)} %bitcast_dynamic-update-slice_fusion.4, f32[1024]{0:T(1024)S(1)} %bitcast.178, f32[4,256]{1,0:T(4,128)S(1)} %mul.170, f32[1024]{0:T(1024)S(1)} %bitcast.179, f32[4,256]{1,0:T(4,128)S(1)} %mul.165, f32[1024]{0:T(1024)S(1)} %bitcast.177, ...), kind=kLoop, calls=%fused_computation.15 | loop fusion | flops 10485760 | bytes 6316032 | tf_op jit(solution)/shard_map/convert_element_type | solution.py:118
  106.7 6.0 %all-to-all-done.1 = bf16[64,16,640]{2,1,0:T(8,128)(2,1)} async-done(((bf16[64,16,640]{2,1,0:T(8,128)(2,1)}), bf16[64,16,640]{2,1,0:T(8,128)(2,1)}, u32[]{:S(2)}, u32[]{:S(2)}) %all-to-all-start.1) | async-done | bytes 1310752 | tf_op jit(solution)/shard_map/all_to_all | solution.py:44
  112.7 4.2 %reshape.470 = bf16[8,128,5,128]{3,2,1,0:T(8,128)(2,1)} reshape(bf16[64,16,640]{2,1,0:T(8,128)(2,1)} %all-to-all-done.1) | data formatting | bytes 2621440 | tf_op jit(solution)/shard_map/reshape | solution.py:45
  116.9 2.0 %fusion.25 = (bf16[128,8,128]{2,1,0:T(8,128)(2,1)S(1)}, bf16[128,8,128]{2,1,0:T(8,128)(2,1)S(1)}, bf16[128,8,128]{2,1,0:T(8,128)(2,1)S(1)}, bf16[128,8,128]{2,1,...) fusion(bf16[8,128,5,128]{3,2,1,0:T(8,128)(2,1)} %reshape.470), kind=kLoop, calls=%fused_computation.61 | loop fusion | bytes 3407872 | tf_op jit(solution)/shard_map/squeeze | solution.py:47
  120.8 2.0 %copy.114 = bf16[128,8,8,128]{3,1,2,0:T(8,128)(2,1)} copy(bf16[128,8,8,128]{3,2,1,0:T(8,128)(2,1)S(1)} %bitcast.162) | data formatting | bytes 4194304
  122.8 4.0 %copy.72 = bf16[1024,1024]{0,1:T(8,128)(2,1)} copy(bf16[1024,1024]{1,0:T(8,128)(2,1)} %bitcast.161) | data formatting | bytes 4194304 | tf_op jit(solution)/shard_map/reshape | solution.py:48
  126.8 10.5 %fusion.6 = bf16[1024,1024]{1,0:T(8,128)(2,1)} fusion(bf16[1024,1024]{0,1:T(8,128)(2,1)} %copy.72, s32[1024]{0:T(1024)S(1)} %copy-done.17, bf16[1024,1024]{1,0:T(8,128)(2,1)} %bitcast.167, bf16[1024,1024]{1,0:T(8,128)(2,1)} %bitcast.166, bf16[128,8,8,128]{3,2,1,0:T(8,128)(2,1)} %bitcast.163), kind=kOutput, calls=%fused_computation.23 | convolution fusion | flops 4310695936 | bytes 10489856 | tf_op jit(solution)/shard_map/dot_general | solution.py:123
  137.4 5.8 %multiply_reduce_fusion.2 = (bf16[1024]{0:T(1024)(128)(2,1)S(1)}, bf16[1024]{0:T(1024)(128)(2,1)S(1)}, bf16[1024]{0:T(1024)(128)(2,1)S(1)}) fusion(f32[1024]{0:T(1024)S(1)} %bitcast.182, f32[1024]{0:T(1024)S(1)} %bitcast.181, f32[1024]{0:T(1024)S(1)} %bitcast.180, bf16[4,256,1024]{2,1,0:T(8,128)(2,1)} %bitcast_dynamic-update-slice_fusion, ...), kind=kOutput, calls=%fused_computation.14 | convolution fusion | flops 2160063488 | bytes 6313984 | tf_op jit(solution)/shard_map/dot_general | solution.py:124
  144.3 1.1 copy.83
  145.4 5.6 %all-to-all-start.3 = ((f32[64,2,3,256]{3,1,2,0:T(2,128)}), f32[64,2,3,256]{3,1,2,0:T(2,128)S(1)}, u32[]{:S(2)}, u32[]{:S(2)}) async-start(f32[64,2,3,256]{3,1,2,0:T(2,128)} %copy.83), calls=%async_computation.3 | async-start | bytes 786432 | tf_op jit(solution)/shard_map/all_to_all | solution.py:136
  151.4 2.1 %reduce.15 = s32[64,2]{1,0:T(8,128)} reduce(s32[64,1,2]{2,1,0:T(1,128)} %copy-done.8, s32[]{:T(128)} %broadcast.687), dimensions={1}, to_apply=%all_to_all.20.reduce_sub_computation.3 | reduce | bytes 1028 | tf_op jit(solution)/shard_map/all_to_all | solution.py:101
  153.5 0.9 eq.123
  154.4 11.2 %all-to-all-done.3 = f32[64,2,3,256]{3,1,2,0:T(2,128)S(1)} async-done(((f32[64,2,3,256]{3,1,2,0:T(2,128)}), f32[64,2,3,256]{3,1,2,0:T(2,128)S(1)}, u32[]{:S(2)}, u32[]{:S(2)}) %all-to-all-start.3) | async-done | bytes 393248 | tf_op jit(solution)/shard_map/all_to_all | solution.py:136
  165.8 0.8 copy.95
  166.6 1.1 copy.85
  168.5 4.5 %collective-permute-done.8 = f32[32,3,256]{2,0,1:T(8,128)S(1)} collective-permute-done((f32[32,3,256]{2,0,1:T(8,128)S(1)}, f32[32,3,256]{2,0,1:T(8,128)S(1)}, u32[]{:S(2)}, u32[]{:S(2)}) %collective-permute-start.8) | collective-permute-done | bytes 98336 | tf_op jit(solution)/shard_map/ppermute | solution.py:58
  173.1 1.7 collective-permute-start.9
  174.8 1.6 copy.86
  176.4 2.9 %collective-permute-done.9 = f32[32,3,256]{2,0,1:T(8,128)S(1)} collective-permute-done((f32[32,3,256]{2,0,1:T(8,128)S(1)}, f32[32,3,256]{2,0,1:T(8,128)S(1)}, u32[]{:S(2)}, u32[]{:S(2)}) %collective-permute-start.9) | collective-permute-done | bytes 98336 | tf_op jit(solution)/shard_map/ppermute | solution.py:58
  179.3 2.3 %multiply_add_fusion = (f32[32,3,256]{2,0,1:T(8,128)}, f32[32,3,256]{2,0,1:T(8,128)}) fusion(f32[32,3,256]{2,0,1:T(8,128)} %param.22, f32[]{:T(128)} %bitcast.57, f32[32,3,256]{2,0,1:T(8,128)S(1)} %add.317, f32[32,3,256]{2,0,1:T(8,128)S(1)} %collective-permute-done.9), kind=kLoop, calls=%fused_computation.81 | loop fusion | flops 98304 | bytes 491524 | tf_op jit(solution)/shard_map/add | solution.py:148
  (116 shorter events, 8.3 us)
Async XLA Ops:
  0.6 86.1 %copy-start = (bf16[4,6,256,256]{3,2,1,0:T(8,128)(2,1)S(1)}, bf16[4,6,256,256]{3,2,1,0:T(8,128)(2,1)}, u32[]{:S(2)}) copy-start(bf16[4,6,256,256]{3,2,1,0:T(8,128)(2,1)} %param.18) | copy-start | bytes 9437188
  0.6 8.7 %copy-start.10 = (bf16[7,4,1024]{2,1,0:T(4,128)(2,1)S(1)}, bf16[7,4,1024]{2,1,0:T(4,128)(2,1)}, u32[]{:S(2)}) copy-start(bf16[7,4,1024]{2,1,0:T(4,128)(2,1)} %param.16) | copy-start | bytes 172036
  0.7 9.3 %copy-start.3 = (bf16[256,4096]{1,0:T(8,128)(2,1)S(1)}, bf16[256,4096]{1,0:T(8,128)(2,1)}, u32[]{:S(2)}) copy-start(bf16[256,4096]{1,0:T(8,128)(2,1)} %param.12) | copy-start | bytes 6291460
  3.4 9.2 %copy-start.11 = (s32[4,6]{1,0:T(4,128)S(1)}, s32[4,6]{1,0:T(4,128)}, u32[]{:S(2)}) copy-start(s32[4,6]{1,0:T(4,128)} %param.19) | copy-start | bytes 292
  3.4 9.4 %copy-start.1 = (s32[2048]{0:T(1024)S(1)}, s32[2048]{0:T(1024)}, u32[]{:S(2)}) copy-start(s32[2048]{0:T(1024)} %param.20) | copy-start | bytes 24580
  3.4 23.2 %copy-start.24 = (s32[64]{0:T(128)S(1)}, s32[64]{0:T(128)}, u32[]{:S(2)}) copy-start(s32[64]{0:T(128)} %param.17) | copy-start | bytes 772
  3.4 25.6 %copy-start.18 = (f32[2]{0:T(128)S(1)}, f32[2]{0:T(128)}, u32[]{:S(2)}) copy-start(f32[2]{0:T(128)} %param.23) | copy-start | bytes 28
  3.4 26.3 %copy-start.12 = (f32[3,1024]{1,0:T(4,128)S(1)}, f32[3,1024]{1,0:T(4,128)}, u32[]{:S(2)}) copy-start(f32[3,1024]{1,0:T(4,128)} %param.14) | copy-start | bytes 36868
  3.5 84.3 %collective-permute-start.5 = (bf16[256,1024]{1,0:T(8,128)(2,1)}, bf16[256,1024]{1,0:T(8,128)(2,1)}, u32[]{:S(2)}, u32[]{:S(2)}) collective-permute-start(bf16[256,1024]{1,0:T(8,128)(2,1)} %get-tuple-element.28), channel_id=1, source_target_pairs={{0,1},{1,2},{2,3},{3,0},{4,5},{5,6},{6,7},{7,4},{8,9},{9,10},{10,1... | collective-permute-start | bytes 1572872 | tf_op jit(solution)/shard_map/ppermute | solution.py:27
  5.1 88.5 %collective-permute-start.6 = (bf16[256,1024]{1,0:T(8,128)(2,1)}, bf16[256,1024]{1,0:T(8,128)(2,1)}, u32[]{:S(2)}, u32[]{:S(2)}) collective-permute-start(bf16[256,1024]{1,0:T(8,128)(2,1)} %get-tuple-element.29), channel_id=1, source_target_pairs={{0,2},{1,3},{2,0},{3,1},{4,6},{5,7},{6,4},{7,5},{8,10},{9,11},{10,... | collective-permute-start | bytes 1572872 | tf_op jit(solution)/shard_map/ppermute | solution.py:27
  8.0 89.3 %collective-permute-start.7 = (bf16[256,1024]{1,0:T(8,128)(2,1)}, bf16[256,1024]{1,0:T(8,128)(2,1)}, u32[]{:S(2)}, u32[]{:S(2)}) collective-permute-start(bf16[256,1024]{1,0:T(8,128)(2,1)} %get-tuple-element.27), channel_id=1, source_target_pairs={{0,3},{1,0},{2,1},{3,2},{4,7},{5,4},{6,5},{7,6},{8,11},{9,8},{10,9... | collective-permute-start | bytes 1572872 | tf_op jit(solution)/shard_map/ppermute | solution.py:27
  9.4 36.3 %collective-permute-start = (bf16[7,4,1024]{2,1,0:T(4,128)(2,1)S(1)}, bf16[7,4,1024]{2,1,0:T(4,128)(2,1)}, u32[]{:S(2)}, u32[]{:S(2)}) collective-permute-start(bf16[7,4,1024]{2,1,0:T(4,128)(2,1)S(1)} %copy-done.10), channel_id=1, source_target_pairs={{0,1},{1,0},{2,3},{3,2},{4,5},{5,4},{6,7},{7,6},{8,9},{9,8},{10,11... | collective-permute-start | bytes 172040 | tf_op jit(solution)/shard_map/ppermute | solution.py:12
  11.3 80.3 %collective-permute-start.2 = (bf16[256,1024]{1,0:T(8,128)(2,1)}, bf16[256,1024]{1,0:T(8,128)(2,1)}, u32[]{:S(2)}, u32[]{:S(2)}) collective-permute-start(bf16[256,1024]{1,0:T(8,128)(2,1)} %get-tuple-element.31), channel_id=1, source_target_pairs={{0,1},{1,2},{2,3},{3,0},{4,5},{5,6},{6,7},{7,4},{8,9},{9,10},{10,1... | collective-permute-start | bytes 1572872 | tf_op jit(solution)/shard_map/ppermute | solution.py:27
  13.8 22.4 %copy-start.20 = (s32[24]{0:T(128)}, s32[24]{0:T(128)S(1)}, u32[]{:S(2)}) copy-start(s32[24]{0:T(128)S(1)} %get-tuple-element.52) | copy-start | bytes 292
  14.6 29.6 %all-to-all-start = ((s32[64,1,2]{2,1,0:T(1,128)}), s32[64,1,2]{2,1,0:T(1,128)S(1)}, u32[]{:S(2)}, u32[]{:S(2)}) async-start(s32[64,1,2]{2,1,0:T(1,128)} %bitcast.2), calls=%async_computation | async-start | bytes 65536 | tf_op jit(solution)/shard_map/all_to_all | solution.py:101
  32.5 6.1 %copy-start.5 = (bf16[256,256]{1,0:T(8,128)(2,1)S(1)}, bf16[256,256]{1,0:T(8,128)(2,1)}, u32[]{:S(2)}) copy-start(bf16[256,256]{1,0:T(8,128)(2,1)} %param.15) | copy-start | bytes 393220
  36.1 6.7 %copy-start.7 = (f32[32,3,256]{2,0,1:T(8,128)S(1)}, f32[32,3,256]{2,0,1:T(8,128)}, u32[]{:S(2)}) copy-start(f32[32,3,256]{2,0,1:T(8,128)} %param.22) | copy-start | bytes 294916
  36.1 6.7 %copy-start.9 = (f32[32,3,256]{2,0,1:T(8,128)S(1)}, f32[32,3,256]{2,0,1:T(8,128)}, u32[]{:S(2)}) copy-start(f32[32,3,256]{2,0,1:T(8,128)} %param.21) | copy-start | bytes 294916
  44.2 0.6 copy-start.8
  47.3 11.5 %collective-permute-start.1 = (bf16[7,8,1024]{2,1,0:T(8,128)(2,1)}, bf16[7,8,1024]{2,1,0:T(8,128)(2,1)}, u32[]{:S(2)}, u32[]{:S(2)}) collective-permute-start(bf16[7,8,1024]{2,1,0:T(8,128)(2,1)} %maximum_select_fusion.1), channel_id=1, source_target_pairs={{0,2},{1,3},{2,0},{3,1},{4,6},{5,7},{6,4},{7,5},{8,10},{9,11},{10,... | collective-permute-start | bytes 344072 | tf_op jit(solution)/shard_map/ppermute | solution.py:12
  47.6 17.7 %copy-start.23 = (pred[64]{0:T(512)(128)(4,1)S(1)}, pred[64]{0:T(512)(128)(4,1)}, u32[]{:S(2)}) copy-start(pred[64]{0:T(512)(128)(4,1)} %compare_and_fusion.2) | copy-start | bytes 196
  48.6 21.1 %all-to-all-start.2 = ((bf16[64,2,3,256]{3,1,2,0:T(2,128)(2,1)}), bf16[64,2,3,256]{3,1,2,0:T(2,128)(2,1)S(1)}, u32[]{:S(2)}, u32[]{:S(2)}) async-start(bf16[64,2,3,256]{3,1,2,0:T(2,128)(2,1)} %broadcast_select_fusion.1), calls=%async_computation.2 | async-start | bytes 393216 | tf_op jit(solution)/shard_map/all_to_all | solution.py:103
  58.9 36.6 %collective-permute-start.3 = (bf16[256,1024]{1,0:T(8,128)(2,1)}, bf16[256,1024]{1,0:T(8,128)(2,1)}, u32[]{:S(2)}, u32[]{:S(2)}) collective-permute-start(bf16[256,1024]{1,0:T(8,128)(2,1)} %get-tuple-element.32), channel_id=1, source_target_pairs={{0,2},{1,3},{2,0},{3,1},{4,6},{5,7},{6,4},{7,5},{8,10},{9,11},{10,... | collective-permute-start | bytes 1572872 | tf_op jit(solution)/shard_map/ppermute | solution.py:27
  65.3 13.1 %copy-start.19 = (s32[24]{0:T(128)S(1)}, s32[24]{0:T(128)}, u32[]{:S(2)}) copy-start(s32[24]{0:T(128)} %fusion.64) | copy-start | bytes 292
  69.7 43.0 %all-to-all-start.1 = ((bf16[64,16,640]{2,1,0:T(8,128)(2,1)}), bf16[64,16,640]{2,1,0:T(8,128)(2,1)}, u32[]{:S(2)}, u32[]{:S(2)}) async-start(bf16[64,16,640]{2,1,0:T(8,128)(2,1)} %broadcast_select_fusion), calls=%async_computation.1 | async-start | bytes 2621440 | tf_op jit(solution)/shard_map/all_to_all | solution.py:44
  78.5 3.4 %copy-start.6 = (bf16[256,256]{1,0:T(8,128)(2,1)S(1)}, bf16[256,256]{1,0:T(8,128)(2,1)}, u32[]{:S(2)}) copy-start(bf16[256,256]{1,0:T(8,128)(2,1)} %param.15) | copy-start | bytes 393220
  82.5 4.2 %copy-start.22 = (pred[4,6]{1,0:T(4,128)(4,1)S(1)}, pred[4,6]{1,0:T(4,128)(4,1)}, u32[]{:S(2)}) copy-start(pred[4,6]{1,0:T(4,128)(4,1)} %compare_and_fusion.1) | copy-start | bytes 76
  86.8 1.0 copy-start.4
  87.8 14.0 %collective-permute-start.4 = (bf16[256,1024]{1,0:T(8,128)(2,1)S(1)}, bf16[256,1024]{1,0:T(8,128)(2,1)S(1)}, u32[]{:S(2)}, u32[]{:S(2)}) collective-permute-start(bf16[256,1024]{1,0:T(8,128)(2,1)S(1)} %copy-done.4), channel_id=1, source_target_pairs={{0,3},{1,0},{2,1},{3,2},{4,7},{5,4},{6,5},{7,6},{8,11},{9,8},{10,9... | collective-permute-start | bytes 1572872 | tf_op jit(solution)/shard_map/ppermute | solution.py:27
  120.8 2.0 %copy-start.2 = (bf16[8,128,8,128]{3,2,1,0:T(8,128)(2,1)}, bf16[8,128,8,128]{3,2,1,0:T(8,128)(2,1)S(1)}, u32[]{:S(2)}) copy-start(bf16[8,128,8,128]{3,2,1,0:T(8,128)(2,1)S(1)} %fusion.32) | copy-start | bytes 6291460
  122.8 4.0 %copy-start.17 = (s32[1024]{0:T(1024)S(1)}, s32[1024]{0:T(1024)}, u32[]{:S(2)}) copy-start(s32[1024]{0:T(1024)} %add_select_fusion.3) | copy-start | bytes 12292
  126.8 10.6 %copy-start.13 = (f32[1,1024]{1,0:T(1,128)S(1)}, f32[1,1024]{1,0:T(1,128)}, u32[]{:S(2)}) copy-start(f32[1,1024]{1,0:T(1,128)} %get-tuple-element.43) | copy-start | bytes 12292
  126.8 10.6 %copy-start.14 = (f32[1,1024]{1,0:T(1,128)S(1)}, f32[1,1024]{1,0:T(1,128)}, u32[]{:S(2)}) copy-start(f32[1,1024]{1,0:T(1,128)} %get-tuple-element.44) | copy-start | bytes 12292
  126.8 10.6 %copy-start.15 = (f32[1,1024]{1,0:T(1,128)S(1)}, f32[1,1024]{1,0:T(1,128)}, u32[]{:S(2)}) copy-start(f32[1,1024]{1,0:T(1,128)} %get-tuple-element.45) | copy-start | bytes 12292
  126.8 10.6 %copy-start.16 = (s32[1024]{0:T(1024)S(1)}, s32[1024]{0:T(1024)}, u32[]{:S(2)}) copy-start(s32[1024]{0:T(1024)} %add_select_fusion.1) | copy-start | bytes 12292
  143.2 0.7 copy-start.21
  145.4 20.3 %all-to-all-start.3 = ((f32[64,2,3,256]{3,1,2,0:T(2,128)}), f32[64,2,3,256]{3,1,2,0:T(2,128)S(1)}, u32[]{:S(2)}, u32[]{:S(2)}) async-start(f32[64,2,3,256]{3,1,2,0:T(2,128)} %copy.83), calls=%async_computation.3 | async-start | bytes 786432 | tf_op jit(solution)/shard_map/all_to_all | solution.py:136
  168.1 5.0 %collective-permute-start.8 = (f32[32,3,256]{2,0,1:T(8,128)S(1)}, f32[32,3,256]{2,0,1:T(8,128)S(1)}, u32[]{:S(2)}, u32[]{:S(2)}) collective-permute-start(f32[32,3,256]{2,0,1:T(8,128)S(1)} %fusion.42), channel_id=1, source_target_pairs={{0,1},{1,0},{2,3},{3,2},{4,5},{5,4},{6,7},{7,6},{8,9},{9,8},{10,11... | collective-permute-start | bytes 294920 | tf_op jit(solution)/shard_map/ppermute | solution.py:58
  173.1 6.2 %collective-permute-start.9 = (f32[32,3,256]{2,0,1:T(8,128)S(1)}, f32[32,3,256]{2,0,1:T(8,128)S(1)}, u32[]{:S(2)}, u32[]{:S(2)}) collective-permute-start(f32[32,3,256]{2,0,1:T(8,128)S(1)} %add.317), channel_id=1, source_target_pairs={{0,2},{1,3},{2,0},{3,1},{4,6},{5,7},{6,4},{7,5},{8,10},{9,11},{10,... | collective-permute-start | bytes 294920 | tf_op jit(solution)/shard_map/ppermute | solution.py:58

commit v8 on v4

--- a/solution.py
+++ b/solution.py
@@ -34,12 +34,18 @@
 
 
 def wafer_sum(x):
+    spot = lax.axis_index("wafer")
     size = lax.axis_size("wafer")
-    bit = 1
-    while bit < size:
-        x = x + lax.ppermute(x, "wafer", [(i, i ^ bit) for i in range(size)])
-        bit *= 2
-    return x
+    terms = [x]
+    for shift in range(1, size):
+        terms.append(lax.ppermute(x, "wafer", [(i, (i + shift) % size) for i in range(size)]))
+    total = None
+    for source in range(size):
+        term = terms[0]
+        for shift in range(1, size):
+            term = jnp.where((spot - source) % size == shift, terms[shift], term)
+        total = term if total is None else total + term
+    return total
 
 
 def shards(

time: 176 us -> 176 us (level)
    ppermute x2 -> x3, waiting for transfers between devices: 4.81 us -> 3.62 us  [wafer_sum(): lax.ppermute(x, 'wafer', [(i, (i + shift) % size) for i in range(size)])]
    ppermute x2 -> x3, starting transfers between devices: 5.64 us -> 5.49 us  [wafer_sum(): lax.ppermute(x, 'wafer', [(i, (i + shift) % size) for i in range(size)])]
  transfers between devices with their start and end apart: 14 -> 15, of which waited for: 7 -> 8; matrix products, arithmetic and copies ran while one was open for 34% -> 34% of each run, Pallas kernels for 0% -> 0%
where the time goes in v8:
time: 176 us; the launch traced here: 174 us
  starting transfers between devices  56.5 us (32%)
  local copies, waits for them, and re-layouts  41.6 us (24%)
  waiting for transfers between devices  36.7 us (21%)
  other arithmetic  22.9 us (13%)
  matrix products  14.9 us (8%)
    dynamic_update_slice x8, local copies, waits for them, and re-layouts, wafer_columns(): placed = lax.dynamic_update_slice_in_dim(placed, piece[None], source, 0)  14 us
    all_to_all x1, starting transfers between devices, shards(): lax.all_to_all(served, 'tm', split_axis=0, concat_axis=0, tiled=True)  12.2 us
    all_to_all x1, starting transfers between devices, shards(): lax.all_to_all(requests, 'tm', split_axis=0, concat_axis=0, tiled=True)  12 us
    all_to_all x1, waiting for transfers between devices, shards(): lax.all_to_all(sent_blocks, 'tm', split_axis=0, concat_axis=0, tiled=True)  11.5 us
    ppermute x6, starting transfers between devices, wafer_columns(): lax.ppermute(piece, 'wafer', [(i, (i + shift) % size) for i in range(size)])  11.4 us
    all_to_all x1, waiting for transfers between devices, shards(): lax.all_to_all(outgoing, 'tm', split_axis=0, concat_axis=0, tiled=True)  11.2 us
    dot_general x1, matrix products, shards(): lax.dot_general(whitened, filter_blocks, (((1,), (1,)), ((), ())), prefer...  8.42 us
    unnamed x44, local copies, waits for them, and re-layouts  7.96 us
  transfers between devices with their start and end apart: 15, of which 8 were waited for; matrix products, arithmetic and copies ran while one was open for 34% of the time, Pallas kernels for 0%

profile of v8, /device:TPU:2, one launch (start us, length us, event | category | flops | bytes accessed | tf_op | source)
XLA Modules:
  0.0 173.7 jit_solution(6029141865720455568)
XLA Ops:
  0.7 2.8 %constant_dynamic-slice_fusion.3 = (bf16[256,1024]{1,0:T(8,128)(2,1)}, bf16[256,1024]{1,0:T(8,128)(2,1)}, bf16[256,1024]{1,0:T(8,128)(2,1)}) fusion(bf16[256,4096]{1,0:T(8,128)(2,1)} %param.12, s32[]{:T(128)S(6)} %select_n.409, s32[]{:T(128)S(6)} %select_n.401, s32[]{:T(128)S(6)} %select_n.405), kind=kLoop, calls=%fused_computation.79 | loop fusion | bytes 3145740 | tf_op jit(solution)/shard_map/dynamic_slice | solution.py:26
  3.5 1.7 collective-permute-start.2
  5.1 2.9 %collective-permute-start.3 = (bf16[256,1024]{1,0:T(8,128)(2,1)}, bf16[256,1024]{1,0:T(8,128)(2,1)}, u32[]{:S(2)}, u32[]{:S(2)}) collective-permute-start(bf16[256,1024]{1,0:T(8,128)(2,1)} %get-tuple-element.32), channel_id=1, source_target_pairs={{0,2},{1,3},{2,0},{3,1},{4,6},{5,7},{6,4},{7,5},{8,10},{9,11},{10,... | collective-permute-start | bytes 1572872 | tf_op jit(solution)/shard_map/ppermute | solution.py:27
  8.0 1.3 collective-permute-start.4
  9.4 1.2 constant_dynamic-slice_fusion
  10.6 0.7 collective-permute-start.5
  11.4 0.7 gather_fusion
  12.5 0.8 all_to_all.19
  13.2 12.0 %all-to-all-start = ((s32[64,1,2]{2,1,0:T(1,128)}), s32[64,1,2]{2,1,0:T(1,128)S(1)}, u32[]{:S(2)}, u32[]{:S(2)}) async-start(s32[64,1,2]{2,1,0:T(1,128)} %bitcast.2), calls=%async_computation | async-start | bytes 65536 | tf_op jit(solution)/shard_map/all_to_all | solution.py:89
  25.4 0.6 fusion.38
  26.5 0.6 add_select_fusion
  27.1 0.6 fusion.45
  27.7 1.6 broadcast.577.clone.1
  29.3 1.9 %bitcast_dynamic-update-slice_fusion.7 = bf16[4,256,1024]{2,1,0:T(8,128)(2,1)} fusion(bf16[4,256,1024]{2,1,0:T(8,128)(2,1)} %broadcast.577.clone.1, s32[]{:T(128)S(6)} %select_n.399, bf16[256,4096]{1,0:T(8,128)(2,1)} %param.12, s32[]{:T(128)S(6)} %select_n.398), kind=kLoop, calls=%fused_computation.27 | loop fusion | bytes 1048584 | tf_op jit(solution)/shard_map/dynamic_update_slice | solution.py:32
  31.2 1.4 fusion.43
  32.6 0.6 pad_clamp_fusion.2
  33.3 0.6 gather.24
  34.5 0.8 gather_fusion.2
  35.4 4.9 %collective-permute-done = bf16[7,4,1024]{2,1,0:T(4,128)(2,1)} collective-permute-done((bf16[7,4,1024]{2,1,0:T(4,128)(2,1)S(1)}, bf16[7,4,1024]{2,1,0:T(4,128)(2,1)}, u32[]{:S(2)}, u32[]{:S(2)}) %collective-permute-start) | collective-permute-done | bytes 57376 | tf_op jit(solution)/shard_map/ppermute | solution.py:12
  40.3 1.6 maximum_select_fusion.1
  41.9 2.9 %collective-permute-start.1 = (bf16[7,8,1024]{2,1,0:T(8,128)(2,1)}, bf16[7,8,1024]{2,1,0:T(8,128)(2,1)}, u32[]{:S(2)}, u32[]{:S(2)}) collective-permute-start(bf16[7,8,1024]{2,1,0:T(8,128)(2,1)} %maximum_select_fusion.1), channel_id=1, source_target_pairs={{0,2},{1,3},{2,0},{3,1},{4,6},{5,7},{6,4},{7,5},{8,10},{9,11},{10,... | collective-permute-start | bytes 344072 | tf_op jit(solution)/shard_map/ppermute | solution.py:12
  44.8 0.9 broadcast_select_fusion.1
  45.8 12.2 %all-to-all-start.2 = ((bf16[64,2,3,256]{3,1,2,0:T(2,128)(2,1)}), bf16[64,2,3,256]{3,1,2,0:T(2,128)(2,1)}, u32[]{:S(2)}, u32[]{:S(2)}) async-start(bf16[64,2,3,256]{3,1,2,0:T(2,128)(2,1)} %broadcast_select_fusion.1), calls=%async_computation.2 | async-start | bytes 393216 | tf_op jit(solution)/shard_map/all_to_all | solution.py:92
  58.0 0.7 collective-permute-start.6
  58.7 1.1 maximum_select_fusion
  59.8 2.2 %gather_fusion.1 = bf16[64,16,1024]{2,1,0:T(8,128)(2,1)} fusion(bf16[7,16,1024]{2,1,0:T(8,128)(2,1)S(1)} %maximum_select_fusion, s32[1024]{0:T(1024)} %pad_clamp_fusion.2), kind=kCustom, calls=%fused_computation.1 | custom fusion | bytes 4194560 | tf_op jit(solution)/shard_map/jit(_take)/gather | solution.py:103
  62.0 3.2 %broadcast_select_fusion = bf16[64,16,1024]{2,1,0:T(8,128)(2,1)} fusion(bf16[64,16,1024]{2,1,0:T(8,128)(2,1)} %gather_fusion.1, pred[64]{0:T(512)(128)(4,1)S(1)} %copy-done.18), kind=kLoop, calls=%fused_computation.17 | loop fusion | flops 1048576 | bytes 4194368 | tf_op jit(solution)/shard_map/jit(_take)/select_n | solution.py:103
  65.3 3.5 %all-to-all-done.2 = bf16[64,2,3,256]{3,1,2,0:T(2,128)(2,1)} async-done(((bf16[64,2,3,256]{3,1,2,0:T(2,128)(2,1)}), bf16[64,2,3,256]{3,1,2,0:T(2,128)(2,1)}, u32[]{:S(2)}, u32[]{:S(2)}) %all-to-all-start.2) | async-done | bytes 196640 | tf_op jit(solution)/shard_map/all_to_all | solution.py:92
  68.7 7.0 %all-to-all-start.1 = ((bf16[64,16,1024]{2,1,0:T(8,128)(2,1)}), bf16[64,16,1024]{2,1,0:T(8,128)(2,1)}, u32[]{:S(2)}, u32[]{:S(2)}) async-start(bf16[64,16,1024]{2,1,0:T(8,128)(2,1)} %broadcast_select_fusion), calls=%async_computation.1 | async-start | bytes 4194304 | tf_op jit(solution)/shard_map/all_to_all | solution.py:104
  75.8 1.6 broadcast.577.clone
  77.5 1.9 %bitcast_dynamic-update-slice_fusion.3 = bf16[4,256,1024]{2,1,0:T(8,128)(2,1)} fusion(bf16[4,256,1024]{2,1,0:T(8,128)(2,1)} %broadcast.577.clone, s32[]{:T(128)S(6)} %select_n.399, bf16[256,4096]{1,0:T(8,128)(2,1)} %param.13, s32[]{:T(128)S(6)} %select_n.398), kind=kLoop, calls=%fused_computation.23 | loop fusion | bytes 1048584 | tf_op jit(solution)/shard_map/dynamic_update_slice | solution.py:32
  79.4 4.2 %compare_select_fusion.1 = bf16[4,256,4,256]{3,2,1,0:T(4,128)(2,1)} fusion(s32[4,256]{1,0:T(4,128)S(1)} %add_select_fusion.1, bf16[256,256]{1,0:T(8,128)(2,1)S(1)} %copy-done.5), kind=kLoop, calls=%fused_computation.10 | loop fusion | flops 2097152 | bytes 2232320 | tf_op jit(solution)/shard_map/jit(_where)/select_n | solution.py:114
  83.7 3.4 %copy.86 = bf16[128,8,4,256]{3,1,2,0:T(8,128)(2,1)} copy(bf16[128,8,4,256]{3,2,1,0:T(4,128)(2,1)} %bitcast.105) | data formatting | bytes 4194304
  87.1 0.5 tile.4
  87.6 1.8 %copy.87 = bf16[128,8,4,256]{3,1,2,0:T(8,128)(2,1)} copy(bf16[128,8,4,256]{3,2,1,0:T(4,128)(2,1)S(1)} %bitcast.106) | data formatting | bytes 4194304
  89.4 1.0 copy.73
  90.5 0.6 gather_fusion.3
  91.1 0.9 convolution_bitcast_fusion
  92.1 4.1 %collective-permute-start.7 = (bf16[256,1024]{1,0:T(8,128)(2,1)S(1)}, bf16[256,1024]{1,0:T(8,128)(2,1)S(1)}, u32[]{:S(2)}, u32[]{:S(2)}) collective-permute-start(bf16[256,1024]{1,0:T(8,128)(2,1)S(1)} %copy-done.4), channel_id=1, source_target_pairs={{0,3},{1,0},{2,1},{3,2},{4,7},{5,4},{6,5},{7,6},{8,11},{9,8},{10,9... | collective-permute-start | bytes 1572872 | tf_op jit(solution)/shard_map/ppermute | solution.py:27
  96.2 1.9 %bitcast_dynamic-update-slice_fusion.6 = bf16[4,256,1024]{2,1,0:T(8,128)(2,1)} fusion(bf16[4,256,1024]{2,1,0:T(8,128)(2,1)} %bitcast_dynamic-update-slice_fusion.7, s32[]{:T(128)S(6)} %select_n.403, bf16[256,1024]{1,0:T(8,128)(2,1)} %collective-permute-done.2), kind=kLoop, calls=%fused_computation.26 | loop fusion | bytes 1048580 | tf_op jit(solution)/shard_map/dynamic_update_slice | solution.py:32
  98.1 1.9 %bitcast_dynamic-update-slice_fusion.2 = bf16[4,256,1024]{2,1,0:T(8,128)(2,1)} fusion(bf16[4,256,1024]{2,1,0:T(8,128)(2,1)} %bitcast_dynamic-update-slice_fusion.3, s32[]{:T(128)S(6)} %select_n.403, bf16[256,1024]{1,0:T(8,128)(2,1)} %collective-permute-done.5), kind=kLoop, calls=%fused_computation.22 | loop fusion | bytes 1048580 | tf_op jit(solution)/shard_map/dynamic_update_slice | solution.py:32
  100.1 1.9 %bitcast_dynamic-update-slice_fusion.5 = bf16[4,256,1024]{2,1,0:T(8,128)(2,1)} fusion(bf16[4,256,1024]{2,1,0:T(8,128)(2,1)} %bitcast_dynamic-update-slice_fusion.6, s32[]{:T(128)S(6)} %select_n.407, bf16[256,1024]{1,0:T(8,128)(2,1)} %collective-permute-done.3), kind=kLoop, calls=%fused_computation.25 | loop fusion | bytes 1048580 | tf_op jit(solution)/shard_map/dynamic_update_slice | solution.py:32
  101.9 1.9 %bitcast_dynamic-update-slice_fusion.1 = bf16[4,256,1024]{2,1,0:T(8,128)(2,1)} fusion(bf16[4,256,1024]{2,1,0:T(8,128)(2,1)} %bitcast_dynamic-update-slice_fusion.2, s32[]{:T(128)S(6)} %select_n.407, bf16[256,1024]{1,0:T(8,128)(2,1)} %collective-permute-done.6), kind=kLoop, calls=%fused_computation.21 | loop fusion | bytes 1048580 | tf_op jit(solution)/shard_map/dynamic_update_slice | solution.py:32
  103.8 1.9 %bitcast_dynamic-update-slice_fusion.4 = bf16[4,256,1024]{2,1,0:T(8,128)(2,1)} fusion(bf16[4,256,1024]{2,1,0:T(8,128)(2,1)} %bitcast_dynamic-update-slice_fusion.5, s32[]{:T(128)S(6)} %select_n.411, bf16[256,1024]{1,0:T(8,128)(2,1)} %collective-permute-done.4), kind=kLoop, calls=%fused_computation.24 | loop fusion | bytes 1048580 | tf_op jit(solution)/shard_map/dynamic_update_slice | solution.py:32
  105.7 2.0 %collective-permute-done.7 = bf16[256,1024]{1,0:T(8,128)(2,1)S(1)} collective-permute-done((bf16[256,1024]{1,0:T(8,128)(2,1)S(1)}, bf16[256,1024]{1,0:T(8,128)(2,1)S(1)}, u32[]{:S(2)}, u32[]{:S(2)}) %collective-permute-start.7) | collective-permute-done | bytes 524320 | tf_op jit(solution)/shard_map/ppermute | solution.py:27
  107.7 0.8 bitcast_dynamic-update-slice_fusion
  108.5 3.2 %multiply_convert_fusion = bf16[4,256,1024]{2,1,0:T(8,128)(2,1)S(1)} fusion(bf16[4,256,1024]{2,1,0:T(8,128)(2,1)} %bitcast_dynamic-update-slice_fusion.4, f32[1024]{0:T(1024)S(1)} %bitcast.118, f32[4,256]{1,0:T(4,128)S(1)} %mul.166, f32[1024]{0:T(1024)S(1)} %bitcast.119, f32[4,256]{1,0:T(4,128)S(1)} %mul.161, f32[1024]{0:T(1024)S(1)} %bitcast.117, ...), kind=kLoop, calls=%fused_computation.8 | loop fusion | flops 10485760 | bytes 6316032 | tf_op jit(solution)/shard_map/convert_element_type | solution.py:111
  111.8 3.7 %fusion.46 = bf16[1024,1024]{1,0:T(8,128)(2,1)} fusion(bf16[1024,1024]{1,0:T(8,128)(2,1)S(1)} %bitcast.110, bf16[1024,1024]{1,0:T(8,128)(2,1)S(1)} %bitcast.109), kind=kOutput, calls=%fused_computation.129 | convolution fusion | flops 2147483648 | bytes 6291456 | tf_op jit(solution)/shard_map/dot_general | solution.py:115
  115.5 11.5 %all-to-all-done.1 = bf16[64,16,1024]{2,1,0:T(8,128)(2,1)} async-done(((bf16[64,16,1024]{2,1,0:T(8,128)(2,1)}), bf16[64,16,1024]{2,1,0:T(8,128)(2,1)}, u32[]{:S(2)}, u32[]{:S(2)}) %all-to-all-start.1) | async-done | bytes 2097184 | tf_op jit(solution)/shard_map/all_to_all | solution.py:104
  126.9 8.4 %multiply_reduce_fusion.2 = (bf16[1024]{0:T(1024)(128)(2,1)S(1)}, bf16[1024]{0:T(1024)(128)(2,1)S(1)}, bf16[1024]{0:T(1024)(128)(2,1)S(1)}) fusion(f32[1024]{0:T(1024)S(1)} %bitcast.122, f32[1024]{0:T(1024)S(1)} %bitcast.121, f32[1024]{0:T(1024)S(1)} %bitcast.120, bf16[4,256,1024]{2,1,0:T(8,128)(2,1)} %bitcast_dynamic-update-slice_fusion, ...), kind=kOutput, calls=%fused_computation.7 | convolution fusion | flops 4308595712 | bytes 8411136 | tf_op jit(solution)/shard_map/dot_general | solution.py:117
  136.4 1.1 copy.78
  137.4 5.4 %all-to-all-start.3 = ((f32[64,2,3,256]{3,1,2,0:T(2,128)}), f32[64,2,3,256]{3,1,2,0:T(2,128)S(1)}, u32[]{:S(2)}, u32[]{:S(2)}) async-start(f32[64,2,3,256]{3,1,2,0:T(2,128)} %copy.78), calls=%async_computation.3 | async-start | bytes 786432 | tf_op jit(solution)/shard_map/all_to_all | solution.py:129
  143.4 2.1 %reduce.15 = s32[64,2]{1,0:T(8,128)} reduce(s32[64,1,2]{2,1,0:T(1,128)} %copy-done.7, s32[]{:T(128)} %broadcast.620), dimensions={1}, to_apply=%all_to_all.20.reduce_sub_computation.3 | reduce | bytes 1028 | tf_op jit(solution)/shard_map/all_to_all | solution.py:89
  145.5 0.9 eq.167
  146.4 11.2 %all-to-all-done.3 = f32[64,2,3,256]{3,1,2,0:T(2,128)S(1)} async-done(((f32[64,2,3,256]{3,1,2,0:T(2,128)}), f32[64,2,3,256]{3,1,2,0:T(2,128)S(1)}, u32[]{:S(2)}, u32[]{:S(2)}) %all-to-all-start.3) | async-done | bytes 393248 | tf_op jit(solution)/shard_map/all_to_all | solution.py:129
  157.7 0.8 copy.89
  158.6 1.1 copy.80
  159.7 1.0 fusion.19
  160.7 2.6 %collective-permute-start.10 = (f32[32,3,256]{2,0,1:T(8,128)}, f32[32,3,256]{2,0,1:T(8,128)S(1)}, u32[]{:S(2)}, u32[]{:S(2)}) collective-permute-start(f32[32,3,256]{2,0,1:T(8,128)} %fusion.19), channel_id=1, source_target_pairs={{0,1},{1,2},{2,3},{3,0},{4,5},{5,6},{6,7},{7,4},{8,9},{9,10},{10,1... | collective-permute-start | bytes 294920 | tf_op jit(solution)/shard_map/ppermute | solution.py:41
  163.3 1.4 collective-permute-start.8
  164.7 1.5 collective-permute-start.9
  166.2 1.6 copy.81
  168.2 3.2 %collective-permute-done.9 = f32[32,3,256]{2,0,1:T(8,128)S(1)} collective-permute-done((f32[32,3,256]{2,0,1:T(8,128)}, f32[32,3,256]{2,0,1:T(8,128)S(1)}, u32[]{:S(2)}, u32[]{:S(2)}) %collective-permute-start.9) | collective-permute-done | bytes 98336 | tf_op jit(solution)/shard_map/ppermute | solution.py:41
  171.4 2.3 %multiply_add_fusion = (f32[32,3,256]{2,0,1:T(8,128)}, f32[32,3,256]{2,0,1:T(8,128)}) fusion(f32[32,3,256]{2,0,1:T(8,128)} %param.22, f32[]{:T(128)} %bitcast.43, f32[32,3,256]{2,0,1:T(8,128)S(1)} %collective-permute-done.8, f32[32,3,256]{2,0,1:T(8,128)S(1)} %collective-permute-done.9, f32[32,3,256]{2,0,1:T(8,128)S(1)} %collective-permute-done.10, ...), kind=kLoop, calls=%fused_computation.33 | loop fusion | flops 442368 | bytes 688144 | tf_op jit(solution)/shard_map/add | solution.py:141
  (84 shorter events, 4.1 us)
Async XLA Ops:
  0.6 90.5 %copy-start = (bf16[4,6,256,256]{3,2,1,0:T(8,128)(2,1)S(1)}, bf16[4,6,256,256]{3,2,1,0:T(8,128)(2,1)}, u32[]{:S(2)}) copy-start(bf16[4,6,256,256]{3,2,1,0:T(8,128)(2,1)} %param.18) | copy-start | bytes 9437188
  0.7 8.7 %copy-start.2 = (bf16[256,4096]{1,0:T(8,128)(2,1)S(1)}, bf16[256,4096]{1,0:T(8,128)(2,1)}, u32[]{:S(2)}) copy-start(bf16[256,4096]{1,0:T(8,128)(2,1)} %param.13) | copy-start | bytes 6291460
  3.5 7.8 %copy-start.10 = (s32[4,6]{1,0:T(4,128)S(1)}, s32[4,6]{1,0:T(4,128)}, u32[]{:S(2)}) copy-start(s32[4,6]{1,0:T(4,128)} %param.19) | copy-start | bytes 292
  3.5 8.0 %copy-start.1 = (s32[2048]{0:T(1024)S(1)}, s32[2048]{0:T(1024)}, u32[]{:S(2)}) copy-start(s32[2048]{0:T(1024)} %param.20) | copy-start | bytes 24580
  3.5 21.8 %copy-start.9 = (bf16[7,4,1024]{2,1,0:T(4,128)(2,1)S(1)}, bf16[7,4,1024]{2,1,0:T(4,128)(2,1)}, u32[]{:S(2)}) copy-start(bf16[7,4,1024]{2,1,0:T(4,128)(2,1)} %param.16) | copy-start | bytes 172036
  3.5 22.5 %copy-start.19 = (s32[64]{0:T(128)S(1)}, s32[64]{0:T(128)}, u32[]{:S(2)}) copy-start(s32[64]{0:T(128)} %param.17) | copy-start | bytes 772
  3.5 23.6 %copy-start.14 = (f32[2]{0:T(128)S(1)}, f32[2]{0:T(128)}, u32[]{:S(2)}) copy-start(f32[2]{0:T(128)} %param.23) | copy-start | bytes 28
  3.5 88.6 %collective-permute-start.2 = (bf16[256,1024]{1,0:T(8,128)(2,1)}, bf16[256,1024]{1,0:T(8,128)(2,1)}, u32[]{:S(2)}, u32[]{:S(2)}) collective-permute-start(bf16[256,1024]{1,0:T(8,128)(2,1)} %get-tuple-element.31), channel_id=1, source_target_pairs={{0,1},{1,2},{2,3},{3,0},{4,5},{5,6},{6,7},{7,4},{8,9},{9,10},{10,1... | collective-permute-start | bytes 1572872 | tf_op jit(solution)/shard_map/ppermute | solution.py:27
  5.1 94.9 %collective-permute-start.3 = (bf16[256,1024]{1,0:T(8,128)(2,1)}, bf16[256,1024]{1,0:T(8,128)(2,1)}, u32[]{:S(2)}, u32[]{:S(2)}) collective-permute-start(bf16[256,1024]{1,0:T(8,128)(2,1)} %get-tuple-element.32), channel_id=1, source_target_pairs={{0,2},{1,3},{2,0},{3,1},{4,6},{5,7},{6,4},{7,5},{8,10},{9,11},{10,... | collective-permute-start | bytes 1572872 | tf_op jit(solution)/shard_map/ppermute | solution.py:27
  8.0 95.8 %collective-permute-start.4 = (bf16[256,1024]{1,0:T(8,128)(2,1)}, bf16[256,1024]{1,0:T(8,128)(2,1)}, u32[]{:S(2)}, u32[]{:S(2)}) collective-permute-start(bf16[256,1024]{1,0:T(8,128)(2,1)} %get-tuple-element.30), channel_id=1, source_target_pairs={{0,3},{1,0},{2,1},{3,2},{4,7},{5,4},{6,5},{7,6},{8,11},{9,8},{10,9... | collective-permute-start | bytes 1572872 | tf_op jit(solution)/shard_map/ppermute | solution.py:27
  10.6 20.6 %copy-start.6 = (f32[32,3,256]{2,0,1:T(8,128)S(1)}, f32[32,3,256]{2,0,1:T(8,128)}, u32[]{:S(2)}) copy-start(f32[32,3,256]{2,0,1:T(8,128)} %param.22) | copy-start | bytes 294916
  10.6 20.6 %copy-start.8 = (f32[32,3,256]{2,0,1:T(8,128)S(1)}, f32[32,3,256]{2,0,1:T(8,128)}, u32[]{:S(2)}) copy-start(f32[32,3,256]{2,0,1:T(8,128)} %param.21) | copy-start | bytes 294916
  10.6 87.6 %collective-permute-start.5 = (bf16[256,1024]{1,0:T(8,128)(2,1)}, bf16[256,1024]{1,0:T(8,128)(2,1)}, u32[]{:S(2)}, u32[]{:S(2)}) collective-permute-start(bf16[256,1024]{1,0:T(8,128)(2,1)} %get-tuple-element.28), channel_id=1, source_target_pairs={{0,1},{1,2},{2,3},{3,0},{4,5},{5,6},{6,7},{7,4},{8,9},{9,10},{10,1... | collective-permute-start | bytes 1572872 | tf_op jit(solution)/shard_map/ppermute | solution.py:27
  12.4 22.0 %copy-start.16 = (s32[24]{0:T(128)}, s32[24]{0:T(128)S(1)}, u32[]{:S(2)}) copy-start(s32[24]{0:T(128)S(1)} %get-tuple-element.42) | copy-start | bytes 292
  13.2 20.7 %all-to-all-start = ((s32[64,1,2]{2,1,0:T(1,128)}), s32[64,1,2]{2,1,0:T(1,128)S(1)}, u32[]{:S(2)}, u32[]{:S(2)}) async-start(s32[64,1,2]{2,1,0:T(1,128)} %bitcast.2), calls=%async_computation | async-start | bytes 65536 | tf_op jit(solution)/shard_map/all_to_all | solution.py:89
  25.3 15.0 %collective-permute-start = (bf16[7,4,1024]{2,1,0:T(4,128)(2,1)S(1)}, bf16[7,4,1024]{2,1,0:T(4,128)(2,1)}, u32[]{:S(2)}, u32[]{:S(2)}) collective-permute-start(bf16[7,4,1024]{2,1,0:T(4,128)(2,1)S(1)} %copy-done.9), channel_id=1, source_target_pairs={{0,1},{1,0},{2,3},{3,2},{4,5},{5,4},{6,7},{7,6},{8,9},{9,8},{10,11... | collective-permute-start | bytes 172040 | tf_op jit(solution)/shard_map/ppermute | solution.py:12
  33.9 0.6 copy-start.7
  41.9 16.0 %collective-permute-start.1 = (bf16[7,8,1024]{2,1,0:T(8,128)(2,1)}, bf16[7,8,1024]{2,1,0:T(8,128)(2,1)}, u32[]{:S(2)}, u32[]{:S(2)}) collective-permute-start(bf16[7,8,1024]{2,1,0:T(8,128)(2,1)} %maximum_select_fusion.1), channel_id=1, source_target_pairs={{0,2},{1,3},{2,0},{3,1},{4,6},{5,7},{6,4},{7,5},{8,10},{9,11},{10,... | collective-permute-start | bytes 344072 | tf_op jit(solution)/shard_map/ppermute | solution.py:12
  45.8 23.0 %all-to-all-start.2 = ((bf16[64,2,3,256]{3,1,2,0:T(2,128)(2,1)}), bf16[64,2,3,256]{3,1,2,0:T(2,128)(2,1)}, u32[]{:S(2)}, u32[]{:S(2)}) async-start(bf16[64,2,3,256]{3,1,2,0:T(2,128)(2,1)} %broadcast_select_fusion.1), calls=%async_computation.2 | async-start | bytes 393216 | tf_op jit(solution)/shard_map/all_to_all | solution.py:92
  58.0 44.0 %collective-permute-start.6 = (bf16[256,1024]{1,0:T(8,128)(2,1)}, bf16[256,1024]{1,0:T(8,128)(2,1)}, u32[]{:S(2)}, u32[]{:S(2)}) collective-permute-start(bf16[256,1024]{1,0:T(8,128)(2,1)} %get-tuple-element.29), channel_id=1, source_target_pairs={{0,2},{1,3},{2,0},{3,1},{4,6},{5,7},{6,4},{7,5},{8,10},{9,11},{10,... | collective-permute-start | bytes 1572872 | tf_op jit(solution)/shard_map/ppermute | solution.py:27
  59.8 2.2 %copy-start.18 = (pred[64]{0:T(512)(128)(4,1)S(1)}, pred[64]{0:T(512)(128)(4,1)}, u32[]{:S(2)}) copy-start(pred[64]{0:T(512)(128)(4,1)} %compare_and_fusion.2) | copy-start | bytes 196
  65.3 10.5 %copy-start.15 = (s32[24]{0:T(128)S(1)}, s32[24]{0:T(128)}, u32[]{:S(2)}) copy-start(s32[24]{0:T(128)} %fusion.38) | copy-start | bytes 292
  68.7 58.2 %all-to-all-start.1 = ((bf16[64,16,1024]{2,1,0:T(8,128)(2,1)}), bf16[64,16,1024]{2,1,0:T(8,128)(2,1)}, u32[]{:S(2)}, u32[]{:S(2)}) async-start(bf16[64,16,1024]{2,1,0:T(8,128)(2,1)} %broadcast_select_fusion), calls=%async_computation.1 | async-start | bytes 4194304 | tf_op jit(solution)/shard_map/all_to_all | solution.py:104
  75.8 3.5 %copy-start.12 = (s32[4,6]{1,0:T(4,128)S(1)}, s32[4,6]{1,0:T(4,128)}, u32[]{:S(2)}) copy-start(s32[4,6]{1,0:T(4,128)} %gather.24) | copy-start | bytes 292
  75.8 3.6 %copy-start.11 = (f32[3,1024]{1,0:T(4,128)S(1)}, f32[3,1024]{1,0:T(4,128)}, u32[]{:S(2)}) copy-start(f32[3,1024]{1,0:T(4,128)} %param.14) | copy-start | bytes 36868
  75.8 3.6 %copy-start.5 = (bf16[256,256]{1,0:T(8,128)(2,1)S(1)}, bf16[256,256]{1,0:T(8,128)(2,1)}, u32[]{:S(2)}) copy-start(bf16[256,256]{1,0:T(8,128)(2,1)} %param.15) | copy-start | bytes 393220
  91.1 1.0 copy-start.4
  92.1 15.6 %collective-permute-start.7 = (bf16[256,1024]{1,0:T(8,128)(2,1)S(1)}, bf16[256,1024]{1,0:T(8,128)(2,1)S(1)}, u32[]{:S(2)}, u32[]{:S(2)}) collective-permute-start(bf16[256,1024]{1,0:T(8,128)(2,1)S(1)} %copy-done.4), channel_id=1, source_target_pairs={{0,3},{1,0},{2,1},{3,2},{4,7},{5,4},{6,5},{7,6},{8,11},{9,8},{10,9... | collective-permute-start | bytes 1572872 | tf_op jit(solution)/shard_map/ppermute | solution.py:27
  108.5 3.2 %copy-start.3 = (bf16[128,8,4,256]{3,1,2,0:T(8,128)(2,1)S(1)}, bf16[128,8,4,256]{3,1,2,0:T(8,128)(2,1)}, u32[]{:S(2)}) copy-start(bf16[128,8,4,256]{3,1,2,0:T(8,128)(2,1)} %copy.86) | copy-start | bytes 6291460
  111.8 15.2 %copy-start.13 = (s32[1024]{0:T(1024)S(1)}, s32[1024]{0:T(1024)}, u32[]{:S(2)}) copy-start(s32[1024]{0:T(1024)} %add_select_fusion) | copy-start | bytes 12292
  135.3 0.6 copy-start.17
  137.4 20.2 %all-to-all-start.3 = ((f32[64,2,3,256]{3,1,2,0:T(2,128)}), f32[64,2,3,256]{3,1,2,0:T(2,128)S(1)}, u32[]{:S(2)}, u32[]{:S(2)}) async-start(f32[64,2,3,256]{3,1,2,0:T(2,128)} %copy.78), calls=%async_computation.3 | async-start | bytes 786432 | tf_op jit(solution)/shard_map/all_to_all | solution.py:129
  160.7 7.4 %collective-permute-start.10 = (f32[32,3,256]{2,0,1:T(8,128)}, f32[32,3,256]{2,0,1:T(8,128)S(1)}, u32[]{:S(2)}, u32[]{:S(2)}) collective-permute-start(f32[32,3,256]{2,0,1:T(8,128)} %fusion.19), channel_id=1, source_target_pairs={{0,1},{1,2},{2,3},{3,0},{4,5},{5,6},{6,7},{7,4},{8,9},{9,10},{10,1... | collective-permute-start | bytes 294920 | tf_op jit(solution)/shard_map/ppermute | solution.py:41
  163.3 4.9 %collective-permute-start.8 = (f32[32,3,256]{2,0,1:T(8,128)}, f32[32,3,256]{2,0,1:T(8,128)S(1)}, u32[]{:S(2)}, u32[]{:S(2)}) collective-permute-start(f32[32,3,256]{2,0,1:T(8,128)} %fusion.19), channel_id=1, source_target_pairs={{0,3},{1,0},{2,1},{3,2},{4,7},{5,4},{6,5},{7,6},{8,11},{9,8},{10,9... | collective-permute-start | bytes 294920 | tf_op jit(solution)/shard_map/ppermute | solution.py:41
  164.7 6.6 %collective-permute-start.9 = (f32[32,3,256]{2,0,1:T(8,128)}, f32[32,3,256]{2,0,1:T(8,128)S(1)}, u32[]{:S(2)}, u32[]{:S(2)}) collective-permute-start(f32[32,3,256]{2,0,1:T(8,128)} %fusion.19), channel_id=1, source_target_pairs={{0,2},{1,3},{2,0},{3,1},{4,6},{5,7},{6,4},{7,5},{8,10},{9,11},{10,... | collective-permute-start | bytes 294920 | tf_op jit(solution)/shard_map/ppermute | solution.py:41

commit v9 on v8

--- a/solution.py
+++ b/solution.py
@@ -118,7 +118,12 @@
         whitened, filter_blocks, (((1,), (1,)), ((), ())), preferred_element_type=jnp.float32
     ).astype(jnp.bfloat16)
     weighted = smoothed.astype(jnp.float32) * column_weights
-    stokes = jnp.stack([jnp.sum(response[j][:, None] * weighted, axis=0) for j in range(comp_count)])
+    tile_rows = 8
+    blocks = [
+        jnp.sum((response[j][:, None] * weighted).reshape(det_total // tile_rows, tile_rows, width), axis=0)
+        for j in range(comp_count)
+    ]
+    stokes = jnp.sum(lax.optimization_barrier(jnp.stack(blocks)), axis=1)
     stokes_short = jnp.transpose(stokes.reshape(comp_count, spans_here, samples), (1, 0, 2)).astype(jnp.bfloat16)
     partial_value = jnp.einsum(
         "cjt,cktp->ckjp", stokes_short, pointing, preferred_element_type=jnp.float32

time: 176 us -> 176 us (level)
  no operation moved by 1% of the time
where the time goes in v9:
time: 176 us; the launch traced here: 174 us
  starting transfers between devices  56.5 us (32%)
  local copies, waits for them, and re-layouts  41.6 us (24%)
  waiting for transfers between devices  36.7 us (21%)
  other arithmetic  22.9 us (13%)
  matrix products  14.9 us (8%)
    dynamic_update_slice x8, local copies, waits for them, and re-layouts, wafer_columns(): placed = lax.dynamic_update_slice_in_dim(placed, piece[None], source, 0)  14 us
    all_to_all x1, starting transfers between devices, shards(): lax.all_to_all(served, 'tm', split_axis=0, concat_axis=0, tiled=True)  12.2 us
    all_to_all x1, starting transfers between devices, shards(): lax.all_to_all(requests, 'tm', split_axis=0, concat_axis=0, tiled=True)  12 us
    all_to_all x1, waiting for transfers between devices, shards(): lax.all_to_all(sent_blocks, 'tm', split_axis=0, concat_axis=0, tiled=True)  11.5 us
    ppermute x6, starting transfers between devices, wafer_columns(): lax.ppermute(piece, 'wafer', [(i, (i + shift) % size) for i in range(size)])  11.4 us
    all_to_all x1, waiting for transfers between devices, shards(): lax.all_to_all(outgoing, 'tm', split_axis=0, concat_axis=0, tiled=True)  11.2 us
    dot_general x1, matrix products, shards(): lax.dot_general(whitened, filter_blocks, (((1,), (1,)), ((), ())), prefer...  8.4 us
    unnamed x44, local copies, waits for them, and re-layouts  7.98 us
  transfers between devices with their start and end apart: 15, of which 8 were waited for; matrix products, arithmetic and copies ran while one was open for 34% of the time, Pallas kernels for 0%

profile of v9, /device:TPU:2, one launch (start us, length us, event | category | flops | bytes accessed | tf_op | source)
XLA Modules:
  0.0 173.7 jit_solution(1418490273847676881)
XLA Ops:
  0.7 2.8 %constant_dynamic-slice_fusion.3 = (bf16[256,1024]{1,0:T(8,128)(2,1)}, bf16[256,1024]{1,0:T(8,128)(2,1)}, bf16[256,1024]{1,0:T(8,128)(2,1)}) fusion(bf16[256,4096]{1,0:T(8,128)(2,1)} %param.12, s32[]{:T(128)S(6)} %select_n.409, s32[]{:T(128)S(6)} %select_n.401, s32[]{:T(128)S(6)} %select_n.405), kind=kLoop, calls=%fused_computation.74 | loop fusion | bytes 3145740 | tf_op jit(solution)/shard_map/dynamic_slice | solution.py:26
  3.5 1.7 collective-permute-start.2
  5.1 2.9 %collective-permute-start.3 = (bf16[256,1024]{1,0:T(8,128)(2,1)}, bf16[256,1024]{1,0:T(8,128)(2,1)}, u32[]{:S(2)}, u32[]{:S(2)}) collective-permute-start(bf16[256,1024]{1,0:T(8,128)(2,1)} %get-tuple-element.32), channel_id=1, source_target_pairs={{0,2},{1,3},{2,0},{3,1},{4,6},{5,7},{6,4},{7,5},{8,10},{9,11},{10,... | collective-permute-start | bytes 1572872 | tf_op jit(solution)/shard_map/ppermute | solution.py:27
  8.0 1.3 collective-permute-start.4
  9.4 1.2 constant_dynamic-slice_fusion
  10.6 0.7 collective-permute-start.5
  11.5 0.7 gather_fusion
  12.5 0.8 all_to_all.19
  13.2 12.0 %all-to-all-start = ((s32[64,1,2]{2,1,0:T(1,128)}), s32[64,1,2]{2,1,0:T(1,128)S(1)}, u32[]{:S(2)}, u32[]{:S(2)}) async-start(s32[64,1,2]{2,1,0:T(1,128)} %bitcast.2), calls=%async_computation | async-start | bytes 65536 | tf_op jit(solution)/shard_map/all_to_all | solution.py:89
  25.9 0.6 compare_and_fusion.2
  26.5 0.6 add_select_fusion
  27.1 0.6 fusion.39
  27.7 1.6 broadcast.577.clone.1
  29.4 1.9 %bitcast_dynamic-update-slice_fusion.7 = bf16[4,256,1024]{2,1,0:T(8,128)(2,1)} fusion(bf16[4,256,1024]{2,1,0:T(8,128)(2,1)} %broadcast.577.clone.1, s32[]{:T(128)S(6)} %select_n.399, bf16[256,4096]{1,0:T(8,128)(2,1)} %param.12, s32[]{:T(128)S(6)} %select_n.398), kind=kLoop, calls=%fused_computation.27 | loop fusion | bytes 1048584 | tf_op jit(solution)/shard_map/dynamic_update_slice | solution.py:32
  31.2 1.4 fusion.37
  32.6 0.6 pad_clamp_fusion.2
  33.3 0.7 gather.24
  34.6 0.8 gather_fusion.2
  35.4 4.8 %collective-permute-done = bf16[7,4,1024]{2,1,0:T(4,128)(2,1)} collective-permute-done((bf16[7,4,1024]{2,1,0:T(4,128)(2,1)S(1)}, bf16[7,4,1024]{2,1,0:T(4,128)(2,1)}, u32[]{:S(2)}, u32[]{:S(2)}) %collective-permute-start) | collective-permute-done | bytes 57376 | tf_op jit(solution)/shard_map/ppermute | solution.py:12
  40.3 1.7 maximum_select_fusion.1
  41.9 2.9 %collective-permute-start.1 = (bf16[7,8,1024]{2,1,0:T(8,128)(2,1)}, bf16[7,8,1024]{2,1,0:T(8,128)(2,1)}, u32[]{:S(2)}, u32[]{:S(2)}) collective-permute-start(bf16[7,8,1024]{2,1,0:T(8,128)(2,1)} %maximum_select_fusion.1), channel_id=1, source_target_pairs={{0,2},{1,3},{2,0},{3,1},{4,6},{5,7},{6,4},{7,5},{8,10},{9,11},{10,... | collective-permute-start | bytes 344072 | tf_op jit(solution)/shard_map/ppermute | solution.py:12
  44.8 0.9 broadcast_select_fusion.1
  45.8 12.2 %all-to-all-start.2 = ((bf16[64,2,3,256]{3,1,2,0:T(2,128)(2,1)}), bf16[64,2,3,256]{3,1,2,0:T(2,128)(2,1)}, u32[]{:S(2)}, u32[]{:S(2)}) async-start(bf16[64,2,3,256]{3,1,2,0:T(2,128)(2,1)} %broadcast_select_fusion.1), calls=%async_computation.2 | async-start | bytes 393216 | tf_op jit(solution)/shard_map/all_to_all | solution.py:92
  58.0 0.7 collective-permute-start.6
  58.7 1.1 maximum_select_fusion
  59.8 2.2 %gather_fusion.1 = bf16[64,16,1024]{2,1,0:T(8,128)(2,1)} fusion(bf16[7,16,1024]{2,1,0:T(8,128)(2,1)S(1)} %maximum_select_fusion, s32[1024]{0:T(1024)} %pad_clamp_fusion.2), kind=kCustom, calls=%fused_computation.1 | custom fusion | bytes 4194560 | tf_op jit(solution)/shard_map/jit(_take)/gather | solution.py:103
  62.0 3.2 %broadcast_select_fusion = bf16[64,16,1024]{2,1,0:T(8,128)(2,1)} fusion(bf16[64,16,1024]{2,1,0:T(8,128)(2,1)} %gather_fusion.1, pred[64]{0:T(512)(128)(4,1)S(1)} %copy-done.18), kind=kLoop, calls=%fused_computation.17 | loop fusion | flops 1048576 | bytes 4194368 | tf_op jit(solution)/shard_map/jit(_take)/select_n | solution.py:103
  65.3 3.5 %all-to-all-done.2 = bf16[64,2,3,256]{3,1,2,0:T(2,128)(2,1)} async-done(((bf16[64,2,3,256]{3,1,2,0:T(2,128)(2,1)}), bf16[64,2,3,256]{3,1,2,0:T(2,128)(2,1)}, u32[]{:S(2)}, u32[]{:S(2)}) %all-to-all-start.2) | async-done | bytes 196640 | tf_op jit(solution)/shard_map/all_to_all | solution.py:92
  68.7 7.0 %all-to-all-start.1 = ((bf16[64,16,1024]{2,1,0:T(8,128)(2,1)}), bf16[64,16,1024]{2,1,0:T(8,128)(2,1)}, u32[]{:S(2)}, u32[]{:S(2)}) async-start(bf16[64,16,1024]{2,1,0:T(8,128)(2,1)} %broadcast_select_fusion), calls=%async_computation.1 | async-start | bytes 4194304 | tf_op jit(solution)/shard_map/all_to_all | solution.py:104
  75.8 1.6 broadcast.577.clone
  77.4 1.9 %bitcast_dynamic-update-slice_fusion.3 = bf16[4,256,1024]{2,1,0:T(8,128)(2,1)} fusion(bf16[4,256,1024]{2,1,0:T(8,128)(2,1)} %broadcast.577.clone, s32[]{:T(128)S(6)} %select_n.399, bf16[256,4096]{1,0:T(8,128)(2,1)} %param.13, s32[]{:T(128)S(6)} %select_n.398), kind=kLoop, calls=%fused_computation.23 | loop fusion | bytes 1048584 | tf_op jit(solution)/shard_map/dynamic_update_slice | solution.py:32
  79.4 4.2 %compare_select_fusion.1 = bf16[4,256,4,256]{3,2,1,0:T(4,128)(2,1)} fusion(s32[4,256]{1,0:T(4,128)S(1)} %add_select_fusion.1, bf16[256,256]{1,0:T(8,128)(2,1)S(1)} %copy-done.5), kind=kLoop, calls=%fused_computation.10 | loop fusion | flops 2097152 | bytes 2232320 | tf_op jit(solution)/shard_map/jit(_where)/select_n | solution.py:114
  83.6 3.4 %copy.74 = bf16[128,8,4,256]{3,1,2,0:T(8,128)(2,1)} copy(bf16[128,8,4,256]{3,2,1,0:T(4,128)(2,1)} %bitcast.115) | data formatting | bytes 4194304
  87.1 0.5 tile.4
  87.6 1.8 %copy.75 = bf16[128,8,4,256]{3,1,2,0:T(8,128)(2,1)} copy(bf16[128,8,4,256]{3,2,1,0:T(4,128)(2,1)S(1)} %bitcast.116) | data formatting | bytes 4194304
  89.4 1.0 copy.64
  90.5 0.6 gather_fusion.3
  91.1 0.9 convolution_bitcast_fusion
  92.1 4.1 %collective-permute-start.7 = (bf16[256,1024]{1,0:T(8,128)(2,1)S(1)}, bf16[256,1024]{1,0:T(8,128)(2,1)S(1)}, u32[]{:S(2)}, u32[]{:S(2)}) collective-permute-start(bf16[256,1024]{1,0:T(8,128)(2,1)S(1)} %copy-done.4), channel_id=1, source_target_pairs={{0,3},{1,0},{2,1},{3,2},{4,7},{5,4},{6,5},{7,6},{8,11},{9,8},{10,9... | collective-permute-start | bytes 1572872 | tf_op jit(solution)/shard_map/ppermute | solution.py:27
  96.2 1.9 %bitcast_dynamic-update-slice_fusion.6 = bf16[4,256,1024]{2,1,0:T(8,128)(2,1)} fusion(bf16[4,256,1024]{2,1,0:T(8,128)(2,1)} %bitcast_dynamic-update-slice_fusion.7, s32[]{:T(128)S(6)} %select_n.403, bf16[256,1024]{1,0:T(8,128)(2,1)} %collective-permute-done.2), kind=kLoop, calls=%fused_computation.26 | loop fusion | bytes 1048580 | tf_op jit(solution)/shard_map/dynamic_update_slice | solution.py:32
  98.1 1.9 %bitcast_dynamic-update-slice_fusion.2 = bf16[4,256,1024]{2,1,0:T(8,128)(2,1)} fusion(bf16[4,256,1024]{2,1,0:T(8,128)(2,1)} %bitcast_dynamic-update-slice_fusion.3, s32[]{:T(128)S(6)} %select_n.403, bf16[256,1024]{1,0:T(8,128)(2,1)} %collective-permute-done.5), kind=kLoop, calls=%fused_computation.22 | loop fusion | bytes 1048580 | tf_op jit(solution)/shard_map/dynamic_update_slice | solution.py:32
  100.0 1.9 %bitcast_dynamic-update-slice_fusion.5 = bf16[4,256,1024]{2,1,0:T(8,128)(2,1)} fusion(bf16[4,256,1024]{2,1,0:T(8,128)(2,1)} %bitcast_dynamic-update-slice_fusion.6, s32[]{:T(128)S(6)} %select_n.407, bf16[256,1024]{1,0:T(8,128)(2,1)} %collective-permute-done.3), kind=kLoop, calls=%fused_computation.25 | loop fusion | bytes 1048580 | tf_op jit(solution)/shard_map/dynamic_update_slice | solution.py:32
  101.9 1.9 %bitcast_dynamic-update-slice_fusion.1 = bf16[4,256,1024]{2,1,0:T(8,128)(2,1)} fusion(bf16[4,256,1024]{2,1,0:T(8,128)(2,1)} %bitcast_dynamic-update-slice_fusion.2, s32[]{:T(128)S(6)} %select_n.407, bf16[256,1024]{1,0:T(8,128)(2,1)} %collective-permute-done.6), kind=kLoop, calls=%fused_computation.21 | loop fusion | bytes 1048580 | tf_op jit(solution)/shard_map/dynamic_update_slice | solution.py:32
  103.8 1.9 %bitcast_dynamic-update-slice_fusion.4 = bf16[4,256,1024]{2,1,0:T(8,128)(2,1)} fusion(bf16[4,256,1024]{2,1,0:T(8,128)(2,1)} %bitcast_dynamic-update-slice_fusion.5, s32[]{:T(128)S(6)} %select_n.411, bf16[256,1024]{1,0:T(8,128)(2,1)} %collective-permute-done.4), kind=kLoop, calls=%fused_computation.24 | loop fusion | bytes 1048580 | tf_op jit(solution)/shard_map/dynamic_update_slice | solution.py:32
  105.6 2.1 %collective-permute-done.7 = bf16[256,1024]{1,0:T(8,128)(2,1)S(1)} collective-permute-done((bf16[256,1024]{1,0:T(8,128)(2,1)S(1)}, bf16[256,1024]{1,0:T(8,128)(2,1)S(1)}, u32[]{:S(2)}, u32[]{:S(2)}) %collective-permute-start.7) | collective-permute-done | bytes 524320 | tf_op jit(solution)/shard_map/ppermute | solution.py:27
  107.7 0.8 bitcast_dynamic-update-slice_fusion
  108.5 3.2 %multiply_convert_fusion = bf16[4,256,1024]{2,1,0:T(8,128)(2,1)S(1)} fusion(bf16[4,256,1024]{2,1,0:T(8,128)(2,1)} %bitcast_dynamic-update-slice_fusion.4, f32[1024]{0:T(1024)S(1)} %bitcast.132, f32[4,256]{1,0:T(4,128)S(1)} %mul.166, f32[1024]{0:T(1024)S(1)} %bitcast.133, f32[4,256]{1,0:T(4,128)S(1)} %mul.161, f32[1024]{0:T(1024)S(1)} %bitcast.131, ...), kind=kLoop, calls=%fused_computation.8 | loop fusion | flops 10485760 | bytes 6316032 | tf_op jit(solution)/shard_map/convert_element_type | solution.py:111
  111.7 3.7 %fusion.40 = bf16[1024,1024]{1,0:T(8,128)(2,1)} fusion(bf16[1024,1024]{1,0:T(8,128)(2,1)S(1)} %bitcast.120, bf16[1024,1024]{1,0:T(8,128)(2,1)S(1)} %bitcast.119), kind=kOutput, calls=%fused_computation.123 | convolution fusion | flops 2147483648 | bytes 6291456 | tf_op jit(solution)/shard_map/dot_general | solution.py:115
  115.4 11.5 %all-to-all-done.1 = bf16[64,16,1024]{2,1,0:T(8,128)(2,1)} async-done(((bf16[64,16,1024]{2,1,0:T(8,128)(2,1)}), bf16[64,16,1024]{2,1,0:T(8,128)(2,1)}, u32[]{:S(2)}, u32[]{:S(2)}) %all-to-all-start.1) | async-done | bytes 2097184 | tf_op jit(solution)/shard_map/all_to_all | solution.py:104
  126.9 8.4 %bitcast_reduce_fusion.2 = (f32[8,1024]{1,0:T(8,128)S(1)}, f32[8,1024]{1,0:T(8,128)S(1)}, f32[8,1024]{1,0:T(8,128)S(1)}) fusion(f32[1024]{0:T(1024)S(1)} %bitcast.136, f32[1024]{0:T(1024)S(1)} %bitcast.135, f32[1024]{0:T(1024)S(1)} %bitcast.134, bf16[4,256,1024]{2,1,0:T(8,128)(2,1)} %bitcast_dynamic-update-slice_fusion, bf16[1024,1024]{1,0:T(8,128)(2,1)} %bitcast.118, ...), kind=kOutput, calls=%fused_computation.6 | convolution fusion | flops 4308574208 | bytes 8503296 | tf_op jit(solution)/shard_map/dot_general | solution.py:117
  136.4 1.0 copy.66
  137.4 5.4 %all-to-all-start.3 = ((f32[64,2,3,256]{3,1,2,0:T(2,128)}), f32[64,2,3,256]{3,1,2,0:T(2,128)S(1)}, u32[]{:S(2)}, u32[]{:S(2)}) async-start(f32[64,2,3,256]{3,1,2,0:T(2,128)} %copy.66), calls=%async_computation.3 | async-start | bytes 786432 | tf_op jit(solution)/shard_map/all_to_all | solution.py:134
  143.4 2.1 %reduce.15 = s32[64,2]{1,0:T(8,128)} reduce(s32[64,1,2]{2,1,0:T(1,128)} %copy-done.7, s32[]{:T(128)} %broadcast.620), dimensions={1}, to_apply=%all_to_all.20.reduce_sub_computation.3 | reduce | bytes 1028 | tf_op jit(solution)/shard_map/all_to_all | solution.py:89
  145.5 0.9 eq.167
  146.4 11.2 %all-to-all-done.3 = f32[64,2,3,256]{3,1,2,0:T(2,128)S(1)} async-done(((f32[64,2,3,256]{3,1,2,0:T(2,128)}), f32[64,2,3,256]{3,1,2,0:T(2,128)S(1)}, u32[]{:S(2)}, u32[]{:S(2)}) %all-to-all-start.3) | async-done | bytes 393248 | tf_op jit(solution)/shard_map/all_to_all | solution.py:134
  157.7 0.8 copy.77
  158.5 1.1 copy.68
  159.7 1.0 fusion.19
  160.7 2.6 %collective-permute-start.10 = (f32[32,3,256]{2,0,1:T(8,128)}, f32[32,3,256]{2,0,1:T(8,128)S(1)}, u32[]{:S(2)}, u32[]{:S(2)}) collective-permute-start(f32[32,3,256]{2,0,1:T(8,128)} %fusion.19), channel_id=1, source_target_pairs={{0,1},{1,2},{2,3},{3,0},{4,5},{5,6},{6,7},{7,4},{8,9},{9,10},{10,1... | collective-permute-start | bytes 294920 | tf_op jit(solution)/shard_map/ppermute | solution.py:41
  163.3 1.4 collective-permute-start.8
  164.7 1.5 collective-permute-start.9
  166.2 1.6 copy.69
  168.2 3.2 %collective-permute-done.9 = f32[32,3,256]{2,0,1:T(8,128)S(1)} collective-permute-done((f32[32,3,256]{2,0,1:T(8,128)}, f32[32,3,256]{2,0,1:T(8,128)S(1)}, u32[]{:S(2)}, u32[]{:S(2)}) %collective-permute-start.9) | collective-permute-done | bytes 98336 | tf_op jit(solution)/shard_map/ppermute | solution.py:41
  171.4 2.4 %multiply_add_fusion = (f32[32,3,256]{2,0,1:T(8,128)}, f32[32,3,256]{2,0,1:T(8,128)}) fusion(f32[32,3,256]{2,0,1:T(8,128)} %param.22, f32[]{:T(128)} %bitcast.50, f32[32,3,256]{2,0,1:T(8,128)S(1)} %collective-permute-done.8, f32[32,3,256]{2,0,1:T(8,128)S(1)} %collective-permute-done.9, f32[32,3,256]{2,0,1:T(8,128)S(1)} %collective-permute-done.10, ...), kind=kLoop, calls=%fused_computation.34 | loop fusion | flops 442368 | bytes 688144 | tf_op jit(solution)/shard_map/add | solution.py:146
  (83 shorter events, 4.2 us)
Async XLA Ops:
  0.6 90.4 %copy-start = (bf16[4,6,256,256]{3,2,1,0:T(8,128)(2,1)S(1)}, bf16[4,6,256,256]{3,2,1,0:T(8,128)(2,1)}, u32[]{:S(2)}) copy-start(bf16[4,6,256,256]{3,2,1,0:T(8,128)(2,1)} %param.18) | copy-start | bytes 9437188
  0.7 8.7 %copy-start.2 = (bf16[256,4096]{1,0:T(8,128)(2,1)S(1)}, bf16[256,4096]{1,0:T(8,128)(2,1)}, u32[]{:S(2)}) copy-start(bf16[256,4096]{1,0:T(8,128)(2,1)} %param.13) | copy-start | bytes 6291460
  3.5 7.8 %copy-start.10 = (s32[4,6]{1,0:T(4,128)S(1)}, s32[4,6]{1,0:T(4,128)}, u32[]{:S(2)}) copy-start(s32[4,6]{1,0:T(4,128)} %param.19) | copy-start | bytes 292
  3.5 8.0 %copy-start.1 = (s32[2048]{0:T(1024)S(1)}, s32[2048]{0:T(1024)}, u32[]{:S(2)}) copy-start(s32[2048]{0:T(1024)} %param.20) | copy-start | bytes 24580
  3.5 21.8 %copy-start.9 = (bf16[7,4,1024]{2,1,0:T(4,128)(2,1)S(1)}, bf16[7,4,1024]{2,1,0:T(4,128)(2,1)}, u32[]{:S(2)}) copy-start(bf16[7,4,1024]{2,1,0:T(4,128)(2,1)} %param.16) | copy-start | bytes 172036
  3.5 22.4 %copy-start.19 = (s32[64]{0:T(128)S(1)}, s32[64]{0:T(128)}, u32[]{:S(2)}) copy-start(s32[64]{0:T(128)} %param.17) | copy-start | bytes 772
  3.5 23.6 %copy-start.14 = (f32[2]{0:T(128)S(1)}, f32[2]{0:T(128)}, u32[]{:S(2)}) copy-start(f32[2]{0:T(128)} %param.23) | copy-start | bytes 28
  3.5 88.6 %collective-permute-start.2 = (bf16[256,1024]{1,0:T(8,128)(2,1)}, bf16[256,1024]{1,0:T(8,128)(2,1)}, u32[]{:S(2)}, u32[]{:S(2)}) collective-permute-start(bf16[256,1024]{1,0:T(8,128)(2,1)} %get-tuple-element.31), channel_id=1, source_target_pairs={{0,1},{1,2},{2,3},{3,0},{4,5},{5,6},{6,7},{7,4},{8,9},{9,10},{10,1... | collective-permute-start | bytes 1572872 | tf_op jit(solution)/shard_map/ppermute | solution.py:27
  5.1 94.9 %collective-permute-start.3 = (bf16[256,1024]{1,0:T(8,128)(2,1)}, bf16[256,1024]{1,0:T(8,128)(2,1)}, u32[]{:S(2)}, u32[]{:S(2)}) collective-permute-start(bf16[256,1024]{1,0:T(8,128)(2,1)} %get-tuple-element.32), channel_id=1, source_target_pairs={{0,2},{1,3},{2,0},{3,1},{4,6},{5,7},{6,4},{7,5},{8,10},{9,11},{10,... | collective-permute-start | bytes 1572872 | tf_op jit(solution)/shard_map/ppermute | solution.py:27
  8.0 95.7 %collective-permute-start.4 = (bf16[256,1024]{1,0:T(8,128)(2,1)}, bf16[256,1024]{1,0:T(8,128)(2,1)}, u32[]{:S(2)}, u32[]{:S(2)}) collective-permute-start(bf16[256,1024]{1,0:T(8,128)(2,1)} %get-tuple-element.30), channel_id=1, source_target_pairs={{0,3},{1,0},{2,1},{3,2},{4,7},{5,4},{6,5},{7,6},{8,11},{9,8},{10,9... | collective-permute-start | bytes 1572872 | tf_op jit(solution)/shard_map/ppermute | solution.py:27
  10.6 20.6 %copy-start.6 = (f32[32,3,256]{2,0,1:T(8,128)S(1)}, f32[32,3,256]{2,0,1:T(8,128)}, u32[]{:S(2)}) copy-start(f32[32,3,256]{2,0,1:T(8,128)} %param.22) | copy-start | bytes 294916
  10.6 20.6 %copy-start.8 = (f32[32,3,256]{2,0,1:T(8,128)S(1)}, f32[32,3,256]{2,0,1:T(8,128)}, u32[]{:S(2)}) copy-start(f32[32,3,256]{2,0,1:T(8,128)} %param.21) | copy-start | bytes 294916
  10.6 87.5 %collective-permute-start.5 = (bf16[256,1024]{1,0:T(8,128)(2,1)}, bf16[256,1024]{1,0:T(8,128)(2,1)}, u32[]{:S(2)}, u32[]{:S(2)}) collective-permute-start(bf16[256,1024]{1,0:T(8,128)(2,1)} %get-tuple-element.28), channel_id=1, source_target_pairs={{0,1},{1,2},{2,3},{3,0},{4,5},{5,6},{6,7},{7,4},{8,9},{9,10},{10,1... | collective-permute-start | bytes 1572872 | tf_op jit(solution)/shard_map/ppermute | solution.py:27
  12.4 22.1 %copy-start.16 = (s32[24]{0:T(128)}, s32[24]{0:T(128)S(1)}, u32[]{:S(2)}) copy-start(s32[24]{0:T(128)S(1)} %get-tuple-element.42) | copy-start | bytes 292
  13.2 20.8 %all-to-all-start = ((s32[64,1,2]{2,1,0:T(1,128)}), s32[64,1,2]{2,1,0:T(1,128)S(1)}, u32[]{:S(2)}, u32[]{:S(2)}) async-start(s32[64,1,2]{2,1,0:T(1,128)} %bitcast.2), calls=%async_computation | async-start | bytes 65536 | tf_op jit(solution)/shard_map/all_to_all | solution.py:89
  25.3 15.0 %collective-permute-start = (bf16[7,4,1024]{2,1,0:T(4,128)(2,1)S(1)}, bf16[7,4,1024]{2,1,0:T(4,128)(2,1)}, u32[]{:S(2)}, u32[]{:S(2)}) collective-permute-start(bf16[7,4,1024]{2,1,0:T(4,128)(2,1)S(1)} %copy-done.9), channel_id=1, source_target_pairs={{0,1},{1,0},{2,3},{3,2},{4,5},{5,4},{6,7},{7,6},{8,9},{9,8},{10,11... | collective-permute-start | bytes 172040 | tf_op jit(solution)/shard_map/ppermute | solution.py:12
  34.0 0.6 copy-start.7
  41.9 16.0 %collective-permute-start.1 = (bf16[7,8,1024]{2,1,0:T(8,128)(2,1)}, bf16[7,8,1024]{2,1,0:T(8,128)(2,1)}, u32[]{:S(2)}, u32[]{:S(2)}) collective-permute-start(bf16[7,8,1024]{2,1,0:T(8,128)(2,1)} %maximum_select_fusion.1), channel_id=1, source_target_pairs={{0,2},{1,3},{2,0},{3,1},{4,6},{5,7},{6,4},{7,5},{8,10},{9,11},{10,... | collective-permute-start | bytes 344072 | tf_op jit(solution)/shard_map/ppermute | solution.py:12
  45.8 23.0 %all-to-all-start.2 = ((bf16[64,2,3,256]{3,1,2,0:T(2,128)(2,1)}), bf16[64,2,3,256]{3,1,2,0:T(2,128)(2,1)}, u32[]{:S(2)}, u32[]{:S(2)}) async-start(bf16[64,2,3,256]{3,1,2,0:T(2,128)(2,1)} %broadcast_select_fusion.1), calls=%async_computation.2 | async-start | bytes 393216 | tf_op jit(solution)/shard_map/all_to_all | solution.py:92
  58.0 43.9 %collective-permute-start.6 = (bf16[256,1024]{1,0:T(8,128)(2,1)}, bf16[256,1024]{1,0:T(8,128)(2,1)}, u32[]{:S(2)}, u32[]{:S(2)}) collective-permute-start(bf16[256,1024]{1,0:T(8,128)(2,1)} %get-tuple-element.29), channel_id=1, source_target_pairs={{0,2},{1,3},{2,0},{3,1},{4,6},{5,7},{6,4},{7,5},{8,10},{9,11},{10,... | collective-permute-start | bytes 1572872 | tf_op jit(solution)/shard_map/ppermute | solution.py:27
  59.8 2.2 %copy-start.18 = (pred[64]{0:T(512)(128)(4,1)S(1)}, pred[64]{0:T(512)(128)(4,1)}, u32[]{:S(2)}) copy-start(pred[64]{0:T(512)(128)(4,1)} %compare_and_fusion.2) | copy-start | bytes 196
  65.3 10.5 %copy-start.15 = (s32[24]{0:T(128)S(1)}, s32[24]{0:T(128)}, u32[]{:S(2)}) copy-start(s32[24]{0:T(128)} %fusion.33) | copy-start | bytes 292
  68.7 58.2 %all-to-all-start.1 = ((bf16[64,16,1024]{2,1,0:T(8,128)(2,1)}), bf16[64,16,1024]{2,1,0:T(8,128)(2,1)}, u32[]{:S(2)}, u32[]{:S(2)}) async-start(bf16[64,16,1024]{2,1,0:T(8,128)(2,1)} %broadcast_select_fusion), calls=%async_computation.1 | async-start | bytes 4194304 | tf_op jit(solution)/shard_map/all_to_all | solution.py:104
  75.8 3.5 %copy-start.12 = (s32[4,6]{1,0:T(4,128)S(1)}, s32[4,6]{1,0:T(4,128)}, u32[]{:S(2)}) copy-start(s32[4,6]{1,0:T(4,128)} %gather.24) | copy-start | bytes 292
  75.8 3.6 %copy-start.11 = (f32[3,1024]{1,0:T(4,128)S(1)}, f32[3,1024]{1,0:T(4,128)}, u32[]{:S(2)}) copy-start(f32[3,1024]{1,0:T(4,128)} %param.14) | copy-start | bytes 36868
  75.8 3.6 %copy-start.5 = (bf16[256,256]{1,0:T(8,128)(2,1)S(1)}, bf16[256,256]{1,0:T(8,128)(2,1)}, u32[]{:S(2)}) copy-start(bf16[256,256]{1,0:T(8,128)(2,1)} %param.15) | copy-start | bytes 393220
  91.1 1.0 copy-start.4
  92.1 15.6 %collective-permute-start.7 = (bf16[256,1024]{1,0:T(8,128)(2,1)S(1)}, bf16[256,1024]{1,0:T(8,128)(2,1)S(1)}, u32[]{:S(2)}, u32[]{:S(2)}) collective-permute-start(bf16[256,1024]{1,0:T(8,128)(2,1)S(1)} %copy-done.4), channel_id=1, source_target_pairs={{0,3},{1,0},{2,1},{3,2},{4,7},{5,4},{6,5},{7,6},{8,11},{9,8},{10,9... | collective-permute-start | bytes 1572872 | tf_op jit(solution)/shard_map/ppermute | solution.py:27
  108.5 3.2 %copy-start.3 = (bf16[128,8,4,256]{3,1,2,0:T(8,128)(2,1)S(1)}, bf16[128,8,4,256]{3,1,2,0:T(8,128)(2,1)}, u32[]{:S(2)}) copy-start(bf16[128,8,4,256]{3,1,2,0:T(8,128)(2,1)} %copy.74) | copy-start | bytes 6291460
  111.7 15.2 %copy-start.13 = (s32[1024]{0:T(1024)S(1)}, s32[1024]{0:T(1024)}, u32[]{:S(2)}) copy-start(s32[1024]{0:T(1024)} %add_select_fusion) | copy-start | bytes 12292
  135.3 0.6 copy-start.17
  137.4 20.2 %all-to-all-start.3 = ((f32[64,2,3,256]{3,1,2,0:T(2,128)}), f32[64,2,3,256]{3,1,2,0:T(2,128)S(1)}, u32[]{:S(2)}, u32[]{:S(2)}) async-start(f32[64,2,3,256]{3,1,2,0:T(2,128)} %copy.66), calls=%async_computation.3 | async-start | bytes 786432 | tf_op jit(solution)/shard_map/all_to_all | solution.py:134
  160.7 7.4 %collective-permute-start.10 = (f32[32,3,256]{2,0,1:T(8,128)}, f32[32,3,256]{2,0,1:T(8,128)S(1)}, u32[]{:S(2)}, u32[]{:S(2)}) collective-permute-start(f32[32,3,256]{2,0,1:T(8,128)} %fusion.19), channel_id=1, source_target_pairs={{0,1},{1,2},{2,3},{3,0},{4,5},{5,6},{6,7},{7,4},{8,9},{9,10},{10,1... | collective-permute-start | bytes 294920 | tf_op jit(solution)/shard_map/ppermute | solution.py:41
  163.3 4.9 %collective-permute-start.8 = (f32[32,3,256]{2,0,1:T(8,128)}, f32[32,3,256]{2,0,1:T(8,128)S(1)}, u32[]{:S(2)}, u32[]{:S(2)}) collective-permute-start(f32[32,3,256]{2,0,1:T(8,128)} %fusion.19), channel_id=1, source_target_pairs={{0,3},{1,0},{2,1},{3,2},{4,7},{5,4},{6,5},{7,6},{8,11},{9,8},{10,9... | collective-permute-start | bytes 294920 | tf_op jit(solution)/shard_map/ppermute | solution.py:41
  164.7 6.6 %collective-permute-start.9 = (f32[32,3,256]{2,0,1:T(8,128)}, f32[32,3,256]{2,0,1:T(8,128)S(1)}, u32[]{:S(2)}, u32[]{:S(2)}) collective-permute-start(f32[32,3,256]{2,0,1:T(8,128)} %fusion.19), channel_id=1, source_target_pairs={{0,2},{1,3},{2,0},{3,1},{4,6},{5,7},{6,4},{7,5},{8,10},{9,11},{10,... | collective-permute-start | bytes 294920 | tf_op jit(solution)/shard_map/ppermute | solution.py:41

commit v10 on v8

--- a/solution.py
+++ b/solution.py
@@ -109,17 +109,17 @@
     parts_flat = jnp.transpose(signal_parts, (1, 0, 2)).reshape(comp_count, width)
     signal = sum(response[j][:, None] * parts_flat[j][None, :] for j in range(comp_count))
     errors = ((columns.astype(jnp.float32) - signal) * column_weights).astype(jnp.bfloat16)
-    block_id = jnp.arange(width, dtype=jnp.int32) // samples
-    same_span = block_id[:, None] == block_id[None, :]
-    filter_blocks = jnp.where(same_span, jnp.tile(band_filter, (spans_here, spans_here)), jnp.zeros((), band_filter.dtype))
-    filtered = jnp.dot(errors, filter_blocks, preferred_element_type=jnp.float32).astype(jnp.bfloat16)
-    whitened = jnp.dot(matrix, filtered, preferred_element_type=jnp.float32).astype(jnp.bfloat16)
-    smoothed = lax.dot_general(
-        whitened, filter_blocks, (((1,), (1,)), ((), ())), preferred_element_type=jnp.float32
-    ).astype(jnp.bfloat16)
-    weighted = smoothed.astype(jnp.float32) * column_weights
-    stokes = jnp.stack([jnp.sum(response[j][:, None] * weighted, axis=0) for j in range(comp_count)])
-    stokes_short = jnp.transpose(stokes.reshape(comp_count, spans_here, samples), (1, 0, 2)).astype(jnp.bfloat16)
+    stokes_spans = []
+    for c in range(spans_here):
+        span = slice(c * samples, (c + 1) * samples)
+        filtered = jnp.dot(errors[:, span], band_filter, preferred_element_type=jnp.float32).astype(jnp.bfloat16)
+        whitened = jnp.dot(matrix, filtered, preferred_element_type=jnp.float32).astype(jnp.bfloat16)
+        smoothed = lax.dot_general(
+            whitened, band_filter, (((1,), (1,)), ((), ())), preferred_element_type=jnp.float32
+        ).astype(jnp.bfloat16)
+        weighted = smoothed.astype(jnp.float32) * column_weights[:, span]
+        stokes_spans.append(jnp.stack([jnp.sum(response[j][:, None] * weighted, axis=0) for j in range(comp_count)]))
+    stokes_short = jnp.stack(stokes_spans).astype(jnp.bfloat16)
     partial_value = jnp.einsum(
         "cjt,cktp->ckjp", stokes_short, pointing, preferred_element_type=jnp.float32
     )

time: 176 us -> 187 us (1.062)
  waiting for transfers between devices: 36.7 us -> 47.1 us
  matrix products: 14.9 us -> 23.5 us
  local copies, waits for them, and re-layouts: 41.6 us -> 37.8 us
  starting transfers between devices: 56.5 us -> 53.6 us
    dot_general x2 -> x8, matrix products: 12.1 us -> 20.7 us  [the longest x4 16.2 us: shards(): lax.dot_general(whitened, band_filter, (((1,), (1,)), ((), ())), preferre...]
    ppermute x2, waiting for transfers between devices: 4.9 us -> 10.7 us  [wafer_gather(): other = lax.ppermute(x, 'wafer', [(i, i ^ bit) for i in range(size)])]
    all_to_all x1, waiting for transfers between devices: 11.5 us -> 16.5 us  [shards(): lax.all_to_all(sent_blocks, 'tm', split_axis=0, concat_axis=0, tiled=True)]
    select_n x3 -> x0, other arithmetic: 4.81 us -> none  [the longest x1 4.21 us: shards(): jnp.where(same_span, jnp.tile(band_filter, (spans_here, spans_here)), jnp...]
    unnamed x44 -> x36, local copies, waits for them, and re-layouts: 7.96 us -> 3.15 us
    ppermute x6, waiting for transfers between devices: 2.03 us -> 6.42 us  [wafer_columns(): lax.ppermute(piece, 'wafer', [(i, (i + shift) % size) for i in range(size)])]
    convert_element_type x0 -> x1, other arithmetic: none -> 3.99 us  [shards(): column_weights = wafer_columns(sample_weight).astype(jnp.float32)]
    ppermute x6, starting transfers between devices: 11.4 us -> 7.55 us  [wafer_columns(): lax.ppermute(piece, 'wafer', [(i, (i + shift) % size) for i in range(size)])]
  transfers between devices with their start and end apart: 15 -> 15, of which waited for: 8 -> 6; matrix products, arithmetic and copies ran while one was open for 34% -> 30% of each run, Pallas kernels for 0% -> 0%
where the time goes in v10:
time: 187 us; the launch traced here: 186 us
  starting transfers between devices  53.6 us (29%)
  waiting for transfers between devices  47.1 us (25%)
  local copies, waits for them, and re-layouts  37.8 us (20%)
  matrix products  23.5 us (13%)
  other arithmetic  22.7 us (12%)
    all_to_all x1, waiting for transfers between devices, shards(): lax.all_to_all(sent_blocks, 'tm', split_axis=0, concat_axis=0, tiled=True)  16.5 us
    dot_general x4, matrix products, shards(): lax.dot_general(whitened, band_filter, (((1,), (1,)), ((), ())), preferre...  16.2 us
    dynamic_update_slice x8, local copies, waits for them, and re-layouts, wafer_columns(): placed = lax.dynamic_update_slice_in_dim(placed, piece[None], source, 0)  13.9 us
    all_to_all x1, starting transfers between devices, shards(): lax.all_to_all(requests, 'tm', split_axis=0, concat_axis=0, tiled=True)  12 us
    all_to_all x1, waiting for transfers between devices, shards(): lax.all_to_all(outgoing, 'tm', split_axis=0, concat_axis=0, tiled=True)  11.2 us
    ppermute x2, waiting for transfers between devices, wafer_gather(): other = lax.ppermute(x, 'wafer', [(i, i ^ bit) for i in range(size)])  10.7 us
    all_to_all x1, starting transfers between devices, shards(): lax.all_to_all(sent_blocks, 'tm', split_axis=0, concat_axis=0, tiled=True)  10.5 us
    all_to_all x1, starting transfers between devices, shards(): lax.all_to_all(served, 'tm', split_axis=0, concat_axis=0, tiled=True)  10.5 us
  transfers between devices with their start and end apart: 15, of which 6 were waited for; matrix products, arithmetic and copies ran while one was open for 30% of the time, Pallas kernels for 0%

profile of v10, /device:TPU:2, one launch (start us, length us, event | category | flops | bytes accessed | tf_op | source)
XLA Modules:
  0.0 185.7 jit_solution(7976450185968886524)
XLA Ops:
  0.6 0.9 reshape.317
  1.6 0.8 reshape.316
  2.4 1.4 gather_fusion
  4.6 0.8 all_to_all.19
  5.3 12.0 %all-to-all-start = ((s32[64,1,2]{2,1,0:T(1,128)}), s32[64,1,2]{2,1,0:T(1,128)S(1)}, u32[]{:S(2)}, u32[]{:S(2)}) async-start(s32[64,1,2]{2,1,0:T(1,128)} %bitcast.2), calls=%async_computation | async-start | bytes 65536 | tf_op jit(solution)/shard_map/all_to_all | solution.py:89
  17.4 1.7 collective-permute-start
  19.0 2.7 %constant_dynamic-slice_fusion.2 = (bf16[256,1024]{1,0:T(8,128)(2,1)}, bf16[256,1024]{1,0:T(8,128)(2,1)}, bf16[256,1024]{1,0:T(8,128)(2,1)}) fusion(bf16[256,4096]{1,0:T(8,128)(2,1)} %param.12, s32[]{:T(128)S(6)} %select_n.377, s32[]{:T(128)S(6)} %select_n.369, s32[]{:T(128)S(6)} %select_n.373), kind=kLoop, calls=%fused_computation.96 | loop fusion | bytes 3145740 | tf_op jit(solution)/shard_map/dynamic_slice | solution.py:26
  21.8 2.3 %collective-permute-start.4 = (bf16[256,1024]{1,0:T(8,128)(2,1)}, bf16[256,1024]{1,0:T(8,128)(2,1)}, u32[]{:S(2)}, u32[]{:S(2)}) collective-permute-start(bf16[256,1024]{1,0:T(8,128)(2,1)} %get-tuple-element.45), channel_id=1, source_target_pairs={{0,3},{1,0},{2,1},{3,2},{4,7},{5,4},{6,5},{7,6},{8,11},{9,8},{10,9... | collective-permute-start | bytes 1572872 | tf_op jit(solution)/shard_map/ppermute | solution.py:27
  24.1 2.7 %collective-permute-start.3 = (bf16[256,1024]{1,0:T(8,128)(2,1)}, bf16[256,1024]{1,0:T(8,128)(2,1)}, u32[]{:S(2)}, u32[]{:S(2)}) collective-permute-start(bf16[256,1024]{1,0:T(8,128)(2,1)} %get-tuple-element.47), channel_id=1, source_target_pairs={{0,2},{1,3},{2,0},{3,1},{4,6},{5,7},{6,4},{7,5},{8,10},{9,11},{10,... | collective-permute-start | bytes 1572872 | tf_op jit(solution)/shard_map/ppermute | solution.py:27
  26.8 1.2 constant_dynamic-slice_fusion.5
  28.0 1.3 collective-permute-start.5
  29.4 0.6 compare_and_fusion.2
  30.8 0.7 fusion.42
  31.4 0.6 compare_and_fusion.1
  32.0 1.4 fusion.39
  33.5 1.6 broadcast.425.clone
  35.1 1.9 %bitcast_dynamic-update-slice_fusion.3 = bf16[4,256,1024]{2,1,0:T(8,128)(2,1)} fusion(bf16[4,256,1024]{2,1,0:T(8,128)(2,1)} %broadcast.425.clone, s32[]{:T(128)S(6)} %select_n.367, bf16[256,4096]{1,0:T(8,128)(2,1)} %param.13, s32[]{:T(128)S(6)} %select_n.366), kind=kLoop, calls=%fused_computation.49 | loop fusion | bytes 1048584 | tf_op jit(solution)/shard_map/dynamic_update_slice | solution.py:32
  38.2 0.8 gather_fusion.2
  39.0 1.7 maximum_select_fusion.1
  40.7 0.8 collective-permute-start.1
  41.5 0.9 broadcast_select_fusion.1
  42.4 10.5 %all-to-all-start.2 = ((bf16[64,2,3,256]{3,1,2,0:T(2,128)(2,1)}), bf16[64,2,3,256]{3,1,2,0:T(2,128)(2,1)}, u32[]{:S(2)}, u32[]{:S(2)}) async-start(bf16[64,2,3,256]{3,1,2,0:T(2,128)(2,1)} %broadcast_select_fusion.1), calls=%async_computation.2 | async-start | bytes 393216 | tf_op jit(solution)/shard_map/all_to_all | solution.py:92
  52.9 10.7 %collective-permute-done.1 = bf16[7,8,1024]{2,1,0:T(8,128)(2,1)} collective-permute-done((bf16[7,8,1024]{2,1,0:T(8,128)(2,1)}, bf16[7,8,1024]{2,1,0:T(8,128)(2,1)}, u32[]{:S(2)}, u32[]{:S(2)}) %collective-permute-start.1) | collective-permute-done | bytes 114720 | tf_op jit(solution)/shard_map/ppermute | solution.py:12
  63.6 1.0 collective-permute-start.6
  64.5 1.1 maximum_select_fusion
  65.7 2.2 %gather_fusion.1 = bf16[64,16,1024]{2,1,0:T(8,128)(2,1)} fusion(bf16[7,16,1024]{2,1,0:T(8,128)(2,1)S(1)} %maximum_select_fusion, s32[1024]{0:T(1024)} %pad_clamp_fusion.2), kind=kCustom, calls=%fused_computation.1 | custom fusion | bytes 4194560 | tf_op jit(solution)/shard_map/jit(_take)/gather | solution.py:103
  67.8 3.2 %broadcast_select_fusion = bf16[64,16,1024]{2,1,0:T(8,128)(2,1)} fusion(bf16[64,16,1024]{2,1,0:T(8,128)(2,1)} %gather_fusion.1, pred[64]{0:T(512)(128)(4,1)S(1)} %copy-done.15), kind=kLoop, calls=%fused_computation.8 | loop fusion | flops 1048576 | bytes 4194368 | tf_op jit(solution)/shard_map/jit(_take)/select_n | solution.py:103
  71.1 10.5 %all-to-all-start.1 = ((bf16[64,16,1024]{2,1,0:T(8,128)(2,1)}), bf16[64,16,1024]{2,1,0:T(8,128)(2,1)}, u32[]{:S(2)}, u32[]{:S(2)}) async-start(bf16[64,16,1024]{2,1,0:T(8,128)(2,1)} %broadcast_select_fusion), calls=%async_computation.1 | async-start | bytes 4194304 | tf_op jit(solution)/shard_map/all_to_all | solution.py:104
  81.6 1.6 broadcast.425.clone.1
  83.2 1.9 bitcast_dynamic-update-slice_fusion.7
  85.1 1.0 copy.64
  86.1 0.6 gather_fusion.3
  86.7 0.9 convolution_bitcast_fusion
  88.0 1.9 %bitcast_dynamic-update-slice_fusion.2 = bf16[4,256,1024]{2,1,0:T(8,128)(2,1)} fusion(bf16[4,256,1024]{2,1,0:T(8,128)(2,1)} %bitcast_dynamic-update-slice_fusion.3, s32[]{:T(128)S(6)} %select_n.371, bf16[256,1024]{1,0:T(8,128)(2,1)} %collective-permute-done.5), kind=kLoop, calls=%fused_computation.48 | loop fusion | bytes 1048580 | tf_op jit(solution)/shard_map/dynamic_update_slice | solution.py:32
  89.9 1.9 %bitcast_dynamic-update-slice_fusion.6 = bf16[4,256,1024]{2,1,0:T(8,128)(2,1)} fusion(bf16[4,256,1024]{2,1,0:T(8,128)(2,1)} %bitcast_dynamic-update-slice_fusion.7, s32[]{:T(128)S(6)} %select_n.371, bf16[256,1024]{1,0:T(8,128)(2,1)} %collective-permute-done.2), kind=kLoop, calls=%fused_computation.52 | loop fusion | bytes 1048580 | tf_op jit(solution)/shard_map/dynamic_update_slice | solution.py:32
  91.8 1.9 bitcast_dynamic-update-slice_fusion.1
  93.6 1.9 %bitcast_dynamic-update-slice_fusion.5 = bf16[4,256,1024]{2,1,0:T(8,128)(2,1)} fusion(bf16[4,256,1024]{2,1,0:T(8,128)(2,1)} %bitcast_dynamic-update-slice_fusion.6, s32[]{:T(128)S(6)} %select_n.375, bf16[256,1024]{1,0:T(8,128)(2,1)} %collective-permute-done.3), kind=kLoop, calls=%fused_computation.51 | loop fusion | bytes 1048580 | tf_op jit(solution)/shard_map/dynamic_update_slice | solution.py:32
  95.5 6.4 %collective-permute-done.7 = bf16[256,1024]{1,0:T(8,128)(2,1)S(1)} collective-permute-done((bf16[256,1024]{1,0:T(8,128)(2,1)S(1)}, bf16[256,1024]{1,0:T(8,128)(2,1)S(1)}, u32[]{:S(2)}, u32[]{:S(2)}) %collective-permute-start.7) | collective-permute-done | bytes 524320 | tf_op jit(solution)/shard_map/ppermute | solution.py:27
  101.9 0.8 bitcast_dynamic-update-slice_fusion
  102.8 1.9 %bitcast_dynamic-update-slice_fusion.4 = bf16[4,256,1024]{2,1,0:T(8,128)(2,1)} fusion(bf16[4,256,1024]{2,1,0:T(8,128)(2,1)} %bitcast_dynamic-update-slice_fusion.5, s32[]{:T(128)S(6)} %select_n.379, bf16[256,1024]{1,0:T(8,128)(2,1)} %collective-permute-done.4), kind=kLoop, calls=%fused_computation.50 | loop fusion | bytes 1048580 | tf_op jit(solution)/shard_map/dynamic_update_slice | solution.py:32
  104.6 3.1 %fusion.1 = bf16[1024,1024]{1,0:T(8,128)(2,1)S(1)} fusion(bf16[4,256,1024]{2,1,0:T(8,128)(2,1)} %bitcast_dynamic-update-slice_fusion.4, f32[1024]{0:T(1024)S(1)} %bitcast.136, f32[1024]{0:T(1024)S(1)} %bitcast.133, f32[1024]{0:T(1024)S(1)} %bitcast.137, f32[1024]{0:T(1024)S(1)} %bitcast.129, f32[1024]{0:T(1024)S(1)} %bitcast.135, f32[1024]{0:T(1024)S(1)} %bitcast.131, ...), kind=kLoop, calls=%fused_computation.6 | loop fusion | flops 10485760 | bytes 6316032 | tf_op jit(solution)/shard_map/convert_element_type | solution.py:111
  107.8 1.1 convolution_convert_fusion.1
  108.9 1.1 convolution_convert_fusion.3
  110.0 1.1 convolution_convert_fusion.5
  111.1 1.1 convolution_convert_fusion.7
  112.2 4.0 %bitcast_convert_fusion = f32[1024,1024]{1,0:T(8,128)} fusion(bf16[4,256,1024]{2,1,0:T(8,128)(2,1)} %bitcast_dynamic-update-slice_fusion), kind=kLoop, calls=%fused_computation.7 | loop fusion | flops 1048576 | bytes 6291456 | tf_op jit(solution)/shard_map/convert_element_type | solution.py:107
  116.2 16.5 %all-to-all-done.1 = bf16[64,16,1024]{2,1,0:T(8,128)(2,1)} async-done(((bf16[64,16,1024]{2,1,0:T(8,128)(2,1)}), bf16[64,16,1024]{2,1,0:T(8,128)(2,1)}, u32[]{:S(2)}, u32[]{:S(2)}) %all-to-all-start.1) | async-done | bytes 2097184 | tf_op jit(solution)/shard_map/all_to_all | solution.py:104
  132.7 3.6 %fusion.4 = f32[1024,256]{1,0:T(8,128)} fusion(bf16[256,256]{1,0:T(8,128)(2,1)S(1)} %copy-done.1, bf16[1024,1024]{1,0:T(8,128)(2,1)} %bitcast.7, bf16[1024,256]{1,0:T(8,128)(2,1)} %convolution_convert_fusion.3), kind=kOutput, calls=%fused_computation.23 | convolution fusion | flops 671875072 | bytes 3801088 | tf_op jit(solution)/shard_map/dot_general | solution.py:117
  136.4 3.6 %fusion.2 = f32[1024,256]{1,0:T(8,128)} fusion(bf16[256,256]{1,0:T(8,128)(2,1)S(1)} %copy-done.1, bf16[1024,1024]{1,0:T(8,128)(2,1)} %bitcast.7, bf16[1024,256]{1,0:T(8,128)(2,1)} %convolution_convert_fusion.7), kind=kOutput, calls=%fused_computation.21 | convolution fusion | flops 671875072 | bytes 3801088 | tf_op jit(solution)/shard_map/dot_general | solution.py:117
  140.0 3.7 %fusion.3 = f32[1024,256]{1,0:T(8,128)} fusion(bf16[256,256]{1,0:T(8,128)(2,1)S(1)} %copy-done.1, bf16[1024,1024]{1,0:T(8,128)(2,1)} %bitcast.7, bf16[1024,256]{1,0:T(8,128)(2,1)} %convolution_convert_fusion.5), kind=kOutput, calls=%fused_computation.22 | convolution fusion | flops 671875072 | bytes 3801088 | tf_op jit(solution)/shard_map/dot_general | solution.py:117
  143.7 5.3 %multiply_reduce_fusion.2 = (bf16[256]{0:T(256)(128)(2,1)S(1)}, bf16[256]{0:T(256)(128)(2,1)S(1)}, bf16[256]{0:T(256)(128)(2,1)S(1)}, bf16[256]{0:T(256)(128)(2,...) fusion(f32[1024]{0:T(1024)S(1)} %bitcast.132, ...), kind=kOutput, calls=%fused_computation.32 | convolution fusion | flops 679212032 | bytes 10110976 | tf_op jit(solution)/shard_map/dot_general | solution.py:117
  150.1 1.0 copy.66
  151.2 5.4 %all-to-all-start.3 = ((f32[64,2,3,256]{3,1,2,0:T(2,128)}), f32[64,2,3,256]{3,1,2,0:T(2,128)S(1)}, u32[]{:S(2)}, u32[]{:S(2)}) async-start(f32[64,2,3,256]{3,1,2,0:T(2,128)} %copy.66), calls=%async_computation.3 | async-start | bytes 786432 | tf_op jit(solution)/shard_map/all_to_all | solution.py:129
  157.1 2.1 %reduce.3 = s32[64,2]{1,0:T(8,128)} reduce(s32[64,1,2]{2,1,0:T(1,128)} %copy-done.5, s32[]{:T(128)} %broadcast.455), dimensions={1}, to_apply=%all_to_all.20.reduce_sub_computation.3 | reduce | bytes 1028 | tf_op jit(solution)/shard_map/all_to_all | solution.py:89
  159.2 0.9 eq.141
  160.1 11.2 %all-to-all-done.3 = f32[64,2,3,256]{3,1,2,0:T(2,128)S(1)} async-done(((f32[64,2,3,256]{3,1,2,0:T(2,128)}), f32[64,2,3,256]{3,1,2,0:T(2,128)S(1)}, u32[]{:S(2)}, u32[]{:S(2)}) %all-to-all-start.3) | async-done | bytes 393248 | tf_op jit(solution)/shard_map/all_to_all | solution.py:129
  171.5 0.8 copy.75
  172.3 1.1 copy.68
  173.4 1.0 fusion.18
  174.4 2.6 %collective-permute-start.9 = (f32[32,3,256]{2,0,1:T(8,128)}, f32[32,3,256]{2,0,1:T(8,128)S(1)}, u32[]{:S(2)}, u32[]{:S(2)}) collective-permute-start(f32[32,3,256]{2,0,1:T(8,128)} %fusion.18), channel_id=1, source_target_pairs={{0,2},{1,3},{2,0},{3,1},{4,6},{5,7},{6,4},{7,5},{8,10},{9,11},{10,... | collective-permute-start | bytes 294920 | tf_op jit(solution)/shard_map/ppermute | solution.py:41
  177.0 2.6 %collective-permute-start.8 = (f32[32,3,256]{2,0,1:T(8,128)}, f32[32,3,256]{2,0,1:T(8,128)S(1)}, u32[]{:S(2)}, u32[]{:S(2)}) collective-permute-start(f32[32,3,256]{2,0,1:T(8,128)} %fusion.18), channel_id=1, source_target_pairs={{0,3},{1,0},{2,1},{3,2},{4,7},{5,4},{6,5},{7,6},{8,11},{9,8},{10,9... | collective-permute-start | bytes 294920 | tf_op jit(solution)/shard_map/ppermute | solution.py:41
  179.6 1.6 copy.69
  181.2 1.7 collective-permute-done.10
  183.4 2.3 %multiply_add_fusion = (f32[32,3,256]{2,0,1:T(8,128)}, f32[32,3,256]{2,0,1:T(8,128)}) fusion(f32[32,3,256]{2,0,1:T(8,128)} %param.22, f32[]{:T(128)} %bitcast.47, f32[32,3,256]{2,0,1:T(8,128)S(1)} %collective-permute-done.8, f32[32,3,256]{2,0,1:T(8,128)S(1)} %collective-permute-done.9, f32[32,3,256]{2,0,1:T(8,128)S(1)} %collective-permute-done.10, ...), kind=kLoop, calls=%fused_computation.59 | loop fusion | flops 442368 | bytes 688144 | tf_op jit(solution)/shard_map/add | solution.py:141
  (89 shorter events, 5.4 us)
Async XLA Ops:
  0.6 86.1 %copy-start = (bf16[4,6,256,256]{3,2,1,0:T(8,128)(2,1)S(1)}, bf16[4,6,256,256]{3,2,1,0:T(8,128)(2,1)}, u32[]{:S(2)}) copy-start(bf16[4,6,256,256]{3,2,1,0:T(8,128)(2,1)} %param.18) | copy-start | bytes 9437188
  4.0 0.5 copy-start.12
  5.3 32.2 %all-to-all-start = ((s32[64,1,2]{2,1,0:T(1,128)}), s32[64,1,2]{2,1,0:T(1,128)S(1)}, u32[]{:S(2)}, u32[]{:S(2)}) async-start(s32[64,1,2]{2,1,0:T(1,128)} %bitcast.2), calls=%async_computation | async-start | bytes 65536 | tf_op jit(solution)/shard_map/all_to_all | solution.py:89
  17.4 21.6 %collective-permute-start = (bf16[7,4,1024]{2,1,0:T(4,128)(2,1)}, bf16[7,4,1024]{2,1,0:T(4,128)(2,1)}, u32[]{:S(2)}, u32[]{:S(2)}) collective-permute-start(bf16[7,4,1024]{2,1,0:T(4,128)(2,1)} %param.16), channel_id=1, source_target_pairs={{0,1},{1,0},{2,3},{3,2},{4,5},{5,4},{6,7},{7,6},{8,9},{9,8},{10,11... | collective-permute-start | bytes 172040 | tf_op jit(solution)/shard_map/ppermute | solution.py:12
  19.0 7.8 %copy-start.2 = (bf16[256,4096]{1,0:T(8,128)(2,1)S(1)}, bf16[256,4096]{1,0:T(8,128)(2,1)}, u32[]{:S(2)}) copy-start(bf16[256,4096]{1,0:T(8,128)(2,1)} %param.13) | copy-start | bytes 6291460
  21.8 7.6 %copy-start.16 = (s32[64]{0:T(128)S(1)}, s32[64]{0:T(128)}, u32[]{:S(2)}) copy-start(s32[64]{0:T(128)} %param.17) | copy-start | bytes 772
  21.8 9.0 %copy-start.10 = (f32[2]{0:T(128)S(1)}, f32[2]{0:T(128)}, u32[]{:S(2)}) copy-start(f32[2]{0:T(128)} %param.23) | copy-start | bytes 28
  21.8 9.6 %copy-start.9 = (f32[3,1024]{1,0:T(4,128)S(1)}, f32[3,1024]{1,0:T(4,128)}, u32[]{:S(2)}) copy-start(f32[3,1024]{1,0:T(4,128)} %param.14) | copy-start | bytes 36868
  21.8 9.7 %copy-start.8 = (s32[4,6]{1,0:T(4,128)S(1)}, s32[4,6]{1,0:T(4,128)}, u32[]{:S(2)}) copy-start(s32[4,6]{1,0:T(4,128)} %param.19) | copy-start | bytes 292
  21.8 10.3 %copy-start.4 = (f32[32,3,256]{2,0,1:T(8,128)S(1)}, f32[32,3,256]{2,0,1:T(8,128)}, u32[]{:S(2)}) copy-start(f32[32,3,256]{2,0,1:T(8,128)} %param.22) | copy-start | bytes 294916
  21.8 10.3 %copy-start.6 = (f32[32,3,256]{2,0,1:T(8,128)S(1)}, f32[32,3,256]{2,0,1:T(8,128)}, u32[]{:S(2)}) copy-start(f32[32,3,256]{2,0,1:T(8,128)} %param.21) | copy-start | bytes 294916
  21.8 81.0 %collective-permute-start.4 = (bf16[256,1024]{1,0:T(8,128)(2,1)}, bf16[256,1024]{1,0:T(8,128)(2,1)}, u32[]{:S(2)}, u32[]{:S(2)}) collective-permute-start(bf16[256,1024]{1,0:T(8,128)(2,1)} %get-tuple-element.45), channel_id=1, source_target_pairs={{0,3},{1,0},{2,1},{3,2},{4,7},{5,4},{6,5},{7,6},{8,11},{9,8},{10,9... | collective-permute-start | bytes 1572872 | tf_op jit(solution)/shard_map/ppermute | solution.py:27
  24.1 65.8 %collective-permute-start.2 = (bf16[256,1024]{1,0:T(8,128)(2,1)}, bf16[256,1024]{1,0:T(8,128)(2,1)}, u32[]{:S(2)}, u32[]{:S(2)}) collective-permute-start(bf16[256,1024]{1,0:T(8,128)(2,1)} %get-tuple-element.46), channel_id=1, source_target_pairs={{0,1},{1,2},{2,3},{3,0},{4,5},{5,6},{6,7},{7,4},{8,9},{9,10},{10,1... | collective-permute-start | bytes 1572872 | tf_op jit(solution)/shard_map/ppermute | solution.py:27
  24.1 69.6 %collective-permute-start.3 = (bf16[256,1024]{1,0:T(8,128)(2,1)}, bf16[256,1024]{1,0:T(8,128)(2,1)}, u32[]{:S(2)}, u32[]{:S(2)}) collective-permute-start(bf16[256,1024]{1,0:T(8,128)(2,1)} %get-tuple-element.47), channel_id=1, source_target_pairs={{0,2},{1,3},{2,0},{3,1},{4,6},{5,7},{6,4},{7,5},{8,10},{9,11},{10,... | collective-permute-start | bytes 1572872 | tf_op jit(solution)/shard_map/ppermute | solution.py:27
  28.0 59.6 %collective-permute-start.5 = (bf16[256,1024]{1,0:T(8,128)(2,1)}, bf16[256,1024]{1,0:T(8,128)(2,1)}, u32[]{:S(2)}, u32[]{:S(2)}) collective-permute-start(bf16[256,1024]{1,0:T(8,128)(2,1)} %get-tuple-element.43), channel_id=1, source_target_pairs={{0,1},{1,2},{2,3},{3,0},{4,5},{5,6},{6,7},{7,4},{8,9},{9,10},{10,1... | collective-permute-start | bytes 1572872 | tf_op jit(solution)/shard_map/ppermute | solution.py:27
  32.0 7.0 %copy-start.7 = (bf16[7,4,1024]{2,1,0:T(4,128)(2,1)S(1)}, bf16[7,4,1024]{2,1,0:T(4,128)(2,1)}, u32[]{:S(2)}) copy-start(bf16[7,4,1024]{2,1,0:T(4,128)(2,1)} %param.16) | copy-start | bytes 172036
  37.6 0.6 copy-start.5
  40.7 22.9 %collective-permute-start.1 = (bf16[7,8,1024]{2,1,0:T(8,128)(2,1)}, bf16[7,8,1024]{2,1,0:T(8,128)(2,1)}, u32[]{:S(2)}, u32[]{:S(2)}) collective-permute-start(bf16[7,8,1024]{2,1,0:T(8,128)(2,1)} %maximum_select_fusion.1), channel_id=1, source_target_pairs={{0,2},{1,3},{2,0},{3,1},{4,6},{5,7},{6,4},{7,5},{8,10},{9,11},{10,... | collective-permute-start | bytes 344072 | tf_op jit(solution)/shard_map/ppermute | solution.py:12
  42.4 28.7 %all-to-all-start.2 = ((bf16[64,2,3,256]{3,1,2,0:T(2,128)(2,1)}), bf16[64,2,3,256]{3,1,2,0:T(2,128)(2,1)}, u32[]{:S(2)}, u32[]{:S(2)}) async-start(bf16[64,2,3,256]{3,1,2,0:T(2,128)(2,1)} %broadcast_select_fusion.1), calls=%async_computation.2 | async-start | bytes 393216 | tf_op jit(solution)/shard_map/all_to_all | solution.py:92
  63.6 28.2 %collective-permute-start.6 = (bf16[256,1024]{1,0:T(8,128)(2,1)}, bf16[256,1024]{1,0:T(8,128)(2,1)}, u32[]{:S(2)}, u32[]{:S(2)}) collective-permute-start(bf16[256,1024]{1,0:T(8,128)(2,1)} %get-tuple-element.44), channel_id=1, source_target_pairs={{0,2},{1,3},{2,0},{3,1},{4,6},{5,7},{6,4},{7,5},{8,10},{9,11},{10,... | collective-permute-start | bytes 1572872 | tf_op jit(solution)/shard_map/ppermute | solution.py:27
  65.6 2.2 %copy-start.15 = (pred[64]{0:T(512)(128)(4,1)S(1)}, pred[64]{0:T(512)(128)(4,1)}, u32[]{:S(2)}) copy-start(pred[64]{0:T(512)(128)(4,1)} %compare_and_fusion.2) | copy-start | bytes 196
  71.1 10.5 %copy-start.11 = (s32[24]{0:T(128)S(1)}, s32[24]{0:T(128)}, u32[]{:S(2)}) copy-start(s32[24]{0:T(128)} %fusion.35) | copy-start | bytes 292
  71.1 61.7 %all-to-all-start.1 = ((bf16[64,16,1024]{2,1,0:T(8,128)(2,1)}), bf16[64,16,1024]{2,1,0:T(8,128)(2,1)}, u32[]{:S(2)}, u32[]{:S(2)}) async-start(bf16[64,16,1024]{2,1,0:T(8,128)(2,1)} %broadcast_select_fusion), calls=%async_computation.1 | async-start | bytes 4194304 | tf_op jit(solution)/shard_map/all_to_all | solution.py:104
  81.6 5.2 %copy-start.14 = (pred[4,6]{1,0:T(4,128)(4,1)S(1)}, pred[4,6]{1,0:T(4,128)(4,1)}, u32[]{:S(2)}) copy-start(pred[4,6]{1,0:T(4,128)(4,1)} %compare_and_fusion.1) | copy-start | bytes 76
  86.7 1.0 copy-start.3
  87.7 14.2 %collective-permute-start.7 = (bf16[256,1024]{1,0:T(8,128)(2,1)S(1)}, bf16[256,1024]{1,0:T(8,128)(2,1)S(1)}, u32[]{:S(2)}, u32[]{:S(2)}) collective-permute-start(bf16[256,1024]{1,0:T(8,128)(2,1)S(1)} %copy-done.3), channel_id=1, source_target_pairs={{0,3},{1,0},{2,1},{3,2},{4,7},{5,4},{6,5},{7,6},{8,11},{9,8},{10,9... | collective-permute-start | bytes 1572872 | tf_op jit(solution)/shard_map/ppermute | solution.py:27
  104.6 3.1 %copy-start.1 = (bf16[256,256]{1,0:T(8,128)(2,1)S(1)}, bf16[256,256]{1,0:T(8,128)(2,1)}, u32[]{:S(2)}) copy-start(bf16[256,256]{1,0:T(8,128)(2,1)} %param.15) | copy-start | bytes 393220
  148.9 0.7 copy-start.13
  151.2 20.2 %all-to-all-start.3 = ((f32[64,2,3,256]{3,1,2,0:T(2,128)}), f32[64,2,3,256]{3,1,2,0:T(2,128)S(1)}, u32[]{:S(2)}, u32[]{:S(2)}) async-start(f32[64,2,3,256]{3,1,2,0:T(2,128)} %copy.66), calls=%async_computation.3 | async-start | bytes 786432 | tf_op jit(solution)/shard_map/all_to_all | solution.py:129
  174.4 8.4 %collective-permute-start.10 = (f32[32,3,256]{2,0,1:T(8,128)}, f32[32,3,256]{2,0,1:T(8,128)S(1)}, u32[]{:S(2)}, u32[]{:S(2)}) collective-permute-start(f32[32,3,256]{2,0,1:T(8,128)} %fusion.18), channel_id=1, source_target_pairs={{0,1},{1,2},{2,3},{3,0},{4,5},{5,6},{6,7},{7,4},{8,9},{9,10},{10,1... | collective-permute-start | bytes 294920 | tf_op jit(solution)/shard_map/ppermute | solution.py:41
  174.4 8.4 %collective-permute-start.9 = (f32[32,3,256]{2,0,1:T(8,128)}, f32[32,3,256]{2,0,1:T(8,128)S(1)}, u32[]{:S(2)}, u32[]{:S(2)}) collective-permute-start(f32[32,3,256]{2,0,1:T(8,128)} %fusion.18), channel_id=1, source_target_pairs={{0,2},{1,3},{2,0},{3,1},{4,6},{5,7},{6,4},{7,5},{8,10},{9,11},{10,... | collective-permute-start | bytes 294920 | tf_op jit(solution)/shard_map/ppermute | solution.py:41
  177.0 6.4 %collective-permute-start.8 = (f32[32,3,256]{2,0,1:T(8,128)}, f32[32,3,256]{2,0,1:T(8,128)S(1)}, u32[]{:S(2)}, u32[]{:S(2)}) collective-permute-start(f32[32,3,256]{2,0,1:T(8,128)} %fusion.18), channel_id=1, source_target_pairs={{0,3},{1,0},{2,1},{3,2},{4,7},{5,4},{6,5},{7,6},{8,11},{9,8},{10,9... | collective-permute-start | bytes 294920 | tf_op jit(solution)/shard_map/ppermute | solution.py:41

commit v11 on v8

--- a/solution.py
+++ b/solution.py
@@ -88,10 +88,13 @@
     requests = requests.reshape(tm_count, capacity)
     asked_slots = lax.all_to_all(requests, "tm", split_axis=0, concat_axis=0, tiled=True)
     served = jnp.take(short_map, asked_slots, axis=0)
-    replies, asked_slots = (
-        lax.all_to_all(served, "tm", split_axis=0, concat_axis=0, tiled=True),
-        asked_slots,
-    )
+    block_rows = wafer_gather(whiten, 1)
+    sent_blocks = jnp.take(block_rows, group_wafer, axis=0).reshape(tm_count, -1)
+    block_size = sent_blocks.shape[1]
+    packed = jnp.concatenate([sent_blocks, served.reshape(tm_count, -1)], axis=1)
+    unpacked = lax.all_to_all(packed, "tm", split_axis=0, concat_axis=0, tiled=True)
+    matrix = unpacked[:, :block_size].reshape(det_total, det_total)
+    replies = unpacked[:, block_size:].reshape(tm_count, capacity, comp_count, pixel_count)
     fetched = jnp.take(
         replies.reshape(tm_count * capacity, comp_count, pixel_count), targets, axis=0
     )
@@ -99,10 +102,6 @@
     signal_parts = jnp.einsum(
         "cktp,ckjp->cjt", pointing, fetched, preferred_element_type=jnp.float32
     )
-    block_rows = wafer_gather(whiten, 1)
-    sent_blocks = jnp.take(block_rows, group_wafer, axis=0)
-    matrix = lax.all_to_all(sent_blocks, "tm", split_axis=0, concat_axis=0, tiled=True)
-    matrix = matrix.reshape(det_total, det_total)
     columns = wafer_columns(timestream)
     column_weights = wafer_columns(sample_weight).astype(jnp.float32)
     width = spans_here * samples

time: 176 us -> 202 us (1.15)
  local copies, waits for them, and re-layouts: 41.6 us -> 73 us
  starting transfers between devices: 56.5 us -> 50.4 us
  other arithmetic: 22.9 us -> 25.6 us
  waiting for transfers between devices: 36.7 us -> 34.1 us
    unnamed x44 -> x24, local copies, waits for them, and re-layouts: 7.96 us -> 28.6 us
    ppermute x6, waiting for transfers between devices: 2.03 us -> 17.8 us  [wafer_columns(): lax.ppermute(piece, 'wafer', [(i, (i + shift) % size) for i in range(size)])]
    all_to_all x2 -> x1, waiting for transfers between devices: 14.9 us -> 0.01 us  [shards(): lax.all_to_all(packed, 'tm', split_axis=0, concat_axis=0, tiled=True)]
    all_to_all x2 -> x1, starting transfers between devices: 19.2 us -> 8.57 us  [shards(): lax.all_to_all(packed, 'tm', split_axis=0, concat_axis=0, tiled=True)]
    all_to_all x0 -> x2, other arithmetic: none -> 6.27 us  [shards(): lax.all_to_all(packed, 'tm', split_axis=0, concat_axis=0, tiled=True)]
    all_to_all x1, starting transfers between devices: 5.43 us -> 10.3 us  [shards(): lax.all_to_all(outgoing, 'tm', split_axis=0, concat_axis=0, tiled=True)]
    reshape x0 -> x1, local copies, waits for them, and re-layouts: none -> 4.19 us  [shards(): matrix = unpacked[:, :block_size].reshape(det_total, det_total)]
    ppermute x6, starting transfers between devices: 11.4 us -> 7.47 us  [wafer_columns(): lax.ppermute(piece, 'wafer', [(i, (i + shift) % size) for i in range(size)])]
  transfers between devices with their start and end apart: 15 -> 14, of which waited for: 8 -> 8; matrix products, arithmetic and copies ran while one was open for 34% -> 23% of each run, Pallas kernels for 0% -> 0%
where the time goes in v11:
time: 202 us; the launch traced here: 199 us
  local copies, waits for them, and re-layouts  73 us (36%)
  starting transfers between devices  50.4 us (25%)
  waiting for transfers between devices  34.1 us (17%)
  other arithmetic  25.6 us (13%)
  matrix products  15 us (7%)
    unnamed x24, local copies, waits for them, and re-layouts  28.6 us
    ppermute x6, waiting for transfers between devices, wafer_columns(): lax.ppermute(piece, 'wafer', [(i, (i + shift) % size) for i in range(size)])  17.8 us
    dynamic_update_slice x8, local copies, waits for them, and re-layouts, wafer_columns(): placed = lax.dynamic_update_slice_in_dim(placed, piece[None], source, 0)  14 us
    all_to_all x1, starting transfers between devices, shards(): lax.all_to_all(requests, 'tm', split_axis=0, concat_axis=0, tiled=True)  12 us
    all_to_all x1, waiting for transfers between devices, shards(): lax.all_to_all(outgoing, 'tm', split_axis=0, concat_axis=0, tiled=True)  11.2 us
    all_to_all x1, starting transfers between devices, shards(): lax.all_to_all(outgoing, 'tm', split_axis=0, concat_axis=0, tiled=True)  10.3 us
    all_to_all x1, starting transfers between devices, shards(): lax.all_to_all(packed, 'tm', split_axis=0, concat_axis=0, tiled=True)  8.57 us
    dot_general x1, matrix products, shards(): lax.dot_general(whitened, filter_blocks, (((1,), (1,)), ((), ())), prefer...  8.41 us
  transfers between devices with their start and end apart: 14, of which 8 were waited for; matrix products, arithmetic and copies ran while one was open for 23% of the time, Pallas kernels for 0%

profile of v11, /device:TPU:2, one launch (start us, length us, event | category | flops | bytes accessed | tf_op | source)
XLA Modules:
  0.0 199.0 jit_solution(16891072391636348385)
XLA Ops:
  0.6 0.9 reshape.448
  2.4 1.4 gather_fusion
  4.8 12.0 %all-to-all-start = ((s32[64,1,2]{2,1,0:T(1,128)}), s32[64,1,2]{2,1,0:T(1,128)S(1)}, u32[]{:S(2)}, u32[]{:S(2)}) async-start(s32[64,1,2]{2,1,0:T(1,128)} %bitcast.2), calls=%async_computation | async-start | bytes 65536 | tf_op jit(solution)/shard_map/all_to_all | solution.py:89
  16.9 1.7 collective-permute-start
  19.8 1.3 fusion.45
  21.2 2.4 %fusion.43 = (bf16[32,3,256]{2,1,0:T(4,128)(2,1)S(1)}, f32[32,3,256]{2,1,0:T(4,128)}) fusion(f32[32,3,256]{2,0,1:T(8,128)} %param.22, f32[]{:T(128)} %bitcast, f32[32,3,256]{2,0,1:T(8,128)} %param.21), kind=kLoop, calls=%fused_computation.127 | loop fusion | flops 73728 | bytes 344068 | tf_op jit(solution)/shard_map/convert_element_type | solution.py:71
  23.5 1.9 all-to-all-done
  26.2 1.5 gather_fusion.2
  27.7 1.0 maximum_select_fusion.1
  28.7 3.3 %collective-permute-start.1 = (bf16[7,8,1024]{2,1,0:T(8,128)(2,1)S(1)}, bf16[7,8,1024]{2,1,0:T(8,128)(2,1)}, u32[]{:S(2)}, u32[]{:S(2)}) collective-permute-start(bf16[7,8,1024]{2,1,0:T(8,128)(2,1)S(1)} %maximum_select_fusion.1), channel_id=1, source_target_pairs={{0,2},{1,3},{2,0},{3,1},{4,6},{5,7},{6,4},{7,5},{8,10},{9,11},{10,... | collective-permute-start | bytes 344072 | tf_op jit(solution)/shard_map/ppermute | solution.py:12
  31.9 1.2 broadcast_select_fusion.1
  33.1 0.9 select_n.406
  34.0 1.2 collective-permute-done.1
  35.3 1.0 maximum_select_fusion
  36.3 2.0 %gather_fusion.1 = bf16[64,16,1024]{2,1,0:T(8,128)(2,1)} fusion(bf16[7,16,1024]{2,1,0:T(8,128)(2,1)S(1)} %maximum_select_fusion, s32[1024]{0:T(1024)S(1)} %pad_clamp_fusion.2), kind=kCustom, calls=%fused_computation.1 | custom fusion | bytes 4194560 | tf_op jit(solution)/shard_map/jit(_take)/gather | solution.py:92
  38.3 2.8 %copy.98 = bf16[8,8,16,1024]{3,1,2,0:T(8,128)(2,1)S(1)} copy(bf16[8,8,16,1024]{3,2,1,0:T(8,128)(2,1)} %bitcast.113) | data formatting | bytes 4194304
  42.0 1.5 maximum_bitcast_fusion
  44.1 4.7 %reduce.16 = bf16[64,17920]{1,0:T(8,128)(2,1)} reduce(bf16[64,1,17920]{2,0,1:T(8,128)(2,1)} %maximum_bitcast_fusion, bf16[]{:T(256)} %broadcast.627), dimensions={1}, to_apply=%copy.84.reduce_sub_computation | reduce | bytes 4587522 | tf_op jit(solution)/shard_map/all_to_all | solution.py:95
  48.8 4.1 %reshape.518 = bf16[64,2,8960]{2,1,0:T(2,128)(2,1)} reshape(bf16[64,17920]{1,0:T(8,128)(2,1)} %reduce.16) | data formatting | bytes 4587520
  52.9 8.6 %all-to-all-start.1 = ((bf16[64,2,8960]{2,1,0:T(2,128)(2,1)}), bf16[64,2,8960]{2,1,0:T(2,128)(2,1)}, u32[]{:S(2)}, u32[]{:S(2)}) async-start(bf16[64,2,8960]{2,1,0:T(2,128)(2,1)} %reshape.518), calls=%async_computation.1 | async-start | bytes 4587520 | tf_op jit(solution)/shard_map/all_to_all | solution.py:95
  61.5 2.7 %constant_dynamic-slice_fusion.3 = (bf16[256,1024]{1,0:T(8,128)(2,1)}, bf16[256,1024]{1,0:T(8,128)(2,1)}, bf16[256,1024]{1,0:T(8,128)(2,1)}) fusion(bf16[256,4096]{1,0:T(8,128)(2,1)} %param.12, s32[]{:T(128)S(6)} %select_n.418, s32[]{:T(128)S(6)} %select_n.410, s32[]{:T(128)S(6)} %select_n.414), kind=kLoop, calls=%fused_computation.81 | loop fusion | bytes 3145740 | tf_op jit(solution)/shard_map/dynamic_slice | solution.py:26
  64.8 3.2 %collective-permute-start.3 = (bf16[256,1024]{1,0:T(8,128)(2,1)}, bf16[256,1024]{1,0:T(8,128)(2,1)}, u32[]{:S(2)}, u32[]{:S(2)}) collective-permute-start(bf16[256,1024]{1,0:T(8,128)(2,1)} %get-tuple-element.35), channel_id=1, source_target_pairs={{0,2},{1,3},{2,0},{3,1},{4,6},{5,7},{6,4},{7,5},{8,10},{9,11},{10,... | collective-permute-start | bytes 1572872 | tf_op jit(solution)/shard_map/ppermute | solution.py:27
  68.0 1.9 collective-permute-start.4
  69.8 1.2 constant_dynamic-slice_fusion
  71.2 1.3 collective-permute-start.6
  72.8 4.2 %compare_select_fusion.1 = bf16[4,256,4,256]{3,2,1,0:T(4,128)(2,1)} fusion(s32[4,256]{1,0:T(4,128)S(1)} %add_select_fusion.1, bf16[256,256]{1,0:T(8,128)(2,1)S(1)} %copy-done.4), kind=kLoop, calls=%fused_computation.10 | loop fusion | flops 2097152 | bytes 2232320 | tf_op jit(solution)/shard_map/jit(_where)/select_n | solution.py:113
  77.0 1.7 broadcast.583.clone.1
  78.7 1.9 bitcast_dynamic-update-slice_fusion.7
  80.6 1.6 broadcast.583.clone
  82.2 1.9 bitcast_dynamic-update-slice_fusion.3
  84.1 3.4 %copy.99 = bf16[128,8,4,256]{3,1,2,0:T(8,128)(2,1)} copy(bf16[128,8,4,256]{3,2,1,0:T(4,128)(2,1)} %bitcast.112) | data formatting | bytes 4194304
  88.1 1.9 copy.100
  90.0 1.4 collective-permute-done.2
  91.8 1.9 bitcast_dynamic-update-slice_fusion.6
  93.7 8.9 %collective-permute-done.5 = bf16[256,1024]{1,0:T(8,128)(2,1)} collective-permute-done((bf16[256,1024]{1,0:T(8,128)(2,1)}, bf16[256,1024]{1,0:T(8,128)(2,1)}, u32[]{:S(2)}, u32[]{:S(2)}) %collective-permute-start.5) | collective-permute-done | bytes 524320 | tf_op jit(solution)/shard_map/ppermute | solution.py:27
  102.7 1.9 bitcast_dynamic-update-slice_fusion.2
  104.5 1.9 bitcast_dynamic-update-slice_fusion.5
  106.5 7.5 %collective-permute-done.6 = bf16[256,1024]{1,0:T(8,128)(2,1)} collective-permute-done((bf16[256,1024]{1,0:T(8,128)(2,1)}, bf16[256,1024]{1,0:T(8,128)(2,1)}, u32[]{:S(2)}, u32[]{:S(2)}) %collective-permute-start.6) | collective-permute-done | bytes 524320 | tf_op jit(solution)/shard_map/ppermute | solution.py:27
  113.9 1.9 bitcast_dynamic-update-slice_fusion.1
  115.8 1.9 bitcast_dynamic-update-slice_fusion.4
  117.7 0.8 bitcast_dynamic-update-slice_fusion
  118.5 10.5 %reshape.519 = bf16[64,1,17920]{2,1,0:T(2,128)(2,1)} reshape(bf16[64,2,8960]{2,1,0:T(2,128)(2,1)} %all-to-all-done.1) | data formatting | bytes 4587520
  129.0 2.6 %copy.117 = bf16[64,1,17920]{2,0,1:T(8,128)(2,1)S(1)} copy(bf16[64,1,17920]{2,1,0:T(2,128)(2,1)} %reshape.519) | data formatting | bytes 4587520
  131.6 1.5 slice.54
  133.1 0.8 reshape_reshape.3
  133.9 1.6 gather_fusion.3
  135.5 0.9 convolution_bitcast_fusion
  136.4 4.2 %reshape.449 = bf16[1024,1024]{1,0:T(8,128)(2,1)} reshape(bf16[64,16384]{1,0:T(8,128)(2,1)} %slice.54) | data formatting | bytes 4194304 | tf_op jit(solution)/shard_map/reshape | solution.py:96
  140.6 3.2 %multiply_convert_fusion = bf16[4,256,1024]{2,1,0:T(8,128)(2,1)S(1)} fusion(bf16[4,256,1024]{2,1,0:T(8,128)(2,1)} %bitcast_dynamic-update-slice_fusion.4, f32[1024]{0:T(1024)S(1)} %bitcast.126, f32[4,256]{1,0:T(4,128)S(1)} %mul.166, f32[1024]{0:T(1024)S(1)} %bitcast.127, f32[4,256]{1,0:T(4,128)S(1)} %mul.161, f32[1024]{0:T(1024)S(1)} %bitcast.125, ...), kind=kLoop, calls=%fused_computation.8 | loop fusion | flops 10485760 | bytes 6316032 | tf_op jit(solution)/shard_map/convert_element_type | solution.py:110
  143.9 3.7 %fusion.46 = bf16[1024,1024]{1,0:T(8,128)(2,1)} fusion(bf16[1024,1024]{1,0:T(8,128)(2,1)S(1)} %bitcast.119, bf16[1024,1024]{1,0:T(8,128)(2,1)S(1)} %bitcast.118), kind=kOutput, calls=%fused_computation.131 | convolution fusion | flops 2147483648 | bytes 6291456 | tf_op jit(solution)/shard_map/dot_general | solution.py:114
  147.6 8.4 %multiply_reduce_fusion.2 = (bf16[1024]{0:T(1024)(128)(2,1)S(1)}, bf16[1024]{0:T(1024)(128)(2,1)S(1)}, bf16[1024]{0:T(1024)(128)(2,1)S(1)}) fusion(f32[1024]{0:T(1024)S(1)} %bitcast.130, f32[1024]{0:T(1024)S(1)} %bitcast.129, f32[1024]{0:T(1024)S(1)} %bitcast.128, bf16[4,256,1024]{2,1,0:T(8,128)(2,1)} %bitcast_dynamic-update-slice_fusion, ...), kind=kOutput, calls=%fused_computation.7 | convolution fusion | flops 4308595712 | bytes 8411136 | tf_op jit(solution)/shard_map/dot_general | solution.py:116
  157.0 1.0 copy.89
  158.1 10.3 %all-to-all-start.2 = ((f32[64,2,3,256]{3,1,2,0:T(2,128)}), f32[64,2,3,256]{3,1,2,0:T(2,128)S(1)}, u32[]{:S(2)}, u32[]{:S(2)}) async-start(f32[64,2,3,256]{3,1,2,0:T(2,128)} %copy.89), calls=%async_computation.2 | async-start | bytes 786432 | tf_op jit(solution)/shard_map/all_to_all | solution.py:128
  168.9 2.1 %reduce.15 = s32[64,2]{1,0:T(8,128)} reduce(s32[64,1,2]{2,1,0:T(1,128)} %copy-done.5, s32[]{:T(128)} %broadcast.626), dimensions={1}, to_apply=%all_to_all.22.reduce_sub_computation.3 | reduce | bytes 1028 | tf_op jit(solution)/shard_map/all_to_all | solution.py:89
  171.0 0.9 eq.167
  171.9 11.2 %all-to-all-done.2 = f32[64,2,3,256]{3,1,2,0:T(2,128)S(1)} async-done(((f32[64,2,3,256]{3,1,2,0:T(2,128)}), f32[64,2,3,256]{3,1,2,0:T(2,128)S(1)}, u32[]{:S(2)}, u32[]{:S(2)}) %all-to-all-start.2) | async-done | bytes 393248 | tf_op jit(solution)/shard_map/all_to_all | solution.py:128
  183.2 0.8 copy.102
  184.1 1.1 copy.91
  185.2 1.0 fusion.19
  186.2 2.6 %collective-permute-start.10 = (f32[32,3,256]{2,0,1:T(8,128)}, f32[32,3,256]{2,0,1:T(8,128)S(1)}, u32[]{:S(2)}, u32[]{:S(2)}) collective-permute-start(f32[32,3,256]{2,0,1:T(8,128)} %fusion.19), channel_id=1, source_target_pairs={{0,1},{1,2},{2,3},{3,0},{4,5},{5,6},{6,7},{7,4},{8,9},{9,10},{10,1... | collective-permute-start | bytes 294920 | tf_op jit(solution)/shard_map/ppermute | solution.py:41
  189.4 3.9 %collective-permute-start.9 = (f32[32,3,256]{2,0,1:T(8,128)}, f32[32,3,256]{2,0,1:T(8,128)S(1)}, u32[]{:S(2)}, u32[]{:S(2)}) collective-permute-start(f32[32,3,256]{2,0,1:T(8,128)} %fusion.19), channel_id=1, source_target_pairs={{0,2},{1,3},{2,0},{3,1},{4,6},{5,7},{6,4},{7,5},{8,10},{9,11},{10,... | collective-permute-start | bytes 294920 | tf_op jit(solution)/shard_map/ppermute | solution.py:41
  193.3 1.6 copy.92
  195.1 1.6 collective-permute-done.9
  196.7 2.2 %multiply_add_fusion = (f32[32,3,256]{2,0,1:T(8,128)}, f32[32,3,256]{2,0,1:T(8,128)}) fusion(f32[32,3,256]{2,0,1:T(8,128)} %param.22, f32[]{:T(128)} %bitcast.42, f32[32,3,256]{2,0,1:T(8,128)S(1)} %collective-permute-done.8, f32[32,3,256]{2,0,1:T(8,128)S(1)} %collective-permute-done.9, f32[32,3,256]{2,0,1:T(8,128)S(1)} %collective-permute-done.10, ...), kind=kLoop, calls=%fused_computation.35 | loop fusion | flops 442368 | bytes 688144 | tf_op jit(solution)/shard_map/add | solution.py:140
  (69 shorter events, 9.9 us)
Async XLA Ops:
  0.6 134.8 %copy-start = (bf16[4,6,256,256]{3,2,1,0:T(8,128)(2,1)S(1)}, bf16[4,6,256,256]{3,2,1,0:T(8,128)(2,1)}, u32[]{:S(2)}) copy-start(bf16[4,6,256,256]{3,2,1,0:T(8,128)(2,1)} %param.18) | copy-start | bytes 9437188
  4.8 20.6 %all-to-all-start = ((s32[64,1,2]{2,1,0:T(1,128)}), s32[64,1,2]{2,1,0:T(1,128)S(1)}, u32[]{:S(2)}, u32[]{:S(2)}) async-start(s32[64,1,2]{2,1,0:T(1,128)} %bitcast.2), calls=%async_computation | async-start | bytes 65536 | tf_op jit(solution)/shard_map/all_to_all | solution.py:89
  16.9 10.8 %collective-permute-start = (bf16[7,4,1024]{2,1,0:T(4,128)(2,1)}, bf16[7,4,1024]{2,1,0:T(4,128)(2,1)S(1)}, u32[]{:S(2)}, u32[]{:S(2)}) collective-permute-start(bf16[7,4,1024]{2,1,0:T(4,128)(2,1)} %param.16), channel_id=1, source_target_pairs={{0,1},{1,0},{2,3},{3,2},{4,5},{5,4},{6,7},{7,6},{8,9},{9,8},{10,11... | collective-permute-start | bytes 172040 | tf_op jit(solution)/shard_map/ppermute | solution.py:12
  25.4 0.6 copy-start.5
  28.7 6.6 %collective-permute-start.1 = (bf16[7,8,1024]{2,1,0:T(8,128)(2,1)S(1)}, bf16[7,8,1024]{2,1,0:T(8,128)(2,1)}, u32[]{:S(2)}, u32[]{:S(2)}) collective-permute-start(bf16[7,8,1024]{2,1,0:T(8,128)(2,1)S(1)} %maximum_select_fusion.1), channel_id=1, source_target_pairs={{0,2},{1,3},{2,0},{3,1},{4,6},{5,7},{6,4},{7,5},{8,10},{9,11},{10,... | collective-permute-start | bytes 344072 | tf_op jit(solution)/shard_map/ppermute | solution.py:12
  41.1 0.9 copy-start.3
  52.9 65.6 %all-to-all-start.1 = ((bf16[64,2,8960]{2,1,0:T(2,128)(2,1)}), bf16[64,2,8960]{2,1,0:T(2,128)(2,1)}, u32[]{:S(2)}, u32[]{:S(2)}) async-start(bf16[64,2,8960]{2,1,0:T(2,128)(2,1)} %reshape.518), calls=%async_computation.1 | async-start | bytes 4587520 | tf_op jit(solution)/shard_map/all_to_all | solution.py:95
  61.5 8.3 %copy-start.1 = (bf16[256,4096]{1,0:T(8,128)(2,1)S(1)}, bf16[256,4096]{1,0:T(8,128)(2,1)}, u32[]{:S(2)}) copy-start(bf16[256,4096]{1,0:T(8,128)(2,1)} %param.13) | copy-start | bytes 6291460
  64.2 8.5 %copy-start.6 = (s32[4,6]{1,0:T(4,128)S(1)}, s32[4,6]{1,0:T(4,128)}, u32[]{:S(2)}) copy-start(s32[4,6]{1,0:T(4,128)} %param.19) | copy-start | bytes 292
  64.2 8.5 %copy-start.7 = (f32[3,1024]{1,0:T(4,128)S(1)}, f32[3,1024]{1,0:T(4,128)}, u32[]{:S(2)}) copy-start(f32[3,1024]{1,0:T(4,128)} %param.14) | copy-start | bytes 36868
  64.2 8.6 %copy-start.4 = (bf16[256,256]{1,0:T(8,128)(2,1)S(1)}, bf16[256,256]{1,0:T(8,128)(2,1)}, u32[]{:S(2)}) copy-start(bf16[256,256]{1,0:T(8,128)(2,1)} %param.15) | copy-start | bytes 393220
  64.2 27.2 %collective-permute-start.2 = (bf16[256,1024]{1,0:T(8,128)(2,1)}, bf16[256,1024]{1,0:T(8,128)(2,1)}, u32[]{:S(2)}, u32[]{:S(2)}) collective-permute-start(bf16[256,1024]{1,0:T(8,128)(2,1)} %get-tuple-element.34), channel_id=1, source_target_pairs={{0,1},{1,2},{2,3},{3,0},{4,5},{5,6},{6,7},{7,4},{8,9},{9,10},{10,1... | collective-permute-start | bytes 1572872 | tf_op jit(solution)/shard_map/ppermute | solution.py:27
  64.8 39.8 %collective-permute-start.3 = (bf16[256,1024]{1,0:T(8,128)(2,1)}, bf16[256,1024]{1,0:T(8,128)(2,1)}, u32[]{:S(2)}, u32[]{:S(2)}) collective-permute-start(bf16[256,1024]{1,0:T(8,128)(2,1)} %get-tuple-element.35), channel_id=1, source_target_pairs={{0,2},{1,3},{2,0},{3,1},{4,6},{5,7},{6,4},{7,5},{8,10},{9,11},{10,... | collective-permute-start | bytes 1572872 | tf_op jit(solution)/shard_map/ppermute | solution.py:27
  68.0 47.9 %collective-permute-start.4 = (bf16[256,1024]{1,0:T(8,128)(2,1)}, bf16[256,1024]{1,0:T(8,128)(2,1)}, u32[]{:S(2)}, u32[]{:S(2)}) collective-permute-start(bf16[256,1024]{1,0:T(8,128)(2,1)} %get-tuple-element.33), channel_id=1, source_target_pairs={{0,3},{1,0},{2,1},{3,2},{4,7},{5,4},{6,5},{7,6},{8,11},{9,8},{10,9... | collective-permute-start | bytes 1572872 | tf_op jit(solution)/shard_map/ppermute | solution.py:27
  71.0 31.6 %collective-permute-start.5 = (bf16[256,1024]{1,0:T(8,128)(2,1)}, bf16[256,1024]{1,0:T(8,128)(2,1)}, u32[]{:S(2)}, u32[]{:S(2)}) collective-permute-start(bf16[256,1024]{1,0:T(8,128)(2,1)} %get-tuple-element.31), channel_id=1, source_target_pairs={{0,1},{1,2},{2,3},{3,0},{4,5},{5,6},{6,7},{7,4},{8,9},{9,10},{10,1... | collective-permute-start | bytes 1572872 | tf_op jit(solution)/shard_map/ppermute | solution.py:27
  71.2 42.8 %collective-permute-start.6 = (bf16[256,1024]{1,0:T(8,128)(2,1)}, bf16[256,1024]{1,0:T(8,128)(2,1)}, u32[]{:S(2)}, u32[]{:S(2)}) collective-permute-start(bf16[256,1024]{1,0:T(8,128)(2,1)} %get-tuple-element.32), channel_id=1, source_target_pairs={{0,2},{1,3},{2,0},{3,1},{4,6},{5,7},{6,4},{7,5},{8,10},{9,11},{10,... | collective-permute-start | bytes 1572872 | tf_op jit(solution)/shard_map/ppermute | solution.py:27
  91.4 26.3 %collective-permute-start.7 = (bf16[256,1024]{1,0:T(8,128)(2,1)}, bf16[256,1024]{1,0:T(8,128)(2,1)S(1)}, u32[]{:S(2)}, u32[]{:S(2)}) collective-permute-start(bf16[256,1024]{1,0:T(8,128)(2,1)} %get-tuple-element.30), channel_id=1, source_target_pairs={{0,3},{1,0},{2,1},{3,2},{4,7},{5,4},{6,5},{7,6},{8,11},{9,8},{10,9... | collective-permute-start | bytes 1572872 | tf_op jit(solution)/shard_map/ppermute | solution.py:27
  140.6 3.2 %copy-start.2 = (bf16[128,8,4,256]{3,1,2,0:T(8,128)(2,1)S(1)}, bf16[128,8,4,256]{3,1,2,0:T(8,128)(2,1)}, u32[]{:S(2)}) copy-start(bf16[128,8,4,256]{3,1,2,0:T(8,128)(2,1)} %copy.99) | copy-start | bytes 6291460
  158.1 25.0 %all-to-all-start.2 = ((f32[64,2,3,256]{3,1,2,0:T(2,128)}), f32[64,2,3,256]{3,1,2,0:T(2,128)S(1)}, u32[]{:S(2)}, u32[]{:S(2)}) async-start(f32[64,2,3,256]{3,1,2,0:T(2,128)} %copy.89), calls=%async_computation.2 | async-start | bytes 786432 | tf_op jit(solution)/shard_map/all_to_all | solution.py:128
  186.2 8.7 %collective-permute-start.10 = (f32[32,3,256]{2,0,1:T(8,128)}, f32[32,3,256]{2,0,1:T(8,128)S(1)}, u32[]{:S(2)}, u32[]{:S(2)}) collective-permute-start(f32[32,3,256]{2,0,1:T(8,128)} %fusion.19), channel_id=1, source_target_pairs={{0,1},{1,2},{2,3},{3,0},{4,5},{5,6},{6,7},{7,4},{8,9},{9,10},{10,1... | collective-permute-start | bytes 294920 | tf_op jit(solution)/shard_map/ppermute | solution.py:41
  188.8 6.4 %collective-permute-start.8 = (f32[32,3,256]{2,0,1:T(8,128)}, f32[32,3,256]{2,0,1:T(8,128)S(1)}, u32[]{:S(2)}, u32[]{:S(2)}) collective-permute-start(f32[32,3,256]{2,0,1:T(8,128)} %fusion.19), channel_id=1, source_target_pairs={{0,3},{1,0},{2,1},{3,2},{4,7},{5,4},{6,5},{7,6},{8,11},{9,8},{10,9... | collective-permute-start | bytes 294920 | tf_op jit(solution)/shard_map/ppermute | solution.py:41
  189.4 7.3 %collective-permute-start.9 = (f32[32,3,256]{2,0,1:T(8,128)}, f32[32,3,256]{2,0,1:T(8,128)S(1)}, u32[]{:S(2)}, u32[]{:S(2)}) collective-permute-start(f32[32,3,256]{2,0,1:T(8,128)} %fusion.19), channel_id=1, source_target_pairs={{0,2},{1,3},{2,0},{3,1},{4,6},{5,7},{6,4},{7,5},{8,10},{9,11},{10,... | collective-permute-start | bytes 294920 | tf_op jit(solution)/shard_map/ppermute | solution.py:41

commit v12 on v6

--- a/solution.py
+++ b/solution.py
@@ -48,16 +48,22 @@
     direct = direct.reshape(det_total, det_total)
     group_of = jnp.arange(det_total, dtype=jnp.int32) // lanes
     use_direct = (group_of[None, :] - group_of[:, None]) % groups < sent_groups
-    return jnp.where(use_direct, direct, direct.T)
+    return lax.optimization_barrier(jnp.where(use_direct, direct, direct.T))
 
 
 def wafer_sum(x):
+    spot = lax.axis_index("wafer")
     size = lax.axis_size("wafer")
-    bit = 1
-    while bit < size:
-        x = x + lax.ppermute(x, "wafer", [(i, i ^ bit) for i in range(size)])
-        bit *= 2
-    return x
+    terms = [x]
+    for shift in range(1, size):
+        terms.append(lax.ppermute(x, "wafer", [(i, (i + shift) % size) for i in range(size)]))
+    total = None
+    for source in range(size):
+        term = terms[0]
+        for shift in range(1, size):
+            term = jnp.where((spot - source) % size == shift, terms[shift], term)
+        total = term if total is None else total + term
+    return total
 
 
 def shards(

time: 183 us -> 184 us (level)
  other arithmetic: 25.4 us -> 29.7 us
  local copies, waits for them, and re-layouts: 55.2 us -> 51.3 us
  matrix products: 18.5 us -> 14.9 us
  starting transfers between devices: 52.2 us -> 54.3 us
    dot_general x1, matrix products: 10.5 us -> 3.66 us  [shards(): jnp.dot(errors, filter_blocks, preferred_element_type=jnp.float32)]
    select_n x0 -> x1, other arithmetic: none -> 5.15 us  [symmetric_gather(): return lax.optimization_barrier(jnp.where(use_direct, direct, direct.T))]
    ppermute x2 -> x3, waiting for transfers between devices: 7.5 us -> 3.62 us  [wafer_sum(): lax.ppermute(x, 'wafer', [(i, (i + shift) % size) for i in range(size)])]
    dynamic_update_slice x8, local copies, waits for them, and re-layouts: 14.2 us -> 10.9 us  [wafer_columns(): placed = lax.dynamic_update_slice_in_dim(placed, piece[None], source, 0)]
    all_to_all x1, waiting for transfers between devices: 6.01 us -> 8.72 us  [symmetric_gather(): got = lax.all_to_all(sent, 'tm', split_axis=0, concat_axis=0, tiled=True)]
    dot_general x1, matrix products: 5.8 us -> 8.42 us  [shards(): lax.dot_general(whitened, filter_blocks, (((1,), (1,)), ((), ())), prefer...]
    ppermute x2 -> x3, starting transfers between devices: 2.1 us -> 4.59 us  [wafer_sum(): lax.ppermute(x, 'wafer', [(i, (i + shift) % size) for i in range(size)])]
    ppermute x2, starting transfers between devices: 0.96 us -> 2.98 us  [wafer_gather(): other = lax.ppermute(x, 'wafer', [(i, i ^ bit) for i in range(size)])]
  transfers between devices with their start and end apart: 14 -> 15, of which waited for: 6 -> 7; matrix products, arithmetic and copies ran while one was open for 32% -> 33% of each run, Pallas kernels for 0% -> 0%
where the time goes in v12:
time: 184 us; the launch traced here: 182 us
  starting transfers between devices  54.3 us (30%)
  local copies, waits for them, and re-layouts  51.3 us (28%)
  waiting for transfers between devices  30.8 us (17%)
  other arithmetic  29.7 us (16%)
  matrix products  14.9 us (8%)
    all_to_all x1, starting transfers between devices, shards(): lax.all_to_all(requests, 'tm', split_axis=0, concat_axis=0, tiled=True)  12 us
    ppermute x6, starting transfers between devices, wafer_columns(): lax.ppermute(piece, 'wafer', [(i, (i + shift) % size) for i in range(size)])  11.2 us
    all_to_all x1, waiting for transfers between devices, shards(): lax.all_to_all(outgoing, 'tm', split_axis=0, concat_axis=0, tiled=True)  11.2 us
    dynamic_update_slice x8, local copies, waits for them, and re-layouts, wafer_columns(): placed = lax.dynamic_update_slice_in_dim(placed, piece[None], source, 0)  10.9 us
    all_to_all x1, starting transfers between devices, shards(): lax.all_to_all(served, 'tm', split_axis=0, concat_axis=0, tiled=True)  10.3 us
    unnamed x59, local copies, waits for them, and re-layouts  10.1 us
    all_to_all x1, waiting for transfers between devices, symmetric_gather(): got = lax.all_to_all(sent, 'tm', split_axis=0, concat_axis=0, tiled=True)  8.72 us
    dot_general x1, matrix products, shards(): lax.dot_general(whitened, filter_blocks, (((1,), (1,)), ((), ())), prefer...  8.42 us
  transfers between devices with their start and end apart: 15, of which 7 were waited for; matrix products, arithmetic and copies ran while one was open for 33% of the time, Pallas kernels for 0%

profile of v12, /device:TPU:2, one launch (start us, length us, event | category | flops | bytes accessed | tf_op | source)
XLA Modules:
  0.0 182.1 jit_solution(11560072857887927959)
XLA Ops:
  0.6 1.7 collective-permute-start
  2.3 2.7 %constant_dynamic-slice_fusion.3 = (bf16[256,1024]{1,0:T(8,128)(2,1)}, bf16[256,1024]{1,0:T(8,128)(2,1)}, bf16[256,1024]{1,0:T(8,128)(2,1)}) fusion(bf16[256,4096]{1,0:T(8,128)(2,1)} %param.12, s32[]{:T(128)S(6)} %select_n.452, s32[]{:T(128)S(6)} %select_n.444, s32[]{:T(128)S(6)} %select_n.448), kind=kLoop, calls=%fused_computation.115 | loop fusion | bytes 3145740 | tf_op jit(solution)/shard_map/dynamic_slice | solution.py:26
  5.1 0.6 collective-permute-start.2
  5.7 3.1 %collective-permute-start.3 = (bf16[256,1024]{1,0:T(8,128)(2,1)}, bf16[256,1024]{1,0:T(8,128)(2,1)}, u32[]{:S(2)}, u32[]{:S(2)}) collective-permute-start(bf16[256,1024]{1,0:T(8,128)(2,1)} %get-tuple-element.32), channel_id=1, source_target_pairs={{0,2},{1,3},{2,0},{3,1},{4,6},{5,7},{6,4},{7,5},{8,10},{9,11},{10,... | collective-permute-start | bytes 1572872 | tf_op jit(solution)/shard_map/ppermute | solution.py:27
  8.8 1.9 %collective-permute-start.4 = (bf16[256,1024]{1,0:T(8,128)(2,1)}, bf16[256,1024]{1,0:T(8,128)(2,1)}, u32[]{:S(2)}, u32[]{:S(2)}) collective-permute-start(bf16[256,1024]{1,0:T(8,128)(2,1)} %get-tuple-element.30), channel_id=1, source_target_pairs={{0,3},{1,0},{2,1},{3,2},{4,7},{5,4},{6,5},{7,6},{8,11},{9,8},{10,9... | collective-permute-start | bytes 1572872 | tf_op jit(solution)/shard_map/ppermute | solution.py:27
  10.7 1.2 constant_dynamic-slice_fusion
  12.2 0.7 gather_fusion
  13.2 0.8 all_to_all.19
  13.9 12.0 %all-to-all-start = ((s32[64,1,2]{2,1,0:T(1,128)}), s32[64,1,2]{2,1,0:T(1,128)S(1)}, u32[]{:S(2)}, u32[]{:S(2)}) async-start(s32[64,1,2]{2,1,0:T(1,128)} %bitcast.2), calls=%async_computation | async-start | bytes 65536 | tf_op jit(solution)/shard_map/all_to_all | solution.py:107
  28.9 1.1 bitcast_dynamic-update-slice_fusion.7
  30.0 1.8 %broadcast.640.clone = bf16[4,256,1024]{2,1,0:T(8,128)(2,1)} broadcast(bf16[]{:T(256)} %constant.263.clone.1), dimensions={} | broadcast | bytes 2097154 | tf_op jit(solution)/shard_map/broadcast.28
  31.8 1.9 %bitcast_dynamic-update-slice_fusion.3 = bf16[4,256,1024]{2,1,0:T(8,128)(2,1)} fusion(bf16[4,256,1024]{2,1,0:T(8,128)(2,1)} %broadcast.640.clone, s32[]{:T(128)S(6)} %select_n.442, bf16[256,4096]{1,0:T(8,128)(2,1)} %param.13, s32[]{:T(128)S(6)} %select_n.441), kind=kLoop, calls=%fused_computation.32 | loop fusion | bytes 1048584 | tf_op jit(solution)/shard_map/dynamic_update_slice | solution.py:32
  33.8 0.7 fusion.67
  34.4 0.6 pad_clamp_fusion
  35.0 0.6 slice_reduce_fusion.2
  36.2 4.2 %compare_select_fusion.1 = bf16[4,256,4,256]{3,2,1,0:T(4,128)(2,1)} fusion(s32[4,256]{1,0:T(4,128)S(1)} %add_select_fusion.2, bf16[256,256]{1,0:T(8,128)(2,1)S(1)} %copy-done.8), kind=kLoop, calls=%fused_computation.18 | loop fusion | flops 2097152 | bytes 2232320 | tf_op jit(solution)/shard_map/jit(_where)/select_n | solution.py:130
  40.4 1.4 fusion.64
  42.4 3.4 %copy.92 = bf16[128,8,4,256]{3,1,2,0:T(8,128)(2,1)} copy(bf16[128,8,4,256]{3,2,1,0:T(4,128)(2,1)} %bitcast.160) | data formatting | bytes 4194304
  46.4 1.8 %copy.93 = bf16[128,8,4,256]{3,1,2,0:T(8,128)(2,1)} copy(bf16[128,8,4,256]{3,2,1,0:T(4,128)(2,1)S(1)} %bitcast.161) | data formatting | bytes 4194304
  48.9 0.8 gather_fusion.2
  49.7 1.7 maximum_select_fusion.1
  51.4 1.3 collective-permute-start.1
  52.7 1.0 broadcast_select_fusion.1
  53.7 10.3 %all-to-all-start.2 = ((bf16[64,2,3,256]{3,1,2,0:T(2,128)(2,1)}), bf16[64,2,3,256]{3,1,2,0:T(2,128)(2,1)S(1)}, u32[]{:S(2)}, u32[]{:S(2)}) async-start(bf16[64,2,3,256]{3,1,2,0:T(2,128)(2,1)} %broadcast_select_fusion.1), calls=%async_computation.2 | async-start | bytes 393216 | tf_op jit(solution)/shard_map/all_to_all | solution.py:110
  64.0 2.3 %collective-permute-start.6 = (bf16[256,1024]{1,0:T(8,128)(2,1)}, bf16[256,1024]{1,0:T(8,128)(2,1)}, u32[]{:S(2)}, u32[]{:S(2)}) collective-permute-start(bf16[256,1024]{1,0:T(8,128)(2,1)} %get-tuple-element.29), channel_id=1, source_target_pairs={{0,2},{1,3},{2,0},{3,1},{4,6},{5,7},{6,4},{7,5},{8,10},{9,11},{10,... | collective-permute-start | bytes 1572872 | tf_op jit(solution)/shard_map/ppermute | solution.py:27
  66.3 1.1 maximum_select_fusion
  67.5 1.9 %gather_fusion.1 = bf16[64,16,640]{2,1,0:T(8,128)(2,1)} fusion(bf16[7,16,640]{2,1,0:T(8,128)(2,1)S(1)} %fusion.29, s32[1024]{0:T(1024)} %pad_clamp_fusion.2), kind=kCustom, calls=%fused_computation.1 | custom fusion | bytes 2621696 | tf_op jit(solution)/shard_map/jit(_take)/gather | solution.py:43
  69.4 2.6 %broadcast_select_fusion = bf16[64,16,640]{2,1,0:T(8,128)(2,1)} fusion(bf16[64,16,640]{2,1,0:T(8,128)(2,1)} %gather_fusion.1, pred[64]{0:T(512)(128)(4,1)S(1)} %copy-done.25), kind=kLoop, calls=%fused_computation.26 | loop fusion | flops 655360 | bytes 2621504 | tf_op jit(solution)/shard_map/jit(_take)/select_n | solution.py:43
  72.0 2.8 %all-to-all-done.2 = bf16[64,2,3,256]{3,1,2,0:T(2,128)(2,1)S(1)} async-done(((bf16[64,2,3,256]{3,1,2,0:T(2,128)(2,1)}), bf16[64,2,3,256]{3,1,2,0:T(2,128)(2,1)S(1)}, u32[]{:S(2)}, u32[]{:S(2)}) %all-to-all-start.2) | async-done | bytes 196640 | tf_op jit(solution)/shard_map/all_to_all | solution.py:110
  74.8 7.7 %all-to-all-start.1 = ((bf16[64,16,640]{2,1,0:T(8,128)(2,1)}), bf16[64,16,640]{2,1,0:T(8,128)(2,1)}, u32[]{:S(2)}, u32[]{:S(2)}) async-start(bf16[64,16,640]{2,1,0:T(8,128)(2,1)} %broadcast_select_fusion), calls=%async_computation.1 | async-start | bytes 2621440 | tf_op jit(solution)/shard_map/all_to_all | solution.py:44
  82.5 0.8 copy.78
  83.3 1.7 gather_fusion.3
  85.0 0.9 convolution_bitcast_fusion
  86.0 3.2 %collective-permute-start.7 = (bf16[256,1024]{1,0:T(8,128)(2,1)S(1)}, bf16[256,1024]{1,0:T(8,128)(2,1)S(1)}, u32[]{:S(2)}, u32[]{:S(2)}) collective-permute-start(bf16[256,1024]{1,0:T(8,128)(2,1)S(1)} %copy-done.7), channel_id=1, source_target_pairs={{0,3},{1,0},{2,1},{3,2},{4,7},{5,4},{6,5},{7,6},{8,11},{9,8},{10,9... | collective-permute-start | bytes 1572872 | tf_op jit(solution)/shard_map/ppermute | solution.py:27
  89.2 1.1 bitcast_dynamic-update-slice_fusion.6
  90.3 1.9 %bitcast_dynamic-update-slice_fusion.2 = bf16[4,256,1024]{2,1,0:T(8,128)(2,1)} fusion(bf16[4,256,1024]{2,1,0:T(8,128)(2,1)} %bitcast_dynamic-update-slice_fusion.3, s32[]{:T(128)S(6)} %select_n.446, bf16[256,1024]{1,0:T(8,128)(2,1)} %collective-permute-done.5), kind=kLoop, calls=%fused_computation.31 | loop fusion | bytes 1048580 | tf_op jit(solution)/shard_map/dynamic_update_slice | solution.py:32
  92.2 1.1 bitcast_dynamic-update-slice_fusion.5
  93.3 1.9 %bitcast_dynamic-update-slice_fusion.1 = bf16[4,256,1024]{2,1,0:T(8,128)(2,1)} fusion(bf16[4,256,1024]{2,1,0:T(8,128)(2,1)} %bitcast_dynamic-update-slice_fusion.2, s32[]{:T(128)S(6)} %select_n.450, bf16[256,1024]{1,0:T(8,128)(2,1)} %collective-permute-done.6), kind=kLoop, calls=%fused_computation.30 | loop fusion | bytes 1048580 | tf_op jit(solution)/shard_map/dynamic_update_slice | solution.py:32
  95.2 1.1 bitcast_dynamic-update-slice_fusion.4
  96.3 4.4 %collective-permute-done.7 = bf16[256,1024]{1,0:T(8,128)(2,1)S(1)} collective-permute-done((bf16[256,1024]{1,0:T(8,128)(2,1)S(1)}, bf16[256,1024]{1,0:T(8,128)(2,1)S(1)}, u32[]{:S(2)}, u32[]{:S(2)}) %collective-permute-start.7) | collective-permute-done | bytes 524320 | tf_op jit(solution)/shard_map/ppermute | solution.py:27
  100.6 0.8 bitcast_dynamic-update-slice_fusion
  101.5 2.9 %multiply_convert_fusion = bf16[4,256,1024]{2,1,0:T(8,128)(2,1)S(1)} fusion(bf16[4,256,1024]{2,1,0:T(8,128)(2,1)S(1)} %bitcast_dynamic-update-slice_fusion.4, f32[1024]{0:T(1024)S(1)} %bitcast.177, f32[4,256]{1,0:T(4,128)S(1)} %copy-done.14, f32[1024]{0:T(1024)S(1)} %bitcast.178, f32[4,256]{1,0:T(4,128)S(1)} %mul.165, f32[1024]{0:T(1024)S(1)} %bitcast.176, ...), kind=kLoop, calls=%fused_computation.15 | loop fusion | flops 10485760 | bytes 6316032 | tf_op jit(solution)/shard_map/convert_element_type | solution.py:127
  104.4 3.7 %fusion.68 = bf16[1024,1024]{1,0:T(8,128)(2,1)} fusion(bf16[1024,1024]{1,0:T(8,128)(2,1)S(1)} %bitcast.166, bf16[1024,1024]{1,0:T(8,128)(2,1)S(1)} %bitcast.165), kind=kOutput, calls=%fused_computation.177 | convolution fusion | flops 2147483648 | bytes 6291456 | tf_op jit(solution)/shard_map/dot_general | solution.py:131
  108.1 8.7 %all-to-all-done.1 = bf16[64,16,640]{2,1,0:T(8,128)(2,1)} async-done(((bf16[64,16,640]{2,1,0:T(8,128)(2,1)}), bf16[64,16,640]{2,1,0:T(8,128)(2,1)}, u32[]{:S(2)}, u32[]{:S(2)}) %all-to-all-start.1) | async-done | bytes 1310752 | tf_op jit(solution)/shard_map/all_to_all | solution.py:44
  116.8 4.1 %reshape.470 = bf16[8,128,5,128]{3,2,1,0:T(8,128)(2,1)} reshape(bf16[64,16,640]{2,1,0:T(8,128)(2,1)} %all-to-all-done.1) | data formatting | bytes 2621440 | tf_op jit(solution)/shard_map/reshape | solution.py:45
  120.9 2.0 %fusion.21 = (bf16[128,8,128]{2,1,0:T(8,128)(2,1)S(1)}, bf16[128,8,128]{2,1,0:T(8,128)(2,1)S(1)}, bf16[128,8,128]{2,1,0:T(8,128)(2,1)S(1)}, bf16[128,8,128]{2,1,...) fusion(bf16[8,128,5,128]{3,2,1,0:T(8,128)(2,1)} %reshape.470), kind=kLoop, calls=%fused_computation.55 | loop fusion | bytes 3407872 | tf_op jit(solution)/shard_map/squeeze | solution.py:47
  124.8 2.1 %copy.113 = bf16[128,8,8,128]{3,1,2,0:T(8,128)(2,1)} copy(bf16[128,8,8,128]{3,2,1,0:T(8,128)(2,1)S(1)} %bitcast.158) | data formatting | bytes 4194304
  126.8 4.0 %copy.72 = bf16[1024,1024]{0,1:T(8,128)(2,1)} copy(bf16[1024,1024]{1,0:T(8,128)(2,1)} %bitcast.162) | data formatting | bytes 4194304 | tf_op jit(solution)/shard_map/reshape | solution.py:48
  130.8 5.1 %fusion.2 = bf16[1024,1024]{1,0:T(8,128)(2,1)} fusion(bf16[1024,1024]{0,1:T(8,128)(2,1)} %copy.72, s32[1024]{0:T(1024)S(1)} %add_select_fusion.3, bf16[128,8,8,128]{3,2,1,0:T(8,128)(2,1)} %bitcast.159), kind=kLoop, calls=%fused_computation.16 | loop fusion | flops 14680064 | bytes 6295552 | tf_op jit(solution)/shard_map/jit(_where)/select_n | solution.py:51
  136.0 8.4 %multiply_reduce_fusion.2 = (bf16[1024]{0:T(1024)(128)(2,1)S(1)}, bf16[1024]{0:T(1024)(128)(2,1)S(1)}, bf16[1024]{0:T(1024)(128)(2,1)S(1)}) fusion(f32[1024]{0:T(1024)S(1)} %bitcast.181, f32[1024]{0:T(1024)S(1)} %bitcast.180, f32[1024]{0:T(1024)S(1)} %bitcast.179, bf16[4,256,1024]{2,1,0:T(8,128)(2,1)} %bitcast_dynamic-update-slice_fusion, ...), kind=kOutput, calls=%fused_computation.14 | convolution fusion | flops 4308595712 | bytes 8411136 | tf_op jit(solution)/shard_map/dot_general | solution.py:133
  145.5 1.1 copy.83
  146.6 5.6 %all-to-all-start.3 = ((f32[64,2,3,256]{3,1,2,0:T(2,128)}), f32[64,2,3,256]{3,1,2,0:T(2,128)S(1)}, u32[]{:S(2)}, u32[]{:S(2)}) async-start(f32[64,2,3,256]{3,1,2,0:T(2,128)} %copy.83), calls=%async_computation.3 | async-start | bytes 786432 | tf_op jit(solution)/shard_map/all_to_all | solution.py:145
  152.7 2.1 %reduce.15 = s32[64,2]{1,0:T(8,128)} reduce(s32[64,1,2]{2,1,0:T(1,128)} %copy-done.10, s32[]{:T(128)} %broadcast.684), dimensions={1}, to_apply=%all_to_all.20.reduce_sub_computation.3 | reduce | bytes 1028 | tf_op jit(solution)/shard_map/all_to_all | solution.py:107
  154.8 0.9 eq.172
  155.7 11.2 %all-to-all-done.3 = f32[64,2,3,256]{3,1,2,0:T(2,128)S(1)} async-done(((f32[64,2,3,256]{3,1,2,0:T(2,128)}), f32[64,2,3,256]{3,1,2,0:T(2,128)S(1)}, u32[]{:S(2)}, u32[]{:S(2)}) %all-to-all-start.3) | async-done | bytes 393248 | tf_op jit(solution)/shard_map/all_to_all | solution.py:145
  167.0 0.8 copy.95
  167.9 1.1 copy.85
  169.0 1.0 fusion.38
  170.0 1.8 collective-permute-start.10
  171.7 1.5 collective-permute-start.8
  173.2 1.4 collective-permute-start.9
  174.6 1.6 copy.86
  176.7 3.0 %collective-permute-done.9 = f32[32,3,256]{2,0,1:T(8,128)S(1)} collective-permute-done((f32[32,3,256]{2,0,1:T(8,128)}, f32[32,3,256]{2,0,1:T(8,128)S(1)}, u32[]{:S(2)}, u32[]{:S(2)}) %collective-permute-start.9) | collective-permute-done | bytes 98336 | tf_op jit(solution)/shard_map/ppermute | solution.py:59
  179.8 2.4 %multiply_add_fusion = (f32[32,3,256]{2,0,1:T(8,128)}, f32[32,3,256]{2,0,1:T(8,128)}) fusion(f32[32,3,256]{2,0,1:T(8,128)} %param.22, f32[]{:T(128)} %bitcast.57, f32[32,3,256]{2,0,1:T(8,128)S(1)} %collective-permute-done.8, f32[32,3,256]{2,0,1:T(8,128)S(1)} %collective-permute-done.9, f32[32,3,256]{2,0,1:T(8,128)S(1)} %collective-permute-done.10, ...), kind=kLoop, calls=%fused_computation.75 | loop fusion | flops 442368 | bytes 688144 | tf_op jit(solution)/shard_map/add | solution.py:157
  (122 shorter events, 10.2 us)
Async XLA Ops:
  0.6 84.3 %copy-start = (bf16[4,6,256,256]{3,2,1,0:T(8,128)(2,1)S(1)}, bf16[4,6,256,256]{3,2,1,0:T(8,128)(2,1)}, u32[]{:S(2)}) copy-start(bf16[4,6,256,256]{3,2,1,0:T(8,128)(2,1)} %param.18) | copy-start | bytes 9437188
  0.6 49.0 %collective-permute-start = (bf16[7,4,1024]{2,1,0:T(4,128)(2,1)}, bf16[7,4,1024]{2,1,0:T(4,128)(2,1)}, u32[]{:S(2)}, u32[]{:S(2)}) collective-permute-start(bf16[7,4,1024]{2,1,0:T(4,128)(2,1)} %param.16), channel_id=1, source_target_pairs={{0,1},{1,0},{2,3},{3,2},{4,5},{5,4},{6,7},{7,6},{8,9},{9,8},{10,11... | collective-permute-start | bytes 172040 | tf_op jit(solution)/shard_map/ppermute | solution.py:12
  2.3 8.4 %copy-start.5 = (bf16[256,4096]{1,0:T(8,128)(2,1)S(1)}, bf16[256,4096]{1,0:T(8,128)(2,1)}, u32[]{:S(2)}) copy-start(bf16[256,4096]{1,0:T(8,128)(2,1)} %param.13) | copy-start | bytes 6291460
  5.0 6.9 %copy-start.13 = (s32[4,6]{1,0:T(4,128)S(1)}, s32[4,6]{1,0:T(4,128)}, u32[]{:S(2)}) copy-start(s32[4,6]{1,0:T(4,128)} %param.19) | copy-start | bytes 292
  5.0 7.1 %copy-start.1 = (s32[2048]{0:T(1024)S(1)}, s32[2048]{0:T(1024)}, u32[]{:S(2)}) copy-start(s32[2048]{0:T(1024)} %param.20) | copy-start | bytes 24580
  5.1 20.9 %copy-start.26 = (s32[64]{0:T(128)S(1)}, s32[64]{0:T(128)}, u32[]{:S(2)}) copy-start(s32[64]{0:T(128)} %param.17) | copy-start | bytes 772
  5.1 80.9 %collective-permute-start.2 = (bf16[256,1024]{1,0:T(8,128)(2,1)}, bf16[256,1024]{1,0:T(8,128)(2,1)}, u32[]{:S(2)}, u32[]{:S(2)}) collective-permute-start(bf16[256,1024]{1,0:T(8,128)(2,1)} %get-tuple-element.31), channel_id=1, source_target_pairs={{0,1},{1,2},{2,3},{3,0},{4,5},{5,6},{6,7},{7,4},{8,9},{9,10},{10,1... | collective-permute-start | bytes 1572872 | tf_op jit(solution)/shard_map/ppermute | solution.py:27
  5.7 86.5 %collective-permute-start.3 = (bf16[256,1024]{1,0:T(8,128)(2,1)}, bf16[256,1024]{1,0:T(8,128)(2,1)}, u32[]{:S(2)}, u32[]{:S(2)}) collective-permute-start(bf16[256,1024]{1,0:T(8,128)(2,1)} %get-tuple-element.32), channel_id=1, source_target_pairs={{0,2},{1,3},{2,0},{3,1},{4,6},{5,7},{6,4},{7,5},{8,10},{9,11},{10,... | collective-permute-start | bytes 1572872 | tf_op jit(solution)/shard_map/ppermute | solution.py:27
  8.8 86.4 %collective-permute-start.4 = (bf16[256,1024]{1,0:T(8,128)(2,1)}, bf16[256,1024]{1,0:T(8,128)(2,1)}, u32[]{:S(2)}, u32[]{:S(2)}) collective-permute-start(bf16[256,1024]{1,0:T(8,128)(2,1)} %get-tuple-element.30), channel_id=1, source_target_pairs={{0,3},{1,0},{2,1},{3,2},{4,7},{5,4},{6,5},{7,6},{8,11},{9,8},{10,9... | collective-permute-start | bytes 1572872 | tf_op jit(solution)/shard_map/ppermute | solution.py:27
  11.8 78.4 %collective-permute-start.5 = (bf16[256,1024]{1,0:T(8,128)(2,1)}, bf16[256,1024]{1,0:T(8,128)(2,1)}, u32[]{:S(2)}, u32[]{:S(2)}) collective-permute-start(bf16[256,1024]{1,0:T(8,128)(2,1)} %get-tuple-element.28), channel_id=1, source_target_pairs={{0,1},{1,2},{2,3},{3,0},{4,5},{5,6},{6,7},{7,4},{8,9},{9,10},{10,1... | collective-permute-start | bytes 1572872 | tf_op jit(solution)/shard_map/ppermute | solution.py:27
  13.1 15.5 %copy-start.21 = (s32[24]{0:T(128)}, s32[24]{0:T(128)S(1)}, u32[]{:S(2)}) copy-start(s32[24]{0:T(128)S(1)} %get-tuple-element.52) | copy-start | bytes 292
  13.9 34.3 %all-to-all-start = ((s32[64,1,2]{2,1,0:T(1,128)}), s32[64,1,2]{2,1,0:T(1,128)S(1)}, u32[]{:S(2)}, u32[]{:S(2)}) async-start(s32[64,1,2]{2,1,0:T(1,128)} %bitcast.2), calls=%async_computation | async-start | bytes 65536 | tf_op jit(solution)/shard_map/all_to_all | solution.py:107
  28.8 4.9 %copy-start.20 = (f32[2]{0:T(128)S(1)}, f32[2]{0:T(128)}, u32[]{:S(2)}) copy-start(f32[2]{0:T(128)} %param.23) | copy-start | bytes 28
  28.9 6.2 %copy-start.15 = (f32[3,1024]{1,0:T(4,128)S(1)}, f32[3,1024]{1,0:T(4,128)}, u32[]{:S(2)}) copy-start(f32[3,1024]{1,0:T(4,128)} %param.14) | copy-start | bytes 36868
  28.9 7.3 %copy-start.8 = (bf16[256,256]{1,0:T(8,128)(2,1)S(1)}, bf16[256,256]{1,0:T(8,128)(2,1)}, u32[]{:S(2)}) copy-start(bf16[256,256]{1,0:T(8,128)(2,1)} %param.15) | copy-start | bytes 393220
  30.0 10.4 %copy-start.3 = (bf16[4,256,1024]{2,1,0:T(8,128)(2,1)}, bf16[4,256,1024]{2,1,0:T(8,128)(2,1)S(1)}, u32[]{:S(2)}) copy-start(bf16[4,256,1024]{2,1,0:T(8,128)(2,1)S(1)} %bitcast_dynamic-update-slice_fusion.7) | copy-start | bytes 6291460
  31.8 8.6 %copy-start.9 = (f32[32,3,256]{2,0,1:T(8,128)S(1)}, f32[32,3,256]{2,0,1:T(8,128)}, u32[]{:S(2)}) copy-start(f32[32,3,256]{2,0,1:T(8,128)} %param.22) | copy-start | bytes 294916
  31.8 8.6 %copy-start.11 = (f32[32,3,256]{2,0,1:T(8,128)S(1)}, f32[32,3,256]{2,0,1:T(8,128)}, u32[]{:S(2)}) copy-start(f32[32,3,256]{2,0,1:T(8,128)} %param.21) | copy-start | bytes 294916
  46.4 3.3 %copy-start.12 = (bf16[7,4,1024]{2,1,0:T(4,128)(2,1)S(1)}, bf16[7,4,1024]{2,1,0:T(4,128)(2,1)}, u32[]{:S(2)}) copy-start(bf16[7,4,1024]{2,1,0:T(4,128)(2,1)} %param.16) | copy-start | bytes 172036
  48.2 0.6 copy-start.10
  51.4 12.6 %collective-permute-start.1 = (bf16[7,8,1024]{2,1,0:T(8,128)(2,1)}, bf16[7,8,1024]{2,1,0:T(8,128)(2,1)}, u32[]{:S(2)}, u32[]{:S(2)}) collective-permute-start(bf16[7,8,1024]{2,1,0:T(8,128)(2,1)} %maximum_select_fusion.1), channel_id=1, source_target_pairs={{0,2},{1,3},{2,0},{3,1},{4,6},{5,7},{6,4},{7,5},{8,10},{9,11},{10,... | collective-permute-start | bytes 344072 | tf_op jit(solution)/shard_map/ppermute | solution.py:12
  52.7 16.7 %copy-start.25 = (pred[64]{0:T(512)(128)(4,1)S(1)}, pred[64]{0:T(512)(128)(4,1)}, u32[]{:S(2)}) copy-start(pred[64]{0:T(512)(128)(4,1)} %compare_and_fusion.2) | copy-start | bytes 196
  53.7 21.1 %all-to-all-start.2 = ((bf16[64,2,3,256]{3,1,2,0:T(2,128)(2,1)}), bf16[64,2,3,256]{3,1,2,0:T(2,128)(2,1)S(1)}, u32[]{:S(2)}, u32[]{:S(2)}) async-start(bf16[64,2,3,256]{3,1,2,0:T(2,128)(2,1)} %broadcast_select_fusion.1), calls=%async_computation.2 | async-start | bytes 393216 | tf_op jit(solution)/shard_map/all_to_all | solution.py:110
  64.0 29.3 %collective-permute-start.6 = (bf16[256,1024]{1,0:T(8,128)(2,1)}, bf16[256,1024]{1,0:T(8,128)(2,1)}, u32[]{:S(2)}, u32[]{:S(2)}) collective-permute-start(bf16[256,1024]{1,0:T(8,128)(2,1)} %get-tuple-element.29), channel_id=1, source_target_pairs={{0,2},{1,3},{2,0},{3,1},{4,6},{5,7},{6,4},{7,5},{8,10},{9,11},{10,... | collective-permute-start | bytes 1572872 | tf_op jit(solution)/shard_map/ppermute | solution.py:27
  72.0 13.0 %copy-start.23 = (pred[4,6]{1,0:T(4,128)(4,1)S(1)}, pred[4,6]{1,0:T(4,128)(4,1)}, u32[]{:S(2)}) copy-start(pred[4,6]{1,0:T(4,128)(4,1)} %compare_and_fusion.1) | copy-start | bytes 76
  74.8 42.0 %all-to-all-start.1 = ((bf16[64,16,640]{2,1,0:T(8,128)(2,1)}), bf16[64,16,640]{2,1,0:T(8,128)(2,1)}, u32[]{:S(2)}, u32[]{:S(2)}) async-start(bf16[64,16,640]{2,1,0:T(8,128)(2,1)} %broadcast_select_fusion), calls=%async_computation.1 | async-start | bytes 2621440 | tf_op jit(solution)/shard_map/all_to_all | solution.py:44
  85.0 1.0 copy-start.7
  85.0 4.2 %copy-start.4 = (bf16[4,256,1024]{2,1,0:T(8,128)(2,1)S(1)}, bf16[4,256,1024]{2,1,0:T(8,128)(2,1)}, u32[]{:S(2)}) copy-start(bf16[4,256,1024]{2,1,0:T(8,128)(2,1)} %copy-done.3) | copy-start | bytes 6291460
  86.0 14.6 %collective-permute-start.7 = (bf16[256,1024]{1,0:T(8,128)(2,1)S(1)}, bf16[256,1024]{1,0:T(8,128)(2,1)S(1)}, u32[]{:S(2)}, u32[]{:S(2)}) collective-permute-start(bf16[256,1024]{1,0:T(8,128)(2,1)S(1)} %copy-done.7), channel_id=1, source_target_pairs={{0,3},{1,0},{2,1},{3,2},{4,7},{5,4},{6,5},{7,6},{8,11},{9,8},{10,9... | collective-permute-start | bytes 1572872 | tf_op jit(solution)/shard_map/ppermute | solution.py:27
  92.2 9.3 %copy-start.14 = (f32[4,256]{1,0:T(4,128)S(1)}, f32[4,256]{1,0:T(4,128)}, u32[]{:S(2)}) copy-start(f32[4,256]{1,0:T(4,128)} %mul.170) | copy-start | bytes 12292
  101.5 2.9 %copy-start.6 = (bf16[128,8,4,256]{3,1,2,0:T(8,128)(2,1)S(1)}, bf16[128,8,4,256]{3,1,2,0:T(8,128)(2,1)}, u32[]{:S(2)}) copy-start(bf16[128,8,4,256]{3,1,2,0:T(8,128)(2,1)} %copy.92) | copy-start | bytes 6291460
  124.8 2.1 %copy-start.2 = (bf16[8,128,8,128]{3,2,1,0:T(8,128)(2,1)}, bf16[8,128,8,128]{3,2,1,0:T(8,128)(2,1)S(1)}, u32[]{:S(2)}) copy-start(bf16[8,128,8,128]{3,2,1,0:T(8,128)(2,1)S(1)} %fusion.28) | copy-start | bytes 6291460
  130.8 5.2 %copy-start.16 = (f32[1,1024]{1,0:T(1,128)S(1)}, f32[1,1024]{1,0:T(1,128)}, u32[]{:S(2)}) copy-start(f32[1,1024]{1,0:T(1,128)} %get-tuple-element.43) | copy-start | bytes 12292
  130.8 5.2 %copy-start.17 = (f32[1,1024]{1,0:T(1,128)S(1)}, f32[1,1024]{1,0:T(1,128)}, u32[]{:S(2)}) copy-start(f32[1,1024]{1,0:T(1,128)} %get-tuple-element.44) | copy-start | bytes 12292
  130.8 5.2 %copy-start.18 = (f32[1,1024]{1,0:T(1,128)S(1)}, f32[1,1024]{1,0:T(1,128)}, u32[]{:S(2)}) copy-start(f32[1,1024]{1,0:T(1,128)} %get-tuple-element.45) | copy-start | bytes 12292
  130.8 5.2 %copy-start.19 = (s32[1024]{0:T(1024)S(1)}, s32[1024]{0:T(1024)}, u32[]{:S(2)}) copy-start(s32[1024]{0:T(1024)} %add_select_fusion.1) | copy-start | bytes 12292
  144.4 0.7 copy-start.22
  144.4 0.7 copy-start.24
  146.6 20.3 %all-to-all-start.3 = ((f32[64,2,3,256]{3,1,2,0:T(2,128)}), f32[64,2,3,256]{3,1,2,0:T(2,128)S(1)}, u32[]{:S(2)}, u32[]{:S(2)}) async-start(f32[64,2,3,256]{3,1,2,0:T(2,128)} %copy.83), calls=%async_computation.3 | async-start | bytes 786432 | tf_op jit(solution)/shard_map/all_to_all | solution.py:145
  170.0 6.5 %collective-permute-start.10 = (f32[32,3,256]{2,0,1:T(8,128)}, f32[32,3,256]{2,0,1:T(8,128)S(1)}, u32[]{:S(2)}, u32[]{:S(2)}) collective-permute-start(f32[32,3,256]{2,0,1:T(8,128)} %fusion.38), channel_id=1, source_target_pairs={{0,1},{1,2},{2,3},{3,0},{4,5},{5,6},{6,7},{7,4},{8,9},{9,10},{10,1... | collective-permute-start | bytes 294920 | tf_op jit(solution)/shard_map/ppermute | solution.py:59
  171.7 5.0 %collective-permute-start.8 = (f32[32,3,256]{2,0,1:T(8,128)}, f32[32,3,256]{2,0,1:T(8,128)S(1)}, u32[]{:S(2)}, u32[]{:S(2)}) collective-permute-start(f32[32,3,256]{2,0,1:T(8,128)} %fusion.38), channel_id=1, source_target_pairs={{0,3},{1,0},{2,1},{3,2},{4,7},{5,4},{6,5},{7,6},{8,11},{9,8},{10,9... | collective-permute-start | bytes 294920 | tf_op jit(solution)/shard_map/ppermute | solution.py:59
  173.2 6.5 %collective-permute-start.9 = (f32[32,3,256]{2,0,1:T(8,128)}, f32[32,3,256]{2,0,1:T(8,128)S(1)}, u32[]{:S(2)}, u32[]{:S(2)}) collective-permute-start(f32[32,3,256]{2,0,1:T(8,128)} %fusion.38), channel_id=1, source_target_pairs={{0,2},{1,3},{2,0},{3,1},{4,6},{5,7},{6,4},{7,5},{8,10},{9,11},{10,... | collective-permute-start | bytes 294920 | tf_op jit(solution)/shard_map/ppermute | solution.py:59
